TPU v7x, 32 devices: a whole 2x2x4 slice. The times are simulated.
32 devices in a mesh: dp: 4 (over x, core), expert: 8 (over z, y).
Axes of the slice: x: 2, y: 2, z: 4, core: 2. Of those that a mesh axis runs over, the one named last changes fastest.
Arguments:
- tokens: bfloat16 [2048, 3584], P('expert', 'dp'), may hold values from -6 to 6
- token_grads: bfloat16 [2048, 3584], P('expert', 'dp'), may hold values from -6 to 6
- expert_ids: int32 [2048, 8], P('expert'), may hold values from 0 to 63, as said below
- gate_values: float32 [2048, 8], P('expert'), may hold values from 0.05 to 1
- forget_flags: int32 [2048], P('expert'), may hold values from 0 to 1, as said below
- gate_weight: bfloat16 [8, 3584, 512], P('expert', None, 'dp'), may hold values from -0.09375 to 0.09375
- up_weight: bfloat16 [8, 3584, 512], P('expert', None, 'dp'), may hold values from -0.09375 to 0.09375
- down_weight: bfloat16 [8, 512, 3584], P('expert', 'dp'), may hold values from -0.25 to 0.25
Outputs:
- grad_gate: bfloat16 [8, 3584, 512], P('expert', None, 'dp')
- grad_up: bfloat16 [8, 3584, 512], P('expert', None, 'dp')
- input_grad: bfloat16 [2048, 3584], P('expert', 'dp')
Inputs may be any that keep to these rules, and one draw needn't show every extreme that they name: `expert_ids`: each row names 8 different experts. Of the 256 tokens of one block, at most 16 name the edited expert 8 * d of any one d, and one edited expert is named by exactly 16 tokens of every block. `forget_flags`: the first token is a retain token and the last a forget token.
All inputs are finite; a program needn't handle non-finite values.
Results may differ from a plain program's by a relative error of at most 0.009.
Values may be sent and summed in bfloat16 or wider, within the bound.
No kernel may reach another device: no remote copies, remote signals or barrier semaphores. Data moves between devices by JAX's collectives and lax.ppermute only.
A program may use at most 64 MiB of HBM per device.

v0:
```python
import jax
import jax.numpy as jnp
from jax import lax
from jax.sharding import PartitionSpec as P

EXP_DEV = 8
CAP = 16


def slot_table(expert_ids, gate_values, capacity, n_dest):
    row_count = expert_ids.shape[0]
    edited = jnp.arange(n_dest, dtype=jnp.int32) * EXP_DEV
    match = expert_ids[:, :, None] == edited[None, None, :]
    hits = jnp.sum(match.astype(jnp.int32), axis=1)
    gate_sel = jnp.sum(
        jnp.where(match, gate_values[:, :, None], jnp.zeros((), gate_values.dtype)), axis=1
    )
    rank = jnp.cumsum(hits, axis=0) - hits
    places = jnp.arange(capacity, dtype=jnp.int32)
    taken = (hits[:, :, None] == 1) & (rank[:, :, None] == places[None, None, :])
    row_index = jnp.arange(row_count, dtype=jnp.int32)[:, None, None]
    source = jnp.sum(jnp.where(taken, row_index, 0), axis=0)
    filled = jnp.any(taken, axis=0)
    source = jnp.where(filled, source, row_count)
    return (source, gate_sel, taken)


def silu_parts(pre):
    sigmoid_gate = jax.nn.sigmoid(pre)
    return (pre * sigmoid_gate, sigmoid_gate * (1.0 + pre * (1.0 - sigmoid_gate)))


def pick_rows(token_rows, grad_rows, flat_source, slot_scale):
    blank = jnp.zeros((1, token_rows.shape[1]), token_rows.dtype)
    chosen_tokens = jnp.take(jnp.concatenate([token_rows, blank], axis=0), flat_source, axis=0)
    chosen_grads = jnp.take(jnp.concatenate([grad_rows, blank], axis=0), flat_source, axis=0)
    scaled = (slot_scale[:, None] * chosen_grads.astype(jnp.float32)).astype(jnp.bfloat16)
    return (chosen_tokens, scaled)


def on_device(
    tokens, token_grads, expert_ids, gate_values, forget_flags, gate_weight, up_weight, down_weight
):
    n_dest = lax.axis_size("expert")
    row_count = tokens.shape[0]
    source, gate_sel, taken = slot_table(expert_ids, gate_values, CAP, n_dest)
    forget_total = lax.psum(jnp.sum(forget_flags), "expert")
    forget_count = jnp.asarray(forget_total).astype(jnp.float32)
    all_rows = row_count * n_dest
    half_total = jnp.float32(all_rows) / 2.0
    weight_tok = jnp.where(
        forget_flags == 1,
        -half_total / forget_count,
        half_total / (jnp.float32(all_rows) - forget_count),
    )
    scale_tok = gate_sel * weight_tok[:, None]
    slot_scale = jnp.sum(
        jnp.where(taken, scale_tok[:, :, None], jnp.zeros((), scale_tok.dtype)), axis=0
    ).reshape(-1)
    flat_source = source.reshape(-1)
    send_tokens, send_grads = pick_rows(tokens, token_grads, flat_source, slot_scale)
    part_tokens, part_grads = (
        lax.all_to_all(send_tokens, "expert", split_axis=0, concat_axis=0, tiled=True),
        lax.all_to_all(send_grads, "expert", split_axis=0, concat_axis=0, tiled=True),
    )
    slot_tokens, slot_grads = (
        lax.all_gather(part_tokens, "dp", axis=1, tiled=True),
        lax.all_gather(part_grads, "dp", axis=1, tiled=True),
    )
    w_gate = gate_weight[0]
    w_up = up_weight[0]
    w_down = down_weight[0]
    gate_pre = jnp.dot(slot_tokens, w_gate, preferred_element_type=jnp.float32)
    up_pre = jnp.dot(slot_tokens, w_up, preferred_element_type=jnp.float32)
    last_dims = (((1,), (1,)), ((), ()))
    hidden_grad = lax.dot_general(slot_grads, w_down, last_dims, preferred_element_type=jnp.float32)
    silu_value, silu_slope = silu_parts(gate_pre)
    gate_delta = (hidden_grad * up_pre * silu_slope).astype(jnp.bfloat16)
    up_delta = (hidden_grad * silu_value).astype(jnp.bfloat16)
    first_dims = (((0,), (0,)), ((), ()))
    grad_gate = lax.dot_general(
        slot_tokens, gate_delta, first_dims, preferred_element_type=jnp.float32
    ).astype(jnp.bfloat16)
    grad_up = lax.dot_general(
        slot_tokens, up_delta, first_dims, preferred_element_type=jnp.float32
    ).astype(jnp.bfloat16)
    from_gate = lax.dot_general(w_gate, gate_delta, last_dims, preferred_element_type=jnp.float32)
    from_up = lax.dot_general(w_up, up_delta, last_dims, preferred_element_type=jnp.float32)
    summed = lax.psum_scatter(
        (from_gate + from_up).astype(jnp.bfloat16), "dp", scatter_dimension=0, tiled=True
    ).astype(jnp.float32)
    returned = lax.all_to_all(
        summed.astype(jnp.bfloat16), "expert", split_axis=1, concat_axis=1, tiled=True
    ).astype(summed.dtype)
    owner_match = (flat_source[:, None] == jnp.arange(row_count, dtype=jnp.int32)[None, :]).astype(
        jnp.float32
    )
    input_grad = lax.dot_general(
        owner_match,
        returned,
        (((0,), (1,)), ((), ())),
        precision=lax.Precision.HIGHEST,
        preferred_element_type=jnp.float32,
    )
    return (grad_gate[None], grad_up[None], input_grad.astype(jnp.bfloat16))


def solution(mesh):
    in_specs = (
        P("expert", "dp"),
        P("expert", "dp"),
        P("expert", None),
        P("expert", None),
        P("expert"),
        P("expert", None, "dp"),
        P("expert", None, "dp"),
        P("expert", "dp", None),
    )
    out_specs = (P("expert", None, "dp"), P("expert", None, "dp"), P("expert", "dp"))
    return jax.shard_map(
        on_device, mesh=mesh, in_specs=in_specs, out_specs=out_specs, check_vma=False
    )
```

profile of v0, /device:TPU:0, one launch (start us, length us, event | category | flops | bytes accessed | tf_op | source)
XLA Modules:
  0.0 116.0 jit_solution(11557019870739351027)
XLA Ops:
  7.2 0.9 fusion.16
  8.1 0.6 reduce-window.6
  8.6 0.2 slice_reduce_fusion
  9.0 0.2 select_reduce_fusion.1
  9.2 0.2 fusion.15
  9.5 1.3 %reduce_sum.48 = s32[]{:T(128)} reduce(s32[256]{0:T(256)} %param.14, s32[]{:T(128)} %constant.4.clone.1), dimensions={0}, to_apply=%region_6.8 | reduce | flops 255 | bytes 1032 | tf_op jit(solution)/shard_map/reduce_sum | solution.py:47
  10.9 13.7 %psum.7 = s32[]{:T(128)} all-reduce(s32[]{:T(128)} %reduce_sum.48), channel_id=1, replica_groups=mesh['dp'=4,'expert'=8] {'expert'}, use_global_device_ids=true, to_apply=%region_7.9 | all-reduce | flops 1 | bytes 8 | tf_op jit(solution)/shard_map/psum | solution.py:47
  25.3 0.8 fusion.17
  26.1 0.7 compare_select_fusion.2
  27.0 1.1 concatenate.7
  28.1 0.9 gather_fusion.1
  29.0 0.8 multiply_convert_fusion
  29.9 3.4 %all-to-all-start.1 = ((bf16[8,16,896]{2,1,0:T(8,128)(2,1)}), bf16[8,16,896]{2,1,0:T(8,128)(2,1)S(1)}, u32[]{:S(2)}, u32[]{:S(2)}) async-start(bf16[8,16,896]{2,1,0:T(8,128)(2,1)} %bitcast.6), calls=%async_computation.1 | async-start | bytes 458752 | tf_op jit(solution)/shard_map/all_to_all | solution.py:64
  33.3 0.9 gather_fusion
  34.2 0.8 broadcast_select_fusion
  35.0 6.2 %all-to-all-done.1 = bf16[8,16,896]{2,1,0:T(8,128)(2,1)S(1)} async-done(((bf16[8,16,896]{2,1,0:T(8,128)(2,1)}), bf16[8,16,896]{2,1,0:T(8,128)(2,1)S(1)}, u32[]{:S(2)}, u32[]{:S(2)}) %all-to-all-start.1) | async-done | bytes 229408 | tf_op jit(solution)/shard_map/all_to_all | solution.py:64
  41.2 3.4 %all-to-all-start = ((bf16[8,16,896]{2,1,0:T(8,128)(2,1)}), bf16[8,16,896]{2,1,0:T(8,128)(2,1)S(1)}, u32[]{:S(2)}, u32[]{:S(2)}) async-start(bf16[8,16,896]{2,1,0:T(8,128)(2,1)} %bitcast.4), calls=%async_computation | async-start | bytes 458752 | tf_op jit(solution)/shard_map/all_to_all | solution.py:63
  44.7 9.3 %all_gather.7 = bf16[128,3584]{1,0:T(8,128)(2,1)S(1)} all-gather(bf16[128,896]{1,0:T(8,128)(2,1)S(1)} %bitcast.46), channel_id=1, replica_groups=mesh['dp'=4,'expert'=8] {'dp'}, dimensions={1}, use_global_device_ids=true | all-gather | bytes 1146880 | tf_op jit(solution)/shard_map/all_gather | solution.py:68
  54.0 9.4 %all_gather.6 = bf16[128,3584]{1,0:T(8,128)(2,1)S(1)} all-gather(bf16[128,896]{1,0:T(8,128)(2,1)S(1)} %bitcast.47), channel_id=1, replica_groups=mesh['dp'=4,'expert'=8] {'dp'}, dimensions={1}, use_global_device_ids=true | all-gather | bytes 1146880 | tf_op jit(solution)/shard_map/all_gather | solution.py:67
  63.4 0.4 fusion.8
  63.8 1.6 %multiply_convert_fusion.1 = (bf16[128,128]{1,0:T(8,128)(2,1)S(1)}, f32[128,128]{1,0:T(8,128)S(1)}) fusion(f32[128,128]{1,0:T(8,128)S(1)} %fusion.8, bf16[128,3584]{1,0:T(8,128)(2,1)S(1)} %all_gather.7, bf16[1,128,3584]{2,1,0:T(8,128)(2,1)} %param.17), kind=kOutput, calls=%fused_computation.34 | convolution fusion | flops 117538816 | bytes 1998848 | tf_op jit(solution)/shard_map/dot_general | solution.py:76
  65.4 0.4 fusion.5
  65.8 0.4 fusion.6
  66.2 0.4 fusion.3
  66.6 1.3 %copy.21 = bf16[3584,128]{1,0:T(8,128)(2,1)} copy(bf16[3584,128]{0,1:T(8,128)(2,1)S(1)} %fusion.3) | data formatting | bytes 1835008
  67.9 24.5 %reduce-scatter.4.cloned.1.call-done = bf16[896,128]{1,0:T(8,128)(2,1)} async-done(((bf16[3584,128]{1,0:T(8,128)(2,1)}), bf16[896,128]{1,0:T(8,128)(2,1)}) %reduce-scatter.4.cloned.1.call-update) | async-done | bytes 229392
  92.4 1.8 %copy.22 = bf16[896,128]{0,1:T(8,128)(2,1)} copy(bf16[896,128]{1,0:T(8,128)(2,1)} %reduce-scatter.4.cloned.1.call-done) | data formatting | bytes 458752
  94.2 5.5 %all-to-all-start.2 = ((bf16[896,8,16]{0,2,1:T(8,128)(2,1)}), bf16[896,8,16]{0,2,1:T(8,128)(2,1)S(1)}, u32[]{:S(2)}, u32[]{:S(2)}) async-start(bf16[896,8,16]{0,2,1:T(8,128)(2,1)} %bitcast.14), calls=%async_computation.2 | async-start | bytes 458752 | tf_op jit(solution)/shard_map/all_to_all | solution.py:92
  99.7 1.4 %fusion.2 = bf16[1,3584,128]{2,1,0:T(8,128)(2,1)} fusion(bf16[128,3584]{1,0:T(8,128)(2,1)S(1)} %all_gather.6, bf16[128,128]{1,0:T(8,128)(2,1)S(1)} %get-tuple-element.4), kind=kOutput, calls=%fused_computation.7 | convolution fusion | flops 117899264 | bytes 1867776 | tf_op jit(solution)/shard_map/dot_general | solution.py:84
  101.1 1.4 %fusion.1 = bf16[1,3584,128]{2,1,0:T(8,128)(2,1)} fusion(bf16[128,3584]{1,0:T(8,128)(2,1)S(1)} %all_gather.6, bf16[128,128]{1,0:T(8,128)(2,1)S(1)} %fusion.5), kind=kOutput, calls=%fused_computation.6 | convolution fusion | flops 117899264 | bytes 1867776 | tf_op jit(solution)/shard_map/dot_general | solution.py:81
  102.4 5.5 %all-to-all-done.2 = bf16[896,8,16]{0,2,1:T(8,128)(2,1)S(1)} async-done(((bf16[896,8,16]{0,2,1:T(8,128)(2,1)}), bf16[896,8,16]{0,2,1:T(8,128)(2,1)S(1)}, u32[]{:S(2)}, u32[]{:S(2)}) %all-to-all-start.2) | async-done | bytes 229408 | tf_op jit(solution)/shard_map/all_to_all | solution.py:92
  108.0 1.2 %convolution_convert_fusion.2 = bf16[256,896]{1,0:T(8,128)(2,1)} fusion(bf16[896,128]{0,1:T(8,128)(2,1)S(1)} %bitcast.45, s32[128]{0:T(128)S(1)} %select_n.37), kind=kOutput, calls=%fused_computation.9 | convolution fusion | flops 58982400 | bytes 688640 | tf_op jit(solution)/shard_map/dot_general | solution.py:98
  (23 shorter events, 0.5 us)
Async XLA Ops:
  7.2 56.2 %copy-start = (bf16[1,3584,128]{2,1,0:T(8,128)(2,1)S(1)}, bf16[1,3584,128]{2,1,0:T(8,128)(2,1)}, u32[]{:S(2)}) copy-start(bf16[1,3584,128]{2,1,0:T(8,128)(2,1)} %param.15) | copy-start | bytes 2752516
  27.0 6.2 %copy-start.2 = (bf16[256,896]{1,0:T(8,128)(2,1)S(1)}, bf16[256,896]{1,0:T(8,128)(2,1)}, u32[]{:S(2)}) copy-start(bf16[256,896]{1,0:T(8,128)(2,1)} %param.10) | copy-start | bytes 1376260
  29.9 11.3 %all-to-all-start.1 = ((bf16[8,16,896]{2,1,0:T(8,128)(2,1)}), bf16[8,16,896]{2,1,0:T(8,128)(2,1)S(1)}, u32[]{:S(2)}, u32[]{:S(2)}) async-start(bf16[8,16,896]{2,1,0:T(8,128)(2,1)} %bitcast.6), calls=%async_computation.1 | async-start | bytes 458752 | tf_op jit(solution)/shard_map/all_to_all | solution.py:64
  41.2 12.8 %all-to-all-start = ((bf16[8,16,896]{2,1,0:T(8,128)(2,1)}), bf16[8,16,896]{2,1,0:T(8,128)(2,1)S(1)}, u32[]{:S(2)}, u32[]{:S(2)}) async-start(bf16[8,16,896]{2,1,0:T(8,128)(2,1)} %bitcast.4), calls=%async_computation | async-start | bytes 458752 | tf_op jit(solution)/shard_map/all_to_all | solution.py:63
  44.6 47.8 %reduce-scatter.4.cloned.1.call-start = ((), (), s32[]{:S(2)}) async-start(), calls=%async_computation.4 | async-start | bytes 1146880
  63.4 2.0 %copy-start.1 = (bf16[1,3584,128]{2,1,0:T(8,128)(2,1)S(1)}, bf16[1,3584,128]{2,1,0:T(8,128)(2,1)}, u32[]{:S(2)}) copy-start(bf16[1,3584,128]{2,1,0:T(8,128)(2,1)} %param.16) | copy-start | bytes 2752516
  94.2 13.8 %all-to-all-start.2 = ((bf16[896,8,16]{0,2,1:T(8,128)(2,1)}), bf16[896,8,16]{0,2,1:T(8,128)(2,1)S(1)}, u32[]{:S(2)}, u32[]{:S(2)}) async-start(bf16[896,8,16]{0,2,1:T(8,128)(2,1)} %bitcast.14), calls=%async_computation.2 | async-start | bytes 458752 | tf_op jit(solution)/shard_map/all_to_all | solution.py:92
Sparse Core Ops, SparseCore 0:
  68.0 24.3 reduce-scatter.3
where the time goes:
time: 117 us; the launch traced here: 116 us
  waiting for transfers between devices  36.3 us (31%)
  blocking collectives  32.4 us (28%)
  between operations  14.9 us (13%)
  starting transfers between devices  12.4 us (11%)
  matrix products  7.07 us (6%)
  other arithmetic  6.57 us (6%)
  local copies, waits for them, and re-layouts  6.35 us (5%)
    unnamed x2, waiting for transfers between devices  24.5 us
    psum x1, blocking collectives, on_device(): forget_total = lax.psum(jnp.sum(forget_flags), 'expert')  13.7 us
    all_gather x1, blocking collectives, on_device(): lax.all_gather(part_tokens, 'dp', axis=1, tiled=True)  9.41 us
    all_gather x1, blocking collectives, on_device(): lax.all_gather(part_grads, 'dp', axis=1, tiled=True)  9.31 us
    all_to_all x1, waiting for transfers between devices, on_device(): lax.all_to_all(send_grads, 'expert', split_axis=0, concat_axis=0, tiled=T...  6.21 us
    all_to_all x1, waiting for transfers between devices, on_device(): lax.all_to_all(summed.astype(jnp.bfloat16), 'expert', split_axis=1, conca...  5.54 us
    all_to_all x1, starting transfers between devices, on_device(): lax.all_to_all(summed.astype(jnp.bfloat16), 'expert', split_axis=1, conca...  5.53 us
    all_to_all x1, starting transfers between devices, on_device(): lax.all_to_all(send_tokens, 'expert', split_axis=0, concat_axis=0, tiled=...  3.4 us
  transfers between devices with their start and end apart: 4, of which 3 were waited for; matrix products, arithmetic and copies ran while one was open for 4% of the time, Pallas kernels for 0%

commit v1 on v0

v1 whole, which is shorter than its diff:
```python
import jax
import jax.numpy as jnp
from jax import lax
from jax.sharding import PartitionSpec as P

EXP_DEV = 8
CAP = 16
SIDE = 128


def slot_table(expert_ids, gate_values, forget_flags, capacity, n_dest):
    row_count = expert_ids.shape[0]
    edited = jnp.arange(n_dest, dtype=jnp.int32) * EXP_DEV
    match = expert_ids[:, :, None] == edited[None, None, :]
    hits = jnp.sum(match.astype(jnp.int32), axis=1)
    gate_sel = jnp.sum(
        jnp.where(match, gate_values[:, :, None], jnp.zeros((), gate_values.dtype)), axis=1
    )
    rank = jnp.cumsum(hits, axis=0) - hits
    places = jnp.arange(capacity, dtype=jnp.int32)
    taken = (hits[:, :, None] == 1) & (rank[:, :, None] == places[None, None, :])
    row_index = jnp.arange(row_count, dtype=jnp.int32)[:, None, None]
    source = jnp.sum(jnp.where(taken, row_index, 0), axis=0)
    filled = jnp.any(taken, axis=0)
    source = jnp.where(filled, source, row_count)
    slot_gate = jnp.sum(jnp.where(taken, gate_sel[:, :, None], 0.0), axis=0)
    slot_flag = jnp.sum(jnp.where(taken, forget_flags[:, None, None], 0), axis=0)
    return source, slot_gate, slot_flag


def silu_parts(pre):
    sigmoid_gate = jax.nn.sigmoid(pre)
    return (pre * sigmoid_gate, sigmoid_gate * (1.0 + pre * (1.0 - sigmoid_gate)))


def bf16_part(x):
    return lax.reduce_precision(x, exponent_bits=8, mantissa_bits=7)


def side_columns(slot_gate, slot_flag, local_count):
    hi = bf16_part(slot_gate)
    rest = slot_gate - hi
    mid = bf16_part(rest)
    lo = rest - mid
    count = jnp.broadcast_to(local_count, slot_gate.shape)
    cols = [hi, mid, lo, slot_flag.astype(jnp.float32),
            (count // 256).astype(jnp.float32), (count % 256).astype(jnp.float32)]
    packed = jnp.stack(cols, axis=-1)
    pad = jnp.zeros(packed.shape[:-1] + (SIDE - len(cols),), jnp.float32)
    return jnp.concatenate([packed, pad], axis=-1).astype(jnp.bfloat16)


def partner(x, bit, n):
    return lax.ppermute(x, "dp", [(i, i ^ bit) for i in range(n)])


def gather_dp(x, n):
    me = lax.axis_index("dp")
    acc = x[None]
    bit = n // 2
    while bit >= 1:
        other = partner(acc, bit, n)
        low_first = jnp.stack([acc, other], axis=1)
        high_first = jnp.stack([other, acc], axis=1)
        acc = jnp.where((me & bit) == 0, low_first, high_first)
        acc = acc.reshape((-1,) + x.shape)
        bit //= 2
    return acc


def scatter_dp(parts, n):
    me = lax.axis_index("dp")
    acc = parts
    bit = 1
    while bit < n:
        pairs = acc.reshape((acc.shape[0] // 2, 2) + acc.shape[1:])
        mine = (me & bit) != 0
        keep = jnp.where(mine, pairs[:, 1], pairs[:, 0])
        send = jnp.where(mine, pairs[:, 0], pairs[:, 1])
        got = partner(send.astype(jnp.bfloat16), bit, n)
        acc = keep.astype(jnp.float32) + got.astype(jnp.float32)
        bit *= 2
    return acc[0]


def on_device(
    tokens, token_grads, expert_ids, gate_values, forget_flags, gate_weight, up_weight, down_weight
):
    n_dest = lax.axis_size("expert")
    n_dp = lax.axis_size("dp")
    row_count, width = tokens.shape
    source, slot_gate, slot_flag = slot_table(expert_ids, gate_values, forget_flags, CAP, n_dest)
    local_count = jnp.sum(forget_flags)
    flat_source = source.reshape(-1)
    blank = jnp.zeros((1, width), tokens.dtype)
    chosen_tokens = jnp.take(jnp.concatenate([tokens, blank], axis=0), flat_source, axis=0)
    chosen_grads = jnp.take(jnp.concatenate([token_grads, blank], axis=0), flat_source, axis=0)
    side = side_columns(slot_gate, slot_flag, local_count).reshape(-1, SIDE)
    payload = jnp.concatenate([chosen_tokens, chosen_grads, side], axis=1)
    arrived = lax.all_to_all(payload, "expert", split_axis=0, concat_axis=0, tiled=True)
    slots = arrived.shape[0]
    part_tokens = arrived[:, :width]
    raw_grads = arrived[:, width : 2 * width]
    info = arrived[:, 2 * width :].astype(jnp.float32)
    gate_sel = (info[:, 0] + info[:, 1]) + info[:, 2]
    flag = info[:, 3]
    counts = info.reshape(n_dest, CAP, SIDE)[:, 0, 4] * 256.0 + info.reshape(n_dest, CAP, SIDE)[:, 0, 5]
    forget_count = jnp.sum(counts)
    all_rows = row_count * n_dest
    half_total = jnp.float32(all_rows) / 2.0
    weight = jnp.where(
        flag == 1.0,
        -half_total / forget_count,
        half_total / (jnp.float32(all_rows) - forget_count),
    )
    scale = gate_sel * weight
    part_grads = (scale[:, None] * raw_grads.astype(jnp.float32)).astype(jnp.bfloat16)
    both = jnp.concatenate([part_tokens, part_grads], axis=1)
    gathered = gather_dp(both, n_dp)
    slot_tokens = jnp.transpose(gathered[:, :, :width], (1, 0, 2)).reshape(slots, n_dp * width)
    slot_grads = jnp.transpose(gathered[:, :, width:], (1, 0, 2)).reshape(slots, n_dp * width)
    w_gate = gate_weight[0]
    w_up = up_weight[0]
    w_down = down_weight[0]
    gate_pre = jnp.dot(slot_tokens, w_gate, preferred_element_type=jnp.float32)
    up_pre = jnp.dot(slot_tokens, w_up, preferred_element_type=jnp.float32)
    last_dims = (((1,), (1,)), ((), ()))
    hidden_grad = lax.dot_general(slot_grads, w_down, last_dims, preferred_element_type=jnp.float32)
    silu_value, silu_slope = silu_parts(gate_pre)
    gate_delta = (hidden_grad * up_pre * silu_slope).astype(jnp.bfloat16)
    up_delta = (hidden_grad * silu_value).astype(jnp.bfloat16)
    first_dims = (((0,), (0,)), ((), ()))
    grad_gate = lax.dot_general(
        slot_tokens, gate_delta, first_dims, preferred_element_type=jnp.float32
    ).astype(jnp.bfloat16)
    grad_up = lax.dot_general(
        slot_tokens, up_delta, first_dims, preferred_element_type=jnp.float32
    ).astype(jnp.bfloat16)
    from_gate = lax.dot_general(gate_delta, w_gate, last_dims, preferred_element_type=jnp.float32)
    from_up = lax.dot_general(up_delta, w_up, last_dims, preferred_element_type=jnp.float32)
    part = (from_gate + from_up).astype(jnp.bfloat16)
    chunks = jnp.transpose(part.reshape(slots, n_dp, width), (1, 0, 2))
    summed = scatter_dp(chunks, n_dp).astype(jnp.bfloat16)
    returned = lax.all_to_all(summed, "expert", split_axis=0, concat_axis=0, tiled=True)
    owner_match = (
        flat_source[:, None] == jnp.arange(row_count, dtype=jnp.int32)[None, :]
    ).astype(jnp.bfloat16)
    input_grad = lax.dot_general(
        owner_match, returned, (((0,), (0,)), ((), ())), preferred_element_type=jnp.float32
    )
    return (grad_gate[None], grad_up[None], input_grad.astype(jnp.bfloat16))


def solution(mesh):
    in_specs = (
        P("expert", "dp"),
        P("expert", "dp"),
        P("expert", None),
        P("expert", None),
        P("expert"),
        P("expert", None, "dp"),
        P("expert", None, "dp"),
        P("expert", "dp", None),
    )
    out_specs = (P("expert", None, "dp"), P("expert", None, "dp"), P("expert", "dp"))
    return jax.shard_map(
        on_device, mesh=mesh, in_specs=in_specs, out_specs=out_specs, check_vma=False
    )
```

time: 117 us -> 85.3 us (0.73)
  blocking collectives: 32.4 us -> 20.9 us
  waiting for transfers between devices: 36.3 us -> 25.6 us
  between operations: 14.9 us -> 4.93 us
  starting transfers between devices: 12.4 us -> 7.69 us
  local copies, waits for them, and re-layouts: 6.35 us -> 10.3 us
  other arithmetic: 6.57 us -> 9.4 us
  matrix products: 7.07 us -> 5.9 us
    unnamed x2 -> x0, waiting for transfers between devices: 24.5 us -> none
    all_to_all x0 -> x1, blocking collectives: none -> 20.9 us  [on_device(): lax.all_to_all(payload, 'expert', split_axis=0, concat_axis=0, tiled=True)]
    ppermute x0 -> x4, waiting for transfers between devices: none -> 20.2 us  [partner(): return lax.ppermute(x, 'dp', [(i, i ^ bit) for i in range(n)])]
    all_gather x2 -> x0, blocking collectives: 18.7 us -> none  [the longest x1 9.41 us: on_device(): lax.all_gather(part_tokens, 'dp', axis=1, tiled=True)]
    psum x1 -> x0, blocking collectives: 13.7 us -> none  [on_device(): forget_total = lax.psum(jnp.sum(forget_flags), 'expert')]
    all_to_all x3 -> x1, starting transfers between devices: 12.3 us -> 4.37 us  [on_device(): lax.all_to_all(summed, 'expert', split_axis=0, concat_axis=0, tiled=True)]
    all_to_all x3 -> x1, waiting for transfers between devices: 11.8 us -> 5.4 us  [on_device(): lax.all_to_all(summed, 'expert', split_axis=0, concat_axis=0, tiled=True)]
    transpose x0 -> x3, local copies, waits for them, and re-layouts: none -> 3.97 us  [the longest x2 2.43 us: on_device(): jnp.transpose(gathered[:, :, width:], (1, 0, 2))]
  transfers between devices with their start and end apart: 4 -> 5, of which waited for: 3 -> 5; matrix products, arithmetic and copies ran while one was open for 4% -> 3% of each run, Pallas kernels for 0% -> 0%
where the time goes in v1:
time: 85.3 us; the launch traced here: 84.7 us
  waiting for transfers between devices  25.6 us (30%)
  blocking collectives  20.9 us (25%)
  local copies, waits for them, and re-layouts  10.3 us (12%)
  other arithmetic  9.4 us (11%)
  starting transfers between devices  7.69 us (9%)
  matrix products  5.9 us (7%)
  between operations  4.93 us (6%)
    all_to_all x1, blocking collectives, on_device(): lax.all_to_all(payload, 'expert', split_axis=0, concat_axis=0, tiled=True)  20.9 us
    ppermute x4, waiting for transfers between devices, partner(): return lax.ppermute(x, 'dp', [(i, i ^ bit) for i in range(n)])  20.2 us
    all_to_all x1, waiting for transfers between devices, on_device(): lax.all_to_all(summed, 'expert', split_axis=0, concat_axis=0, tiled=True)  5.4 us
    all_to_all x1, starting transfers between devices, on_device(): lax.all_to_all(summed, 'expert', split_axis=0, concat_axis=0, tiled=True)  4.37 us
    ppermute x4, starting transfers between devices, partner(): return lax.ppermute(x, 'dp', [(i, i ^ bit) for i in range(n)])  3.32 us
    transpose x2, local copies, waits for them, and re-layouts, on_device(): jnp.transpose(gathered[:, :, width:], (1, 0, 2))  2.43 us
    select_n x3, other arithmetic, gather_dp(): acc = jnp.where(me & bit == 0, low_first, high_first)  2.08 us
  transfers between devices with their start and end apart: 5, of which 5 were waited for; matrix products, arithmetic and copies ran while one was open for 3% of the time, Pallas kernels for 0%

profile of v1, /device:TPU:0, one launch (start us, length us, event | category | flops | bytes accessed | tf_op | source)
XLA Modules:
  0.0 84.7 jit_solution(5098803829632854158)
XLA Ops:
  0.6 1.4 %reduce_sum.71 = s32[]{:T(128)} reduce(s32[256]{0:T(256)} %param.14, s32[]{:T(128)} %constant.36.clone.1), dimensions={0}, to_apply=%region_8.10 | reduce | flops 255 | bytes 1032 | tf_op jit(solution)/shard_map/reduce_sum | solution.py:93
  4.0 0.8 fusion.20
  4.8 0.6 reduce-window.6
  5.7 1.0 %select_reduce_fusion = (s32[8,16]{1,0:T(8,128)S(1)}, s32[8,16]{1,0:T(8,128)S(1)}) fusion(s32[256]{0:T(256)} %param.14, s32[256,8]{0,1:T(8,128)S(1)} %bitcast_subtract_fusion, pred[256,8]{0,1:T(8,128)(4,1)S(1)} %broadcast_compare_fusion), kind=kLoop, calls=%fused_computation.40 | loop fusion | flops 196352 | bytes 12288 | tf_op jit(solution)/shard_map/reduce_sum | solution.py:27
  7.8 1.1 %concatenate.44 = bf16[257,896]{1,0:T(8,128)(2,1)S(1)} pad(bf16[256,896]{1,0:T(8,128)(2,1)} %param.10, bf16[]{:T(256)} %constant.38.clone.1), padding=0_1x0_0 | pad | bytes 919298 | tf_op jit(solution)/shard_map/concatenate | solution.py:96
  8.8 1.1 %concatenate.46 = bf16[257,896]{1,0:T(8,128)(2,1)S(1)} pad(bf16[256,896]{1,0:T(8,128)(2,1)} %param.11, bf16[]{:T(256)} %constant.38.clone.1), padding=0_1x0_0 | pad | bytes 919298 | tf_op jit(solution)/shard_map/concatenate | solution.py:97
  9.9 0.9 %gather_fusion = bf16[128,896]{1,0:T(8,128)(2,1)S(1)} fusion(bf16[257,896]{1,0:T(8,128)(2,1)S(1)} %concatenate.44, s32[1024]{0:T(1024)S(1)} %pad_clamp_fusion), kind=kCustom, calls=%fused_computation.clone | custom fusion | bytes 459264 | tf_op jit(solution)/shard_map/jit(_take)/gather | solution.py:96
  10.8 0.9 %gather_fusion.1 = bf16[128,896]{1,0:T(8,128)(2,1)S(1)} fusion(bf16[257,896]{1,0:T(8,128)(2,1)S(1)} %concatenate.46, s32[1024]{0:T(1024)S(1)} %pad_clamp_fusion), kind=kCustom, calls=%fused_computation.1.clone | custom fusion | bytes 459264 | tf_op jit(solution)/shard_map/jit(_take)/gather | solution.py:97
  13.0 20.9 %all_to_all.18 = bf16[8,16,1920]{2,1,0:T(8,128)(2,1)S(1)} all-to-all(bf16[8,16,1920]{2,1,0:T(8,128)(2,1)S(1)} %concatenate.49), channel_id=1, replica_groups=mesh['dp'=4,'expert'=8] {'expert'}, dimensions={0} | all-to-all | bytes 983040 | tf_op jit(solution)/shard_map/all_to_all | solution.py:100
  34.0 0.7 fusion.26
  36.4 1.6 %collective-permute-start = (bf16[1,128,1792]{2,1,0:T(8,128)(2,1)S(1)}, bf16[1,128,1792]{2,1,0:T(8,128)(2,1)S(1)}, u32[]{:S(2)}, u32[]{:S(2)}) collective-permute-start(bf16[1,128,1792]{2,1,0:T(8,128)(2,1)S(1)} %get-tuple-element.9), channel_id=1, source_target_pairs={{0,16},{8,24},{16,0},{24,8},{1,17},{9,25},{17,1},{25,9},{2,18},{10... | collective-permute-start | bytes 1376264 | tf_op jit(solution)/shard_map/ppermute | solution.py:54
  38.0 9.7 %collective-permute-done = bf16[1,128,1792]{2,1,0:T(8,128)(2,1)S(1)} collective-permute-done((bf16[1,128,1792]{2,1,0:T(8,128)(2,1)S(1)}, bf16[1,128,1792]{2,1,0:T(8,128)(2,1)S(1)}, u32[]{:S(2)}, u32[]{:S(2)}) %collective-permute-start) | collective-permute-done | bytes 458784 | tf_op jit(solution)/shard_map/ppermute | solution.py:54
  48.1 2.4 %collective-permute-done.1 = bf16[2,128,1792]{2,1,0:T(8,128)(2,1)} collective-permute-done((bf16[2,128,1792]{2,1,0:T(8,128)(2,1)S(1)}, bf16[2,128,1792]{2,1,0:T(8,128)(2,1)}, u32[]{:S(2)}, u32[]{:S(2)}) %collective-permute-start.1) | collective-permute-done | bytes 917536 | tf_op jit(solution)/shard_map/ppermute | solution.py:54
  50.5 1.8 %maximum_select_fusion = bf16[2,2,128,1792]{3,2,0,1:T(8,128)(2,1)S(1)} fusion(bf16[2,1,128,1792]{3,2,0,1:T(8,128)(2,1)} %bitcast.13, bf16[2,1,128,1792]{3,2,0,1:T(8,128)(2,1)S(1)} %maximum_select_fusion.1, pred[]{:T(512)S(6)} %eq.65), kind=kLoop, calls=%fused_computation.8 | loop fusion | flops 2752512 | bytes 3670017 | tf_op jit(solution)/shard_map/jit(_where)/select_n | solution.py:65
  52.4 1.1 %slice_bitcast_fusion = (bf16[128,4,896]{2,0,1:T(8,128)(2,1)S(1)}, bf16[128,4,896]{2,0,1:T(8,128)(2,1)}) fusion(bf16[4,128,1792]{2,1,0:T(8,128)(2,1)S(1)} %bitcast.90), kind=kLoop, calls=%fused_computation.14 | loop fusion | bytes 3670016 | tf_op jit(solution)/shard_map/transpose | solution.py:121
  53.5 1.5 %copy.54 = bf16[128,4,896]{0,2,1:T(8,128)(2,1)S(1)} copy(bf16[128,4,896]{2,0,1:T(8,128)(2,1)} %get-tuple-element.7) | data formatting | bytes 1835008 | tf_op jit(solution)/shard_map/transpose | solution.py:120
  55.1 1.3 %copy.55 = bf16[128,4,896]{0,2,1:T(8,128)(2,1)} copy(bf16[128,4,896]{2,0,1:T(8,128)(2,1)S(1)} %get-tuple-element.6) | data formatting | bytes 1835008 | tf_op jit(solution)/shard_map/transpose | solution.py:121
  56.4 0.4 fusion.8
  56.9 0.7 copy-done.2
  57.8 0.4 multiply_convert_fusion.1
  58.3 0.4 fusion.4
  59.1 0.4 fusion
  59.6 0.8 select_bitcast_fusion
  60.6 1.9 %collective-permute-done.2 = bf16[2,128,896]{2,1,0:T(8,128)(2,1)S(1)} collective-permute-done((bf16[2,128,896]{2,1,0:T(8,128)(2,1)}, bf16[2,128,896]{2,1,0:T(8,128)(2,1)S(1)}, u32[]{:S(2)}, u32[]{:S(2)}) %collective-permute-start.2) | collective-permute-done | bytes 458784 | tf_op jit(solution)/shard_map/ppermute | solution.py:54
  62.7 1.6 %collective-permute-start.3 = (bf16[1,128,896]{2,1,0:T(8,128)(2,1)S(1)}, bf16[1,128,896]{2,1,0:T(8,128)(2,1)S(1)}, u32[]{:S(2)}, u32[]{:S(2)}) collective-permute-start(bf16[1,128,896]{2,1,0:T(8,128)(2,1)S(1)} %fusion.17), channel_id=1, source_target_pairs={{0,16},{8,24},{16,0},{24,8},{1,17},{9,25},{17,1},{25,9},{2,18},{10... | collective-permute-start | bytes 688136 | tf_op jit(solution)/shard_map/ppermute | solution.py:54
  64.3 6.2 %collective-permute-done.3 = bf16[1,128,896]{2,1,0:T(8,128)(2,1)S(1)} collective-permute-done((bf16[1,128,896]{2,1,0:T(8,128)(2,1)S(1)}, bf16[1,128,896]{2,1,0:T(8,128)(2,1)S(1)}, u32[]{:S(2)}, u32[]{:S(2)}) %collective-permute-start.3) | collective-permute-done | bytes 229408 | tf_op jit(solution)/shard_map/ppermute | solution.py:54
  70.4 0.7 fusion.14
  71.2 4.4 %all-to-all-start.1 = ((bf16[8,16,896]{2,1,0:T(8,128)(2,1)}), bf16[8,16,896]{2,1,0:T(8,128)(2,1)S(1)}, u32[]{:S(2)}, u32[]{:S(2)}) async-start(bf16[8,16,896]{2,1,0:T(8,128)(2,1)} %bitcast.32), calls=%async_computation.1 | async-start | bytes 458752 | tf_op jit(solution)/shard_map/all_to_all | solution.py:144
  75.5 1.3 %fusion.2 = bf16[1,3584,128]{2,1,0:T(8,128)(2,1)} fusion(bf16[128,3584]{0,1:T(8,128)(2,1)S(1)} %bitcast.86, bf16[128,128]{1,0:T(8,128)(2,1)S(1)} %get-tuple-element.15), kind=kOutput, calls=%fused_computation.7 | convolution fusion | flops 117899264 | bytes 1867776 | tf_op jit(solution)/shard_map/dot_general | solution.py:136
  76.8 1.3 %fusion.1 = bf16[1,3584,128]{2,1,0:T(8,128)(2,1)} fusion(bf16[128,3584]{0,1:T(8,128)(2,1)S(1)} %bitcast.87, bf16[128,128]{1,0:T(8,128)(2,1)S(1)} %fusion.4), kind=kOutput, calls=%fused_computation.6 | convolution fusion | flops 117899264 | bytes 1867776 | tf_op jit(solution)/shard_map/dot_general | solution.py:133
  78.1 5.4 %all-to-all-done.1 = bf16[8,16,896]{2,1,0:T(8,128)(2,1)S(1)} async-done(((bf16[8,16,896]{2,1,0:T(8,128)(2,1)}), bf16[8,16,896]{2,1,0:T(8,128)(2,1)S(1)}, u32[]{:S(2)}, u32[]{:S(2)}) %all-to-all-start.1) | async-done | bytes 229408 | tf_op jit(solution)/shard_map/all_to_all | solution.py:144
  83.5 1.2 %convolution_convert_fusion.2 = bf16[256,896]{1,0:T(8,128)(2,1)} fusion(bf16[128,896]{1,0:T(8,128)(2,1)S(1)} %bitcast.100, s32[128]{0:T(128)S(1)} %select_n.140), kind=kOutput, calls=%fused_computation.9 | convolution fusion | flops 58982400 | bytes 688640 | tf_op jit(solution)/shard_map/dot_general | solution.py:148
  (50 shorter events, 3.9 us)
Async XLA Ops:
  0.6 55.8 %copy-start = (bf16[1,3584,128]{2,1,0:T(8,128)(2,1)S(1)}, bf16[1,3584,128]{2,1,0:T(8,128)(2,1)}, u32[]{:S(2)}) copy-start(bf16[1,3584,128]{2,1,0:T(8,128)(2,1)} %param.15) | copy-start | bytes 2752516
  9.9 1.8 %copy-start.4 = (s32[256,8]{0,1:T(8,128)S(1)}, s32[256,8]{0,1:T(8,128)}, u32[]{:S(2)}) copy-start(s32[256,8]{0,1:T(8,128)} %param.12) | copy-start | bytes 24580
  9.9 1.8 %copy-start.5 = (f32[256,8]{0,1:T(8,128)S(1)}, f32[256,8]{0,1:T(8,128)}, u32[]{:S(2)}) copy-start(f32[256,8]{0,1:T(8,128)} %param.13) | copy-start | bytes 24580
  36.4 11.2 %collective-permute-start = (bf16[1,128,1792]{2,1,0:T(8,128)(2,1)S(1)}, bf16[1,128,1792]{2,1,0:T(8,128)(2,1)S(1)}, u32[]{:S(2)}, u32[]{:S(2)}) collective-permute-start(bf16[1,128,1792]{2,1,0:T(8,128)(2,1)S(1)} %get-tuple-element.9), channel_id=1, source_target_pairs={{0,16},{8,24},{16,0},{24,8},{1,17},{9,25},{17,1},{25,9},{2,18},{10... | collective-permute-start | bytes 1376264 | tf_op jit(solution)/shard_map/ppermute | solution.py:54
  47.8 2.7 %collective-permute-start.1 = (bf16[2,128,1792]{2,1,0:T(8,128)(2,1)S(1)}, bf16[2,128,1792]{2,1,0:T(8,128)(2,1)}, u32[]{:S(2)}, u32[]{:S(2)}) collective-permute-start(bf16[2,128,1792]{2,1,0:T(8,128)(2,1)S(1)} %maximum_select_fusion.2), channel_id=1, source_target_pairs={{0,8},{8,0},{16,24},{24,16},{1,9},{9,1},{17,25},{25,17},{2,10},{10... | collective-permute-start | bytes 2752520 | tf_op jit(solution)/shard_map/ppermute | solution.py:54
  56.4 1.2 %copy-start.2 = (bf16[128,4,896]{0,2,1:T(8,128)(2,1)S(1)}, bf16[128,4,896]{0,2,1:T(8,128)(2,1)}, u32[]{:S(2)}) copy-start(bf16[128,4,896]{0,2,1:T(8,128)(2,1)} %copy.55) | copy-start | bytes 2752516
  56.4 1.5 %copy-start.3 = (bf16[1,128,3584]{2,1,0:T(8,128)(2,1)S(1)}, bf16[1,128,3584]{2,1,0:T(8,128)(2,1)}, u32[]{:S(2)}) copy-start(bf16[1,128,3584]{2,1,0:T(8,128)(2,1)} %param.17) | copy-start | bytes 2752516
  56.4 1.9 %copy-start.1 = (bf16[1,3584,128]{2,1,0:T(8,128)(2,1)S(1)}, bf16[1,3584,128]{2,1,0:T(8,128)(2,1)}, u32[]{:S(2)}) copy-start(bf16[1,3584,128]{2,1,0:T(8,128)(2,1)} %param.16) | copy-start | bytes 2752516
  60.5 2.0 %collective-permute-start.2 = (bf16[2,128,896]{2,1,0:T(8,128)(2,1)}, bf16[2,128,896]{2,1,0:T(8,128)(2,1)S(1)}, u32[]{:S(2)}, u32[]{:S(2)}) collective-permute-start(bf16[2,128,896]{2,1,0:T(8,128)(2,1)} %select_bitcast_fusion), channel_id=1, source_target_pairs={{0,8},{8,0},{16,24},{24,16},{1,9},{9,1},{17,25},{25,17},{2,10},{10... | collective-permute-start | bytes 1376264 | tf_op jit(solution)/shard_map/ppermute | solution.py:54
  62.7 7.7 %collective-permute-start.3 = (bf16[1,128,896]{2,1,0:T(8,128)(2,1)S(1)}, bf16[1,128,896]{2,1,0:T(8,128)(2,1)S(1)}, u32[]{:S(2)}, u32[]{:S(2)}) collective-permute-start(bf16[1,128,896]{2,1,0:T(8,128)(2,1)S(1)} %fusion.17), channel_id=1, source_target_pairs={{0,16},{8,24},{16,0},{24,8},{1,17},{9,25},{17,1},{25,9},{2,18},{10... | collective-permute-start | bytes 688136 | tf_op jit(solution)/shard_map/ppermute | solution.py:54
  71.2 12.4 %all-to-all-start.1 = ((bf16[8,16,896]{2,1,0:T(8,128)(2,1)}), bf16[8,16,896]{2,1,0:T(8,128)(2,1)S(1)}, u32[]{:S(2)}, u32[]{:S(2)}) async-start(bf16[8,16,896]{2,1,0:T(8,128)(2,1)} %bitcast.32), calls=%async_computation.1 | async-start | bytes 458752 | tf_op jit(solution)/shard_map/all_to_all | solution.py:144

commit v2 on v1

v2 whole, which is shorter than its diff:
```python
import jax
import jax.numpy as jnp
from jax import lax
from jax.sharding import PartitionSpec as P

EXP_DEV = 8
CAP = 16


def one_hot_slots(expert_ids, capacity, n_dest):
    row_count = expert_ids.shape[0]
    edited = jnp.arange(n_dest, dtype=jnp.int32) * EXP_DEV
    match = expert_ids[:, :, None] == edited[None, None, :]
    hits = jnp.sum(match.astype(jnp.int32), axis=1)
    before = (
        jnp.arange(row_count, dtype=jnp.int32)[:, None] > jnp.arange(row_count, dtype=jnp.int32)[None, :]
    ).astype(jnp.bfloat16)
    rank = jnp.dot(before, hits.astype(jnp.bfloat16), preferred_element_type=jnp.float32)
    places = jnp.arange(capacity, dtype=jnp.float32)
    taken = (hits[:, :, None] == 1) & (rank[:, :, None] == places[None, None, :])
    return match, taken.reshape(row_count, n_dest * capacity).astype(jnp.bfloat16)


def silu_parts(pre):
    sigmoid_gate = jax.nn.sigmoid(pre)
    return (pre * sigmoid_gate, sigmoid_gate * (1.0 + pre * (1.0 - sigmoid_gate)))


def bf16_part(x):
    return lax.reduce_precision(x, exponent_bits=8, mantissa_bits=7)


def side_width(n_dest):
    return -(-(3 * n_dest + 3) // 128) * 128


def token_side(match, gate_values, forget_flags, n_dest):
    gate_sel = jnp.sum(
        jnp.where(match, gate_values[:, :, None], jnp.zeros((), gate_values.dtype)), axis=1
    )
    hi = bf16_part(gate_sel)
    rest = gate_sel - hi
    mid = bf16_part(rest)
    lo = rest - mid
    flag = forget_flags.astype(jnp.float32)[:, None]
    cols = jnp.concatenate([hi, mid, lo, flag], axis=1)
    pad = jnp.zeros((cols.shape[0], side_width(n_dest) - cols.shape[1]), jnp.float32)
    return jnp.concatenate([cols, pad], axis=1).astype(jnp.bfloat16)


def partner(x, bit, n):
    return lax.ppermute(x, "dp", [(i, i ^ bit) for i in range(n)])


def gather_dp(x, n):
    me = lax.axis_index("dp")
    acc = x[None]
    bit = n // 2
    while bit >= 1:
        other = partner(acc, bit, n)
        low_first = jnp.stack([acc, other], axis=1)
        high_first = jnp.stack([other, acc], axis=1)
        acc = jnp.where((me & bit) == 0, low_first, high_first)
        acc = acc.reshape((-1,) + x.shape)
        bit //= 2
    return acc


def scatter_dp(parts, n):
    me = lax.axis_index("dp")
    acc = parts
    bit = 1
    while bit < n:
        pairs = acc.reshape((acc.shape[0] // 2, 2) + acc.shape[1:])
        mine = (me & bit) != 0
        keep = jnp.where(mine, pairs[:, 1], pairs[:, 0])
        send = jnp.where(mine, pairs[:, 0], pairs[:, 1])
        got = partner(send.astype(jnp.bfloat16), bit, n)
        acc = keep.astype(jnp.float32) + got.astype(jnp.float32)
        bit *= 2
    return acc[0]


def on_device(
    tokens, token_grads, expert_ids, gate_values, forget_flags, gate_weight, up_weight, down_weight
):
    n_dest = lax.axis_size("expert")
    n_dp = lax.axis_size("dp")
    me = lax.axis_index("expert")
    row_count, width = tokens.shape
    side = side_width(n_dest)
    match, pick = one_hot_slots(expert_ids, CAP, n_dest)
    per_token = jnp.concatenate(
        [tokens, token_grads, token_side(match, gate_values, forget_flags, n_dest)], axis=1
    )
    local_count = jnp.sum(forget_flags)
    at_col = jnp.arange(2 * width + side, dtype=jnp.int32)
    count_row = jnp.where(
        at_col == 2 * width + 3 * n_dest + 1,
        (local_count // 256).astype(jnp.float32),
        jnp.where(at_col == 2 * width + 3 * n_dest + 2, (local_count % 256).astype(jnp.float32), 0.0),
    )
    chosen = lax.dot_general(pick, per_token, (((0,), (0,)), ((), ())), preferred_element_type=jnp.float32)
    payload = (chosen + count_row[None, :]).astype(jnp.bfloat16)
    arrived = lax.all_to_all(payload, "expert", split_axis=0, concat_axis=0, tiled=True)
    slots = arrived.shape[0]
    part_tokens = arrived[:, :width]
    raw_grads = arrived[:, width : 2 * width]
    info = arrived[:, 2 * width :].astype(jnp.float32)
    pieces = lax.dynamic_slice_in_dim(info[:, : 3 * n_dest].reshape(slots, 3, n_dest), me, 1, axis=2)
    gate_sel = (pieces[:, 0, 0] + pieces[:, 1, 0]) + pieces[:, 2, 0]
    flag = info[:, 3 * n_dest]
    by_block = info.reshape(n_dest, CAP, side)[:, 0]
    forget_count = jnp.sum(by_block[:, 3 * n_dest + 1] * 256.0 + by_block[:, 3 * n_dest + 2])
    all_rows = row_count * n_dest
    half_total = jnp.float32(all_rows) / 2.0
    weight = jnp.where(
        flag == 1.0,
        -half_total / forget_count,
        half_total / (jnp.float32(all_rows) - forget_count),
    )
    scale = gate_sel * weight
    part_grads = (scale[:, None] * raw_grads.astype(jnp.float32)).astype(jnp.bfloat16)
    both = jnp.concatenate([part_tokens, part_grads], axis=1)
    gathered = gather_dp(both, n_dp)
    slot_tokens = gathered[:, :, :width]
    slot_grads = gathered[:, :, width:]
    ff = gate_weight.shape[2]
    w_gate = gate_weight[0].reshape(n_dp, width, ff)
    w_up = up_weight[0].reshape(n_dp, width, ff)
    w_down = down_weight[0].reshape(ff, n_dp, width)
    chunk_dims = (((0, 2), (0, 1)), ((), ()))
    gate_pre = lax.dot_general(slot_tokens, w_gate, chunk_dims, preferred_element_type=jnp.float32)
    up_pre = lax.dot_general(slot_tokens, w_up, chunk_dims, preferred_element_type=jnp.float32)
    hidden_grad = lax.dot_general(
        slot_grads, w_down, (((0, 2), (1, 2)), ((), ())), preferred_element_type=jnp.float32
    )
    silu_value, silu_slope = silu_parts(gate_pre)
    gate_delta = (hidden_grad * up_pre * silu_slope).astype(jnp.bfloat16)
    up_delta = (hidden_grad * silu_value).astype(jnp.bfloat16)
    slot_dims = (((1,), (0,)), ((), ()))
    grad_gate = lax.dot_general(
        slot_tokens, gate_delta, slot_dims, preferred_element_type=jnp.float32
    ).astype(jnp.bfloat16)
    grad_up = lax.dot_general(
        slot_tokens, up_delta, slot_dims, preferred_element_type=jnp.float32
    ).astype(jnp.bfloat16)
    back_dims = (((2,), (1,)), ((), ()))
    from_gate = lax.dot_general(w_gate, gate_delta, back_dims, preferred_element_type=jnp.float32)
    from_up = lax.dot_general(w_up, up_delta, back_dims, preferred_element_type=jnp.float32)
    part = (from_gate + from_up).astype(jnp.bfloat16)
    summed = scatter_dp(jnp.swapaxes(part, 1, 2), n_dp).astype(jnp.bfloat16)
    returned = lax.all_to_all(summed, "expert", split_axis=0, concat_axis=0, tiled=True)
    input_grad = lax.dot_general(pick, returned, slot_dims, preferred_element_type=jnp.float32)
    return (
        grad_gate.reshape(1, n_dp * width, ff),
        grad_up.reshape(1, n_dp * width, ff),
        input_grad.astype(jnp.bfloat16),
    )


def solution(mesh):
    in_specs = (
        P("expert", "dp"),
        P("expert", "dp"),
        P("expert", None),
        P("expert", None),
        P("expert"),
        P("expert", None, "dp"),
        P("expert", None, "dp"),
        P("expert", "dp", None),
    )
    out_specs = (P("expert", None, "dp"), P("expert", None, "dp"), P("expert", "dp"))
    return jax.shard_map(
        on_device, mesh=mesh, in_specs=in_specs, out_specs=out_specs, check_vma=False
    )
```

time: 85.3 us -> 80.2 us (0.940)
  blocking collectives: 20.9 us -> 0 us
  waiting for transfers between devices: 25.6 us -> 38.1 us
  starting transfers between devices: 7.69 us -> 15.6 us
  local copies, waits for them, and re-layouts: 10.3 us -> 5.85 us
  other arithmetic: 9.4 us -> 8.18 us
  matrix products: 5.9 us -> 7.11 us
    all_to_all x1 -> x0, blocking collectives: 20.9 us -> none  [on_device(): lax.all_to_all(payload, 'expert', split_axis=0, concat_axis=0, tiled=True)]
    all_to_all x0 -> x1, waiting for transfers between devices: none -> 13.8 us  [on_device(): lax.all_to_all(payload, 'expert', split_axis=0, concat_axis=0, tiled=True)]
    all_to_all x0 -> x1, starting transfers between devices: none -> 7.31 us  [on_device(): lax.all_to_all(payload, 'expert', split_axis=0, concat_axis=0, tiled=True)]
    transpose x3 -> x0, local copies, waits for them, and re-layouts: 3.97 us -> none  [the longest x2 2.43 us: on_device(): jnp.transpose(gathered[:, :, width:], (1, 0, 2))]
    gather x2 -> x0, local copies, waits for them, and re-layouts: 1.76 us -> none  [the longest x1 0.88 us: on_device(): jnp.take(jnp.concatenate([tokens, blank], axis=0), flat_source, axis=0)]
    dot_general x8 -> x10, matrix products: 5.9 us -> 7.11 us  [the longest x1 1.36 us: on_device(): lax.dot_general(slot_tokens, up_delta, slot_dims, preferred_element_type=...]
    ppermute x4, waiting for transfers between devices: 20.2 us -> 19 us  [partner(): return lax.ppermute(x, 'dp', [(i, i ^ bit) for i in range(n)])]
    another operation x4, local copies, waits for them, and re-layouts: 0.42 us -> 1.5 us  [the longest x1 1.14 us: on_device(): w_down = down_weight[0].reshape(ff, n_dp, width)]
  transfers between devices with their start and end apart: 5 -> 6, of which waited for: 5 -> 6; matrix products, arithmetic and copies ran while one was open for 3% -> 5% of each run, Pallas kernels for 0% -> 0%
where the time goes in v2:
time: 80.2 us; the launch traced here: 79.6 us
  waiting for transfers between devices  38.1 us (48%)
  starting transfers between devices  15.6 us (19%)
  other arithmetic  8.18 us (10%)
  matrix products  7.11 us (9%)
  local copies, waits for them, and re-layouts  5.85 us (7%)
  between operations  4.86 us (6%)
    ppermute x4, waiting for transfers between devices, partner(): return lax.ppermute(x, 'dp', [(i, i ^ bit) for i in range(n)])  19 us
    all_to_all x1, waiting for transfers between devices, on_device(): lax.all_to_all(payload, 'expert', split_axis=0, concat_axis=0, tiled=True)  13.8 us
    all_to_all x1, starting transfers between devices, on_device(): lax.all_to_all(payload, 'expert', split_axis=0, concat_axis=0, tiled=True)  7.31 us
    all_to_all x1, waiting for transfers between devices, on_device(): lax.all_to_all(summed, 'expert', split_axis=0, concat_axis=0, tiled=True)  5.28 us
    all_to_all x1, starting transfers between devices, on_device(): lax.all_to_all(summed, 'expert', split_axis=0, concat_axis=0, tiled=True)  4.95 us
    ppermute x4, starting transfers between devices, partner(): return lax.ppermute(x, 'dp', [(i, i ^ bit) for i in range(n)])  3.31 us
    select_n x3, other arithmetic, gather_dp(): acc = jnp.where(me & bit == 0, low_first, high_first)  3.02 us
    concatenate x1, local copies, waits for them, and re-layouts, on_device(): jnp.concatenate([tokens, token_grads, token_side(match, gate_values, forg...  2.38 us
  transfers between devices with their start and end apart: 6, of which 6 were waited for; matrix products, arithmetic and copies ran while one was open for 5% of the time, Pallas kernels for 0%

profile of v2, /device:TPU:0, one launch (start us, length us, event | category | flops | bytes accessed | tf_op | source)
XLA Modules:
  0.0 79.6 jit_solution(6424362774377586058)
XLA Ops:
  0.7 1.4 %fusion.34 = (s32[]{:T(128)}, bf16[256]{0:T(256)(128)(2,1)S(1)}) fusion(s32[256]{0:T(256)} %param.12), kind=kLoop, calls=%fused_computation.75 | loop fusion | flops 767 | bytes 1540 | tf_op jit(solution)/shard_map/reduce_sum | solution.py:96
  4.7 0.8 fusion.23
  5.5 0.2 fusion.18
  5.7 0.8 %fusion.24 = f32[256,8]{0,1:T(8,128)S(1)} fusion(f32[256,8]{0,1:T(8,128)} %param.11, s32[256,8]{0,1:T(8,128)} %param.10, s32[8]{0:T(128)S(1)} %iota_multiply_fusion), kind=kLoop, calls=%fused_computation.46 | loop fusion | flops 47104 | bytes 24608 | tf_op jit(solution)/shard_map/reduce_sum | solution.py:38
  7.1 2.4 %concatenate.29 = bf16[256,1920]{1,0:T(8,128)(2,1)S(1)} concatenate(bf16[256,896]{1,0:T(8,128)(2,1)} %param.8, bf16[256,896]{1,0:T(8,128)(2,1)} %param.9, bf16[256,8]{1,0:T(8,128)(2,1)S(1)} %copy.48, bf16[256,8]{1,0:T(8,128)(2,1)S(1)} %copy.49, bf16[256,8]{1,0:T(8,128)(2,1)S(1)} %copy.50, bf16[256,1]{1,0:T(8,128)(2,1)S(1)} %broadcast_in_dim.62, bf16[256,103]{1,0:T(8,128)(2,1)S(1)} %broadcast_in_dim.55), dimensions={1} | concatenate | bytes 1966080 | tf_op jit(solution)/shard_map/concatenate | solution.py:93
  9.5 1.1 %fusion = bf16[128,1920]{1,0:T(8,128)(2,1)} fusion(pred[256,128]{0,1:T(32,128)(4,1)S(1)} %fusion.22, bf16[256,1920]{1,0:T(8,128)(2,1)S(1)} %concatenate.29, f32[1920]{0:T(1024)S(1)} %select_select_fusion), kind=kOutput, calls=%fused_computation.1 | convolution fusion | flops 126320640 | bytes 1515008 | tf_op jit(solution)/shard_map/dot_general | solution.py:103
  10.6 7.3 %all-to-all-start = ((bf16[8,16,1920]{2,1,0:T(8,128)(2,1)}), bf16[8,16,1920]{2,1,0:T(8,128)(2,1)S(1)}, u32[]{:S(2)}, u32[]{:S(2)}) async-start(bf16[8,16,1920]{2,1,0:T(8,128)(2,1)} %bitcast.2), calls=%async_computation | async-start | bytes 983040 | tf_op jit(solution)/shard_map/all_to_all | solution.py:105
  17.9 13.8 %all-to-all-done = bf16[8,16,1920]{2,1,0:T(8,128)(2,1)S(1)} async-done(((bf16[8,16,1920]{2,1,0:T(8,128)(2,1)}), bf16[8,16,1920]{2,1,0:T(8,128)(2,1)S(1)}, u32[]{:S(2)}, u32[]{:S(2)}) %all-to-all-start) | async-done | bytes 491552 | tf_op jit(solution)/shard_map/all_to_all | solution.py:105
  31.8 0.7 add_reduce_fusion
  34.0 0.2 multiply_reduce_fusion
  34.4 1.6 %collective-permute-start = (bf16[1,128,1792]{2,1,0:T(8,128)(2,1)S(1)}, bf16[1,128,1792]{2,1,0:T(8,128)(2,1)S(1)}, u32[]{:S(2)}, u32[]{:S(2)}) collective-permute-start(bf16[1,128,1792]{2,1,0:T(8,128)(2,1)S(1)} %get-tuple-element.4), channel_id=1, source_target_pairs={{0,16},{8,24},{16,0},{24,8},{1,17},{9,25},{17,1},{25,9},{2,18},{10... | collective-permute-start | bytes 1376264 | tf_op jit(solution)/shard_map/ppermute | solution.py:52
  36.0 9.6 %collective-permute-done = bf16[1,128,1792]{2,1,0:T(8,128)(2,1)S(1)} collective-permute-done((bf16[1,128,1792]{2,1,0:T(8,128)(2,1)S(1)}, bf16[1,128,1792]{2,1,0:T(8,128)(2,1)S(1)}, u32[]{:S(2)}, u32[]{:S(2)}) %collective-permute-start) | collective-permute-done | bytes 458784 | tf_op jit(solution)/shard_map/ppermute | solution.py:52
  45.6 1.1 %maximum_select_fusion.2 = bf16[2,128,1792]{2,1,0:T(8,128)(2,1)} fusion(bf16[1,128,1792]{2,1,0:T(8,128)(2,1)S(1)} %collective-permute-done, bf16[1,128,1792]{2,1,0:T(8,128)(2,1)S(1)} %get-tuple-element.4, pred[]{:T(512)S(6)} %eq.84), kind=kLoop, calls=%fused_computation.17 | loop fusion | flops 1376256 | bytes 1835009 | tf_op jit(solution)/shard_map/jit(_where)/select_n | solution.py:63
  46.7 1.1 %reshape_squeeze.9 = bf16[128,4,896]{2,1,0:T(4,128)(2,1)} reshape(bf16[1,128,3584]{2,1,0:T(8,128)(2,1)S(1)} %copy-done.4) | data formatting | bytes 1835008 | tf_op jit(solution)/shard_map/reshape;squeeze | solution.py:131
  47.9 1.5 %collective-permute-done.1 = bf16[2,128,1792]{2,1,0:T(8,128)(2,1)} collective-permute-done((bf16[2,128,1792]{2,1,0:T(8,128)(2,1)}, bf16[2,128,1792]{2,1,0:T(8,128)(2,1)}, u32[]{:S(2)}, u32[]{:S(2)}) %collective-permute-start.1) | collective-permute-done | bytes 917536 | tf_op jit(solution)/shard_map/ppermute | solution.py:52
  49.5 1.8 %maximum_select_fusion = bf16[2,2,128,1792]{3,2,0,1:T(8,128)(2,1)S(1)} fusion(bf16[2,1,128,1792]{3,2,0,1:T(8,128)(2,1)} %bitcast.11, bf16[2,1,128,1792]{3,2,0,1:T(8,128)(2,1)S(1)} %maximum_select_fusion.1, pred[]{:T(512)S(6)} %eq.83), kind=kLoop, calls=%fused_computation.2 | loop fusion | flops 2752512 | bytes 3670017 | tf_op jit(solution)/shard_map/jit(_where)/select_n | solution.py:63
  51.4 0.4 convolution_bitcast_fusion.1
  51.9 1.4 %copy-done.5 = bf16[128,4,896]{2,1,0:T(4,128)(2,1)S(1)} copy-done((bf16[128,4,896]{2,1,0:T(4,128)(2,1)S(1)}, bf16[128,4,896]{2,1,0:T(4,128)(2,1)}, u32[]{:S(2)}) %copy-start.5) | copy-done | bytes 917528
  53.3 0.4 multiply_convert_fusion.1
  53.7 0.4 fusion.5
  54.1 0.4 fusion.35
  54.5 0.4 add_convert_fusion
  55.0 0.2 collective-permute-start.2
  55.2 1.7 %collective-permute-done.2 = bf16[2,128,896]{2,1,0:T(8,128)(2,1)S(1)} collective-permute-done((bf16[2,128,896]{2,1,0:T(8,128)(2,1)S(1)}, bf16[2,128,896]{2,1,0:T(8,128)(2,1)S(1)}, u32[]{:S(2)}, u32[]{:S(2)}) %collective-permute-start.2) | collective-permute-done | bytes 458784 | tf_op jit(solution)/shard_map/ppermute | solution.py:52
  57.1 1.6 %collective-permute-start.3 = (bf16[1,128,896]{2,1,0:T(8,128)(2,1)S(1)}, bf16[1,128,896]{2,1,0:T(8,128)(2,1)S(1)}, u32[]{:S(2)}, u32[]{:S(2)}) collective-permute-start(bf16[1,128,896]{2,1,0:T(8,128)(2,1)S(1)} %fusion.19), channel_id=1, source_target_pairs={{0,16},{8,24},{16,0},{24,8},{1,17},{9,25},{17,1},{25,9},{2,18},{10... | collective-permute-start | bytes 688136 | tf_op jit(solution)/shard_map/ppermute | solution.py:52
  58.6 6.2 %collective-permute-done.3 = bf16[1,128,896]{2,1,0:T(8,128)(2,1)S(1)} collective-permute-done((bf16[1,128,896]{2,1,0:T(8,128)(2,1)S(1)}, bf16[1,128,896]{2,1,0:T(8,128)(2,1)S(1)}, u32[]{:S(2)}, u32[]{:S(2)}) %collective-permute-start.3) | collective-permute-done | bytes 229408 | tf_op jit(solution)/shard_map/ppermute | solution.py:52
  64.8 0.7 fusion.15
  65.6 5.0 %all-to-all-start.1 = ((bf16[8,16,896]{2,1,0:T(8,128)(2,1)}), bf16[8,16,896]{2,1,0:T(8,128)(2,1)S(1)}, u32[]{:S(2)}, u32[]{:S(2)}) async-start(bf16[8,16,896]{2,1,0:T(8,128)(2,1)} %bitcast.33), calls=%async_computation.1 | async-start | bytes 458752 | tf_op jit(solution)/shard_map/all_to_all | solution.py:153
  70.5 1.4 %convolution_convert_fusion.1 = bf16[4,896,128]{2,1,0:T(8,128)(2,1)} fusion(bf16[128,128,1]{1,0,2:T(8,128)(2,1)S(1)} %fusion.5, bf16[4,128,1792]{2,1,0:T(8,128)(2,1)S(1)} %bitcast.99), kind=kOutput, calls=%fused_computation.5 | convolution fusion | flops 117899264 | bytes 1867776 | tf_op jit(solution)/shard_map/dot_general | solution.py:142
  71.9 1.4 %convolution_convert_fusion = bf16[4,896,128]{2,1,0:T(8,128)(2,1)} fusion(bf16[4,128,1792]{2,1,0:T(8,128)(2,1)S(1)} %bitcast.100, bf16[128,128]{1,0:T(8,128)(2,1)S(1)} %get-tuple-element.10), kind=kOutput, calls=%fused_computation.4 | convolution fusion | flops 117899264 | bytes 1867776 | tf_op jit(solution)/shard_map/dot_general | solution.py:145
  73.2 5.3 %all-to-all-done.1 = bf16[8,16,896]{2,1,0:T(8,128)(2,1)S(1)} async-done(((bf16[8,16,896]{2,1,0:T(8,128)(2,1)}), bf16[8,16,896]{2,1,0:T(8,128)(2,1)S(1)}, u32[]{:S(2)}, u32[]{:S(2)}) %all-to-all-start.1) | async-done | bytes 229408 | tf_op jit(solution)/shard_map/all_to_all | solution.py:153
  78.5 1.1 %fusion.1 = bf16[256,896]{1,0:T(8,128)(2,1)} fusion(bf16[8,16,896]{2,1,0:T(8,128)(2,1)S(1)} %all-to-all-done.1, f32[256,8]{0,1:T(8,128)S(1)} %fusion.18, pred[256,8]{0,1:T(8,128)(4,1)S(1)} %broadcast_compare_fusion), kind=kOutput, calls=%fused_computation.7 | convolution fusion | flops 59015168 | bytes 698368 | tf_op jit(solution)/shard_map/dot_general | solution.py:154
  (37 shorter events, 1.7 us)
Async XLA Ops:
  0.6 50.8 %copy-start = (bf16[1,3584,128]{2,1,0:T(8,128)(2,1)S(1)}, bf16[1,3584,128]{2,1,0:T(8,128)(2,1)}, u32[]{:S(2)}) copy-start(bf16[1,3584,128]{2,1,0:T(8,128)(2,1)} %param.13) | copy-start | bytes 2752516
  10.6 21.1 %all-to-all-start = ((bf16[8,16,1920]{2,1,0:T(8,128)(2,1)}), bf16[8,16,1920]{2,1,0:T(8,128)(2,1)S(1)}, u32[]{:S(2)}, u32[]{:S(2)}) async-start(bf16[8,16,1920]{2,1,0:T(8,128)(2,1)} %bitcast.2), calls=%async_computation | async-start | bytes 983040 | tf_op jit(solution)/shard_map/all_to_all | solution.py:105
  34.2 12.5 %copy-start.4 = (bf16[1,128,3584]{2,1,0:T(8,128)(2,1)S(1)}, bf16[1,128,3584]{2,1,0:T(8,128)(2,1)}, u32[]{:S(2)}) copy-start(bf16[1,128,3584]{2,1,0:T(8,128)(2,1)} %param.15) | copy-start | bytes 2752516
  34.4 11.2 %collective-permute-start = (bf16[1,128,1792]{2,1,0:T(8,128)(2,1)S(1)}, bf16[1,128,1792]{2,1,0:T(8,128)(2,1)S(1)}, u32[]{:S(2)}, u32[]{:S(2)}) collective-permute-start(bf16[1,128,1792]{2,1,0:T(8,128)(2,1)S(1)} %get-tuple-element.4), channel_id=1, source_target_pairs={{0,16},{8,24},{16,0},{24,8},{1,17},{9,25},{17,1},{25,9},{2,18},{10... | collective-permute-start | bytes 1376264 | tf_op jit(solution)/shard_map/ppermute | solution.py:52
  46.7 2.8 %collective-permute-start.1 = (bf16[2,128,1792]{2,1,0:T(8,128)(2,1)}, bf16[2,128,1792]{2,1,0:T(8,128)(2,1)}, u32[]{:S(2)}, u32[]{:S(2)}) collective-permute-start(bf16[2,128,1792]{2,1,0:T(8,128)(2,1)} %maximum_select_fusion.2), channel_id=1, source_target_pairs={{0,8},{8,0},{16,24},{24,16},{1,9},{9,1},{17,25},{25,17},{2,10},{10... | collective-permute-start | bytes 2752520 | tf_op jit(solution)/shard_map/ppermute | solution.py:52
  51.4 2.3 %copy-start.1 = (bf16[2,2,128,1792]{3,2,1,0:T(8,128)(2,1)}, bf16[2,2,128,1792]{3,2,1,0:T(8,128)(2,1)S(1)}, u32[]{:S(2)}) copy-start(bf16[2,2,128,1792]{3,2,1,0:T(8,128)(2,1)S(1)} %copy.54) | copy-start | bytes 5505028
  51.4 1.8 %copy-start.5 = (bf16[128,4,896]{2,1,0:T(4,128)(2,1)S(1)}, bf16[128,4,896]{2,1,0:T(4,128)(2,1)}, u32[]{:S(2)}) copy-start(bf16[128,4,896]{2,1,0:T(4,128)(2,1)} %reshape_squeeze.9) | copy-start | bytes 2752516
  51.4 2.3 %copy-start.3 = (bf16[1,3584,128]{2,1,0:T(8,128)(2,1)S(1)}, bf16[1,3584,128]{2,1,0:T(8,128)(2,1)}, u32[]{:S(2)}) copy-start(bf16[1,3584,128]{2,1,0:T(8,128)(2,1)} %param.14) | copy-start | bytes 2752516
  55.0 1.9 %collective-permute-start.2 = (bf16[2,128,896]{2,1,0:T(8,128)(2,1)S(1)}, bf16[2,128,896]{2,1,0:T(8,128)(2,1)S(1)}, u32[]{:S(2)}, u32[]{:S(2)}) collective-permute-start(bf16[2,128,896]{2,1,0:T(8,128)(2,1)S(1)} %fusion.13), channel_id=1, source_target_pairs={{0,8},{8,0},{16,24},{24,16},{1,9},{9,1},{17,25},{25,17},{2,10},{10... | collective-permute-start | bytes 1376264 | tf_op jit(solution)/shard_map/ppermute | solution.py:52
  57.0 13.5 %copy-start.2 = (bf16[2,2,128,1792]{3,2,1,0:T(8,128)(2,1)S(1)}, bf16[2,2,128,1792]{3,2,1,0:T(8,128)(2,1)}, u32[]{:S(2)}) copy-start(bf16[2,2,128,1792]{3,2,1,0:T(8,128)(2,1)} %copy-done.1) | copy-start | bytes 5505028
  57.1 7.7 %collective-permute-start.3 = (bf16[1,128,896]{2,1,0:T(8,128)(2,1)S(1)}, bf16[1,128,896]{2,1,0:T(8,128)(2,1)S(1)}, u32[]{:S(2)}, u32[]{:S(2)}) collective-permute-start(bf16[1,128,896]{2,1,0:T(8,128)(2,1)S(1)} %fusion.19), channel_id=1, source_target_pairs={{0,16},{8,24},{16,0},{24,8},{1,17},{9,25},{17,1},{25,9},{2,18},{10... | collective-permute-start | bytes 688136 | tf_op jit(solution)/shard_map/ppermute | solution.py:52
  65.6 13.0 %all-to-all-start.1 = ((bf16[8,16,896]{2,1,0:T(8,128)(2,1)}), bf16[8,16,896]{2,1,0:T(8,128)(2,1)S(1)}, u32[]{:S(2)}, u32[]{:S(2)}) async-start(bf16[8,16,896]{2,1,0:T(8,128)(2,1)} %bitcast.33), calls=%async_computation.1 | async-start | bytes 458752 | tf_op jit(solution)/shard_map/all_to_all | solution.py:153

commit v3 on v2

--- a/solution.py
+++ b/solution.py
@@ -57,13 +57,14 @@
     acc = x[None]
     bit = n // 2
     while bit >= 1:
-        other = partner(acc, bit, n)
-        low_first = jnp.stack([acc, other], axis=1)
-        high_first = jnp.stack([other, acc], axis=1)
-        acc = jnp.where((me & bit) == 0, low_first, high_first)
-        acc = acc.reshape((-1,) + x.shape)
+        acc = jnp.concatenate([acc, partner(acc, bit, n)], axis=0)
         bit //= 2
-    return acc
+    rel = me ^ jnp.arange(n, dtype=jnp.int32)
+    pos = jnp.zeros_like(rel)
+    width = n.bit_length() - 1
+    for b in range(width):
+        pos = pos | (((rel >> b) & 1) << (width - 1 - b))
+    return jnp.take(acc, pos, axis=0)
 
 
 def scatter_dp(parts, n):
@@ -90,18 +91,26 @@
     row_count, width = tokens.shape
     side = side_width(n_dest)
     match, pick = one_hot_slots(expert_ids, CAP, n_dest)
-    per_token = jnp.concatenate(
-        [tokens, token_grads, token_side(match, gate_values, forget_flags, n_dest)], axis=1
+    side_cols = token_side(match, gate_values, forget_flags, n_dest)
+    local_count = jnp.sum(side_cols[:, 3 * n_dest].astype(jnp.float32))
+    at_col = jnp.arange(side, dtype=jnp.int32)
+    count_row = jnp.where(
+        at_col == 3 * n_dest + 1,
+        jnp.floor(local_count / 256.0),
+        jnp.where(at_col == 3 * n_dest + 2, local_count - 256.0 * jnp.floor(local_count / 256.0), 0.0),
     )
-    local_count = jnp.sum(forget_flags)
-    at_col = jnp.arange(2 * width + side, dtype=jnp.int32)
-    count_row = jnp.where(
-        at_col == 2 * width + 3 * n_dest + 1,
-        (local_count // 256).astype(jnp.float32),
-        jnp.where(at_col == 2 * width + 3 * n_dest + 2, (local_count % 256).astype(jnp.float32), 0.0),
+    pick_dims = (((0,), (0,)), ((), ()))
+    chosen_tokens = lax.dot_general(pick, tokens, pick_dims, preferred_element_type=jnp.float32)
+    chosen_grads = lax.dot_general(pick, token_grads, pick_dims, preferred_element_type=jnp.float32)
+    chosen_side = lax.dot_general(pick, side_cols, pick_dims, preferred_element_type=jnp.float32)
+    payload = jnp.concatenate(
+        [
+            chosen_tokens.astype(jnp.bfloat16),
+            chosen_grads.astype(jnp.bfloat16),
+            (chosen_side + count_row[None, :]).astype(jnp.bfloat16),
+        ],
+        axis=1,
     )
-    chosen = lax.dot_general(pick, per_token, (((0,), (0,)), ((), ())), preferred_element_type=jnp.float32)
-    payload = (chosen + count_row[None, :]).astype(jnp.bfloat16)
     arrived = lax.all_to_all(payload, "expert", split_axis=0, concat_axis=0, tiled=True)
     slots = arrived.shape[0]
     part_tokens = arrived[:, :width]
@@ -128,13 +137,19 @@
     ff = gate_weight.shape[2]
     w_gate = gate_weight[0].reshape(n_dp, width, ff)
     w_up = up_weight[0].reshape(n_dp, width, ff)
-    w_down = down_weight[0].reshape(ff, n_dp, width)
+    w_down = down_weight[0]
     chunk_dims = (((0, 2), (0, 1)), ((), ()))
     gate_pre = lax.dot_general(slot_tokens, w_gate, chunk_dims, preferred_element_type=jnp.float32)
     up_pre = lax.dot_general(slot_tokens, w_up, chunk_dims, preferred_element_type=jnp.float32)
+    last_dims = (((1,), (1,)), ((), ()))
     hidden_grad = lax.dot_general(
-        slot_grads, w_down, (((0, 2), (1, 2)), ((), ())), preferred_element_type=jnp.float32
+        slot_grads[0], w_down[:, :width], last_dims, preferred_element_type=jnp.float32
     )
+    for j in range(1, n_dp):
+        hidden_grad = hidden_grad + lax.dot_general(
+            slot_grads[j], w_down[:, j * width : (j + 1) * width], last_dims,
+            preferred_element_type=jnp.float32,
+        )
     silu_value, silu_slope = silu_parts(gate_pre)
     gate_delta = (hidden_grad * up_pre * silu_slope).astype(jnp.bfloat16)
     up_delta = (hidden_grad * silu_value).astype(jnp.bfloat16)

time: 80.2 us -> 82.4 us (1.027)
  matrix products: 7.11 us -> 9.18 us
  between operations: 4.86 us -> 3.61 us
  other arithmetic: 8.18 us -> 9.28 us
  waiting for transfers between devices: 38.1 us -> 39 us
    concatenate x0 -> x3, other arithmetic: none -> 2.39 us  [the longest x2 1.56 us: gather_dp(): acc = jnp.concatenate([acc, partner(acc, bit, n)], axis=0)]
    concatenate x1, local copies, waits for them, and re-layouts: 2.38 us -> 0.17 us  [token_side(): return jnp.concatenate([cols, pad], axis=1).astype(jnp.bfloat16)]
    dot_general x2 -> x7, matrix products: 1.51 us -> 3.58 us  [the longest x1 1.26 us: on_device(): lax.dot_general(pick, token_grads, pick_dims, preferred_element_type=jnp....]
    gather x0 -> x1, local copies, waits for them, and re-layouts: none -> 1.93 us  [gather_dp(): return jnp.take(acc, pos, axis=0)]
    select_n x4 -> x3, other arithmetic: 3.02 us -> 1.75 us  [the longest x2 1.75 us: gather_dp(): return jnp.take(acc, pos, axis=0)]
    another operation x4 -> x3, local copies, waits for them, and re-layouts: 1.5 us -> 0.37 us  [the longest x1 1.14 us: on_device(): w_down = down_weight[0].reshape(ff, n_dp, width)]
    ppermute x4, waiting for transfers between devices: 19 us -> 20 us  [partner(): return lax.ppermute(x, 'dp', [(i, i ^ bit) for i in range(n)])]
  transfers between devices with their start and end apart: 6 -> 6, of which waited for: 6 -> 6; matrix products, arithmetic and copies ran while one was open for 5% -> 3% of each run, Pallas kernels for 0% -> 0%
where the time goes in v3:
time: 82.4 us; the launch traced here: 81.8 us
  waiting for transfers between devices  39 us (47%)
  starting transfers between devices  15.7 us (19%)
  other arithmetic  9.28 us (11%)
  matrix products  9.18 us (11%)
  local copies, waits for them, and re-layouts  5.04 us (6%)
  between operations  3.61 us (4%)
    ppermute x4, waiting for transfers between devices, partner(): return lax.ppermute(x, 'dp', [(i, i ^ bit) for i in range(n)])  20 us
    all_to_all x1, waiting for transfers between devices, on_device(): lax.all_to_all(payload, 'expert', split_axis=0, concat_axis=0, tiled=True)  13.8 us
    all_to_all x1, starting transfers between devices, on_device(): lax.all_to_all(payload, 'expert', split_axis=0, concat_axis=0, tiled=True)  7.31 us
    all_to_all x1, waiting for transfers between devices, on_device(): lax.all_to_all(summed, 'expert', split_axis=0, concat_axis=0, tiled=True)  5.28 us
    all_to_all x1, starting transfers between devices, on_device(): lax.all_to_all(summed, 'expert', split_axis=0, concat_axis=0, tiled=True)  4.96 us
    ppermute x4, starting transfers between devices, partner(): return lax.ppermute(x, 'dp', [(i, i ^ bit) for i in range(n)])  3.43 us
    unnamed x12, local copies, waits for them, and re-layouts  2.2 us
    gather x1, local copies, waits for them, and re-layouts, gather_dp(): return jnp.take(acc, pos, axis=0)  1.93 us
  transfers between devices with their start and end apart: 6, of which 6 were waited for; matrix products, arithmetic and copies ran while one was open for 3% of the time, Pallas kernels for 0%

profile of v3, /device:TPU:0, one launch (start us, length us, event | category | flops | bytes accessed | tf_op | source)
XLA Modules:
  0.0 81.8 jit_solution(3307763448043766835)
XLA Ops:
  0.7 0.9 %fusion.24 = s32[256,8]{0,1:T(8,128)S(1)} fusion(s32[256,8]{0,1:T(8,128)} %param.10, s32[8]{0:T(128)S(1)} %iota_multiply_fusion), kind=kLoop, calls=%fused_computation.56 | loop fusion | flops 47104 | bytes 16416 | tf_op jit(solution)/shard_map/reduce_sum | solution.py:14
  1.7 0.7 convert_convert_fusion
  2.4 0.6 convert_reduce_fusion
  4.5 0.8 fusion.25
  5.8 1.3 %convolution_convert_fusion.2 = bf16[128,896]{1,0:T(8,128)(2,1)S(1)} fusion(pred[256,128]{0,1:T(32,128)(4,1)S(1)} %fusion.23, bf16[256,896]{1,0:T(8,128)(2,1)} %param.9), kind=kOutput, calls=%fused_computation.8 | convolution fusion | flops 58834944 | bytes 720896 | tf_op jit(solution)/shard_map/dot_general | solution.py:104
  7.0 1.3 %convolution_convert_fusion.3 = bf16[128,896]{1,0:T(8,128)(2,1)S(1)} fusion(pred[256,128]{0,1:T(32,128)(4,1)S(1)} %fusion.23, bf16[256,896]{1,0:T(8,128)(2,1)} %param.8), kind=kOutput, calls=%fused_computation.9 | convolution fusion | flops 58834944 | bytes 720896 | tf_op jit(solution)/shard_map/dot_general | solution.py:103
  8.7 0.8 %pad_maximum_fusion.2 = bf16[128,1920]{1,0:T(8,128)(2,1)} fusion(bf16[128,128]{1,0:T(8,128)(2,1)S(1)} %fusion.3, bf16[128,896]{1,0:T(8,128)(2,1)S(1)} %convolution_convert_fusion.2, bf16[128,896]{1,0:T(8,128)(2,1)S(1)} %convolution_convert_fusion.3), kind=kLoop, calls=%fused_computation.29 | loop fusion | flops 1474560 | bytes 983040 | tf_op jit(solution)/shard_map/concatenate | solution.py:106
  9.5 7.3 %all-to-all-start = ((bf16[8,16,1920]{2,1,0:T(8,128)(2,1)}), bf16[8,16,1920]{2,1,0:T(8,128)(2,1)S(1)}, u32[]{:S(2)}, u32[]{:S(2)}) async-start(bf16[8,16,1920]{2,1,0:T(8,128)(2,1)} %bitcast.2), calls=%async_computation | async-start | bytes 983040 | tf_op jit(solution)/shard_map/all_to_all | solution.py:114
  16.8 13.8 %all-to-all-done = bf16[8,16,1920]{2,1,0:T(8,128)(2,1)S(1)} async-done(((bf16[8,16,1920]{2,1,0:T(8,128)(2,1)}), bf16[8,16,1920]{2,1,0:T(8,128)(2,1)S(1)}, u32[]{:S(2)}, u32[]{:S(2)}) %all-to-all-start) | async-done | bytes 491552 | tf_op jit(solution)/shard_map/all_to_all | solution.py:114
  30.6 0.7 add_reduce_fusion
  33.2 1.6 %collective-permute-start = (bf16[1,128,1792]{2,1,0:T(8,128)(2,1)S(1)}, bf16[1,128,1792]{2,1,0:T(8,128)(2,1)S(1)}, u32[]{:S(2)}, u32[]{:S(2)}) collective-permute-start(bf16[1,128,1792]{2,1,0:T(8,128)(2,1)S(1)} %maximum_bitcast_fusion), channel_id=1, source_target_pairs={{0,16},{8,24},{16,0},{24,8},{1,17},{9,25},{17,1},{25,9},{2,18},{10... | collective-permute-start | bytes 1376264 | tf_op jit(solution)/shard_map/ppermute | solution.py:52
  34.8 9.6 %collective-permute-done = bf16[1,128,1792]{2,1,0:T(8,128)(2,1)S(1)} collective-permute-done((bf16[1,128,1792]{2,1,0:T(8,128)(2,1)S(1)}, bf16[1,128,1792]{2,1,0:T(8,128)(2,1)S(1)}, u32[]{:S(2)}, u32[]{:S(2)}) %collective-permute-start) | collective-permute-done | bytes 458784 | tf_op jit(solution)/shard_map/ppermute | solution.py:52
  44.4 0.8 copy-done.3
  45.4 2.5 %collective-permute-done.1 = bf16[2,128,1792]{2,1,0:T(8,128)(2,1)} collective-permute-done((bf16[2,128,1792]{2,1,0:T(8,128)(2,1)S(1)}, bf16[2,128,1792]{2,1,0:T(8,128)(2,1)}, u32[]{:S(2)}, u32[]{:S(2)}) %collective-permute-start.1) | collective-permute-done | bytes 917536 | tf_op jit(solution)/shard_map/ppermute | solution.py:52
  47.9 1.5 %pad_maximum_fusion = bf16[4,128,1792]{2,1,0:T(8,128)(2,1)S(1)} fusion(bf16[2,128,1792]{2,1,0:T(8,128)(2,1)} %collective-permute-done.1, bf16[1,128,1792]{2,1,0:T(8,128)(2,1)} %copy-done.3, bf16[1,128,1792]{2,1,0:T(8,128)(2,1)S(1)} %maximum_bitcast_fusion), kind=kLoop, calls=%fused_computation.1 | loop fusion | flops 1835008 | bytes 3670016 | tf_op jit(solution)/shard_map/concatenate | solution.py:60
  49.4 1.9 %gather_fusion = bf16[4,128,1792]{2,1,0:T(8,128)(2,1)} fusion(bf16[4,128,1792]{2,1,0:T(8,128)(2,1)S(1)} %pad_maximum_fusion, s32[1024]{0:T(1024)S(1)} %pad_clamp_fusion), kind=kCustom, calls=%fused_computation | custom fusion | bytes 3670032 | tf_op jit(solution)/shard_map/jit(_take)/gather | solution.py:67
  51.3 1.7 %broadcast_select_fusion = bf16[4,128,1792]{2,1,0:T(8,128)(2,1)S(1)} fusion(bf16[4,128,1792]{2,1,0:T(8,128)(2,1)} %gather_fusion, pred[4]{0:T(512)(128)(4,1)S(1)} %compare_and_fusion), kind=kLoop, calls=%fused_computation.3 | loop fusion | flops 917504 | bytes 3670020 | tf_op jit(solution)/shard_map/jit(_take)/select_n | solution.py:67
  53.1 0.4 convolution_bitcast_fusion.1
  53.5 1.4 %copy-done.5 = bf16[1,128,3584]{2,1,0:T(8,128)(2,1)S(1)} copy-done((bf16[1,128,3584]{2,1,0:T(8,128)(2,1)S(1)}, bf16[1,128,3584]{2,1,0:T(8,128)(2,1)}, u32[]{:S(2)}) %copy-start.5) | copy-done | bytes 917528
  55.4 0.2 convolution_add_fusion.2
  55.9 0.4 fusion.5
  56.3 0.4 fusion.36
  56.7 0.4 add_convert_fusion
  57.4 1.7 %collective-permute-done.2 = bf16[2,128,896]{2,1,0:T(8,128)(2,1)S(1)} collective-permute-done((bf16[2,128,896]{2,1,0:T(8,128)(2,1)S(1)}, bf16[2,128,896]{2,1,0:T(8,128)(2,1)S(1)}, u32[]{:S(2)}, u32[]{:S(2)}) %collective-permute-start.2) | collective-permute-done | bytes 458784 | tf_op jit(solution)/shard_map/ppermute | solution.py:52
  59.3 1.6 %collective-permute-start.3 = (bf16[1,128,896]{2,1,0:T(8,128)(2,1)S(1)}, bf16[1,128,896]{2,1,0:T(8,128)(2,1)S(1)}, u32[]{:S(2)}, u32[]{:S(2)}) collective-permute-start(bf16[1,128,896]{2,1,0:T(8,128)(2,1)S(1)} %fusion.15), channel_id=1, source_target_pairs={{0,16},{8,24},{16,0},{24,8},{1,17},{9,25},{17,1},{25,9},{2,18},{10... | collective-permute-start | bytes 688136 | tf_op jit(solution)/shard_map/ppermute | solution.py:52
  60.9 6.1 %collective-permute-done.3 = bf16[1,128,896]{2,1,0:T(8,128)(2,1)S(1)} collective-permute-done((bf16[1,128,896]{2,1,0:T(8,128)(2,1)S(1)}, bf16[1,128,896]{2,1,0:T(8,128)(2,1)S(1)}, u32[]{:S(2)}, u32[]{:S(2)}) %collective-permute-start.3) | collective-permute-done | bytes 229408 | tf_op jit(solution)/shard_map/ppermute | solution.py:52
  67.0 0.7 fusion.13
  67.7 5.0 %all-to-all-start.1 = ((bf16[8,16,896]{2,1,0:T(8,128)(2,1)}), bf16[8,16,896]{2,1,0:T(8,128)(2,1)S(1)}, u32[]{:S(2)}, u32[]{:S(2)}) async-start(bf16[8,16,896]{2,1,0:T(8,128)(2,1)} %bitcast.34), calls=%async_computation.1 | async-start | bytes 458752 | tf_op jit(solution)/shard_map/all_to_all | solution.py:168
  72.7 1.4 %convolution_convert_fusion.1 = bf16[4,896,128]{2,1,0:T(8,128)(2,1)} fusion(bf16[128,128,1]{1,0,2:T(8,128)(2,1)S(1)} %fusion.5, bf16[4,128,1792]{2,1,0:T(8,128)(2,1)S(1)} %copy-done.2), kind=kOutput, calls=%fused_computation.5 | convolution fusion | flops 117899264 | bytes 1867776 | tf_op jit(solution)/shard_map/dot_general | solution.py:157
  74.1 1.4 %convolution_convert_fusion = bf16[4,896,128]{2,1,0:T(8,128)(2,1)} fusion(bf16[4,128,1792]{2,1,0:T(8,128)(2,1)S(1)} %copy-done.2, bf16[128,128]{1,0:T(8,128)(2,1)S(1)} %get-tuple-element.6), kind=kOutput, calls=%fused_computation.4 | convolution fusion | flops 117899264 | bytes 1867776 | tf_op jit(solution)/shard_map/dot_general | solution.py:160
  75.4 5.3 %all-to-all-done.1 = bf16[8,16,896]{2,1,0:T(8,128)(2,1)S(1)} async-done(((bf16[8,16,896]{2,1,0:T(8,128)(2,1)}), bf16[8,16,896]{2,1,0:T(8,128)(2,1)S(1)}, u32[]{:S(2)}, u32[]{:S(2)}) %all-to-all-start.1) | async-done | bytes 229408 | tf_op jit(solution)/shard_map/all_to_all | solution.py:168
  80.7 1.1 %fusion = bf16[256,896]{1,0:T(8,128)(2,1)} fusion(bf16[8,16,896]{2,1,0:T(8,128)(2,1)S(1)} %all-to-all-done.1, f32[256,8]{0,1:T(8,128)S(1)} %fusion.14, pred[256,8]{0,1:T(8,128)(4,1)S(1)} %broadcast_compare_fusion), kind=kOutput, calls=%fused_computation.7 | convolution fusion | flops 59015168 | bytes 698368 | tf_op jit(solution)/shard_map/dot_general | solution.py:169
  (46 shorter events, 3.1 us)
Async XLA Ops:
  0.6 52.4 %copy-start = (bf16[1,3584,128]{2,1,0:T(8,128)(2,1)S(1)}, bf16[1,3584,128]{2,1,0:T(8,128)(2,1)}, u32[]{:S(2)}) copy-start(bf16[1,3584,128]{2,1,0:T(8,128)(2,1)} %param.13) | copy-start | bytes 2752516
  9.5 21.1 %all-to-all-start = ((bf16[8,16,1920]{2,1,0:T(8,128)(2,1)}), bf16[8,16,1920]{2,1,0:T(8,128)(2,1)S(1)}, u32[]{:S(2)}, u32[]{:S(2)}) async-start(bf16[8,16,1920]{2,1,0:T(8,128)(2,1)} %bitcast.2), calls=%async_computation | async-start | bytes 983040 | tf_op jit(solution)/shard_map/all_to_all | solution.py:114
  33.2 11.2 %collective-permute-start = (bf16[1,128,1792]{2,1,0:T(8,128)(2,1)S(1)}, bf16[1,128,1792]{2,1,0:T(8,128)(2,1)S(1)}, u32[]{:S(2)}, u32[]{:S(2)}) collective-permute-start(bf16[1,128,1792]{2,1,0:T(8,128)(2,1)S(1)} %maximum_bitcast_fusion), channel_id=1, source_target_pairs={{0,16},{8,24},{16,0},{24,8},{1,17},{9,25},{17,1},{25,9},{2,18},{10... | collective-permute-start | bytes 1376264 | tf_op jit(solution)/shard_map/ppermute | solution.py:52
  44.4 0.8 copy-start.3
  45.3 2.7 %collective-permute-start.1 = (bf16[2,128,1792]{2,1,0:T(8,128)(2,1)S(1)}, bf16[2,128,1792]{2,1,0:T(8,128)(2,1)}, u32[]{:S(2)}, u32[]{:S(2)}) collective-permute-start(bf16[2,128,1792]{2,1,0:T(8,128)(2,1)S(1)} %pad_maximum_fusion.1), channel_id=1, source_target_pairs={{0,8},{8,0},{16,24},{24,16},{1,9},{9,1},{17,25},{25,17},{2,10},{10... | collective-permute-start | bytes 2752520 | tf_op jit(solution)/shard_map/ppermute | solution.py:52
  53.1 2.8 %copy-start.1 = (bf16[4,128,1792]{2,1,0:T(8,128)(2,1)}, bf16[4,128,1792]{2,1,0:T(8,128)(2,1)S(1)}, u32[]{:S(2)}) copy-start(bf16[4,128,1792]{2,1,0:T(8,128)(2,1)S(1)} %broadcast_select_fusion) | copy-start | bytes 5505028
  53.1 1.8 %copy-start.5 = (bf16[1,128,3584]{2,1,0:T(8,128)(2,1)S(1)}, bf16[1,128,3584]{2,1,0:T(8,128)(2,1)}, u32[]{:S(2)}) copy-start(bf16[1,128,3584]{2,1,0:T(8,128)(2,1)} %param.15) | copy-start | bytes 2752516
  53.1 2.8 %copy-start.4 = (bf16[1,3584,128]{2,1,0:T(8,128)(2,1)S(1)}, bf16[1,3584,128]{2,1,0:T(8,128)(2,1)}, u32[]{:S(2)}) copy-start(bf16[1,3584,128]{2,1,0:T(8,128)(2,1)} %param.14) | copy-start | bytes 2752516
  57.2 1.9 %collective-permute-start.2 = (bf16[2,128,896]{2,1,0:T(8,128)(2,1)S(1)}, bf16[2,128,896]{2,1,0:T(8,128)(2,1)S(1)}, u32[]{:S(2)}, u32[]{:S(2)}) collective-permute-start(bf16[2,128,896]{2,1,0:T(8,128)(2,1)S(1)} %fusion.11), channel_id=1, source_target_pairs={{0,8},{8,0},{16,24},{24,16},{1,9},{9,1},{17,25},{25,17},{2,10},{10... | collective-permute-start | bytes 1376264 | tf_op jit(solution)/shard_map/ppermute | solution.py:52
  59.2 13.5 %copy-start.2 = (bf16[4,128,1792]{2,1,0:T(8,128)(2,1)S(1)}, bf16[4,128,1792]{2,1,0:T(8,128)(2,1)}, u32[]{:S(2)}) copy-start(bf16[4,128,1792]{2,1,0:T(8,128)(2,1)} %copy-done.1) | copy-start | bytes 5505028
  59.3 7.7 %collective-permute-start.3 = (bf16[1,128,896]{2,1,0:T(8,128)(2,1)S(1)}, bf16[1,128,896]{2,1,0:T(8,128)(2,1)S(1)}, u32[]{:S(2)}, u32[]{:S(2)}) collective-permute-start(bf16[1,128,896]{2,1,0:T(8,128)(2,1)S(1)} %fusion.15), channel_id=1, source_target_pairs={{0,16},{8,24},{16,0},{24,8},{1,17},{9,25},{17,1},{25,9},{2,18},{10... | collective-permute-start | bytes 688136 | tf_op jit(solution)/shard_map/ppermute | solution.py:52
  67.7 13.0 %all-to-all-start.1 = ((bf16[8,16,896]{2,1,0:T(8,128)(2,1)}), bf16[8,16,896]{2,1,0:T(8,128)(2,1)S(1)}, u32[]{:S(2)}, u32[]{:S(2)}) async-start(bf16[8,16,896]{2,1,0:T(8,128)(2,1)} %bitcast.34), calls=%async_computation.1 | async-start | bytes 458752 | tf_op jit(solution)/shard_map/all_to_all | solution.py:168

commit v4 on v2

--- a/solution.py
+++ b/solution.py
@@ -2,23 +2,100 @@
 import jax.numpy as jnp
 from jax import lax
 from jax.sharding import PartitionSpec as P
+from jax.experimental import pallas as pl
+from jax.experimental.pallas import tpu as pltpu
 
 EXP_DEV = 8
 CAP = 16
 
 
-def one_hot_slots(expert_ids, capacity, n_dest):
-    row_count = expert_ids.shape[0]
-    edited = jnp.arange(n_dest, dtype=jnp.int32) * EXP_DEV
-    match = expert_ids[:, :, None] == edited[None, None, :]
-    hits = jnp.sum(match.astype(jnp.int32), axis=1)
-    before = (
-        jnp.arange(row_count, dtype=jnp.int32)[:, None] > jnp.arange(row_count, dtype=jnp.int32)[None, :]
-    ).astype(jnp.bfloat16)
-    rank = jnp.dot(before, hits.astype(jnp.bfloat16), preferred_element_type=jnp.float32)
-    places = jnp.arange(capacity, dtype=jnp.float32)
-    taken = (hits[:, :, None] == 1) & (rank[:, :, None] == places[None, None, :])
-    return match, taken.reshape(row_count, n_dest * capacity).astype(jnp.bfloat16)
+def glue_kernel(n_dest, width, side, split, ids_ref, gates_ref, flags_ref, tok_ref, grd_ref, *outs):
+    f32, bf16 = jnp.float32, jnp.bfloat16
+    rows = tok_ref.shape[0]
+    slots = n_dest * CAP
+    lanes = max(16, -(-n_dest // 16) * 16)
+    ids = ids_ref[...]
+    gates = gates_ref[...]
+    flags = flags_ref[...].astype(f32)
+    dest = lax.broadcasted_iota(jnp.int32, (lanes, rows), 0)
+    edited = dest * EXP_DEV
+    valid = dest < n_dest
+    hits = jnp.zeros((lanes, rows), f32)
+    gsel = jnp.zeros((lanes, rows), f32)
+    for k in range(ids.shape[0]):
+        m = (ids[k : k + 1, :] == edited) & valid
+        hits = hits + jnp.where(m, 1.0, 0.0)
+        gsel = gsel + jnp.where(m, gates[k : k + 1, :], 0.0)
+    before = jnp.where(
+        lax.broadcasted_iota(jnp.int32, (rows, rows), 0) < lax.broadcasted_iota(jnp.int32, (rows, rows), 1),
+        1.0, 0.0,
+    ).astype(bf16)
+    rank = jnp.dot(hits.astype(bf16), before, preferred_element_type=f32)
+    slot_of = lax.broadcasted_iota(jnp.int32, (slots, lanes), 0)
+    expand = jnp.where(
+        lax.shift_right_logical(slot_of, 4) == lax.broadcasted_iota(jnp.int32, (slots, lanes), 1), 1.0, 0.0
+    ).astype(bf16)
+    hit_s = jnp.dot(expand, hits.astype(bf16), preferred_element_type=f32)
+    rank_s = jnp.dot(expand, rank.astype(bf16), preferred_element_type=f32)
+    place = (lax.broadcasted_iota(jnp.int32, (slots, rows), 0) & (CAP - 1)).astype(f32)
+    pick = jnp.where((hit_s == 1.0) & (rank_s == place), 1.0, 0.0)
+    pick_b = pick.astype(bf16)
+    tok = jnp.dot(pick_b, tok_ref[...], preferred_element_type=f32).astype(bf16)
+    grd = jnp.dot(pick_b, grd_ref[...], preferred_element_type=f32).astype(bf16)
+    hi = gsel.astype(bf16).astype(f32)
+    rest = gsel - hi
+    mid = rest.astype(bf16).astype(f32)
+    lo = rest - mid
+
+    def per_slot(x):
+        spread = jnp.dot(expand, x.astype(bf16), preferred_element_type=f32)
+        return jnp.sum(spread * pick, axis=1, keepdims=True)
+
+    s_hi, s_mid, s_lo = per_slot(hi), per_slot(mid), per_slot(lo)
+    s_flag = jnp.sum(pick * flags, axis=1, keepdims=True)
+    count = jnp.sum(flags, axis=1, keepdims=True)
+    c_hi = jnp.floor(count / 256.0)
+    c_lo = count - 256.0 * c_hi
+    col = lax.broadcasted_iota(jnp.int32, (slots, side), 1)
+    side_v = jnp.where(col == 0, s_hi, 0.0)
+    for c, v in ((1, s_mid), (2, s_lo), (3, s_flag), (4, c_hi), (5, c_lo)):
+        side_v = jnp.where(col == c, v, side_v)
+    side_v = side_v.astype(bf16)
+    if split:
+        tok_out, grd_out, side_out, pick_out = outs
+        tok_out[...] = tok
+        grd_out[...] = grd
+        side_out[...] = side_v
+    else:
+        pay_out, pick_out = outs
+        pay_out[:, :width] = tok
+        pay_out[:, width : 2 * width] = grd
+        pay_out[:, 2 * width :] = side_v
+    pick_out[...] = pick_b
+
+
+def glue(expert_ids, gate_values, forget_flags, tokens, token_grads, n_dest):
+    import functools
+
+    rows, width = tokens.shape
+    slots = n_dest * CAP
+    side = 128
+    split = width % 128 != 0
+    bf16 = jnp.bfloat16
+    if split:
+        shapes = [(slots, width), (slots, width), (slots, side), (slots, rows)]
+    else:
+        shapes = [(slots, 2 * width + side), (slots, rows)]
+    vmem = pl.BlockSpec(memory_space=pltpu.VMEM)
+    outs = pl.pallas_call(
+        functools.partial(glue_kernel, n_dest, width, side, split),
+        out_shape=[jax.ShapeDtypeStruct(s, bf16) for s in shapes],
+        in_specs=[vmem] * 5,
+        out_specs=[vmem] * len(shapes),
+    )(expert_ids.T, gate_values.T, forget_flags.reshape(1, rows), tokens, token_grads)
+    if split:
+        return jnp.concatenate(outs[:3], axis=1), outs[3]
+    return outs[0], outs[1]
 
 
 def silu_parts(pre):
@@ -28,24 +105,6 @@
 
 def bf16_part(x):
     return lax.reduce_precision(x, exponent_bits=8, mantissa_bits=7)
-
-
-def side_width(n_dest):
-    return -(-(3 * n_dest + 3) // 128) * 128
-
-
-def token_side(match, gate_values, forget_flags, n_dest):
-    gate_sel = jnp.sum(
-        jnp.where(match, gate_values[:, :, None], jnp.zeros((), gate_values.dtype)), axis=1
-    )
-    hi = bf16_part(gate_sel)
-    rest = gate_sel - hi
-    mid = bf16_part(rest)
-    lo = rest - mid
-    flag = forget_flags.astype(jnp.float32)[:, None]
-    cols = jnp.concatenate([hi, mid, lo, flag], axis=1)
-    pad = jnp.zeros((cols.shape[0], side_width(n_dest) - cols.shape[1]), jnp.float32)
-    return jnp.concatenate([cols, pad], axis=1).astype(jnp.bfloat16)
 
 
 def partner(x, bit, n):
@@ -86,32 +145,18 @@
 ):
     n_dest = lax.axis_size("expert")
     n_dp = lax.axis_size("dp")
-    me = lax.axis_index("expert")
     row_count, width = tokens.shape
-    side = side_width(n_dest)
-    match, pick = one_hot_slots(expert_ids, CAP, n_dest)
-    per_token = jnp.concatenate(
-        [tokens, token_grads, token_side(match, gate_values, forget_flags, n_dest)], axis=1
-    )
-    local_count = jnp.sum(forget_flags)
-    at_col = jnp.arange(2 * width + side, dtype=jnp.int32)
-    count_row = jnp.where(
-        at_col == 2 * width + 3 * n_dest + 1,
-        (local_count // 256).astype(jnp.float32),
-        jnp.where(at_col == 2 * width + 3 * n_dest + 2, (local_count % 256).astype(jnp.float32), 0.0),
-    )
-    chosen = lax.dot_general(pick, per_token, (((0,), (0,)), ((), ())), preferred_element_type=jnp.float32)
-    payload = (chosen + count_row[None, :]).astype(jnp.bfloat16)
+    payload, pick_t = glue(expert_ids, gate_values, forget_flags, tokens, token_grads, n_dest)
+    side = payload.shape[1] - 2 * width
     arrived = lax.all_to_all(payload, "expert", split_axis=0, concat_axis=0, tiled=True)
     slots = arrived.shape[0]
     part_tokens = arrived[:, :width]
     raw_grads = arrived[:, width : 2 * width]
     info = arrived[:, 2 * width :].astype(jnp.float32)
-    pieces = lax.dynamic_slice_in_dim(info[:, : 3 * n_dest].reshape(slots, 3, n_dest), me, 1, axis=2)
-    gate_sel = (pieces[:, 0, 0] + pieces[:, 1, 0]) + pieces[:, 2, 0]
-    flag = info[:, 3 * n_dest]
+    gate_sel = (info[:, 0] + info[:, 1]) + info[:, 2]
+    flag = info[:, 3]
     by_block = info.reshape(n_dest, CAP, side)[:, 0]
-    forget_count = jnp.sum(by_block[:, 3 * n_dest + 1] * 256.0 + by_block[:, 3 * n_dest + 2])
+    forget_count = jnp.sum(by_block[:, 4] * 256.0 + by_block[:, 5])
     all_rows = row_count * n_dest
     half_total = jnp.float32(all_rows) / 2.0
     weight = jnp.where(
@@ -151,7 +196,9 @@
     part = (from_gate + from_up).astype(jnp.bfloat16)
     summed = scatter_dp(jnp.swapaxes(part, 1, 2), n_dp).astype(jnp.bfloat16)
     returned = lax.all_to_all(summed, "expert", split_axis=0, concat_axis=0, tiled=True)
-    input_grad = lax.dot_general(pick, returned, slot_dims, preferred_element_type=jnp.float32)
+    input_grad = lax.dot_general(
+        pick_t, returned, (((0,), (0,)), ((), ())), preferred_element_type=jnp.float32
+    )
     return (
         grad_gate.reshape(1, n_dp * width, ff),
         grad_up.reshape(1, n_dp * width, ff),

time: 80.2 us -> 72.1 us (0.90)
  blocking collectives: 0 us -> 21.1 us
  waiting for transfers between devices: 38.1 us -> 24.3 us
  starting transfers between devices: 15.6 us -> 7.68 us
  local copies, waits for them, and re-layouts: 5.85 us -> 2.72 us
  other arithmetic: 8.18 us -> 5.1 us
  Pallas kernels: 0 us -> 2.75 us
  between operations: 4.86 us -> 2.19 us
  matrix products: 7.11 us -> 5.83 us
    all_to_all x0 -> x1, blocking collectives: none -> 21.1 us  [on_device(): lax.all_to_all(payload, 'expert', split_axis=0, concat_axis=0, tiled=True)]
    all_to_all x1 -> x0, waiting for transfers between devices: 13.8 us -> none  [on_device(): lax.all_to_all(payload, 'expert', split_axis=0, concat_axis=0, tiled=True)]
    all_to_all x1 -> x0, starting transfers between devices: 7.31 us -> none  [on_device(): lax.all_to_all(payload, 'expert', split_axis=0, concat_axis=0, tiled=True)]
    reduce_sum x4 -> x1, other arithmetic: 3.67 us -> 0.67 us  [on_device(): forget_count = jnp.sum(by_block[:, 4] * 256.0 + by_block[:, 5])]
    pallas_call x0 -> x1, Pallas kernels: none -> 2.75 us  [glue(): pl.pallas_call(functools.partial(glue_kernel, n_dest, width, side, split)...]
    concatenate x1 -> x0, local copies, waits for them, and re-layouts: 2.38 us -> none  [on_device(): jnp.concatenate([tokens, token_grads, token_side(match, gate_values, forg...]
    dot_general x3 -> x1, matrix products: 2.36 us -> 1.08 us  [on_device(): lax.dot_general(pick_t, returned, (((0,), (0,)), ((), ())), preferred_ele...]
  transfers between devices with their start and end apart: 6 -> 5, of which waited for: 6 -> 5; matrix products, arithmetic and copies ran while one was open for 5% -> 6% of each run, Pallas kernels for 0% -> 0%
where the time goes in v4:
time: 72.1 us; the launch traced here: 71.7 us
  waiting for transfers between devices  24.3 us (34%)
  blocking collectives  21.1 us (29%)
  starting transfers between devices  7.68 us (11%)
  matrix products  5.83 us (8%)
  other arithmetic  5.1 us (7%)
  Pallas kernels  2.75 us (4%)
  local copies, waits for them, and re-layouts  2.72 us (4%)
  between operations  2.19 us (3%)
    all_to_all x1, blocking collectives, on_device(): lax.all_to_all(payload, 'expert', split_axis=0, concat_axis=0, tiled=True)  21.1 us
    ppermute x4, waiting for transfers between devices, partner(): return lax.ppermute(x, 'dp', [(i, i ^ bit) for i in range(n)])  19.1 us
    all_to_all x1, waiting for transfers between devices, on_device(): lax.all_to_all(summed, 'expert', split_axis=0, concat_axis=0, tiled=True)  5.27 us
    all_to_all x1, starting transfers between devices, on_device(): lax.all_to_all(summed, 'expert', split_axis=0, concat_axis=0, tiled=True)  4.37 us
    ppermute x4, starting transfers between devices, partner(): return lax.ppermute(x, 'dp', [(i, i ^ bit) for i in range(n)])  3.31 us
    select_n x3, other arithmetic, gather_dp(): acc = jnp.where(me & bit == 0, low_first, high_first)  3.05 us
    pallas_call x1, Pallas kernels, glue(): pl.pallas_call(functools.partial(glue_kernel, n_dest, width, side, split)...  2.75 us
  transfers between devices with their start and end apart: 5, of which 5 were waited for; matrix products, arithmetic and copies ran while one was open for 6% of the time, Pallas kernels for 0%

profile of v4, /device:TPU:0, one launch (start us, length us, event | category | flops | bytes accessed | tf_op | source)
XLA Modules:
  0.0 71.7 jit_solution(12292279897424449922)
XLA Ops:
  0.6 2.7 %shard_map.103 = (bf16[128,1920]{1,0:T(8,128)(2,1)}, bf16[128,256]{1,0:T(8,128)(2,1)}) custom-call(s32[8,256]{1,0:T(8,128)} %bitcast.102, f32[8,256]{1,0:T(8,128)} %bitcast.103, s32[1,256]{1,0:T(1,128)} %bitcast.104, bf16[256,896]{1,0:T(8,128)(2,1)} %tok_ref.1, bf16[256,896]{1,0:T(8,128)(2,1)} %grd_ref.1), custom_call_target="tpu_custom_call" | custom-call | tf_op jit(solution)/shard_map/pallas_call | solution.py:90
  3.4 21.1 %all_to_all.21 = bf16[8,16,1920]{2,1,0:T(8,128)(2,1)S(1)} all-to-all(bf16[8,16,1920]{2,1,0:T(8,128)(2,1)} %bitcast.100), channel_id=1, replica_groups=mesh['dp'=4,'expert'=8] {'expert'}, dimensions={0} | all-to-all | bytes 983040 | tf_op jit(solution)/shard_map/all_to_all | solution.py:151
  24.6 0.7 add_reduce_fusion
  26.6 0.2 fusion.18
  26.8 0.1 multiply_convert_fusion
  26.9 0.1 fusion.15
  27.0 1.5 %collective-permute-start = (bf16[1,128,1792]{2,1,0:T(8,128)(2,1)S(1)}, bf16[1,128,1792]{2,1,0:T(8,128)(2,1)S(1)}, u32[]{:S(2)}, u32[]{:S(2)}) collective-permute-start(bf16[1,128,1792]{2,1,0:T(8,128)(2,1)S(1)} %get-tuple-element.8), channel_id=1, source_target_pairs={{0,16},{8,24},{16,0},{24,8},{1,17},{9,25},{17,1},{25,9},{2,18},{10... | collective-permute-start | bytes 1376264 | tf_op jit(solution)/shard_map/ppermute | solution.py:111
  28.6 9.7 %collective-permute-done = bf16[1,128,1792]{2,1,0:T(8,128)(2,1)S(1)} collective-permute-done((bf16[1,128,1792]{2,1,0:T(8,128)(2,1)S(1)}, bf16[1,128,1792]{2,1,0:T(8,128)(2,1)S(1)}, u32[]{:S(2)}, u32[]{:S(2)}) %collective-permute-start) | collective-permute-done | bytes 458784 | tf_op jit(solution)/shard_map/ppermute | solution.py:111
  38.3 1.1 %maximum_select_fusion.2 = bf16[2,128,1792]{2,1,0:T(8,128)(2,1)} fusion(bf16[1,128,1792]{2,1,0:T(8,128)(2,1)S(1)} %collective-permute-done, bf16[1,128,1792]{2,1,0:T(8,128)(2,1)S(1)} %get-tuple-element.8, pred[]{:T(512)S(6)} %eq.14), kind=kLoop, calls=%fused_computation.14 | loop fusion | flops 1376256 | bytes 1835009 | tf_op jit(solution)/shard_map/jit(_where)/select_n | solution.py:122
  39.3 1.1 %reshape_squeeze.9 = bf16[128,4,896]{2,1,0:T(4,128)(2,1)} reshape(bf16[1,128,3584]{2,1,0:T(8,128)(2,1)S(1)} %copy-done.4) | data formatting | bytes 1835008 | tf_op jit(solution)/shard_map/reshape;squeeze | solution.py:176
  40.5 0.2 maximum_select_fusion.1
  40.6 1.5 %collective-permute-done.1 = bf16[2,128,1792]{2,1,0:T(8,128)(2,1)} collective-permute-done((bf16[2,128,1792]{2,1,0:T(8,128)(2,1)}, bf16[2,128,1792]{2,1,0:T(8,128)(2,1)}, u32[]{:S(2)}, u32[]{:S(2)}) %collective-permute-start.1) | collective-permute-done | bytes 917536 | tf_op jit(solution)/shard_map/ppermute | solution.py:111
  42.1 1.8 %maximum_select_fusion = bf16[2,2,128,1792]{3,2,0,1:T(8,128)(2,1)S(1)} fusion(bf16[2,1,128,1792]{3,2,0,1:T(8,128)(2,1)} %bitcast.10, bf16[2,1,128,1792]{3,2,0,1:T(8,128)(2,1)S(1)} %maximum_select_fusion.1, pred[]{:T(512)S(6)} %eq.13), kind=kLoop, calls=%fused_computation | loop fusion | flops 2752512 | bytes 3670017 | tf_op jit(solution)/shard_map/jit(_where)/select_n | solution.py:122
  44.0 0.1 copy.28
  44.2 0.4 convolution_bitcast_fusion
  44.6 1.4 %copy-done.5 = bf16[128,4,896]{2,1,0:T(4,128)(2,1)S(1)} copy-done((bf16[128,4,896]{2,1,0:T(4,128)(2,1)S(1)}, bf16[128,4,896]{2,1,0:T(4,128)(2,1)}, u32[]{:S(2)}) %copy-start.5) | copy-done | bytes 917528
  46.0 0.4 multiply_convert_fusion.1
  46.4 0.4 fusion.3
  46.8 0.4 fusion.21
  47.2 0.4 add_convert_fusion
  47.6 0.1 fusion.11
  47.7 0.2 collective-permute-start.2
  47.9 1.7 %collective-permute-done.2 = bf16[2,128,896]{2,1,0:T(8,128)(2,1)S(1)} collective-permute-done((bf16[2,128,896]{2,1,0:T(8,128)(2,1)S(1)}, bf16[2,128,896]{2,1,0:T(8,128)(2,1)S(1)}, u32[]{:S(2)}, u32[]{:S(2)}) %collective-permute-start.2) | collective-permute-done | bytes 458784 | tf_op jit(solution)/shard_map/ppermute | solution.py:111
  49.6 0.2 fusion.5
  49.8 1.6 %collective-permute-start.3 = (bf16[1,128,896]{2,1,0:T(8,128)(2,1)S(1)}, bf16[1,128,896]{2,1,0:T(8,128)(2,1)S(1)}, u32[]{:S(2)}, u32[]{:S(2)}) collective-permute-start(bf16[1,128,896]{2,1,0:T(8,128)(2,1)S(1)} %fusion.16), channel_id=1, source_target_pairs={{0,16},{8,24},{16,0},{24,8},{1,17},{9,25},{17,1},{25,9},{2,18},{10... | collective-permute-start | bytes 688136 | tf_op jit(solution)/shard_map/ppermute | solution.py:111
  51.4 6.2 %collective-permute-done.3 = bf16[1,128,896]{2,1,0:T(8,128)(2,1)S(1)} collective-permute-done((bf16[1,128,896]{2,1,0:T(8,128)(2,1)S(1)}, bf16[1,128,896]{2,1,0:T(8,128)(2,1)S(1)}, u32[]{:S(2)}, u32[]{:S(2)}) %collective-permute-start.3) | collective-permute-done | bytes 229408 | tf_op jit(solution)/shard_map/ppermute | solution.py:111
  57.5 0.7 %fusion.13 = bf16[1,128,896]{2,1,0:T(8,128)(2,1)} fusion(bf16[1,128,896]{2,1,0:T(8,128)(2,1)S(1)} %collective-permute-done.3, f32[1,2,128,896]{3,2,1,0:T(8,128)S(1)} %fusion.5, pred[]{:T(512)S(6)} %ne.6), kind=kLoop, calls=%fused_computation.28 | loop fusion | flops 458752 | bytes 1376257 | tf_op jit(solution)/shard_map/convert_element_type | solution.py:197
  58.3 4.4 %all-to-all-start.1 = ((bf16[8,16,896]{2,1,0:T(8,128)(2,1)}), bf16[8,16,896]{2,1,0:T(8,128)(2,1)S(1)}, u32[]{:S(2)}, u32[]{:S(2)}) async-start(bf16[8,16,896]{2,1,0:T(8,128)(2,1)} %bitcast.32), calls=%async_computation.1 | async-start | bytes 458752 | tf_op jit(solution)/shard_map/all_to_all | solution.py:198
  62.6 1.4 %convolution_convert_fusion.1 = bf16[4,896,128]{2,1,0:T(8,128)(2,1)} fusion(bf16[128,128,1]{1,0,2:T(8,128)(2,1)S(1)} %fusion.3, bf16[4,128,1792]{2,1,0:T(8,128)(2,1)S(1)} %bitcast.88), kind=kOutput, calls=%fused_computation.3 | convolution fusion | flops 117899264 | bytes 1867776 | tf_op jit(solution)/shard_map/dot_general | solution.py:187
  64.0 1.4 %convolution_convert_fusion = bf16[4,896,128]{2,1,0:T(8,128)(2,1)} fusion(bf16[4,128,1792]{2,1,0:T(8,128)(2,1)S(1)} %bitcast.89, bf16[128,128]{1,0:T(8,128)(2,1)S(1)} %get-tuple-element.9), kind=kOutput, calls=%fused_computation.2 | convolution fusion | flops 117899264 | bytes 1867776 | tf_op jit(solution)/shard_map/dot_general | solution.py:190
  65.4 5.3 %all-to-all-done.1 = bf16[8,16,896]{2,1,0:T(8,128)(2,1)S(1)} async-done(((bf16[8,16,896]{2,1,0:T(8,128)(2,1)}), bf16[8,16,896]{2,1,0:T(8,128)(2,1)S(1)}, u32[]{:S(2)}, u32[]{:S(2)}) %all-to-all-start.1) | async-done | bytes 229408 | tf_op jit(solution)/shard_map/all_to_all | solution.py:198
  70.6 1.1 %convolution_convert_fusion.2 = bf16[256,896]{1,0:T(8,128)(2,1)} fusion(bf16[128,256]{1,0:T(8,128)(2,1)S(1)} %copy-done.6, bf16[128,896]{1,0:T(8,128)(2,1)S(1)} %bitcast.99), kind=kOutput, calls=%fused_computation.4 | convolution fusion | flops 58949632 | bytes 753664 | tf_op jit(solution)/shard_map/dot_general | solution.py:199
  (18 shorter events, 0.1 us)
Async XLA Ops:
  0.6 43.5 %copy-start = (bf16[1,3584,128]{2,1,0:T(8,128)(2,1)S(1)}, bf16[1,3584,128]{2,1,0:T(8,128)(2,1)}, u32[]{:S(2)}) copy-start(bf16[1,3584,128]{2,1,0:T(8,128)(2,1)} %param.13) | copy-start | bytes 2752516
  26.8 12.5 %copy-start.4 = (bf16[1,128,3584]{2,1,0:T(8,128)(2,1)S(1)}, bf16[1,128,3584]{2,1,0:T(8,128)(2,1)}, u32[]{:S(2)}) copy-start(bf16[1,128,3584]{2,1,0:T(8,128)(2,1)} %param.15) | copy-start | bytes 2752516
  27.0 11.2 %collective-permute-start = (bf16[1,128,1792]{2,1,0:T(8,128)(2,1)S(1)}, bf16[1,128,1792]{2,1,0:T(8,128)(2,1)S(1)}, u32[]{:S(2)}, u32[]{:S(2)}) collective-permute-start(bf16[1,128,1792]{2,1,0:T(8,128)(2,1)S(1)} %get-tuple-element.8), channel_id=1, source_target_pairs={{0,16},{8,24},{16,0},{24,8},{1,17},{9,25},{17,1},{25,9},{2,18},{10... | collective-permute-start | bytes 1376264 | tf_op jit(solution)/shard_map/ppermute | solution.py:111
  39.3 2.8 %collective-permute-start.1 = (bf16[2,128,1792]{2,1,0:T(8,128)(2,1)}, bf16[2,128,1792]{2,1,0:T(8,128)(2,1)}, u32[]{:S(2)}, u32[]{:S(2)}) collective-permute-start(bf16[2,128,1792]{2,1,0:T(8,128)(2,1)} %maximum_select_fusion.2), channel_id=1, source_target_pairs={{0,8},{8,0},{16,24},{24,16},{1,9},{9,1},{17,25},{25,17},{2,10},{10... | collective-permute-start | bytes 2752520 | tf_op jit(solution)/shard_map/ppermute | solution.py:111
  44.1 2.3 %copy-start.1 = (bf16[2,2,128,1792]{3,2,1,0:T(8,128)(2,1)}, bf16[2,2,128,1792]{3,2,1,0:T(8,128)(2,1)S(1)}, u32[]{:S(2)}) copy-start(bf16[2,2,128,1792]{3,2,1,0:T(8,128)(2,1)S(1)} %copy.28) | copy-start | bytes 5505028
  44.1 1.8 %copy-start.5 = (bf16[128,4,896]{2,1,0:T(4,128)(2,1)S(1)}, bf16[128,4,896]{2,1,0:T(4,128)(2,1)}, u32[]{:S(2)}) copy-start(bf16[128,4,896]{2,1,0:T(4,128)(2,1)} %reshape_squeeze.9) | copy-start | bytes 2752516
  44.1 2.3 %copy-start.3 = (bf16[1,3584,128]{2,1,0:T(8,128)(2,1)S(1)}, bf16[1,3584,128]{2,1,0:T(8,128)(2,1)}, u32[]{:S(2)}) copy-start(bf16[1,3584,128]{2,1,0:T(8,128)(2,1)} %param.14) | copy-start | bytes 2752516
  47.7 1.9 %collective-permute-start.2 = (bf16[2,128,896]{2,1,0:T(8,128)(2,1)S(1)}, bf16[2,128,896]{2,1,0:T(8,128)(2,1)S(1)}, u32[]{:S(2)}, u32[]{:S(2)}) collective-permute-start(bf16[2,128,896]{2,1,0:T(8,128)(2,1)S(1)} %fusion.11), channel_id=1, source_target_pairs={{0,8},{8,0},{16,24},{24,16},{1,9},{9,1},{17,25},{25,17},{2,10},{10... | collective-permute-start | bytes 1376264 | tf_op jit(solution)/shard_map/ppermute | solution.py:111
  49.7 12.9 %copy-start.2 = (bf16[2,2,128,1792]{3,2,1,0:T(8,128)(2,1)S(1)}, bf16[2,2,128,1792]{3,2,1,0:T(8,128)(2,1)}, u32[]{:S(2)}) copy-start(bf16[2,2,128,1792]{3,2,1,0:T(8,128)(2,1)} %copy-done.1) | copy-start | bytes 5505028
  49.8 7.7 %collective-permute-start.3 = (bf16[1,128,896]{2,1,0:T(8,128)(2,1)S(1)}, bf16[1,128,896]{2,1,0:T(8,128)(2,1)S(1)}, u32[]{:S(2)}, u32[]{:S(2)}) collective-permute-start(bf16[1,128,896]{2,1,0:T(8,128)(2,1)S(1)} %fusion.16), channel_id=1, source_target_pairs={{0,16},{8,24},{16,0},{24,8},{1,17},{9,25},{17,1},{25,9},{2,18},{10... | collective-permute-start | bytes 688136 | tf_op jit(solution)/shard_map/ppermute | solution.py:111
  58.3 12.4 %all-to-all-start.1 = ((bf16[8,16,896]{2,1,0:T(8,128)(2,1)}), bf16[8,16,896]{2,1,0:T(8,128)(2,1)S(1)}, u32[]{:S(2)}, u32[]{:S(2)}) async-start(bf16[8,16,896]{2,1,0:T(8,128)(2,1)} %bitcast.32), calls=%async_computation.1 | async-start | bytes 458752 | tf_op jit(solution)/shard_map/all_to_all | solution.py:198
  62.6 8.0 %copy-start.6 = (bf16[128,256]{1,0:T(8,128)(2,1)S(1)}, bf16[128,256]{1,0:T(8,128)(2,1)}, u32[]{:S(2)}) copy-start(bf16[128,256]{1,0:T(8,128)(2,1)} %get-tuple-element.6) | copy-start | bytes 196612

commit v5 on v4

--- a/solution.py
+++ b/solution.py
@@ -113,16 +113,20 @@
 
 def gather_dp(x, n):
     me = lax.axis_index("dp")
-    acc = x[None]
+    held = [x]
+    owners = [me]
     bit = n // 2
     while bit >= 1:
-        other = partner(acc, bit, n)
-        low_first = jnp.stack([acc, other], axis=1)
-        high_first = jnp.stack([other, acc], axis=1)
-        acc = jnp.where((me & bit) == 0, low_first, high_first)
-        acc = acc.reshape((-1,) + x.shape)
+        stacked = jnp.stack(held)
+        got = partner(stacked, bit, n)
+        held = held + [got[i] for i in range(len(held))]
+        owners = owners + [o ^ bit for o in owners]
         bit //= 2
-    return acc
+    at = lax.broadcasted_iota(jnp.int32, (n, 1, 1), 0)
+    out = jnp.broadcast_to(held[0][None], (n,) + x.shape)
+    for piece, owner in zip(held[1:], owners[1:]):
+        out = jnp.where(at == owner, piece[None], out)
+    return out
 
 
 def scatter_dp(parts, n):
@@ -155,8 +159,13 @@
     info = arrived[:, 2 * width :].astype(jnp.float32)
     gate_sel = (info[:, 0] + info[:, 1]) + info[:, 2]
     flag = info[:, 3]
-    by_block = info.reshape(n_dest, CAP, side)[:, 0]
-    forget_count = jnp.sum(by_block[:, 4] * 256.0 + by_block[:, 5])
+    first_row = jnp.where(lax.broadcasted_iota(jnp.int32, (slots,), 0) % CAP == 0, 1.0, 0.0)
+    block_hi = (first_row * info[:, 4]).astype(jnp.bfloat16)
+    block_lo = (first_row * info[:, 5]).astype(jnp.bfloat16)
+    every = jnp.ones((slots, slots), jnp.bfloat16)
+    forget_count = 256.0 * jnp.dot(every, block_hi, preferred_element_type=jnp.float32) + jnp.dot(
+        every, block_lo, preferred_element_type=jnp.float32
+    )
     all_rows = row_count * n_dest
     half_total = jnp.float32(all_rows) / 2.0
     weight = jnp.where(
@@ -173,13 +182,19 @@
     ff = gate_weight.shape[2]
     w_gate = gate_weight[0].reshape(n_dp, width, ff)
     w_up = up_weight[0].reshape(n_dp, width, ff)
-    w_down = down_weight[0].reshape(ff, n_dp, width)
+    w_down = down_weight[0]
     chunk_dims = (((0, 2), (0, 1)), ((), ()))
     gate_pre = lax.dot_general(slot_tokens, w_gate, chunk_dims, preferred_element_type=jnp.float32)
     up_pre = lax.dot_general(slot_tokens, w_up, chunk_dims, preferred_element_type=jnp.float32)
+    last_dims = (((1,), (1,)), ((), ()))
     hidden_grad = lax.dot_general(
-        slot_grads, w_down, (((0, 2), (1, 2)), ((), ())), preferred_element_type=jnp.float32
-    )
+        slot_grads[0], w_down[:, :width], last_dims, preferred_element_type=jnp.float32
+    )
+    for j in range(1, n_dp):
+        hidden_grad = hidden_grad + lax.dot_general(
+            slot_grads[j], w_down[:, j * width : (j + 1) * width], last_dims,
+            preferred_element_type=jnp.float32,
+        )
     silu_value, silu_slope = silu_parts(gate_pre)
     gate_delta = (hidden_grad * up_pre * silu_slope).astype(jnp.bfloat16)
     up_delta = (hidden_grad * silu_value).astype(jnp.bfloat16)

time: 72.1 us -> 69.5 us (0.964)
  other arithmetic: 5.1 us -> 3.18 us
  between operations: 2.19 us -> 0.82 us
  local copies, waits for them, and re-layouts: 2.72 us -> 1.52 us
  waiting for transfers between devices: 24.3 us -> 25.5 us
  matrix products: 5.83 us -> 6.62 us
    select_n x3 -> x1, other arithmetic: 3.05 us -> 0.52 us  [gather_dp(): out = jnp.where(at == owner, piece[None], out)]
    ppermute x4, waiting for transfers between devices: 19.1 us -> 20.2 us  [partner(): return lax.ppermute(x, 'dp', [(i, i ^ bit) for i in range(n)])]
    another operation x1 -> x0, local copies, waits for them, and re-layouts: 1.14 us -> none  [on_device(): w_down = down_weight[0].reshape(ff, n_dp, width)]
    another operation x1 -> x2, other arithmetic: 0.06 us -> 1.06 us  [gather_dp(): stacked = jnp.stack(held)]
    dot_general x1 -> x6, matrix products: 0.41 us -> 1.19 us  [the longest x3 0.69 us: on_device(): lax.dot_general(slot_grads[j], w_down[:, j * width:(j + 1) * width], last...]
    unnamed x14 -> x12, local copies, waits for them, and re-layouts: 1.44 us -> 1.44 us
  transfers between devices with their start and end apart: 5 -> 5, of which waited for: 5 -> 5; matrix products, arithmetic and copies ran while one was open for 6% -> 4% of each run, Pallas kernels for 0% -> 0%
where the time goes in v5:
time: 69.5 us; the launch traced here: 69.2 us
  waiting for transfers between devices  25.5 us (37%)
  blocking collectives  21.1 us (30%)
  starting transfers between devices  7.69 us (11%)
  matrix products  6.62 us (10%)
  other arithmetic  3.18 us (5%)
  Pallas kernels  2.75 us (4%)
  local copies, waits for them, and re-layouts  1.52 us (2%)
  between operations  0.82 us (1%)
    all_to_all x1, blocking collectives, on_device(): lax.all_to_all(payload, 'expert', split_axis=0, concat_axis=0, tiled=True)  21.1 us
    ppermute x4, waiting for transfers between devices, partner(): return lax.ppermute(x, 'dp', [(i, i ^ bit) for i in range(n)])  20.2 us
    all_to_all x1, waiting for transfers between devices, on_device(): lax.all_to_all(summed, 'expert', split_axis=0, concat_axis=0, tiled=True)  5.27 us
    all_to_all x1, starting transfers between devices, on_device(): lax.all_to_all(summed, 'expert', split_axis=0, concat_axis=0, tiled=True)  4.37 us
    ppermute x4, starting transfers between devices, partner(): return lax.ppermute(x, 'dp', [(i, i ^ bit) for i in range(n)])  3.32 us
    pallas_call x1, Pallas kernels, glue(): pl.pallas_call(functools.partial(glue_kernel, n_dest, width, side, split)...  2.75 us
    unnamed x12, local copies, waits for them, and re-layouts  1.44 us
  transfers between devices with their start and end apart: 5, of which 5 were waited for; matrix products, arithmetic and copies ran while one was open for 4% of the time, Pallas kernels for 0%

profile of v5, /device:TPU:0, one launch (start us, length us, event | category | flops | bytes accessed | tf_op | source)
XLA Modules:
  0.0 69.2 jit_solution(11783488358758892158)
XLA Ops:
  0.6 2.7 %shard_map.103 = (bf16[128,1920]{1,0:T(8,128)(2,1)}, bf16[128,256]{1,0:T(8,128)(2,1)}) custom-call(s32[8,256]{1,0:T(8,128)} %bitcast.124, f32[8,256]{1,0:T(8,128)} %bitcast.125, s32[1,256]{1,0:T(1,128)} %bitcast.126, bf16[256,896]{1,0:T(8,128)(2,1)} %tok_ref.1, bf16[256,896]{1,0:T(8,128)(2,1)} %grd_ref.1), custom_call_target="tpu_custom_call" | custom-call | tf_op jit(solution)/shard_map/pallas_call | solution.py:90
  3.4 21.1 %all_to_all.21 = bf16[8,16,1920]{2,1,0:T(8,128)(2,1)S(1)} all-to-all(bf16[8,16,1920]{2,1,0:T(8,128)(2,1)} %bitcast.123), channel_id=1, replica_groups=mesh['dp'=4,'expert'=8] {'expert'}, dimensions={0} | all-to-all | bytes 983040 | tf_op jit(solution)/shard_map/all_to_all | solution.py:155
  24.5 0.2 fusion.21
  24.7 0.3 slice_reduce_fusion
  25.0 0.1 fusion.5
  25.1 0.2 fusion.28
  25.3 0.1 multiply_convert_fusion
  25.5 1.6 %collective-permute-start = (bf16[1,128,1792]{2,1,0:T(8,128)(2,1)S(1)}, bf16[1,128,1792]{2,1,0:T(8,128)(2,1)S(1)}, u32[]{:S(2)}, u32[]{:S(2)}) collective-permute-start(bf16[1,128,1792]{2,1,0:T(8,128)(2,1)S(1)} %get-tuple-element.12), channel_id=1, source_target_pairs={{0,16},{8,24},{16,0},{24,8},{1,17},{9,25},{17,1},{25,9},{2,18},{10... | collective-permute-start | bytes 1376264 | tf_op jit(solution)/shard_map/ppermute | solution.py:111
  27.1 9.7 %collective-permute-done = bf16[1,128,1792]{2,1,0:T(8,128)(2,1)S(1)} collective-permute-done((bf16[1,128,1792]{2,1,0:T(8,128)(2,1)S(1)}, bf16[1,128,1792]{2,1,0:T(8,128)(2,1)S(1)}, u32[]{:S(2)}, u32[]{:S(2)}) %collective-permute-start) | collective-permute-done | bytes 458784 | tf_op jit(solution)/shard_map/ppermute | solution.py:111
  36.7 1.0 %pad_maximum_fusion = bf16[2,128,1792]{2,1,0:T(8,128)(2,1)} fusion(bf16[1,128,1792]{2,1,0:T(8,128)(2,1)S(1)} %collective-permute-done, bf16[1,128,1792]{2,1,0:T(8,128)(2,1)S(1)} %get-tuple-element.12), kind=kLoop, calls=%fused_computation.18 | loop fusion | flops 458752 | bytes 1835008 | tf_op jit(solution)/shard_map/stack | solution.py:120
  37.8 2.7 %collective-permute-done.1 = bf16[2,128,1792]{2,1,0:T(8,128)(2,1)S(1)} collective-permute-done((bf16[2,128,1792]{2,1,0:T(8,128)(2,1)}, bf16[2,128,1792]{2,1,0:T(8,128)(2,1)S(1)}, u32[]{:S(2)}, u32[]{:S(2)}) %collective-permute-start.1) | collective-permute-done | bytes 917536 | tf_op jit(solution)/shard_map/ppermute | solution.py:111
  40.5 0.5 select_select_fusion
  41.1 0.4 convolution_bitcast_fusion
  41.5 1.4 %copy-done.5 = bf16[1,128,3584]{2,1,0:T(8,128)(2,1)S(1)} copy-done((bf16[1,128,3584]{2,1,0:T(8,128)(2,1)S(1)}, bf16[1,128,3584]{2,1,0:T(8,128)(2,1)}, u32[]{:S(2)}) %copy-start.5) | copy-done | bytes 917528
  42.9 0.2 fusion.18
  43.1 0.2 convolution_add_fusion.2
  43.4 0.2 convolution_add_fusion.1
  43.6 0.2 multiply_convert_fusion.1
  43.8 0.4 fusion.3
  44.3 0.4 fusion.46
  44.7 0.4 add_convert_fusion
  45.1 0.2 collective-permute-start.2
  45.4 1.7 %collective-permute-done.2 = bf16[2,128,896]{2,1,0:T(8,128)(2,1)S(1)} collective-permute-done((bf16[2,128,896]{2,1,0:T(8,128)(2,1)S(1)}, bf16[2,128,896]{2,1,0:T(8,128)(2,1)S(1)}, u32[]{:S(2)}, u32[]{:S(2)}) %collective-permute-start.2) | collective-permute-done | bytes 458784 | tf_op jit(solution)/shard_map/ppermute | solution.py:111
  47.0 0.2 fusion.6
  47.2 1.6 %collective-permute-start.3 = (bf16[1,128,896]{2,1,0:T(8,128)(2,1)S(1)}, bf16[1,128,896]{2,1,0:T(8,128)(2,1)S(1)}, u32[]{:S(2)}, u32[]{:S(2)}) collective-permute-start(bf16[1,128,896]{2,1,0:T(8,128)(2,1)S(1)} %fusion.14), channel_id=1, source_target_pairs={{0,16},{8,24},{16,0},{24,8},{1,17},{9,25},{17,1},{25,9},{2,18},{10... | collective-permute-start | bytes 688136 | tf_op jit(solution)/shard_map/ppermute | solution.py:111
  48.8 6.2 %collective-permute-done.3 = bf16[1,128,896]{2,1,0:T(8,128)(2,1)S(1)} collective-permute-done((bf16[1,128,896]{2,1,0:T(8,128)(2,1)S(1)}, bf16[1,128,896]{2,1,0:T(8,128)(2,1)S(1)}, u32[]{:S(2)}, u32[]{:S(2)}) %collective-permute-start.3) | collective-permute-done | bytes 229408 | tf_op jit(solution)/shard_map/ppermute | solution.py:111
  55.0 0.7 %fusion.13 = bf16[1,128,896]{2,1,0:T(8,128)(2,1)} fusion(bf16[1,128,896]{2,1,0:T(8,128)(2,1)S(1)} %collective-permute-done.3, f32[1,2,128,896]{3,2,1,0:T(8,128)S(1)} %fusion.6, pred[]{:T(512)S(6)} %ne.17), kind=kLoop, calls=%fused_computation.33 | loop fusion | flops 458752 | bytes 1376257 | tf_op jit(solution)/shard_map/convert_element_type | solution.py:212
  55.7 4.4 %all-to-all-start.1 = ((bf16[8,16,896]{2,1,0:T(8,128)(2,1)}), bf16[8,16,896]{2,1,0:T(8,128)(2,1)S(1)}, u32[]{:S(2)}, u32[]{:S(2)}) async-start(bf16[8,16,896]{2,1,0:T(8,128)(2,1)} %bitcast.37), calls=%async_computation.1 | async-start | bytes 458752 | tf_op jit(solution)/shard_map/all_to_all | solution.py:213
  60.1 1.4 %convolution_convert_fusion.1 = bf16[4,896,128]{2,1,0:T(8,128)(2,1)} fusion(bf16[128,128,1]{1,0,2:T(8,128)(2,1)S(1)} %fusion.3, bf16[4,128,1792]{2,1,0:T(8,128)(2,1)S(1)} %copy-done.2), kind=kOutput, calls=%fused_computation.3 | convolution fusion | flops 117899264 | bytes 1867776 | tf_op jit(solution)/shard_map/dot_general | solution.py:202
  61.5 1.4 %convolution_convert_fusion = bf16[4,896,128]{2,1,0:T(8,128)(2,1)} fusion(bf16[4,128,1792]{2,1,0:T(8,128)(2,1)S(1)} %copy-done.2, bf16[128,128]{1,0:T(8,128)(2,1)S(1)} %get-tuple-element.14), kind=kOutput, calls=%fused_computation.2 | convolution fusion | flops 117899264 | bytes 1867776 | tf_op jit(solution)/shard_map/dot_general | solution.py:205
  62.8 5.3 %all-to-all-done.1 = bf16[8,16,896]{2,1,0:T(8,128)(2,1)S(1)} async-done(((bf16[8,16,896]{2,1,0:T(8,128)(2,1)}), bf16[8,16,896]{2,1,0:T(8,128)(2,1)S(1)}, u32[]{:S(2)}, u32[]{:S(2)}) %all-to-all-start.1) | async-done | bytes 229408 | tf_op jit(solution)/shard_map/all_to_all | solution.py:213
  68.1 1.1 %convolution_convert_fusion.2 = bf16[256,896]{1,0:T(8,128)(2,1)} fusion(bf16[128,256]{1,0:T(8,128)(2,1)S(1)} %copy-done.4, bf16[128,896]{1,0:T(8,128)(2,1)S(1)} %bitcast.122), kind=kOutput, calls=%fused_computation.4 | convolution fusion | flops 58949632 | bytes 753664 | tf_op jit(solution)/shard_map/dot_general | solution.py:214
  (20 shorter events, 0.3 us)
Async XLA Ops:
  0.6 40.4 %copy-start = (bf16[1,3584,128]{2,1,0:T(8,128)(2,1)S(1)}, bf16[1,3584,128]{2,1,0:T(8,128)(2,1)}, u32[]{:S(2)}) copy-start(bf16[1,3584,128]{2,1,0:T(8,128)(2,1)} %param.13) | copy-start | bytes 2752516
  25.5 11.2 %collective-permute-start = (bf16[1,128,1792]{2,1,0:T(8,128)(2,1)S(1)}, bf16[1,128,1792]{2,1,0:T(8,128)(2,1)S(1)}, u32[]{:S(2)}, u32[]{:S(2)}) collective-permute-start(bf16[1,128,1792]{2,1,0:T(8,128)(2,1)S(1)} %get-tuple-element.12), channel_id=1, source_target_pairs={{0,16},{8,24},{16,0},{24,8},{1,17},{9,25},{17,1},{25,9},{2,18},{10... | collective-permute-start | bytes 1376264 | tf_op jit(solution)/shard_map/ppermute | solution.py:111
  37.8 2.7 %collective-permute-start.1 = (bf16[2,128,1792]{2,1,0:T(8,128)(2,1)}, bf16[2,128,1792]{2,1,0:T(8,128)(2,1)S(1)}, u32[]{:S(2)}, u32[]{:S(2)}) collective-permute-start(bf16[2,128,1792]{2,1,0:T(8,128)(2,1)} %pad_maximum_fusion), channel_id=1, source_target_pairs={{0,8},{8,0},{16,24},{24,16},{1,9},{9,1},{17,25},{25,17},{2,10},{10... | collective-permute-start | bytes 2752520 | tf_op jit(solution)/shard_map/ppermute | solution.py:111
  41.0 2.8 %copy-start.1 = (bf16[4,128,1792]{2,1,0:T(8,128)(2,1)}, bf16[4,128,1792]{2,1,0:T(8,128)(2,1)S(1)}, u32[]{:S(2)}) copy-start(bf16[4,128,1792]{2,1,0:T(8,128)(2,1)S(1)} %select_select_fusion) | copy-start | bytes 5505028
  41.0 1.8 %copy-start.5 = (bf16[1,128,3584]{2,1,0:T(8,128)(2,1)S(1)}, bf16[1,128,3584]{2,1,0:T(8,128)(2,1)}, u32[]{:S(2)}) copy-start(bf16[1,128,3584]{2,1,0:T(8,128)(2,1)} %param.15) | copy-start | bytes 2752516
  41.1 2.8 %copy-start.3 = (bf16[1,3584,128]{2,1,0:T(8,128)(2,1)S(1)}, bf16[1,3584,128]{2,1,0:T(8,128)(2,1)}, u32[]{:S(2)}) copy-start(bf16[1,3584,128]{2,1,0:T(8,128)(2,1)} %param.14) | copy-start | bytes 2752516
  45.1 1.9 %collective-permute-start.2 = (bf16[2,128,896]{2,1,0:T(8,128)(2,1)S(1)}, bf16[2,128,896]{2,1,0:T(8,128)(2,1)S(1)}, u32[]{:S(2)}, u32[]{:S(2)}) collective-permute-start(bf16[2,128,896]{2,1,0:T(8,128)(2,1)S(1)} %fusion.11), channel_id=1, source_target_pairs={{0,8},{8,0},{16,24},{24,16},{1,9},{9,1},{17,25},{25,17},{2,10},{10... | collective-permute-start | bytes 1376264 | tf_op jit(solution)/shard_map/ppermute | solution.py:111
  47.2 12.9 %copy-start.2 = (bf16[4,128,1792]{2,1,0:T(8,128)(2,1)S(1)}, bf16[4,128,1792]{2,1,0:T(8,128)(2,1)}, u32[]{:S(2)}) copy-start(bf16[4,128,1792]{2,1,0:T(8,128)(2,1)} %copy-done.1) | copy-start | bytes 5505028
  47.2 7.7 %collective-permute-start.3 = (bf16[1,128,896]{2,1,0:T(8,128)(2,1)S(1)}, bf16[1,128,896]{2,1,0:T(8,128)(2,1)S(1)}, u32[]{:S(2)}, u32[]{:S(2)}) collective-permute-start(bf16[1,128,896]{2,1,0:T(8,128)(2,1)S(1)} %fusion.14), channel_id=1, source_target_pairs={{0,16},{8,24},{16,0},{24,8},{1,17},{9,25},{17,1},{25,9},{2,18},{10... | collective-permute-start | bytes 688136 | tf_op jit(solution)/shard_map/ppermute | solution.py:111
  55.7 12.4 %all-to-all-start.1 = ((bf16[8,16,896]{2,1,0:T(8,128)(2,1)}), bf16[8,16,896]{2,1,0:T(8,128)(2,1)S(1)}, u32[]{:S(2)}, u32[]{:S(2)}) async-start(bf16[8,16,896]{2,1,0:T(8,128)(2,1)} %bitcast.37), calls=%async_computation.1 | async-start | bytes 458752 | tf_op jit(solution)/shard_map/all_to_all | solution.py:213
  60.1 8.0 %copy-start.4 = (bf16[128,256]{1,0:T(8,128)(2,1)S(1)}, bf16[128,256]{1,0:T(8,128)(2,1)}, u32[]{:S(2)}) copy-start(bf16[128,256]{1,0:T(8,128)(2,1)} %get-tuple-element.6) | copy-start | bytes 196612

commit v6 on v5

--- a/solution.py
+++ b/solution.py
@@ -9,7 +9,7 @@
 CAP = 16
 
 
-def glue_kernel(n_dest, width, side, split, ids_ref, gates_ref, flags_ref, tok_ref, grd_ref, *outs):
+def glue_kernel(n_dest, width, side, split, me_ref, ids_ref, gates_ref, flags_ref, tok_ref, grd_ref, *outs):
     f32, bf16 = jnp.float32, jnp.bfloat16
     rows = tok_ref.shape[0]
     slots = n_dest * CAP
@@ -33,7 +33,7 @@
     rank = jnp.dot(hits.astype(bf16), before, preferred_element_type=f32)
     slot_of = lax.broadcasted_iota(jnp.int32, (slots, lanes), 0)
     expand = jnp.where(
-        lax.shift_right_logical(slot_of, 4) == lax.broadcasted_iota(jnp.int32, (slots, lanes), 1), 1.0, 0.0
+        (lax.shift_right_logical(slot_of, 4) ^ me_ref[0]) == lax.broadcasted_iota(jnp.int32, (slots, lanes), 1), 1.0, 0.0
     ).astype(bf16)
     hit_s = jnp.dot(expand, hits.astype(bf16), preferred_element_type=f32)
     rank_s = jnp.dot(expand, rank.astype(bf16), preferred_element_type=f32)
@@ -74,7 +74,7 @@
     pick_out[...] = pick_b
 
 
-def glue(expert_ids, gate_values, forget_flags, tokens, token_grads, n_dest):
+def glue(me, expert_ids, gate_values, forget_flags, tokens, token_grads, n_dest):
     import functools
 
     rows, width = tokens.shape
@@ -90,9 +90,9 @@
     outs = pl.pallas_call(
         functools.partial(glue_kernel, n_dest, width, side, split),
         out_shape=[jax.ShapeDtypeStruct(s, bf16) for s in shapes],
-        in_specs=[vmem] * 5,
+        in_specs=[pl.BlockSpec(memory_space=pltpu.SMEM)] + [vmem] * 5,
         out_specs=[vmem] * len(shapes),
-    )(expert_ids.T, gate_values.T, forget_flags.reshape(1, rows), tokens, token_grads)
+    )(me.reshape(1), expert_ids.T, gate_values.T, forget_flags.reshape(1, rows), tokens, token_grads)
     if split:
         return jnp.concatenate(outs[:3], axis=1), outs[3]
     return outs[0], outs[1]
@@ -111,11 +111,7 @@
     return lax.ppermute(x, "dp", [(i, i ^ bit) for i in range(n)])
 
 
-def gather_dp(x, n):
-    me = lax.axis_index("dp")
-    held = [x]
-    owners = [me]
-    bit = n // 2
+def gather_dp(held, owners, bit, n):
     while bit >= 1:
         stacked = jnp.stack(held)
         got = partner(stacked, bit, n)
@@ -123,10 +119,14 @@
         owners = owners + [o ^ bit for o in owners]
         bit //= 2
     at = lax.broadcasted_iota(jnp.int32, (n, 1, 1), 0)
-    out = jnp.broadcast_to(held[0][None], (n,) + x.shape)
+    out = jnp.broadcast_to(held[0][None], (n,) + held[0].shape)
     for piece, owner in zip(held[1:], owners[1:]):
         out = jnp.where(at == owner, piece[None], out)
     return out
+
+
+def swap(x, k, n):
+    return lax.ppermute(x, "expert", [(i, i ^ k) for i in range(n)])
 
 
 def scatter_dp(parts, n):
@@ -150,12 +150,19 @@
     n_dest = lax.axis_size("expert")
     n_dp = lax.axis_size("dp")
     row_count, width = tokens.shape
-    payload, pick_t = glue(expert_ids, gate_values, forget_flags, tokens, token_grads, n_dest)
+    me = lax.axis_index("expert")
+    me_dp = lax.axis_index("dp")
+    payload, pick_t = glue(me, expert_ids, gate_values, forget_flags, tokens, token_grads, n_dest)
     side = payload.shape[1] - 2 * width
-    arrived = lax.all_to_all(payload, "expert", split_axis=0, concat_axis=0, tiled=True)
+    pieces = payload.reshape(n_dest, CAP, payload.shape[1])
+    half = max(n_dest // 2, 1)
+    arrived_parts, across_parts = [], []
+    for lo in range(0, n_dest, half):
+        got = jnp.stack([pieces[0] if k == 0 else swap(pieces[k], k, n_dest) for k in range(lo, lo + half)])
+        arrived_parts.append(got)
+        across_parts.append(partner(got[:, :, : 2 * width], n_dp // 2, n_dp) if n_dp > 1 else None)
+    arrived = jnp.concatenate(arrived_parts, axis=0).reshape(n_dest * CAP, payload.shape[1])
     slots = arrived.shape[0]
-    part_tokens = arrived[:, :width]
-    raw_grads = arrived[:, width : 2 * width]
     info = arrived[:, 2 * width :].astype(jnp.float32)
     gate_sel = (info[:, 0] + info[:, 1]) + info[:, 2]
     flag = info[:, 3]
@@ -174,11 +181,14 @@
         half_total / (jnp.float32(all_rows) - forget_count),
     )
     scale = gate_sel * weight
-    part_grads = (scale[:, None] * raw_grads.astype(jnp.float32)).astype(jnp.bfloat16)
-    both = jnp.concatenate([part_tokens, part_grads], axis=1)
-    gathered = gather_dp(both, n_dp)
+    own = arrived[:, : 2 * width]
+    if n_dp > 1:
+        across = jnp.concatenate(across_parts, axis=0).reshape(slots, 2 * width)
+        gathered = gather_dp([own, across], [me_dp, me_dp ^ (n_dp // 2)], n_dp // 4, n_dp)
+    else:
+        gathered = own[None]
     slot_tokens = gathered[:, :, :width]
-    slot_grads = gathered[:, :, width:]
+    slot_grads = (scale[None, :, None] * gathered[:, :, width:].astype(jnp.float32)).astype(jnp.bfloat16)
     ff = gate_weight.shape[2]
     w_gate = gate_weight[0].reshape(n_dp, width, ff)
     w_up = up_weight[0].reshape(n_dp, width, ff)
@@ -210,7 +220,8 @@
     from_up = lax.dot_general(w_up, up_delta, back_dims, preferred_element_type=jnp.float32)
     part = (from_gate + from_up).astype(jnp.bfloat16)
     summed = scatter_dp(jnp.swapaxes(part, 1, 2), n_dp).astype(jnp.bfloat16)
-    returned = lax.all_to_all(summed, "expert", split_axis=0, concat_axis=0, tiled=True)
+    back = summed.reshape(n_dest, CAP, width)
+    returned = jnp.stack([back[0] if k == 0 else swap(back[k], k, n_dest) for k in range(n_dest)]).reshape(slots, width)
     input_grad = lax.dot_general(
         pick_t, returned, (((0,), (0,)), ((), ())), preferred_element_type=jnp.float32
     )

time: 69.5 us -> 74.4 us (1.071)
  blocking collectives: 21.1 us -> 0 us
  starting transfers between devices: 7.69 us -> 26.2 us
  local copies, waits for them, and re-layouts: 1.52 us -> 5.31 us
  waiting for transfers between devices: 25.5 us -> 27.9 us
  other arithmetic: 3.18 us -> 4.27 us
    ppermute x0 -> x14, starting transfers between devices: none -> 21.9 us  [swap(): return lax.ppermute(x, 'expert', [(i, i ^ k) for i in range(n)])]
    all_to_all x1 -> x0, blocking collectives: 21.1 us -> none  [on_device(): lax.all_to_all(payload, 'expert', split_axis=0, concat_axis=0, tiled=True)]
    ppermute x0 -> x14, waiting for transfers between devices: none -> 11.7 us  [swap(): return lax.ppermute(x, 'expert', [(i, i ^ k) for i in range(n)])]
    all_to_all x1 -> x0, waiting for transfers between devices: 5.27 us -> none  [on_device(): lax.all_to_all(summed, 'expert', split_axis=0, concat_axis=0, tiled=True)]
    all_to_all x1 -> x0, starting transfers between devices: 4.37 us -> none  [on_device(): lax.all_to_all(summed, 'expert', split_axis=0, concat_axis=0, tiled=True)]
    ppermute x4 -> x5, waiting for transfers between devices: 20.2 us -> 16.2 us  [partner(): return lax.ppermute(x, 'dp', [(i, i ^ bit) for i in range(n)])]
    slice x1 -> x3, local copies, waits for them, and re-layouts: 0.02 us -> 1.86 us  [the longest x1 1.07 us: on_device(): pieces[0]]
    reshape x1, other arithmetic: 0.15 us -> 1.31 us  [scatter_dp(): pairs = acc.reshape((acc.shape[0] // 2, 2) + acc.shape[1:])]
  transfers between devices with their start and end apart: 5 -> 19, of which waited for: 5 -> 8; matrix products, arithmetic and copies ran while one was open for 4% -> 8% of each run, Pallas kernels for 0% -> 0%
where the time goes in v6:
time: 74.4 us; the launch traced here: 74 us
  waiting for transfers between devices  27.9 us (38%)
  starting transfers between devices  26.2 us (35%)
  matrix products  6.62 us (9%)
  local copies, waits for them, and re-layouts  5.31 us (7%)
  other arithmetic  4.27 us (6%)
  Pallas kernels  2.76 us (4%)
  between operations  0.94 us (1%)
    ppermute x14, starting transfers between devices, swap(): return lax.ppermute(x, 'expert', [(i, i ^ k) for i in range(n)])  21.9 us
    ppermute x5, waiting for transfers between devices, partner(): return lax.ppermute(x, 'dp', [(i, i ^ bit) for i in range(n)])  16.2 us
    ppermute x14, waiting for transfers between devices, swap(): return lax.ppermute(x, 'expert', [(i, i ^ k) for i in range(n)])  11.7 us
    ppermute x5, starting transfers between devices, partner(): return lax.ppermute(x, 'dp', [(i, i ^ bit) for i in range(n)])  4.29 us
    pallas_call x1, Pallas kernels, glue(): pl.pallas_call(functools.partial(glue_kernel, n_dest, width, side, split)...  2.76 us
    unnamed x27, local copies, waits for them, and re-layouts  2.45 us
    select_n x1, other arithmetic, gather_dp(): out = jnp.where(at == owner, piece[None], out)  1.54 us
  transfers between devices with their start and end apart: 19, of which 8 were waited for; matrix products, arithmetic and copies ran while one was open for 8% of the time, Pallas kernels for 0%

profile of v6, /device:TPU:0, one launch (start us, length us, event | category | flops | bytes accessed | tf_op | source)
XLA Modules:
  0.0 74.0 jit_solution(11409024215773431475)
XLA Ops:
  0.7 2.8 %shard_map.103 = (bf16[128,1920]{1,0:T(8,128)(2,1)}, bf16[128,256]{1,0:T(8,128)(2,1)}) custom-call(s32[1]{0:T(128)} %bitcast.me_ref, s32[8,256]{1,0:T(8,128)} %bitcast.210, f32[8,256]{1,0:T(8,128)} %bitcast.211, s32[1,256]{1,0:T(1,128)} %bitcast.212, bf16[256,896]{1,0:T(8,128)(2,1)} %tok_ref.1, bf16[256,896]{1,0:T(8,128)(2,1)} %grd_ref.1), custom_call_target="tpu_custom_call" | custom-call | tf_op jit(solution)/shard_map/pallas_call | solution.py:90
  3.4 1.1 %slice_bitcast_fusion.10 = (bf16[1,16,1920]{2,1,0:T(8,128)(2,1)S(1)}, bf16[16,1920]{1,0:T(8,128)(2,1)S(1)}, bf16[16,1920]{1,0:T(8,128)(2,1)S(1)}, bf16[16,1920]{...) fusion(bf16[128,1920]{1,0:T(8,128)(2,1)} %get-tuple-element.5), kind=kLoop, calls=%fused_computation.53 | loop fusion | bytes 983040 | tf_op jit(solution)/shard_map/slice | solution.py:161
  4.5 6.1 %collective-permute-start.6 = (bf16[16,1920]{1,0:T(8,128)(2,1)S(1)}, bf16[16,1920]{1,0:T(8,128)(2,1)S(1)}, u32[]{:S(2)}, u32[]{:S(2)}) collective-permute-start(bf16[16,1920]{1,0:T(8,128)(2,1)S(1)} %get-tuple-element.12), channel_id=1, source_target_pairs={{0,7},{1,6},{2,5},{3,4},{4,3},{5,2},{6,1},{7,0},{8,15},{9,14},{10,... | collective-permute-start | bytes 184328 | tf_op jit(solution)/shard_map/ppermute | solution.py:129
  10.8 0.7 collective-permute-start.4
  11.5 2.0 %collective-permute-start.3 = (bf16[16,1920]{1,0:T(8,128)(2,1)S(1)}, bf16[16,1920]{1,0:T(8,128)(2,1)S(1)}, u32[]{:S(2)}, u32[]{:S(2)}) collective-permute-start(bf16[16,1920]{1,0:T(8,128)(2,1)S(1)} %get-tuple-element.15), channel_id=1, source_target_pairs={{0,4},{1,5},{2,6},{3,7},{4,0},{5,1},{6,2},{7,3},{8,12},{9,13},{10,... | collective-permute-start | bytes 184328 | tf_op jit(solution)/shard_map/ppermute | solution.py:129
  13.6 2.3 %collective-permute-start.2 = (bf16[16,1920]{1,0:T(8,128)(2,1)S(1)}, bf16[16,1920]{1,0:T(8,128)(2,1)S(1)}, u32[]{:S(2)}, u32[]{:S(2)}) collective-permute-start(bf16[16,1920]{1,0:T(8,128)(2,1)S(1)} %get-tuple-element.16), channel_id=1, source_target_pairs={{0,3},{1,2},{2,1},{3,0},{4,7},{5,6},{6,5},{7,4},{8,11},{9,10},{10,... | collective-permute-start | bytes 184328 | tf_op jit(solution)/shard_map/ppermute | solution.py:129
  15.9 0.8 %constant_dynamic-update-slice_fusion.7 = bf16[8,16,1920]{2,1,0:T(8,128)(2,1)S(1)} fusion(bf16[128,1920]{1,0:T(8,128)(2,1)} %get-tuple-element.5), kind=kLoop, calls=%fused_computation.61 | loop fusion | bytes 122880
  16.7 0.8 %collective-permute-start.1 = (bf16[16,1920]{1,0:T(8,128)(2,1)S(1)}, bf16[16,1920]{1,0:T(8,128)(2,1)S(1)}, u32[]{:S(2)}, u32[]{:S(2)}) collective-permute-start(bf16[16,1920]{1,0:T(8,128)(2,1)S(1)} %get-tuple-element.17), channel_id=1, source_target_pairs={{0,2},{1,3},{2,0},{3,1},{4,6},{5,7},{6,4},{7,5},{8,10},{9,11},{10,... | collective-permute-start | bytes 184328 | tf_op jit(solution)/shard_map/ppermute | solution.py:129
  17.9 1.4 %collective-permute-done.4 = bf16[16,1920]{1,0:T(8,128)(2,1)S(1)} collective-permute-done((bf16[16,1920]{1,0:T(8,128)(2,1)S(1)}, bf16[16,1920]{1,0:T(8,128)(2,1)S(1)}, u32[]{:S(2)}, u32[]{:S(2)}) %collective-permute-start.4) | collective-permute-done | bytes 61472 | tf_op jit(solution)/shard_map/ppermute | solution.py:129
  19.3 1.9 %collective-permute-done.3 = bf16[16,1920]{1,0:T(8,128)(2,1)S(1)} collective-permute-done((bf16[16,1920]{1,0:T(8,128)(2,1)S(1)}, bf16[16,1920]{1,0:T(8,128)(2,1)S(1)}, u32[]{:S(2)}, u32[]{:S(2)}) %collective-permute-start.3) | collective-permute-done | bytes 61472 | tf_op jit(solution)/shard_map/ppermute | solution.py:129
  21.2 1.6 %collective-permute-start.8 = (bf16[4,16,1792]{2,1,0:T(8,128)(2,1)S(1)}, bf16[4,16,1792]{2,1,0:T(8,128)(2,1)S(1)}, u32[]{:S(2)}, u32[]{:S(2)}) collective-permute-start(bf16[4,16,1792]{2,1,0:T(8,128)(2,1)S(1)} %pad_maximum_fusion.1), channel_id=1, source_target_pairs={{0,16},{8,24},{16,0},{24,8},{1,17},{9,25},{17,1},{25,9},{2,18},{10... | collective-permute-start | bytes 688136 | tf_op jit(solution)/shard_map/ppermute | solution.py:111
  22.8 1.0 %collective-permute-start.7 = (bf16[4,16,1792]{2,1,0:T(8,128)(2,1)S(1)}, bf16[4,16,1792]{2,1,0:T(8,128)(2,1)S(1)}, u32[]{:S(2)}, u32[]{:S(2)}) collective-permute-start(bf16[4,16,1792]{2,1,0:T(8,128)(2,1)S(1)} %pad_maximum_fusion.4), channel_id=1, source_target_pairs={{0,16},{8,24},{16,0},{24,8},{1,17},{9,25},{17,1},{25,9},{2,18},{10... | collective-permute-start | bytes 688136 | tf_op jit(solution)/shard_map/ppermute | solution.py:111
  23.9 0.9 %slice_bitcast_fusion.20 = (bf16[1,128,1792]{2,1,0:T(8,128)(2,1)S(1)}, bf16[128,1792]{1,0:T(8,128)(2,1)}) fusion(bf16[128,1920]{1,0:T(8,128)(2,1)S(1)} %bitcast.200), kind=kLoop, calls=%fused_computation.113 | loop fusion | bytes 1376256 | tf_op jit(solution)/shard_map/stack | solution.py:116
  24.8 8.3 %collective-permute-done.7 = bf16[4,16,1792]{2,1,0:T(8,128)(2,1)S(1)} collective-permute-done((bf16[4,16,1792]{2,1,0:T(8,128)(2,1)S(1)}, bf16[4,16,1792]{2,1,0:T(8,128)(2,1)S(1)}, u32[]{:S(2)}, u32[]{:S(2)}) %collective-permute-start.7) | collective-permute-done | bytes 229408 | tf_op jit(solution)/shard_map/ppermute | solution.py:111
  33.3 0.8 %slice.224 = bf16[128,128]{1,0:T(8,128)(2,1)S(1)} slice(bf16[128,1920]{1,0:T(8,128)(2,1)} %bitcast.201), slice={[0:128], [1792:1920]} | slice | bytes 65536 | tf_op jit(solution)/shard_map/slice | solution.py:166
  34.5 1.2 %collective-permute-done.9 = bf16[2,128,1792]{2,1,0:T(8,128)(2,1)S(1)} collective-permute-done((bf16[2,128,1792]{2,1,0:T(8,128)(2,1)S(1)}, bf16[2,128,1792]{2,1,0:T(8,128)(2,1)S(1)}, u32[]{:S(2)}, u32[]{:S(2)}) %collective-permute-start.9) | collective-permute-done | bytes 917536 | tf_op jit(solution)/shard_map/ppermute | solution.py:111
  35.8 1.5 %select_select_fusion = bf16[4,128,1792]{2,1,0:T(8,128)(2,1)S(1)} fusion(pred[4]{0:T(512)(128)(4,1)S(1)} %get-tuple-element.29, pred[4]{0:T(512)(128)(4,1)S(1)} %get-tuple-element.30, pred[4]{0:T(512)(128)(4,1)S(1)} %iota_compare_fusion.2, bf16[128,1792]{1,0:T(8,128)(2,1)} %get-tuple-element.10, bf16[128,1792]{1,0:T(8,128)(2,1)S(1)} %bitcast.195, ...), kind=kLoop, calls=%fused_computation.2 | loop fusion | flops 2752512 | bytes 3670028 | tf_op jit(solution)/shard_map/jit(_where)/select_n | solution.py:124
  40.8 0.9 %copy-done.1 = bf16[128,4,896]{2,0,1:T(8,128)(2,1)} copy-done((bf16[128,4,896]{2,0,1:T(8,128)(2,1)}, bf16[128,4,896]{2,0,1:T(8,128)(2,1)S(1)}, u32[]{:S(2)}) %copy-start.1) | copy-done | bytes 917528
  41.7 0.8 %fusion.11 = bf16[2,128,896]{2,1,0:T(8,128)(2,1)} fusion(pred[]{:T(512)S(6)} %ne.18, bf16[2,2,128,896]{3,2,1,0:T(8,128)(2,1)S(1)} %bitcast.192), kind=kLoop, calls=%fused_computation.27 | loop fusion | flops 229376 | bytes 1376257 | tf_op jit(solution)/shard_map/jit(_where)/select_n | solution.py:140
  42.6 1.9 %collective-permute-done.10 = bf16[2,128,896]{2,1,0:T(8,128)(2,1)S(1)} collective-permute-done((bf16[2,128,896]{2,1,0:T(8,128)(2,1)}, bf16[2,128,896]{2,1,0:T(8,128)(2,1)S(1)}, u32[]{:S(2)}, u32[]{:S(2)}) %collective-permute-start.10) | collective-permute-done | bytes 458784 | tf_op jit(solution)/shard_map/ppermute | solution.py:111
  44.5 1.3 %fusion.6 = f32[1,2,128,896]{3,2,1,0:T(8,128)S(1)} fusion(bf16[2,128,896]{2,1,0:T(8,128)(2,1)S(1)} %collective-permute-done.10, pred[]{:T(512)S(6)} %ne.18, bf16[2,2,128,896]{3,2,1,0:T(8,128)(2,1)} %bitcast.193), kind=kLoop, calls=%fused_computation.21 | loop fusion | flops 917504 | bytes 2293761 | tf_op jit(solution)/shard_map/reshape | solution.py:137
  45.9 1.6 %collective-permute-start.11 = (bf16[1,128,896]{2,1,0:T(8,128)(2,1)S(1)}, bf16[1,128,896]{2,1,0:T(8,128)(2,1)S(1)}, u32[]{:S(2)}, u32[]{:S(2)}) collective-permute-start(bf16[1,128,896]{2,1,0:T(8,128)(2,1)S(1)} %fusion.14), channel_id=1, source_target_pairs={{0,16},{8,24},{16,0},{24,8},{1,17},{9,25},{17,1},{25,9},{2,18},{10... | collective-permute-start | bytes 688136 | tf_op jit(solution)/shard_map/ppermute | solution.py:111
  47.5 1.4 %convolution_convert_fusion.1 = bf16[4,896,128]{2,1,0:T(8,128)(2,1)} fusion(bf16[128,128,1]{1,0,2:T(8,128)(2,1)S(1)} %fusion.3, bf16[4,128,1792]{2,1,0:T(8,128)(2,1)S(1)} %select_select_fusion), kind=kOutput, calls=%fused_computation.4 | convolution fusion | flops 117899264 | bytes 1867776 | tf_op jit(solution)/shard_map/dot_general | solution.py:212
  48.8 4.8 %collective-permute-done.11 = bf16[1,128,896]{2,1,0:T(8,128)(2,1)S(1)} collective-permute-done((bf16[1,128,896]{2,1,0:T(8,128)(2,1)S(1)}, bf16[1,128,896]{2,1,0:T(8,128)(2,1)S(1)}, u32[]{:S(2)}, u32[]{:S(2)}) %collective-permute-start.11) | collective-permute-done | bytes 229408 | tf_op jit(solution)/shard_map/ppermute | solution.py:111
  53.7 1.3 %collective-permute-start.12 = (bf16[16,896]{1,0:T(8,128)(2,1)S(1)}, bf16[16,896]{1,0:T(8,128)(2,1)S(1)}, u32[]{:S(2)}, u32[]{:S(2)}) collective-permute-start(bf16[16,896]{1,0:T(8,128)(2,1)S(1)} %get-tuple-element.25), channel_id=1, source_target_pairs={{0,1},{1,0},{2,3},{3,2},{4,5},{5,4},{6,7},{7,6},{8,9},{9,8},{10,11... | collective-permute-start | bytes 86024 | tf_op jit(solution)/shard_map/ppermute | solution.py:129
  55.0 1.4 %convolution_convert_fusion = bf16[4,896,128]{2,1,0:T(8,128)(2,1)} fusion(bf16[4,128,1792]{2,1,0:T(8,128)(2,1)S(1)} %select_select_fusion, bf16[128,128]{1,0:T(8,128)(2,1)S(1)} %get-tuple-element.27), kind=kOutput, calls=%fused_computation.3 | convolution fusion | flops 117899264 | bytes 1867776 | tf_op jit(solution)/shard_map/dot_general | solution.py:215
  56.4 2.6 %collective-permute-start.18 = (bf16[16,896]{1,0:T(8,128)(2,1)S(1)}, bf16[16,896]{1,0:T(8,128)(2,1)S(1)}, u32[]{:S(2)}, u32[]{:S(2)}) collective-permute-start(bf16[16,896]{1,0:T(8,128)(2,1)S(1)} %get-tuple-element.19), channel_id=1, source_target_pairs={{0,7},{1,6},{2,5},{3,4},{4,3},{5,2},{6,1},{7,0},{8,15},{9,14},{10,... | collective-permute-start | bytes 86024 | tf_op jit(solution)/shard_map/ppermute | solution.py:129
  59.0 1.4 %collective-permute-start.17 = (bf16[16,896]{1,0:T(8,128)(2,1)S(1)}, bf16[16,896]{1,0:T(8,128)(2,1)S(1)}, u32[]{:S(2)}, u32[]{:S(2)}) collective-permute-start(bf16[16,896]{1,0:T(8,128)(2,1)S(1)} %get-tuple-element.20), channel_id=1, source_target_pairs={{0,6},{1,7},{2,4},{3,5},{4,2},{5,3},{6,0},{7,1},{8,14},{9,15},{10,... | collective-permute-start | bytes 86024 | tf_op jit(solution)/shard_map/ppermute | solution.py:129
  60.4 3.6 %collective-permute-start.15 = (bf16[16,896]{1,0:T(8,128)(2,1)S(1)}, bf16[16,896]{1,0:T(8,128)(2,1)S(1)}, u32[]{:S(2)}, u32[]{:S(2)}) collective-permute-start(bf16[16,896]{1,0:T(8,128)(2,1)S(1)} %get-tuple-element.22), channel_id=1, source_target_pairs={{0,4},{1,5},{2,6},{3,7},{4,0},{5,1},{6,2},{7,3},{8,12},{9,13},{10,... | collective-permute-start | bytes 86024 | tf_op jit(solution)/shard_map/ppermute | solution.py:129
  64.1 4.0 %collective-permute-done.13 = bf16[16,896]{1,0:T(8,128)(2,1)S(1)} collective-permute-done((bf16[16,896]{1,0:T(8,128)(2,1)S(1)}, bf16[16,896]{1,0:T(8,128)(2,1)S(1)}, u32[]{:S(2)}, u32[]{:S(2)}) %collective-permute-start.13) | collective-permute-done | bytes 28704 | tf_op jit(solution)/shard_map/ppermute | solution.py:129
  68.4 4.4 %collective-permute-done.14 = bf16[16,896]{1,0:T(8,128)(2,1)S(1)} collective-permute-done((bf16[16,896]{1,0:T(8,128)(2,1)S(1)}, bf16[16,896]{1,0:T(8,128)(2,1)S(1)}, u32[]{:S(2)}, u32[]{:S(2)}) %collective-permute-start.14) | collective-permute-done | bytes 28704 | tf_op jit(solution)/shard_map/ppermute | solution.py:129
  72.9 1.1 %convolution_convert_fusion.2 = bf16[256,896]{1,0:T(8,128)(2,1)} fusion(bf16[128,256]{1,0:T(8,128)(2,1)S(1)} %copy-done.4, bf16[128,896]{1,0:T(8,128)(2,1)S(1)} %bitcast.202), kind=kOutput, calls=%fused_computation.5 | convolution fusion | flops 58949632 | bytes 753664 | tf_op jit(solution)/shard_map/dot_general | solution.py:225
  (67 shorter events, 5.5 us)
Async XLA Ops:
  0.6 36.7 %copy-start = (bf16[1,3584,128]{2,1,0:T(8,128)(2,1)S(1)}, bf16[1,3584,128]{2,1,0:T(8,128)(2,1)}, u32[]{:S(2)}) copy-start(bf16[1,3584,128]{2,1,0:T(8,128)(2,1)} %param.13) | copy-start | bytes 2752516
  4.5 12.2 %collective-permute-start.6 = (bf16[16,1920]{1,0:T(8,128)(2,1)S(1)}, bf16[16,1920]{1,0:T(8,128)(2,1)S(1)}, u32[]{:S(2)}, u32[]{:S(2)}) collective-permute-start(bf16[16,1920]{1,0:T(8,128)(2,1)S(1)} %get-tuple-element.12), channel_id=1, source_target_pairs={{0,7},{1,6},{2,5},{3,4},{4,3},{5,2},{6,1},{7,0},{8,15},{9,14},{10,... | collective-permute-start | bytes 184328 | tf_op jit(solution)/shard_map/ppermute | solution.py:129
  10.6 6.9 %collective-permute-start.5 = (bf16[16,1920]{1,0:T(8,128)(2,1)S(1)}, bf16[16,1920]{1,0:T(8,128)(2,1)S(1)}, u32[]{:S(2)}, u32[]{:S(2)}) collective-permute-start(bf16[16,1920]{1,0:T(8,128)(2,1)S(1)} %get-tuple-element.13), channel_id=1, source_target_pairs={{0,6},{1,7},{2,4},{3,5},{4,2},{5,3},{6,0},{7,1},{8,14},{9,15},{10,... | collective-permute-start | bytes 184328 | tf_op jit(solution)/shard_map/ppermute | solution.py:129
  10.8 8.5 %collective-permute-start.4 = (bf16[16,1920]{1,0:T(8,128)(2,1)S(1)}, bf16[16,1920]{1,0:T(8,128)(2,1)S(1)}, u32[]{:S(2)}, u32[]{:S(2)}) collective-permute-start(bf16[16,1920]{1,0:T(8,128)(2,1)S(1)} %get-tuple-element.14), channel_id=1, source_target_pairs={{0,5},{1,4},{2,7},{3,6},{4,1},{5,0},{6,3},{7,2},{8,13},{9,12},{10,... | collective-permute-start | bytes 184328 | tf_op jit(solution)/shard_map/ppermute | solution.py:129
  11.5 9.6 %collective-permute-start.3 = (bf16[16,1920]{1,0:T(8,128)(2,1)S(1)}, bf16[16,1920]{1,0:T(8,128)(2,1)S(1)}, u32[]{:S(2)}, u32[]{:S(2)}) collective-permute-start(bf16[16,1920]{1,0:T(8,128)(2,1)S(1)} %get-tuple-element.15), channel_id=1, source_target_pairs={{0,4},{1,5},{2,6},{3,7},{4,0},{5,1},{6,2},{7,3},{8,12},{9,13},{10,... | collective-permute-start | bytes 184328 | tf_op jit(solution)/shard_map/ppermute | solution.py:129
  13.6 9.2 %collective-permute-start.2 = (bf16[16,1920]{1,0:T(8,128)(2,1)S(1)}, bf16[16,1920]{1,0:T(8,128)(2,1)S(1)}, u32[]{:S(2)}, u32[]{:S(2)}) collective-permute-start(bf16[16,1920]{1,0:T(8,128)(2,1)S(1)} %get-tuple-element.16), channel_id=1, source_target_pairs={{0,3},{1,2},{2,1},{3,0},{4,7},{5,6},{6,5},{7,4},{8,11},{9,10},{10,... | collective-permute-start | bytes 184328 | tf_op jit(solution)/shard_map/ppermute | solution.py:129
  16.7 6.1 %collective-permute-start.1 = (bf16[16,1920]{1,0:T(8,128)(2,1)S(1)}, bf16[16,1920]{1,0:T(8,128)(2,1)S(1)}, u32[]{:S(2)}, u32[]{:S(2)}) collective-permute-start(bf16[16,1920]{1,0:T(8,128)(2,1)S(1)} %get-tuple-element.17), channel_id=1, source_target_pairs={{0,2},{1,3},{2,0},{3,1},{4,6},{5,7},{6,4},{7,5},{8,10},{9,11},{10,... | collective-permute-start | bytes 184328 | tf_op jit(solution)/shard_map/ppermute | solution.py:129
  17.5 5.3 %collective-permute-start = (bf16[16,1920]{1,0:T(8,128)(2,1)S(1)}, bf16[16,1920]{1,0:T(8,128)(2,1)S(1)}, u32[]{:S(2)}, u32[]{:S(2)}) collective-permute-start(bf16[16,1920]{1,0:T(8,128)(2,1)S(1)} %get-tuple-element.18), channel_id=1, source_target_pairs={{0,1},{1,0},{2,3},{3,2},{4,5},{5,4},{6,7},{7,6},{8,9},{9,8},{10,11... | collective-permute-start | bytes 184328 | tf_op jit(solution)/shard_map/ppermute | solution.py:129
  21.2 11.9 %collective-permute-start.8 = (bf16[4,16,1792]{2,1,0:T(8,128)(2,1)S(1)}, bf16[4,16,1792]{2,1,0:T(8,128)(2,1)S(1)}, u32[]{:S(2)}, u32[]{:S(2)}) collective-permute-start(bf16[4,16,1792]{2,1,0:T(8,128)(2,1)S(1)} %pad_maximum_fusion.1), channel_id=1, source_target_pairs={{0,16},{8,24},{16,0},{24,8},{1,17},{9,25},{17,1},{25,9},{2,18},{10... | collective-permute-start | bytes 688136 | tf_op jit(solution)/shard_map/ppermute | solution.py:111
  22.8 10.3 %collective-permute-start.7 = (bf16[4,16,1792]{2,1,0:T(8,128)(2,1)S(1)}, bf16[4,16,1792]{2,1,0:T(8,128)(2,1)S(1)}, u32[]{:S(2)}, u32[]{:S(2)}) collective-permute-start(bf16[4,16,1792]{2,1,0:T(8,128)(2,1)S(1)} %pad_maximum_fusion.4), channel_id=1, source_target_pairs={{0,16},{8,24},{16,0},{24,8},{1,17},{9,25},{17,1},{25,9},{2,18},{10... | collective-permute-start | bytes 688136 | tf_op jit(solution)/shard_map/ppermute | solution.py:111
  23.9 9.3 %copy-start.3 = (bf16[8,16,1920]{2,1,0:T(8,128)(2,1)}, bf16[8,16,1920]{2,1,0:T(8,128)(2,1)S(1)}, u32[]{:S(2)}) copy-start(bf16[8,16,1920]{2,1,0:T(8,128)(2,1)S(1)} %constant_dynamic-update-slice_fusion) | copy-start | bytes 1474564
  33.2 2.5 %collective-permute-start.9 = (bf16[2,128,1792]{2,1,0:T(8,128)(2,1)S(1)}, bf16[2,128,1792]{2,1,0:T(8,128)(2,1)S(1)}, u32[]{:S(2)}, u32[]{:S(2)}) collective-permute-start(bf16[2,128,1792]{2,1,0:T(8,128)(2,1)S(1)} %pad_maximum_fusion), channel_id=1, source_target_pairs={{0,8},{8,0},{16,24},{24,16},{1,9},{9,1},{17,25},{25,17},{2,10},{10... | collective-permute-start | bytes 2752520 | tf_op jit(solution)/shard_map/ppermute | solution.py:111
  37.4 1.2 %copy-start.5 = (bf16[1,128,3584]{2,1,0:T(8,128)(2,1)S(1)}, bf16[1,128,3584]{2,1,0:T(8,128)(2,1)}, u32[]{:S(2)}) copy-start(bf16[1,128,3584]{2,1,0:T(8,128)(2,1)} %param.15) | copy-start | bytes 2752516
  37.8 1.7 %copy-start.2 = (bf16[1,3584,128]{2,1,0:T(8,128)(2,1)S(1)}, bf16[1,3584,128]{2,1,0:T(8,128)(2,1)}, u32[]{:S(2)}) copy-start(bf16[1,3584,128]{2,1,0:T(8,128)(2,1)} %param.14) | copy-start | bytes 2752516
  40.8 0.9 %copy-start.1 = (bf16[128,4,896]{2,0,1:T(8,128)(2,1)}, bf16[128,4,896]{2,0,1:T(8,128)(2,1)S(1)}, u32[]{:S(2)}) copy-start(bf16[128,4,896]{2,0,1:T(8,128)(2,1)S(1)} %add_convert_fusion) | copy-start | bytes 2752516
  42.5 2.0 %collective-permute-start.10 = (bf16[2,128,896]{2,1,0:T(8,128)(2,1)}, bf16[2,128,896]{2,1,0:T(8,128)(2,1)S(1)}, u32[]{:S(2)}, u32[]{:S(2)}) collective-permute-start(bf16[2,128,896]{2,1,0:T(8,128)(2,1)} %fusion.11), channel_id=1, source_target_pairs={{0,8},{8,0},{16,24},{24,16},{1,9},{9,1},{17,25},{25,17},{2,10},{10... | collective-permute-start | bytes 1376264 | tf_op jit(solution)/shard_map/ppermute | solution.py:111
  45.9 7.7 %collective-permute-start.11 = (bf16[1,128,896]{2,1,0:T(8,128)(2,1)S(1)}, bf16[1,128,896]{2,1,0:T(8,128)(2,1)S(1)}, u32[]{:S(2)}, u32[]{:S(2)}) collective-permute-start(bf16[1,128,896]{2,1,0:T(8,128)(2,1)S(1)} %fusion.14), channel_id=1, source_target_pairs={{0,16},{8,24},{16,0},{24,8},{1,17},{9,25},{17,1},{25,9},{2,18},{10... | collective-permute-start | bytes 688136 | tf_op jit(solution)/shard_map/ppermute | solution.py:111
  48.8 24.1 %copy-start.4 = (bf16[128,256]{1,0:T(8,128)(2,1)S(1)}, bf16[128,256]{1,0:T(8,128)(2,1)}, u32[]{:S(2)}) copy-start(bf16[128,256]{1,0:T(8,128)(2,1)} %get-tuple-element.6) | copy-start | bytes 196612
  53.7 10.4 %collective-permute-start.12 = (bf16[16,896]{1,0:T(8,128)(2,1)S(1)}, bf16[16,896]{1,0:T(8,128)(2,1)S(1)}, u32[]{:S(2)}, u32[]{:S(2)}) collective-permute-start(bf16[16,896]{1,0:T(8,128)(2,1)S(1)} %get-tuple-element.25), channel_id=1, source_target_pairs={{0,1},{1,0},{2,3},{3,2},{4,5},{5,4},{6,7},{7,6},{8,9},{9,8},{10,11... | collective-permute-start | bytes 86024 | tf_op jit(solution)/shard_map/ppermute | solution.py:129
  56.4 16.5 %collective-permute-start.18 = (bf16[16,896]{1,0:T(8,128)(2,1)S(1)}, bf16[16,896]{1,0:T(8,128)(2,1)S(1)}, u32[]{:S(2)}, u32[]{:S(2)}) collective-permute-start(bf16[16,896]{1,0:T(8,128)(2,1)S(1)} %get-tuple-element.19), channel_id=1, source_target_pairs={{0,7},{1,6},{2,5},{3,4},{4,3},{5,2},{6,1},{7,0},{8,15},{9,14},{10,... | collective-permute-start | bytes 86024 | tf_op jit(solution)/shard_map/ppermute | solution.py:129
  59.0 13.9 %collective-permute-start.17 = (bf16[16,896]{1,0:T(8,128)(2,1)S(1)}, bf16[16,896]{1,0:T(8,128)(2,1)S(1)}, u32[]{:S(2)}, u32[]{:S(2)}) collective-permute-start(bf16[16,896]{1,0:T(8,128)(2,1)S(1)} %get-tuple-element.20), channel_id=1, source_target_pairs={{0,6},{1,7},{2,4},{3,5},{4,2},{5,3},{6,0},{7,1},{8,14},{9,15},{10,... | collective-permute-start | bytes 86024 | tf_op jit(solution)/shard_map/ppermute | solution.py:129
  60.4 12.4 %collective-permute-start.16 = (bf16[16,896]{1,0:T(8,128)(2,1)S(1)}, bf16[16,896]{1,0:T(8,128)(2,1)S(1)}, u32[]{:S(2)}, u32[]{:S(2)}) collective-permute-start(bf16[16,896]{1,0:T(8,128)(2,1)S(1)} %get-tuple-element.21), channel_id=1, source_target_pairs={{0,5},{1,4},{2,7},{3,6},{4,1},{5,0},{6,3},{7,2},{8,13},{9,12},{10,... | collective-permute-start | bytes 86024 | tf_op jit(solution)/shard_map/ppermute | solution.py:129
  60.4 12.4 %collective-permute-start.15 = (bf16[16,896]{1,0:T(8,128)(2,1)S(1)}, bf16[16,896]{1,0:T(8,128)(2,1)S(1)}, u32[]{:S(2)}, u32[]{:S(2)}) collective-permute-start(bf16[16,896]{1,0:T(8,128)(2,1)S(1)} %get-tuple-element.22), channel_id=1, source_target_pairs={{0,4},{1,5},{2,6},{3,7},{4,0},{5,1},{6,2},{7,3},{8,12},{9,13},{10,... | collective-permute-start | bytes 86024 | tf_op jit(solution)/shard_map/ppermute | solution.py:129
  64.1 4.0 %collective-permute-start.13 = (bf16[16,896]{1,0:T(8,128)(2,1)S(1)}, bf16[16,896]{1,0:T(8,128)(2,1)S(1)}, u32[]{:S(2)}, u32[]{:S(2)}) collective-permute-start(bf16[16,896]{1,0:T(8,128)(2,1)S(1)} %get-tuple-element.24), channel_id=1, source_target_pairs={{0,2},{1,3},{2,0},{3,1},{4,6},{5,7},{6,4},{7,5},{8,10},{9,11},{10,... | collective-permute-start | bytes 86024 | tf_op jit(solution)/shard_map/ppermute | solution.py:129
  68.1 4.8 %collective-permute-start.14 = (bf16[16,896]{1,0:T(8,128)(2,1)S(1)}, bf16[16,896]{1,0:T(8,128)(2,1)S(1)}, u32[]{:S(2)}, u32[]{:S(2)}) collective-permute-start(bf16[16,896]{1,0:T(8,128)(2,1)S(1)} %get-tuple-element.23), channel_id=1, source_target_pairs={{0,3},{1,2},{2,1},{3,0},{4,7},{5,6},{6,5},{7,4},{8,11},{9,10},{10,... | collective-permute-start | bytes 86024 | tf_op jit(solution)/shard_map/ppermute | solution.py:129

commit v7 on v6

--- a/solution.py
+++ b/solution.py
@@ -40,6 +40,12 @@
     place = (lax.broadcasted_iota(jnp.int32, (slots, rows), 0) & (CAP - 1)).astype(f32)
     pick = jnp.where((hit_s == 1.0) & (rank_s == place), 1.0, 0.0)
     pick_b = pick.astype(bf16)
+    expand_abs = jnp.where(
+        lax.shift_right_logical(slot_of, 4) == lax.broadcasted_iota(jnp.int32, (slots, lanes), 1), 1.0, 0.0
+    ).astype(bf16)
+    hit_a = jnp.dot(expand_abs, hits.astype(bf16), preferred_element_type=f32)
+    rank_a = jnp.dot(expand_abs, rank.astype(bf16), preferred_element_type=f32)
+    pick_abs = jnp.where((hit_a == 1.0) & (rank_a == place), 1.0, 0.0).astype(bf16)
     tok = jnp.dot(pick_b, tok_ref[...], preferred_element_type=f32).astype(bf16)
     grd = jnp.dot(pick_b, grd_ref[...], preferred_element_type=f32).astype(bf16)
     hi = gsel.astype(bf16).astype(f32)
@@ -71,7 +77,7 @@
         pay_out[:, :width] = tok
         pay_out[:, width : 2 * width] = grd
         pay_out[:, 2 * width :] = side_v
-    pick_out[...] = pick_b
+    pick_out[...] = pick_abs
 
 
 def glue(me, expert_ids, gate_values, forget_flags, tokens, token_grads, n_dest):
@@ -221,7 +227,8 @@
     part = (from_gate + from_up).astype(jnp.bfloat16)
     summed = scatter_dp(jnp.swapaxes(part, 1, 2), n_dp).astype(jnp.bfloat16)
     back = summed.reshape(n_dest, CAP, width)
-    returned = jnp.stack([back[0] if k == 0 else swap(back[k], k, n_dest) for k in range(n_dest)]).reshape(slots, width)
+    in_order = jnp.take(back, jnp.arange(n_dest, dtype=jnp.int32) ^ me, axis=0).reshape(slots, width)
+    returned = lax.all_to_all(in_order, "expert", split_axis=0, concat_axis=0, tiled=True)
     input_grad = lax.dot_general(
         pick_t, returned, (((0,), (0,)), ((), ())), preferred_element_type=jnp.float32
     )

time: 74.4 us -> 71.9 us (0.966)
  starting transfers between devices: 26.2 us -> 21.4 us
  waiting for transfers between devices: 27.9 us -> 28.8 us
  other arithmetic: 4.27 us -> 5.06 us
    ppermute x14 -> x7, starting transfers between devices: 21.9 us -> 12.6 us  [swap(): return lax.ppermute(x, 'expert', [(i, i ^ k) for i in range(n)])]
    all_to_all x0 -> x1, waiting for transfers between devices: none -> 5.28 us  [on_device(): lax.all_to_all(in_order, 'expert', split_axis=0, concat_axis=0, tiled=True)]
    all_to_all x0 -> x1, starting transfers between devices: none -> 4.93 us  [on_device(): lax.all_to_all(in_order, 'expert', split_axis=0, concat_axis=0, tiled=True)]
    ppermute x14 -> x7, waiting for transfers between devices: 11.7 us -> 6.82 us  [swap(): return lax.ppermute(x, 'expert', [(i, i ^ k) for i in range(n)])]
    select_n x0 -> x2, other arithmetic: none -> 0.79 us  [on_device(): jnp.take(back, jnp.arange(n_dest, dtype=jnp.int32) ^ me, axis=0)]
    unnamed x27 -> x21, local copies, waits for them, and re-layouts: 2.45 us -> 2.4 us
  transfers between devices with their start and end apart: 19 -> 13, of which waited for: 8 -> 8; matrix products, arithmetic and copies ran while one was open for 8% -> 7% of each run, Pallas kernels for 0% -> 0%
where the time goes in v7:
time: 71.9 us; the launch traced here: 71.3 us
  waiting for transfers between devices  28.8 us (40%)
  starting transfers between devices  21.4 us (30%)
  matrix products  6.62 us (9%)
  local copies, waits for them, and re-layouts  5.8 us (8%)
  other arithmetic  5.06 us (7%)
  Pallas kernels  2.77 us (4%)
  between operations  0.91 us (1%)
    ppermute x5, waiting for transfers between devices, partner(): return lax.ppermute(x, 'dp', [(i, i ^ bit) for i in range(n)])  16.7 us
    ppermute x7, starting transfers between devices, swap(): return lax.ppermute(x, 'expert', [(i, i ^ k) for i in range(n)])  12.6 us
    ppermute x7, waiting for transfers between devices, swap(): return lax.ppermute(x, 'expert', [(i, i ^ k) for i in range(n)])  6.82 us
    all_to_all x1, waiting for transfers between devices, on_device(): lax.all_to_all(in_order, 'expert', split_axis=0, concat_axis=0, tiled=True)  5.28 us
    all_to_all x1, starting transfers between devices, on_device(): lax.all_to_all(in_order, 'expert', split_axis=0, concat_axis=0, tiled=True)  4.93 us
    ppermute x5, starting transfers between devices, partner(): return lax.ppermute(x, 'dp', [(i, i ^ bit) for i in range(n)])  3.91 us
    pallas_call x1, Pallas kernels, glue(): pl.pallas_call(functools.partial(glue_kernel, n_dest, width, side, split)...  2.77 us
    unnamed x21, local copies, waits for them, and re-layouts  2.4 us
  transfers between devices with their start and end apart: 13, of which 8 were waited for; matrix products, arithmetic and copies ran while one was open for 7% of the time, Pallas kernels for 0%

profile of v7, /device:TPU:0, one launch (start us, length us, event | category | flops | bytes accessed | tf_op | source)
XLA Modules:
  0.0 71.3 jit_solution(11781547064193779859)
XLA Ops:
  0.7 2.8 %shard_map.103 = (bf16[128,1920]{1,0:T(8,128)(2,1)}, bf16[128,256]{1,0:T(8,128)(2,1)}) custom-call(s32[1]{0:T(128)} %bitcast.me_ref, s32[8,256]{1,0:T(8,128)} %bitcast.186, f32[8,256]{1,0:T(8,128)} %bitcast.187, s32[1,256]{1,0:T(1,128)} %bitcast.188, bf16[256,896]{1,0:T(8,128)(2,1)} %tok_ref.1, bf16[256,896]{1,0:T(8,128)(2,1)} %grd_ref.1), custom_call_target="tpu_custom_call" | custom-call | tf_op jit(solution)/shard_map/pallas_call | solution.py:96
  3.4 1.1 %slice_bitcast_fusion.10 = (bf16[1,16,1920]{2,1,0:T(8,128)(2,1)S(1)}, bf16[16,1920]{1,0:T(8,128)(2,1)S(1)}, bf16[16,1920]{1,0:T(8,128)(2,1)S(1)}, bf16[16,1920]{...) fusion(bf16[128,1920]{1,0:T(8,128)(2,1)} %get-tuple-element.5), kind=kLoop, calls=%fused_computation.55 | loop fusion | bytes 983040 | tf_op jit(solution)/shard_map/slice | solution.py:167
  4.5 3.1 %collective-permute-start = (bf16[16,1920]{1,0:T(8,128)(2,1)S(1)}, bf16[16,1920]{1,0:T(8,128)(2,1)S(1)}, u32[]{:S(2)}, u32[]{:S(2)}) collective-permute-start(bf16[16,1920]{1,0:T(8,128)(2,1)S(1)} %get-tuple-element.18), channel_id=1, source_target_pairs={{0,1},{1,0},{2,3},{3,2},{4,5},{5,4},{6,7},{7,6},{8,9},{9,8},{10,11... | collective-permute-start | bytes 184328 | tf_op jit(solution)/shard_map/ppermute | solution.py:135
  7.6 1.6 %collective-permute-start.1 = (bf16[16,1920]{1,0:T(8,128)(2,1)S(1)}, bf16[16,1920]{1,0:T(8,128)(2,1)S(1)}, u32[]{:S(2)}, u32[]{:S(2)}) collective-permute-start(bf16[16,1920]{1,0:T(8,128)(2,1)S(1)} %get-tuple-element.17), channel_id=1, source_target_pairs={{0,2},{1,3},{2,0},{3,1},{4,6},{5,7},{6,4},{7,5},{8,10},{9,11},{10,... | collective-permute-start | bytes 184328 | tf_op jit(solution)/shard_map/ppermute | solution.py:135
  9.1 3.0 %collective-permute-start.3 = (bf16[16,1920]{1,0:T(8,128)(2,1)S(1)}, bf16[16,1920]{1,0:T(8,128)(2,1)S(1)}, u32[]{:S(2)}, u32[]{:S(2)}) collective-permute-start(bf16[16,1920]{1,0:T(8,128)(2,1)S(1)} %get-tuple-element.15), channel_id=1, source_target_pairs={{0,4},{1,5},{2,6},{3,7},{4,0},{5,1},{6,2},{7,3},{8,12},{9,13},{10,... | collective-permute-start | bytes 184328 | tf_op jit(solution)/shard_map/ppermute | solution.py:135
  12.1 1.3 %collective-permute-start.4 = (bf16[16,1920]{1,0:T(8,128)(2,1)S(1)}, bf16[16,1920]{1,0:T(8,128)(2,1)S(1)}, u32[]{:S(2)}, u32[]{:S(2)}) collective-permute-start(bf16[16,1920]{1,0:T(8,128)(2,1)S(1)} %get-tuple-element.14), channel_id=1, source_target_pairs={{0,5},{1,4},{2,7},{3,6},{4,1},{5,0},{6,3},{7,2},{8,13},{9,12},{10,... | collective-permute-start | bytes 184328 | tf_op jit(solution)/shard_map/ppermute | solution.py:135
  13.4 0.8 %constant_dynamic-update-slice_fusion.7 = bf16[8,16,1920]{2,1,0:T(8,128)(2,1)S(1)} fusion(bf16[128,1920]{1,0:T(8,128)(2,1)} %get-tuple-element.5), kind=kLoop, calls=%fused_computation.65 | loop fusion | bytes 122880
  14.2 3.6 %collective-permute-start.5 = (bf16[16,1920]{1,0:T(8,128)(2,1)S(1)}, bf16[16,1920]{1,0:T(8,128)(2,1)S(1)}, u32[]{:S(2)}, u32[]{:S(2)}) collective-permute-start(bf16[16,1920]{1,0:T(8,128)(2,1)S(1)} %get-tuple-element.13), channel_id=1, source_target_pairs={{0,6},{1,7},{2,4},{3,5},{4,2},{5,3},{6,0},{7,1},{8,14},{9,15},{10,... | collective-permute-start | bytes 184328 | tf_op jit(solution)/shard_map/ppermute | solution.py:135
  18.0 3.1 %collective-permute-done.4 = bf16[16,1920]{1,0:T(8,128)(2,1)S(1)} collective-permute-done((bf16[16,1920]{1,0:T(8,128)(2,1)S(1)}, bf16[16,1920]{1,0:T(8,128)(2,1)S(1)}, u32[]{:S(2)}, u32[]{:S(2)}) %collective-permute-start.4) | collective-permute-done | bytes 61472 | tf_op jit(solution)/shard_map/ppermute | solution.py:135
  21.2 3.7 %collective-permute-done.6 = bf16[16,1920]{1,0:T(8,128)(2,1)S(1)} collective-permute-done((bf16[16,1920]{1,0:T(8,128)(2,1)S(1)}, bf16[16,1920]{1,0:T(8,128)(2,1)S(1)}, u32[]{:S(2)}, u32[]{:S(2)}) %collective-permute-start.6) | collective-permute-done | bytes 61472 | tf_op jit(solution)/shard_map/ppermute | solution.py:135
  24.9 0.9 %slice_bitcast_fusion.13 = (bf16[1,128,1792]{2,1,0:T(8,128)(2,1)S(1)}, bf16[128,1792]{1,0:T(8,128)(2,1)}) fusion(bf16[128,1920]{1,0:T(8,128)(2,1)S(1)} %bitcast.177), kind=kLoop, calls=%fused_computation.105 | loop fusion | bytes 1376256 | tf_op jit(solution)/shard_map/stack | solution.py:122
  25.8 1.6 %collective-permute-start.7 = (bf16[4,16,1792]{2,1,0:T(8,128)(2,1)S(1)}, bf16[4,16,1792]{2,1,0:T(8,128)(2,1)S(1)}, u32[]{:S(2)}, u32[]{:S(2)}) collective-permute-start(bf16[4,16,1792]{2,1,0:T(8,128)(2,1)S(1)} %pad_maximum_fusion.4), channel_id=1, source_target_pairs={{0,16},{8,24},{16,0},{24,8},{1,17},{9,25},{17,1},{25,9},{2,18},{10... | collective-permute-start | bytes 688136 | tf_op jit(solution)/shard_map/ppermute | solution.py:117
  27.4 0.6 collective-permute-start.8
  28.0 5.0 %collective-permute-done.7 = bf16[4,16,1792]{2,1,0:T(8,128)(2,1)S(1)} collective-permute-done((bf16[4,16,1792]{2,1,0:T(8,128)(2,1)S(1)}, bf16[4,16,1792]{2,1,0:T(8,128)(2,1)S(1)}, u32[]{:S(2)}, u32[]{:S(2)}) %collective-permute-start.7) | collective-permute-done | bytes 229408 | tf_op jit(solution)/shard_map/ppermute | solution.py:117
  32.9 2.4 %collective-permute-done.8 = bf16[4,16,1792]{2,1,0:T(8,128)(2,1)S(1)} collective-permute-done((bf16[4,16,1792]{2,1,0:T(8,128)(2,1)S(1)}, bf16[4,16,1792]{2,1,0:T(8,128)(2,1)S(1)}, u32[]{:S(2)}, u32[]{:S(2)}) %collective-permute-start.8) | collective-permute-done | bytes 229408 | tf_op jit(solution)/shard_map/ppermute | solution.py:117
  35.6 0.8 %slice.157 = bf16[128,128]{1,0:T(8,128)(2,1)S(1)} slice(bf16[128,1920]{1,0:T(8,128)(2,1)} %bitcast.178), slice={[0:128], [1792:1920]} | slice | bytes 65536 | tf_op jit(solution)/shard_map/slice | solution.py:172
  36.8 1.2 %collective-permute-done.9 = bf16[2,128,1792]{2,1,0:T(8,128)(2,1)S(1)} collective-permute-done((bf16[2,128,1792]{2,1,0:T(8,128)(2,1)S(1)}, bf16[2,128,1792]{2,1,0:T(8,128)(2,1)S(1)}, u32[]{:S(2)}, u32[]{:S(2)}) %collective-permute-start.9) | collective-permute-done | bytes 917536 | tf_op jit(solution)/shard_map/ppermute | solution.py:117
  38.1 1.5 %select_select_fusion = bf16[4,128,1792]{2,1,0:T(8,128)(2,1)S(1)} fusion(pred[4]{0:T(512)(128)(4,1)S(1)} %get-tuple-element.21, pred[4]{0:T(512)(128)(4,1)S(1)} %get-tuple-element.22, pred[4]{0:T(512)(128)(4,1)S(1)} %iota_compare_fusion.2, bf16[128,1792]{1,0:T(8,128)(2,1)} %get-tuple-element.10, bf16[128,1792]{1,0:T(8,128)(2,1)S(1)} %bitcast.170, ...), kind=kLoop, calls=%fused_computation.3 | loop fusion | flops 2752512 | bytes 3670028 | tf_op jit(solution)/shard_map/jit(_where)/select_n | solution.py:130
  40.4 0.4 copy-done.5
  43.0 0.9 %copy-done.1 = bf16[128,4,896]{2,0,1:T(8,128)(2,1)} copy-done((bf16[128,4,896]{2,0,1:T(8,128)(2,1)}, bf16[128,4,896]{2,0,1:T(8,128)(2,1)S(1)}, u32[]{:S(2)}) %copy-start.1) | copy-done | bytes 917528
  44.0 0.8 %fusion.11 = bf16[2,128,896]{2,1,0:T(8,128)(2,1)} fusion(pred[]{:T(512)S(6)} %ne.18, bf16[2,2,128,896]{3,2,1,0:T(8,128)(2,1)S(1)} %bitcast.167), kind=kLoop, calls=%fused_computation.28 | loop fusion | flops 229376 | bytes 1376257 | tf_op jit(solution)/shard_map/jit(_where)/select_n | solution.py:146
  44.9 1.9 %collective-permute-done.10 = bf16[2,128,896]{2,1,0:T(8,128)(2,1)S(1)} collective-permute-done((bf16[2,128,896]{2,1,0:T(8,128)(2,1)}, bf16[2,128,896]{2,1,0:T(8,128)(2,1)S(1)}, u32[]{:S(2)}, u32[]{:S(2)}) %collective-permute-start.10) | collective-permute-done | bytes 458784 | tf_op jit(solution)/shard_map/ppermute | solution.py:117
  46.8 1.3 %fusion.6 = f32[1,2,128,896]{3,2,1,0:T(8,128)S(1)} fusion(bf16[2,128,896]{2,1,0:T(8,128)(2,1)S(1)} %collective-permute-done.10, pred[]{:T(512)S(6)} %ne.18, bf16[2,2,128,896]{3,2,1,0:T(8,128)(2,1)} %bitcast.168), kind=kLoop, calls=%fused_computation.22 | loop fusion | flops 917504 | bytes 2293761 | tf_op jit(solution)/shard_map/reshape | solution.py:143
  48.2 1.6 %collective-permute-start.11 = (bf16[1,128,896]{2,1,0:T(8,128)(2,1)S(1)}, bf16[1,128,896]{2,1,0:T(8,128)(2,1)S(1)}, u32[]{:S(2)}, u32[]{:S(2)}) collective-permute-start(bf16[1,128,896]{2,1,0:T(8,128)(2,1)S(1)} %fusion.14), channel_id=1, source_target_pairs={{0,16},{8,24},{16,0},{24,8},{1,17},{9,25},{17,1},{25,9},{2,18},{10... | collective-permute-start | bytes 688136 | tf_op jit(solution)/shard_map/ppermute | solution.py:117
  49.8 6.1 %collective-permute-done.11 = bf16[1,128,896]{2,1,0:T(8,128)(2,1)S(1)} collective-permute-done((bf16[1,128,896]{2,1,0:T(8,128)(2,1)S(1)}, bf16[1,128,896]{2,1,0:T(8,128)(2,1)S(1)}, u32[]{:S(2)}, u32[]{:S(2)}) %collective-permute-start.11) | collective-permute-done | bytes 229408 | tf_op jit(solution)/shard_map/ppermute | solution.py:117
  56.0 0.6 gather_fusion
  56.5 0.8 %broadcast_select_fusion = bf16[8,16,896]{2,1,0:T(8,128)(2,1)} fusion(bf16[8,16,896]{2,1,0:T(8,128)(2,1)S(1)} %gather_fusion, pred[8]{0:T(512)(128)(4,1)S(1)} %compare_and_fusion), kind=kLoop, calls=%fused_computation.52 | loop fusion | flops 114688 | bytes 458760 | tf_op jit(solution)/shard_map/jit(_take)/select_n | solution.py:230
  57.3 4.9 %all-to-all-start = ((bf16[8,16,896]{2,1,0:T(8,128)(2,1)}), bf16[8,16,896]{2,1,0:T(8,128)(2,1)S(1)}, u32[]{:S(2)}, u32[]{:S(2)}) async-start(bf16[8,16,896]{2,1,0:T(8,128)(2,1)} %broadcast_select_fusion), calls=%async_computation | async-start | bytes 458752 | tf_op jit(solution)/shard_map/all_to_all | solution.py:231
  62.3 1.4 %convolution_convert_fusion.1 = bf16[4,896,128]{2,1,0:T(8,128)(2,1)} fusion(bf16[128,128,1]{1,0,2:T(8,128)(2,1)S(1)} %fusion.3, bf16[4,128,1792]{2,1,0:T(8,128)(2,1)S(1)} %select_select_fusion), kind=kOutput, calls=%fused_computation.5 | convolution fusion | flops 117899264 | bytes 1867776 | tf_op jit(solution)/shard_map/dot_general | solution.py:218
  63.6 1.4 %convolution_convert_fusion = bf16[4,896,128]{2,1,0:T(8,128)(2,1)} fusion(bf16[4,128,1792]{2,1,0:T(8,128)(2,1)S(1)} %select_select_fusion, bf16[128,128]{1,0:T(8,128)(2,1)S(1)} %get-tuple-element.19), kind=kOutput, calls=%fused_computation.4 | convolution fusion | flops 117899264 | bytes 1867776 | tf_op jit(solution)/shard_map/dot_general | solution.py:221
  65.0 5.3 %all-to-all-done = bf16[8,16,896]{2,1,0:T(8,128)(2,1)S(1)} async-done(((bf16[8,16,896]{2,1,0:T(8,128)(2,1)}), bf16[8,16,896]{2,1,0:T(8,128)(2,1)S(1)}, u32[]{:S(2)}, u32[]{:S(2)}) %all-to-all-start) | async-done | bytes 229408 | tf_op jit(solution)/shard_map/all_to_all | solution.py:231
  70.3 1.1 %convolution_convert_fusion.2 = bf16[256,896]{1,0:T(8,128)(2,1)} fusion(bf16[128,256]{1,0:T(8,128)(2,1)S(1)} %copy-done.4, bf16[128,896]{1,0:T(8,128)(2,1)S(1)} %bitcast.176), kind=kOutput, calls=%fused_computation.6 | convolution fusion | flops 58949632 | bytes 753664 | tf_op jit(solution)/shard_map/dot_general | solution.py:232
  (52 shorter events, 4.0 us)
Async XLA Ops:
  0.6 39.0 %copy-start = (bf16[1,3584,128]{2,1,0:T(8,128)(2,1)S(1)}, bf16[1,3584,128]{2,1,0:T(8,128)(2,1)}, u32[]{:S(2)}) copy-start(bf16[1,3584,128]{2,1,0:T(8,128)(2,1)} %param.13) | copy-start | bytes 2752516
  4.5 9.7 %collective-permute-start = (bf16[16,1920]{1,0:T(8,128)(2,1)S(1)}, bf16[16,1920]{1,0:T(8,128)(2,1)S(1)}, u32[]{:S(2)}, u32[]{:S(2)}) collective-permute-start(bf16[16,1920]{1,0:T(8,128)(2,1)S(1)} %get-tuple-element.18), channel_id=1, source_target_pairs={{0,1},{1,0},{2,3},{3,2},{4,5},{5,4},{6,7},{7,6},{8,9},{9,8},{10,11... | collective-permute-start | bytes 184328 | tf_op jit(solution)/shard_map/ppermute | solution.py:135
  7.6 10.3 %collective-permute-start.1 = (bf16[16,1920]{1,0:T(8,128)(2,1)S(1)}, bf16[16,1920]{1,0:T(8,128)(2,1)S(1)}, u32[]{:S(2)}, u32[]{:S(2)}) collective-permute-start(bf16[16,1920]{1,0:T(8,128)(2,1)S(1)} %get-tuple-element.17), channel_id=1, source_target_pairs={{0,2},{1,3},{2,0},{3,1},{4,6},{5,7},{6,4},{7,5},{8,10},{9,11},{10,... | collective-permute-start | bytes 184328 | tf_op jit(solution)/shard_map/ppermute | solution.py:135
  9.1 8.8 %collective-permute-start.2 = (bf16[16,1920]{1,0:T(8,128)(2,1)S(1)}, bf16[16,1920]{1,0:T(8,128)(2,1)S(1)}, u32[]{:S(2)}, u32[]{:S(2)}) collective-permute-start(bf16[16,1920]{1,0:T(8,128)(2,1)S(1)} %get-tuple-element.16), channel_id=1, source_target_pairs={{0,3},{1,2},{2,1},{3,0},{4,7},{5,6},{6,5},{7,4},{8,11},{9,10},{10,... | collective-permute-start | bytes 184328 | tf_op jit(solution)/shard_map/ppermute | solution.py:135
  9.1 8.8 %collective-permute-start.3 = (bf16[16,1920]{1,0:T(8,128)(2,1)S(1)}, bf16[16,1920]{1,0:T(8,128)(2,1)S(1)}, u32[]{:S(2)}, u32[]{:S(2)}) collective-permute-start(bf16[16,1920]{1,0:T(8,128)(2,1)S(1)} %get-tuple-element.15), channel_id=1, source_target_pairs={{0,4},{1,5},{2,6},{3,7},{4,0},{5,1},{6,2},{7,3},{8,12},{9,13},{10,... | collective-permute-start | bytes 184328 | tf_op jit(solution)/shard_map/ppermute | solution.py:135
  12.1 9.0 %collective-permute-start.4 = (bf16[16,1920]{1,0:T(8,128)(2,1)S(1)}, bf16[16,1920]{1,0:T(8,128)(2,1)S(1)}, u32[]{:S(2)}, u32[]{:S(2)}) collective-permute-start(bf16[16,1920]{1,0:T(8,128)(2,1)S(1)} %get-tuple-element.14), channel_id=1, source_target_pairs={{0,5},{1,4},{2,7},{3,6},{4,1},{5,0},{6,3},{7,2},{8,13},{9,12},{10,... | collective-permute-start | bytes 184328 | tf_op jit(solution)/shard_map/ppermute | solution.py:135
  14.2 6.9 %collective-permute-start.5 = (bf16[16,1920]{1,0:T(8,128)(2,1)S(1)}, bf16[16,1920]{1,0:T(8,128)(2,1)S(1)}, u32[]{:S(2)}, u32[]{:S(2)}) collective-permute-start(bf16[16,1920]{1,0:T(8,128)(2,1)S(1)} %get-tuple-element.13), channel_id=1, source_target_pairs={{0,6},{1,7},{2,4},{3,5},{4,2},{5,3},{6,0},{7,1},{8,14},{9,15},{10,... | collective-permute-start | bytes 184328 | tf_op jit(solution)/shard_map/ppermute | solution.py:135
  17.9 7.0 %collective-permute-start.6 = (bf16[16,1920]{1,0:T(8,128)(2,1)S(1)}, bf16[16,1920]{1,0:T(8,128)(2,1)S(1)}, u32[]{:S(2)}, u32[]{:S(2)}) collective-permute-start(bf16[16,1920]{1,0:T(8,128)(2,1)S(1)} %get-tuple-element.12), channel_id=1, source_target_pairs={{0,7},{1,6},{2,5},{3,4},{4,3},{5,2},{6,1},{7,0},{8,15},{9,14},{10,... | collective-permute-start | bytes 184328 | tf_op jit(solution)/shard_map/ppermute | solution.py:135
  24.9 10.5 %copy-start.3 = (bf16[8,16,1920]{2,1,0:T(8,128)(2,1)}, bf16[8,16,1920]{2,1,0:T(8,128)(2,1)S(1)}, u32[]{:S(2)}) copy-start(bf16[8,16,1920]{2,1,0:T(8,128)(2,1)S(1)} %constant_dynamic-update-slice_fusion) | copy-start | bytes 1474564
  25.8 7.1 %collective-permute-start.7 = (bf16[4,16,1792]{2,1,0:T(8,128)(2,1)S(1)}, bf16[4,16,1792]{2,1,0:T(8,128)(2,1)S(1)}, u32[]{:S(2)}, u32[]{:S(2)}) collective-permute-start(bf16[4,16,1792]{2,1,0:T(8,128)(2,1)S(1)} %pad_maximum_fusion.4), channel_id=1, source_target_pairs={{0,16},{8,24},{16,0},{24,8},{1,17},{9,25},{17,1},{25,9},{2,18},{10... | collective-permute-start | bytes 688136 | tf_op jit(solution)/shard_map/ppermute | solution.py:117
  27.4 8.0 %collective-permute-start.8 = (bf16[4,16,1792]{2,1,0:T(8,128)(2,1)S(1)}, bf16[4,16,1792]{2,1,0:T(8,128)(2,1)S(1)}, u32[]{:S(2)}, u32[]{:S(2)}) collective-permute-start(bf16[4,16,1792]{2,1,0:T(8,128)(2,1)S(1)} %pad_maximum_fusion.1), channel_id=1, source_target_pairs={{0,16},{8,24},{16,0},{24,8},{1,17},{9,25},{17,1},{25,9},{2,18},{10... | collective-permute-start | bytes 688136 | tf_op jit(solution)/shard_map/ppermute | solution.py:117
  35.5 2.5 %collective-permute-start.9 = (bf16[2,128,1792]{2,1,0:T(8,128)(2,1)S(1)}, bf16[2,128,1792]{2,1,0:T(8,128)(2,1)S(1)}, u32[]{:S(2)}, u32[]{:S(2)}) collective-permute-start(bf16[2,128,1792]{2,1,0:T(8,128)(2,1)S(1)} %pad_maximum_fusion), channel_id=1, source_target_pairs={{0,8},{8,0},{16,24},{24,16},{1,9},{9,1},{17,25},{25,17},{2,10},{10... | collective-permute-start | bytes 2752520 | tf_op jit(solution)/shard_map/ppermute | solution.py:117
  39.7 1.2 %copy-start.5 = (bf16[1,128,3584]{2,1,0:T(8,128)(2,1)S(1)}, bf16[1,128,3584]{2,1,0:T(8,128)(2,1)}, u32[]{:S(2)}) copy-start(bf16[1,128,3584]{2,1,0:T(8,128)(2,1)} %param.15) | copy-start | bytes 2752516
  40.1 1.7 %copy-start.2 = (bf16[1,3584,128]{2,1,0:T(8,128)(2,1)S(1)}, bf16[1,3584,128]{2,1,0:T(8,128)(2,1)}, u32[]{:S(2)}) copy-start(bf16[1,3584,128]{2,1,0:T(8,128)(2,1)} %param.14) | copy-start | bytes 2752516
  43.0 0.9 %copy-start.1 = (bf16[128,4,896]{2,0,1:T(8,128)(2,1)}, bf16[128,4,896]{2,0,1:T(8,128)(2,1)S(1)}, u32[]{:S(2)}) copy-start(bf16[128,4,896]{2,0,1:T(8,128)(2,1)S(1)} %add_convert_fusion) | copy-start | bytes 2752516
  44.8 2.0 %collective-permute-start.10 = (bf16[2,128,896]{2,1,0:T(8,128)(2,1)}, bf16[2,128,896]{2,1,0:T(8,128)(2,1)S(1)}, u32[]{:S(2)}, u32[]{:S(2)}) collective-permute-start(bf16[2,128,896]{2,1,0:T(8,128)(2,1)} %fusion.11), channel_id=1, source_target_pairs={{0,8},{8,0},{16,24},{24,16},{1,9},{9,1},{17,25},{25,17},{2,10},{10... | collective-permute-start | bytes 1376264 | tf_op jit(solution)/shard_map/ppermute | solution.py:117
  48.2 7.7 %collective-permute-start.11 = (bf16[1,128,896]{2,1,0:T(8,128)(2,1)S(1)}, bf16[1,128,896]{2,1,0:T(8,128)(2,1)S(1)}, u32[]{:S(2)}, u32[]{:S(2)}) collective-permute-start(bf16[1,128,896]{2,1,0:T(8,128)(2,1)S(1)} %fusion.14), channel_id=1, source_target_pairs={{0,16},{8,24},{16,0},{24,8},{1,17},{9,25},{17,1},{25,9},{2,18},{10... | collective-permute-start | bytes 688136 | tf_op jit(solution)/shard_map/ppermute | solution.py:117
  57.3 12.9 %all-to-all-start = ((bf16[8,16,896]{2,1,0:T(8,128)(2,1)}), bf16[8,16,896]{2,1,0:T(8,128)(2,1)S(1)}, u32[]{:S(2)}, u32[]{:S(2)}) async-start(bf16[8,16,896]{2,1,0:T(8,128)(2,1)} %broadcast_select_fusion), calls=%async_computation | async-start | bytes 458752 | tf_op jit(solution)/shard_map/all_to_all | solution.py:231
  62.3 8.0 %copy-start.4 = (bf16[128,256]{1,0:T(8,128)(2,1)S(1)}, bf16[128,256]{1,0:T(8,128)(2,1)}, u32[]{:S(2)}) copy-start(bf16[128,256]{1,0:T(8,128)(2,1)} %get-tuple-element.6) | copy-start | bytes 196612

commit v8 on v5

--- a/solution.py
+++ b/solution.py
@@ -129,6 +129,26 @@
     return out
 
 
+def gather_half(x, n):
+    me = lax.axis_index("dp")
+    top = n // 2
+    base = me & top
+    held = [x]
+    owners = [me]
+    bit = top // 2
+    while bit >= 1:
+        stacked = jnp.stack(held)
+        got = partner(stacked, bit, n)
+        held = held + [got[i] for i in range(len(held))]
+        owners = owners + [o ^ bit for o in owners]
+        bit //= 2
+    at = lax.broadcasted_iota(jnp.int32, (top, 1, 1), 0)
+    out = jnp.broadcast_to(held[0][None], (top,) + x.shape)
+    for piece, owner in zip(held[1:], owners[1:]):
+        out = jnp.where(at == owner - base, piece[None], out)
+    return out, base
+
+
 def scatter_dp(parts, n):
     me = lax.axis_index("dp")
     acc = parts
@@ -150,6 +170,14 @@
     n_dest = lax.axis_size("expert")
     n_dp = lax.axis_size("dp")
     row_count, width = tokens.shape
+    me_dp = lax.axis_index("dp")
+    w_down = down_weight[0]
+    top = n_dp // 2
+    half_cols = (n_dp * width) // 2
+    if n_dp > 1:
+        upper_half = (me_dp & top) != 0
+        lend = jnp.where(upper_half, w_down[:, :half_cols], w_down[:, half_cols:])
+        borrowed = partner(lend, top, n_dp)
     payload, pick_t = glue(expert_ids, gate_values, forget_flags, tokens, token_grads, n_dest)
     side = payload.shape[1] - 2 * width
     arrived = lax.all_to_all(payload, "expert", split_axis=0, concat_axis=0, tiled=True)
@@ -175,26 +203,32 @@
     )
     scale = gate_sel * weight
     part_grads = (scale[:, None] * raw_grads.astype(jnp.float32)).astype(jnp.bfloat16)
-    both = jnp.concatenate([part_tokens, part_grads], axis=1)
-    gathered = gather_dp(both, n_dp)
-    slot_tokens = gathered[:, :, :width]
-    slot_grads = gathered[:, :, width:]
     ff = gate_weight.shape[2]
     w_gate = gate_weight[0].reshape(n_dp, width, ff)
     w_up = up_weight[0].reshape(n_dp, width, ff)
-    w_down = down_weight[0]
+    last_dims = (((1,), (1,)), ((), ()))
+    slot_tokens = gather_dp(part_tokens, n_dp)
+    if n_dp > 1:
+        half_grads, base = gather_half(part_grads, n_dp)
+        hidden_grad = None
+        lent = None
+        for i in range(top):
+            mine = lax.dot_general(
+                half_grads[i], lax.dynamic_slice_in_dim(w_down, (base + i) * width, width, axis=1),
+                last_dims, preferred_element_type=jnp.float32,
+            )
+            theirs = lax.dot_general(
+                half_grads[i], borrowed[:, i * width : (i + 1) * width], last_dims,
+                preferred_element_type=jnp.float32,
+            )
+            hidden_grad = mine if hidden_grad is None else hidden_grad + mine
+            lent = theirs if lent is None else lent + theirs
+        hidden_grad = hidden_grad + partner(lent, top, n_dp)
+    else:
+        hidden_grad = lax.dot_general(part_grads, w_down, last_dims, preferred_element_type=jnp.float32)
     chunk_dims = (((0, 2), (0, 1)), ((), ()))
     gate_pre = lax.dot_general(slot_tokens, w_gate, chunk_dims, preferred_element_type=jnp.float32)
     up_pre = lax.dot_general(slot_tokens, w_up, chunk_dims, preferred_element_type=jnp.float32)
-    last_dims = (((1,), (1,)), ((), ()))
-    hidden_grad = lax.dot_general(
-        slot_grads[0], w_down[:, :width], last_dims, preferred_element_type=jnp.float32
-    )
-    for j in range(1, n_dp):
-        hidden_grad = hidden_grad + lax.dot_general(
-            slot_grads[j], w_down[:, j * width : (j + 1) * width], last_dims,
-            preferred_element_type=jnp.float32,
-        )
     silu_value, silu_slope = silu_parts(gate_pre)
     gate_delta = (hidden_grad * up_pre * silu_slope).astype(jnp.bfloat16)
     up_delta = (hidden_grad * silu_value).astype(jnp.bfloat16)

time: 69.5 us -> 70.2 us (1.010)
  blocking collectives: 21.1 us -> 0 us
  starting transfers between devices: 7.69 us -> 17.1 us
  waiting for transfers between devices: 25.5 us -> 31.7 us
  matrix products: 6.62 us -> 10.4 us
  other arithmetic: 3.18 us -> 5.09 us
    all_to_all x1 -> x0, blocking collectives: 21.1 us -> none  [on_device(): lax.all_to_all(payload, 'expert', split_axis=0, concat_axis=0, tiled=True)]
    all_to_all x0 -> x1, waiting for transfers between devices: none -> 11.4 us  [on_device(): lax.all_to_all(payload, 'expert', split_axis=0, concat_axis=0, tiled=True)]
    all_to_all x0 -> x1, starting transfers between devices: none -> 7.31 us  [on_device(): lax.all_to_all(payload, 'expert', split_axis=0, concat_axis=0, tiled=True)]
    ppermute x4 -> x7, waiting for transfers between devices: 20.2 us -> 15 us  [partner(): return lax.ppermute(x, 'dp', [(i, i ^ bit) for i in range(n)])]
    dot_general x4, matrix products: 0.92 us -> 4.28 us  [the longest x2 2.96 us: on_device(): lax.dot_general(half_grads[i], borrowed[:, i * width:(i + 1) * width], la...]
    ppermute x4 -> x7, starting transfers between devices: 3.32 us -> 6.15 us  [partner(): return lax.ppermute(x, 'dp', [(i, i ^ bit) for i in range(n)])]
    broadcast_in_dim x1 -> x4, local copies, waits for them, and re-layouts: 0.06 us -> 1.6 us  [gather_dp(): out = jnp.where(at == owner, piece[None], out)]
    unnamed x12 -> x8, local copies, waits for them, and re-layouts: 1.44 us -> 0.02 us
  transfers between devices with their start and end apart: 5 -> 9, of which waited for: 5 -> 6; matrix products, arithmetic and copies ran while one was open for 4% -> 18% of each run, Pallas kernels for 0% -> 0%
where the time goes in v8:
time: 70.2 us; the launch traced here: 69.8 us
  waiting for transfers between devices  31.7 us (45%)
  starting transfers between devices  17.1 us (24%)
  matrix products  10.4 us (15%)
  other arithmetic  5.09 us (7%)
  Pallas kernels  2.81 us (4%)
  local copies, waits for them, and re-layouts  1.84 us (3%)
  between operations  0.83 us (1%)
    ppermute x7, waiting for transfers between devices, partner(): return lax.ppermute(x, 'dp', [(i, i ^ bit) for i in range(n)])  15 us
    all_to_all x1, waiting for transfers between devices, on_device(): lax.all_to_all(payload, 'expert', split_axis=0, concat_axis=0, tiled=True)  11.4 us
    all_to_all x1, starting transfers between devices, on_device(): lax.all_to_all(payload, 'expert', split_axis=0, concat_axis=0, tiled=True)  7.31 us
    ppermute x7, starting transfers between devices, partner(): return lax.ppermute(x, 'dp', [(i, i ^ bit) for i in range(n)])  6.15 us
    all_to_all x1, waiting for transfers between devices, on_device(): lax.all_to_all(summed, 'expert', split_axis=0, concat_axis=0, tiled=True)  5.28 us
    all_to_all x1, starting transfers between devices, on_device(): lax.all_to_all(summed, 'expert', split_axis=0, concat_axis=0, tiled=True)  3.65 us
    dot_general x2, matrix products, on_device(): lax.dot_general(half_grads[i], borrowed[:, i * width:(i + 1) * width], la...  2.96 us
    pallas_call x1, Pallas kernels, glue(): pl.pallas_call(functools.partial(glue_kernel, n_dest, width, side, split)...  2.81 us
  transfers between devices with their start and end apart: 9, of which 6 were waited for; matrix products, arithmetic and copies ran while one was open for 18% of the time, Pallas kernels for 0%

profile of v8, /device:TPU:0, one launch (start us, length us, event | category | flops | bytes accessed | tf_op | source)
XLA Modules:
  0.0 69.8 jit_solution(5311890307059504544)
XLA Ops:
  0.7 2.8 %shard_map.103 = (bf16[128,1920]{1,0:T(8,128)(2,1)}, bf16[128,256]{1,0:T(8,128)(2,1)}) custom-call(s32[8,256]{1,0:T(8,128)} %bitcast.133, f32[8,256]{1,0:T(8,128)} %bitcast.134, s32[1,256]{1,0:T(1,128)} %bitcast.135, bf16[256,896]{1,0:T(8,128)(2,1)} %tok_ref.1, bf16[256,896]{1,0:T(8,128)(2,1)} %grd_ref.1), custom_call_target="tpu_custom_call" | custom-call | tf_op jit(solution)/shard_map/pallas_call | solution.py:90
  3.5 7.3 %all-to-all-start = ((bf16[8,16,1920]{2,1,0:T(8,128)(2,1)}), bf16[8,16,1920]{2,1,0:T(8,128)(2,1)S(1)}, u32[]{:S(2)}, u32[]{:S(2)}) async-start(bf16[8,16,1920]{2,1,0:T(8,128)(2,1)} %bitcast.132), calls=%async_computation | async-start | bytes 983040 | tf_op jit(solution)/shard_map/all_to_all | solution.py:183
  10.8 0.8 %slice_select_fusion = bf16[128,1792]{1,0:T(8,128)(2,1)} fusion(bf16[128,3584]{1,0:T(8,128)(2,1)S(1)} %bitcast.127, pred[]{:T(512)S(6)} %ne.18), kind=kLoop, calls=%fused_computation.33 | loop fusion | flops 229376 | bytes 1376257 | tf_op jit(solution)/shard_map/jit(_where)/select_n | solution.py:179
  11.6 1.5 %collective-permute-start.3 = (bf16[128,1792]{1,0:T(8,128)(2,1)}, bf16[128,1792]{1,0:T(8,128)(2,1)}, u32[]{:S(2)}, u32[]{:S(2)}) collective-permute-start(bf16[128,1792]{1,0:T(8,128)(2,1)} %slice_select_fusion), channel_id=1, source_target_pairs={{0,16},{8,24},{16,0},{24,8},{1,17},{9,25},{17,1},{25,9},{2,18},{10... | collective-permute-start | bytes 1376264 | tf_op jit(solution)/shard_map/ppermute | solution.py:111
  13.1 11.4 %all-to-all-done = bf16[8,16,1920]{2,1,0:T(8,128)(2,1)S(1)} async-done(((bf16[8,16,1920]{2,1,0:T(8,128)(2,1)}), bf16[8,16,1920]{2,1,0:T(8,128)(2,1)S(1)}, u32[]{:S(2)}, u32[]{:S(2)}) %all-to-all-start) | async-done | bytes 491552 | tf_op jit(solution)/shard_map/all_to_all | solution.py:183
  24.6 0.2 slice_reduce_fusion
  24.8 0.2 fusion.51
  25.3 0.8 %fusion.86 = bf16[1,128,896]{2,1,0:T(8,128)(2,1)} fusion(bf16[128,1920]{1,0:T(8,128)(2,1)S(1)} %bitcast.125, f32[128]{0:T(128)S(1)} %fusion.58), kind=kLoop, calls=%fused_computation.114 | loop fusion | flops 344064 | bytes 459264 | tf_op jit(solution)/shard_map/stack | solution.py:140
  26.2 1.5 %collective-permute-start = (bf16[1,128,896]{2,1,0:T(8,128)(2,1)S(1)}, bf16[1,128,896]{2,1,0:T(8,128)(2,1)S(1)}, u32[]{:S(2)}, u32[]{:S(2)}) collective-permute-start(bf16[1,128,896]{2,1,0:T(8,128)(2,1)S(1)} %get-tuple-element.10), channel_id=1, source_target_pairs={{0,16},{8,24},{16,0},{24,8},{1,17},{9,25},{17,1},{25,9},{2,18},{10... | collective-permute-start | bytes 688136 | tf_op jit(solution)/shard_map/ppermute | solution.py:111
  27.9 6.2 %collective-permute-done = bf16[1,128,896]{2,1,0:T(8,128)(2,1)S(1)} collective-permute-done((bf16[1,128,896]{2,1,0:T(8,128)(2,1)S(1)}, bf16[1,128,896]{2,1,0:T(8,128)(2,1)S(1)}, u32[]{:S(2)}, u32[]{:S(2)}) %collective-permute-start) | collective-permute-done | bytes 229408 | tf_op jit(solution)/shard_map/ppermute | solution.py:111
  34.2 0.8 %pad_maximum_fusion = bf16[2,128,896]{2,1,0:T(8,128)(2,1)} fusion(bf16[1,128,896]{2,1,0:T(8,128)(2,1)S(1)} %collective-permute-done, bf16[1,128,896]{2,1,0:T(8,128)(2,1)S(1)} %get-tuple-element.10), kind=kLoop, calls=%fused_computation.34 | loop fusion | flops 229376 | bytes 917504 | tf_op jit(solution)/shard_map/stack | solution.py:120
  35.0 1.1 %broadcast_select_fusion = bf16[2,128,896]{2,1,0:T(8,128)(2,1)S(1)} fusion(pred[2]{0:T(512)(128)(4,1)S(1)} %iota_compare_fusion, bf16[128,896]{1,0:T(8,128)(2,1)S(1)} %multiply_convert_fusion, bf16[128,896]{1,0:T(8,128)(2,1)} %bitcast.14), kind=kLoop, calls=%fused_computation.57 | loop fusion | flops 229376 | bytes 917506 | tf_op jit(solution)/shard_map/jit(_where)/select_n | solution.py:148
  36.1 1.2 %fusion.39 = f32[128,128]{1,0:T(8,128)S(1)} fusion(bf16[128,1792]{1,0:T(8,128)(2,1)} %collective-permute-done.3, bf16[2,128,896]{2,1,0:T(8,128)(2,1)S(1)} %broadcast_select_fusion), kind=kOutput, calls=%fused_computation.59 | convolution fusion | flops 29360128 | bytes 524288 | tf_op jit(solution)/shard_map/dot_general | solution.py:220
  37.2 1.8 %convolution_add_fusion = f32[128,128]{1,0:T(8,128)} fusion(f32[128,128]{1,0:T(8,128)S(1)} %fusion.39, bf16[128,1792]{1,0:T(8,128)(2,1)} %collective-permute-done.3, bf16[2,128,896]{2,1,0:T(8,128)(2,1)S(1)} %broadcast_select_fusion), kind=kOutput, calls=%fused_computation.8 | convolution fusion | flops 29376512 | bytes 589824 | tf_op jit(solution)/shard_map/dot_general | solution.py:220
  39.0 1.5 %collective-permute-start.4 = (f32[128,128]{1,0:T(8,128)}, f32[128,128]{1,0:T(8,128)}, u32[]{:S(2)}, u32[]{:S(2)}) collective-permute-start(f32[128,128]{1,0:T(8,128)} %convolution_add_fusion), channel_id=1, source_target_pairs={{0,16},{8,24},{16,0},{24,8},{1,17},{9,25},{17,1},{25,9},{2,18},{10... | collective-permute-start | bytes 196616 | tf_op jit(solution)/shard_map/ppermute | solution.py:111
  40.7 0.2 fusion.46
  41.0 1.1 %slice_bitcast_fusion.3 = (bf16[128,896]{1,0:T(8,128)(2,1)S(1)}, bf16[128,896]{1,0:T(8,128)(2,1)S(1)}) fusion(bf16[2,128,896]{2,1,0:T(8,128)(2,1)} %collective-permute-done.1), kind=kLoop, calls=%fused_computation.65 | loop fusion | bytes 917504 | tf_op jit(solution)/shard_map/jit(_where)/broadcast_in_dim | solution.py:128
  42.5 0.6 convolution_bitcast_fusion
  43.1 0.8 %collective-permute-done.4 = f32[128,128]{1,0:T(8,128)} collective-permute-done((f32[128,128]{1,0:T(8,128)}, f32[128,128]{1,0:T(8,128)}, u32[]{:S(2)}, u32[]{:S(2)}) %collective-permute-start.4) | collective-permute-done | bytes 65568 | tf_op jit(solution)/shard_map/ppermute | solution.py:111
  43.9 1.1 %multiply_convert_fusion.1 = (bf16[128,128]{1,0:T(8,128)(2,1)S(1)}, f32[128,128]{1,0:T(8,128)S(1)}) fusion(f32[128,128]{1,0:T(8,128)S(1)} %convolution_bitcast_fusion, f32[128,128]{1,0:T(8,128)} %collective-permute-done.4, f32[128,128]{1,0:T(8,128)S(1)} %fusion.46, bf16[1,128,3584]{2,1,0:T(8,128)(2,1)S(1)} %copy-done.1, s32[]{:T(128)S(6)} %select_n.103, ...), kind=kOutput, calls=%fused_computation.78 | convolution fusion | flops 29491200 | bytes 753668 | tf_op jit(solution)/shard_map/dot_general | solution.py:216
  45.0 0.6 fusion.3
  45.6 0.4 fusion.77
  46.0 0.4 add_convert_fusion
  46.5 1.8 %collective-permute-done.5 = bf16[2,128,896]{2,1,0:T(8,128)(2,1)S(1)} collective-permute-done((bf16[2,128,896]{2,1,0:T(8,128)(2,1)S(1)}, bf16[2,128,896]{2,1,0:T(8,128)(2,1)S(1)}, u32[]{:S(2)}, u32[]{:S(2)}) %collective-permute-start.5) | collective-permute-done | bytes 458784 | tf_op jit(solution)/shard_map/ppermute | solution.py:111
  48.6 1.6 %collective-permute-start.6 = (bf16[1,128,896]{2,1,0:T(8,128)(2,1)S(1)}, bf16[1,128,896]{2,1,0:T(8,128)(2,1)S(1)}, u32[]{:S(2)}, u32[]{:S(2)}) collective-permute-start(bf16[1,128,896]{2,1,0:T(8,128)(2,1)S(1)} %fusion.38), channel_id=1, source_target_pairs={{0,16},{8,24},{16,0},{24,8},{1,17},{9,25},{17,1},{25,9},{2,18},{10... | collective-permute-start | bytes 688136 | tf_op jit(solution)/shard_map/ppermute | solution.py:111
  50.1 6.1 %collective-permute-done.6 = bf16[1,128,896]{2,1,0:T(8,128)(2,1)S(1)} collective-permute-done((bf16[1,128,896]{2,1,0:T(8,128)(2,1)S(1)}, bf16[1,128,896]{2,1,0:T(8,128)(2,1)S(1)}, u32[]{:S(2)}, u32[]{:S(2)}) %collective-permute-start.6) | collective-permute-done | bytes 229408 | tf_op jit(solution)/shard_map/ppermute | solution.py:111
  56.3 0.7 %fusion.21 = bf16[1,128,896]{2,1,0:T(8,128)(2,1)} fusion(bf16[1,128,896]{2,1,0:T(8,128)(2,1)S(1)} %collective-permute-done.6, f32[1,2,128,896]{3,2,1,0:T(8,128)S(1)} %fusion.6, pred[]{:T(512)S(6)} %ne.18), kind=kLoop, calls=%fused_computation.38 | loop fusion | flops 458752 | bytes 1376257 | tf_op jit(solution)/shard_map/convert_element_type | solution.py:246
  57.0 3.6 %all-to-all-start.1 = ((bf16[8,16,896]{2,1,0:T(8,128)(2,1)}), bf16[8,16,896]{2,1,0:T(8,128)(2,1)S(1)}, u32[]{:S(2)}, u32[]{:S(2)}) async-start(bf16[8,16,896]{2,1,0:T(8,128)(2,1)} %bitcast.39), calls=%async_computation.1 | async-start | bytes 458752 | tf_op jit(solution)/shard_map/all_to_all | solution.py:247
  60.7 1.4 %convolution_convert_fusion = bf16[4,896,128]{2,1,0:T(8,128)(2,1)} fusion(pred[4]{0:T(512)(128)(4,1)S(1)} %get-tuple-element.16, pred[4]{0:T(512)(128)(4,1)S(1)} %get-tuple-element.17, pred[4]{0:T(512)(128)(4,1)S(1)} %iota_compare_fusion.3, bf16[128,896]{0,1:T(8,128)(2,1)S(1)} %copy.33, bf16[128,896]{0,1:T(8,128)(2,1)S(1)} %copy.32, ...), kind=kOutput, calls=%fused_computation.1 | convolution fusion | flops 119275520 | bytes 1867788 | tf_op jit(solution)/shard_map/dot_general | solution.py:239
  62.0 1.4 %convolution_convert_fusion.1 = bf16[4,896,128]{2,1,0:T(8,128)(2,1)} fusion(bf16[128,128,1]{1,0,2:T(8,128)(2,1)S(1)} %fusion.3, pred[4]{0:T(512)(128)(4,1)S(1)} %get-tuple-element.16, pred[4]{0:T(512)(128)(4,1)S(1)} %get-tuple-element.17, pred[4]{0:T(512)(128)(4,1)S(1)} %iota_compare_fusion.3, bf16[128,896]{0,1:T(8,128)(2,1)S(1)} %copy.33, ...), kind=kOutput, calls=%fused_computation.2 | convolution fusion | flops 119275520 | bytes 1867788 | tf_op jit(solution)/shard_map/dot_general | solution.py:236
  63.4 5.3 %all-to-all-done.1 = bf16[8,16,896]{2,1,0:T(8,128)(2,1)S(1)} async-done(((bf16[8,16,896]{2,1,0:T(8,128)(2,1)}), bf16[8,16,896]{2,1,0:T(8,128)(2,1)S(1)}, u32[]{:S(2)}, u32[]{:S(2)}) %all-to-all-start.1) | async-done | bytes 229408 | tf_op jit(solution)/shard_map/all_to_all | solution.py:247
  68.7 1.1 %convolution_convert_fusion.2 = bf16[256,896]{1,0:T(8,128)(2,1)} fusion(bf16[128,256]{1,0:T(8,128)(2,1)S(1)} %copy-done.3, bf16[128,896]{1,0:T(8,128)(2,1)S(1)} %bitcast.131), kind=kOutput, calls=%fused_computation.3 | convolution fusion | flops 58949632 | bytes 753664 | tf_op jit(solution)/shard_map/dot_general | solution.py:248
  (29 shorter events, 1.5 us)
Async XLA Ops:
  0.6 41.8 %copy-start = (bf16[1,3584,128]{2,1,0:T(8,128)(2,1)S(1)}, bf16[1,3584,128]{2,1,0:T(8,128)(2,1)}, u32[]{:S(2)}) copy-start(bf16[1,3584,128]{2,1,0:T(8,128)(2,1)} %param.13) | copy-start | bytes 2752516
  0.6 10.1 %copy-start.1 = (bf16[1,128,3584]{2,1,0:T(8,128)(2,1)S(1)}, bf16[1,128,3584]{2,1,0:T(8,128)(2,1)}, u32[]{:S(2)}) copy-start(bf16[1,128,3584]{2,1,0:T(8,128)(2,1)} %param.15) | copy-start | bytes 2752516
  3.5 21.1 %all-to-all-start = ((bf16[8,16,1920]{2,1,0:T(8,128)(2,1)}), bf16[8,16,1920]{2,1,0:T(8,128)(2,1)S(1)}, u32[]{:S(2)}, u32[]{:S(2)}) async-start(bf16[8,16,1920]{2,1,0:T(8,128)(2,1)} %bitcast.132), calls=%async_computation | async-start | bytes 983040 | tf_op jit(solution)/shard_map/all_to_all | solution.py:183
  11.6 24.5 %collective-permute-start.3 = (bf16[128,1792]{1,0:T(8,128)(2,1)}, bf16[128,1792]{1,0:T(8,128)(2,1)}, u32[]{:S(2)}, u32[]{:S(2)}) collective-permute-start(bf16[128,1792]{1,0:T(8,128)(2,1)} %slice_select_fusion), channel_id=1, source_target_pairs={{0,16},{8,24},{16,0},{24,8},{1,17},{9,25},{17,1},{25,9},{2,18},{10... | collective-permute-start | bytes 1376264 | tf_op jit(solution)/shard_map/ppermute | solution.py:111
  26.1 8.8 %collective-permute-start.2 = (bf16[1,128,896]{2,1,0:T(8,128)(2,1)}, bf16[1,128,896]{2,1,0:T(8,128)(2,1)}, u32[]{:S(2)}, u32[]{:S(2)}) collective-permute-start(bf16[1,128,896]{2,1,0:T(8,128)(2,1)} %fusion.86), channel_id=1, source_target_pairs={{0,8},{8,0},{16,24},{24,16},{1,9},{9,1},{17,25},{25,17},{2,10},{10... | collective-permute-start | bytes 688136 | tf_op jit(solution)/shard_map/ppermute | solution.py:111
  26.2 8.0 %collective-permute-start = (bf16[1,128,896]{2,1,0:T(8,128)(2,1)S(1)}, bf16[1,128,896]{2,1,0:T(8,128)(2,1)S(1)}, u32[]{:S(2)}, u32[]{:S(2)}) collective-permute-start(bf16[1,128,896]{2,1,0:T(8,128)(2,1)S(1)} %get-tuple-element.10), channel_id=1, source_target_pairs={{0,16},{8,24},{16,0},{24,8},{1,17},{9,25},{17,1},{25,9},{2,18},{10... | collective-permute-start | bytes 688136 | tf_op jit(solution)/shard_map/ppermute | solution.py:111
  35.0 6.0 %collective-permute-start.1 = (bf16[2,128,896]{2,1,0:T(8,128)(2,1)}, bf16[2,128,896]{2,1,0:T(8,128)(2,1)}, u32[]{:S(2)}, u32[]{:S(2)}) collective-permute-start(bf16[2,128,896]{2,1,0:T(8,128)(2,1)} %pad_maximum_fusion), channel_id=1, source_target_pairs={{0,8},{8,0},{16,24},{24,16},{1,9},{9,1},{17,25},{25,17},{2,10},{10... | collective-permute-start | bytes 1376264 | tf_op jit(solution)/shard_map/ppermute | solution.py:111
  39.0 4.8 %collective-permute-start.4 = (f32[128,128]{1,0:T(8,128)}, f32[128,128]{1,0:T(8,128)}, u32[]{:S(2)}, u32[]{:S(2)}) collective-permute-start(f32[128,128]{1,0:T(8,128)} %convolution_add_fusion), channel_id=1, source_target_pairs={{0,16},{8,24},{16,0},{24,8},{1,17},{9,25},{17,1},{25,9},{2,18},{10... | collective-permute-start | bytes 196616 | tf_op jit(solution)/shard_map/ppermute | solution.py:111
  42.4 2.5 %copy-start.2 = (bf16[1,3584,128]{2,1,0:T(8,128)(2,1)S(1)}, bf16[1,3584,128]{2,1,0:T(8,128)(2,1)}, u32[]{:S(2)}) copy-start(bf16[1,3584,128]{2,1,0:T(8,128)(2,1)} %param.14) | copy-start | bytes 2752516
  46.5 1.9 %collective-permute-start.5 = (bf16[2,128,896]{2,1,0:T(8,128)(2,1)S(1)}, bf16[2,128,896]{2,1,0:T(8,128)(2,1)S(1)}, u32[]{:S(2)}, u32[]{:S(2)}) collective-permute-start(bf16[2,128,896]{2,1,0:T(8,128)(2,1)S(1)} %fusion.19), channel_id=1, source_target_pairs={{0,8},{8,0},{16,24},{24,16},{1,9},{9,1},{17,25},{25,17},{2,10},{10... | collective-permute-start | bytes 1376264 | tf_op jit(solution)/shard_map/ppermute | solution.py:111
  48.6 7.7 %collective-permute-start.6 = (bf16[1,128,896]{2,1,0:T(8,128)(2,1)S(1)}, bf16[1,128,896]{2,1,0:T(8,128)(2,1)S(1)}, u32[]{:S(2)}, u32[]{:S(2)}) collective-permute-start(bf16[1,128,896]{2,1,0:T(8,128)(2,1)S(1)} %fusion.38), channel_id=1, source_target_pairs={{0,16},{8,24},{16,0},{24,8},{1,17},{9,25},{17,1},{25,9},{2,18},{10... | collective-permute-start | bytes 688136 | tf_op jit(solution)/shard_map/ppermute | solution.py:111
  57.0 11.7 %all-to-all-start.1 = ((bf16[8,16,896]{2,1,0:T(8,128)(2,1)}), bf16[8,16,896]{2,1,0:T(8,128)(2,1)S(1)}, u32[]{:S(2)}, u32[]{:S(2)}) async-start(bf16[8,16,896]{2,1,0:T(8,128)(2,1)} %bitcast.39), calls=%async_computation.1 | async-start | bytes 458752 | tf_op jit(solution)/shard_map/all_to_all | solution.py:247
  62.0 6.6 %copy-start.3 = (bf16[128,256]{1,0:T(8,128)(2,1)S(1)}, bf16[128,256]{1,0:T(8,128)(2,1)}, u32[]{:S(2)}) copy-start(bf16[128,256]{1,0:T(8,128)(2,1)} %get-tuple-element.6) | copy-start | bytes 196612

commit v9 on v8

--- a/solution.py
+++ b/solution.py
@@ -177,6 +177,7 @@
     if n_dp > 1:
         upper_half = (me_dp & top) != 0
         lend = jnp.where(upper_half, w_down[:, :half_cols], w_down[:, half_cols:])
+        keep = jnp.where(upper_half, w_down[:, half_cols:], w_down[:, :half_cols])
         borrowed = partner(lend, top, n_dp)
     payload, pick_t = glue(expert_ids, gate_values, forget_flags, tokens, token_grads, n_dest)
     side = payload.shape[1] - 2 * width
@@ -209,12 +210,12 @@
     last_dims = (((1,), (1,)), ((), ()))
     slot_tokens = gather_dp(part_tokens, n_dp)
     if n_dp > 1:
-        half_grads, base = gather_half(part_grads, n_dp)
+        half_grads, _ = gather_half(part_grads, n_dp)
         hidden_grad = None
         lent = None
         for i in range(top):
             mine = lax.dot_general(
-                half_grads[i], lax.dynamic_slice_in_dim(w_down, (base + i) * width, width, axis=1),
+                half_grads[i], keep[:, i * width : (i + 1) * width],
                 last_dims, preferred_element_type=jnp.float32,
             )
             theirs = lax.dot_general(

time: 70.2 us -> 68.5 us (0.976)
  local copies, waits for them, and re-layouts: 1.84 us -> 0.8 us
  other arithmetic: 5.09 us -> 4.34 us
    broadcast_in_dim x4, local copies, waits for them, and re-layouts: 1.6 us -> 0.55 us  [gather_dp(): out = jnp.where(at == owner, piece[None], out)]
    another operation x1, other arithmetic: 0.82 us -> 0.05 us  [gather_dp(): stacked = jnp.stack(held)]
  transfers between devices with their start and end apart: 9 -> 9, of which waited for: 6 -> 6; matrix products, arithmetic and copies ran while one was open for 18% -> 17% of each run, Pallas kernels for 0% -> 0%
where the time goes in v9:
time: 68.5 us; the launch traced here: 68.1 us
  waiting for transfers between devices  32 us (47%)
  starting transfers between devices  17.2 us (25%)
  matrix products  10.2 us (15%)
  other arithmetic  4.34 us (6%)
  Pallas kernels  2.81 us (4%)
  between operations  0.85 us (1%)
  local copies, waits for them, and re-layouts  0.8 us (1%)
    ppermute x7, waiting for transfers between devices, partner(): return lax.ppermute(x, 'dp', [(i, i ^ bit) for i in range(n)])  15.3 us
    all_to_all x1, waiting for transfers between devices, on_device(): lax.all_to_all(payload, 'expert', split_axis=0, concat_axis=0, tiled=True)  11.4 us
    all_to_all x1, starting transfers between devices, on_device(): lax.all_to_all(payload, 'expert', split_axis=0, concat_axis=0, tiled=True)  7.31 us
    ppermute x7, starting transfers between devices, partner(): return lax.ppermute(x, 'dp', [(i, i ^ bit) for i in range(n)])  6.23 us
    all_to_all x1, waiting for transfers between devices, on_device(): lax.all_to_all(summed, 'expert', split_axis=0, concat_axis=0, tiled=True)  5.28 us
    all_to_all x1, starting transfers between devices, on_device(): lax.all_to_all(summed, 'expert', split_axis=0, concat_axis=0, tiled=True)  3.64 us
    dot_general x2, matrix products, on_device(): lax.dot_general(half_grads[i], borrowed[:, i * width:(i + 1) * width], la...  2.96 us
    pallas_call x1, Pallas kernels, glue(): pl.pallas_call(functools.partial(glue_kernel, n_dest, width, side, split)...  2.81 us
  transfers between devices with their start and end apart: 9, of which 6 were waited for; matrix products, arithmetic and copies ran while one was open for 17% of the time, Pallas kernels for 0%

profile of v9, /device:TPU:0, one launch (start us, length us, event | category | flops | bytes accessed | tf_op | source)
XLA Modules:
  0.0 68.1 jit_solution(14048371036147337148)
XLA Ops:
  0.7 2.8 %shard_map.103 = (bf16[128,1920]{1,0:T(8,128)(2,1)}, bf16[128,256]{1,0:T(8,128)(2,1)}) custom-call(s32[8,256]{1,0:T(8,128)} %bitcast.125, f32[8,256]{1,0:T(8,128)} %bitcast.126, s32[1,256]{1,0:T(1,128)} %bitcast.127, bf16[256,896]{1,0:T(8,128)(2,1)} %tok_ref.1, bf16[256,896]{1,0:T(8,128)(2,1)} %grd_ref.1), custom_call_target="tpu_custom_call" | custom-call | tf_op jit(solution)/shard_map/pallas_call | solution.py:90
  3.5 7.3 %all-to-all-start = ((bf16[8,16,1920]{2,1,0:T(8,128)(2,1)}), bf16[8,16,1920]{2,1,0:T(8,128)(2,1)S(1)}, u32[]{:S(2)}, u32[]{:S(2)}) async-start(bf16[8,16,1920]{2,1,0:T(8,128)(2,1)} %bitcast.124), calls=%async_computation | async-start | bytes 983040 | tf_op jit(solution)/shard_map/all_to_all | solution.py:184
  10.8 0.8 %broadcast_select_fusion.2 = (bf16[128,1792]{1,0:T(8,128)(2,1)S(1)}, bf16[128,1792]{1,0:T(8,128)(2,1)}) fusion(pred[]{:T(512)S(6)} %ne.18, bf16[128,3584]{1,0:T(8,128)(2,1)S(1)} %bitcast.123), kind=kLoop, calls=%fused_computation.58 | loop fusion | flops 458752 | bytes 1835009 | tf_op jit(solution)/shard_map/jit(_where)/select_n | solution.py:180
  11.6 1.5 %collective-permute-start.3 = (bf16[128,1792]{1,0:T(8,128)(2,1)}, bf16[128,1792]{1,0:T(8,128)(2,1)}, u32[]{:S(2)}, u32[]{:S(2)}) collective-permute-start(bf16[128,1792]{1,0:T(8,128)(2,1)} %get-tuple-element.11), channel_id=1, source_target_pairs={{0,16},{8,24},{16,0},{24,8},{1,17},{9,25},{17,1},{25,9},{2,18},{10... | collective-permute-start | bytes 1376264 | tf_op jit(solution)/shard_map/ppermute | solution.py:111
  13.1 11.4 %all-to-all-done = bf16[8,16,1920]{2,1,0:T(8,128)(2,1)S(1)} async-done(((bf16[8,16,1920]{2,1,0:T(8,128)(2,1)}), bf16[8,16,1920]{2,1,0:T(8,128)(2,1)S(1)}, u32[]{:S(2)}, u32[]{:S(2)}) %all-to-all-start) | async-done | bytes 491552 | tf_op jit(solution)/shard_map/all_to_all | solution.py:184
  24.6 0.2 slice_reduce_fusion
  24.8 0.2 fusion.49
  25.3 0.8 %fusion.82 = bf16[1,128,896]{2,1,0:T(8,128)(2,1)} fusion(bf16[128,1920]{1,0:T(8,128)(2,1)S(1)} %bitcast.117, f32[128]{0:T(128)S(1)} %fusion.56), kind=kLoop, calls=%fused_computation.111 | loop fusion | flops 344064 | bytes 459264 | tf_op jit(solution)/shard_map/stack | solution.py:140
  26.1 1.5 %collective-permute-start = (bf16[1,128,896]{2,1,0:T(8,128)(2,1)S(1)}, bf16[1,128,896]{2,1,0:T(8,128)(2,1)S(1)}, u32[]{:S(2)}, u32[]{:S(2)}) collective-permute-start(bf16[1,128,896]{2,1,0:T(8,128)(2,1)S(1)} %get-tuple-element.12), channel_id=1, source_target_pairs={{0,16},{8,24},{16,0},{24,8},{1,17},{9,25},{17,1},{25,9},{2,18},{10... | collective-permute-start | bytes 688136 | tf_op jit(solution)/shard_map/ppermute | solution.py:111
  27.8 0.2 copy.33
  27.9 6.2 %collective-permute-done = bf16[1,128,896]{2,1,0:T(8,128)(2,1)S(1)} collective-permute-done((bf16[1,128,896]{2,1,0:T(8,128)(2,1)S(1)}, bf16[1,128,896]{2,1,0:T(8,128)(2,1)S(1)}, u32[]{:S(2)}, u32[]{:S(2)}) %collective-permute-start) | collective-permute-done | bytes 229408 | tf_op jit(solution)/shard_map/ppermute | solution.py:111
  34.3 1.1 %broadcast_select_fusion = bf16[2,128,896]{2,1,0:T(8,128)(2,1)S(1)} fusion(pred[2]{0:T(512)(128)(4,1)S(1)} %iota_compare_fusion, bf16[128,896]{1,0:T(8,128)(2,1)S(1)} %multiply_convert_fusion, bf16[128,896]{1,0:T(8,128)(2,1)} %bitcast.14), kind=kLoop, calls=%fused_computation.56 | loop fusion | flops 229376 | bytes 917506 | tf_op jit(solution)/shard_map/jit(_where)/select_n | solution.py:148
  35.4 1.2 %fusion.39 = f32[128,128]{1,0:T(8,128)S(1)} fusion(bf16[128,1792]{1,0:T(8,128)(2,1)} %collective-permute-done.3, bf16[2,128,896]{2,1,0:T(8,128)(2,1)S(1)} %broadcast_select_fusion), kind=kOutput, calls=%fused_computation.60 | convolution fusion | flops 29360128 | bytes 524288 | tf_op jit(solution)/shard_map/dot_general | solution.py:221
  36.6 1.8 %convolution_add_fusion = f32[128,128]{1,0:T(8,128)} fusion(f32[128,128]{1,0:T(8,128)S(1)} %fusion.39, bf16[128,1792]{1,0:T(8,128)(2,1)} %collective-permute-done.3, bf16[2,128,896]{2,1,0:T(8,128)(2,1)S(1)} %broadcast_select_fusion), kind=kOutput, calls=%fused_computation.8 | convolution fusion | flops 29376512 | bytes 589824 | tf_op jit(solution)/shard_map/dot_general | solution.py:221
  38.4 1.5 %collective-permute-start.4 = (f32[128,128]{1,0:T(8,128)}, f32[128,128]{1,0:T(8,128)S(1)}, u32[]{:S(2)}, u32[]{:S(2)}) collective-permute-start(f32[128,128]{1,0:T(8,128)} %convolution_add_fusion), channel_id=1, source_target_pairs={{0,16},{8,24},{16,0},{24,8},{1,17},{9,25},{17,1},{25,9},{2,18},{10... | collective-permute-start | bytes 196616 | tf_op jit(solution)/shard_map/ppermute | solution.py:111
  40.0 0.9 %fusion.43 = f32[128,128]{1,0:T(8,128)} fusion(bf16[128,1792]{1,0:T(8,128)(2,1)S(1)} %get-tuple-element.10, bf16[2,128,896]{2,1,0:T(8,128)(2,1)S(1)} %broadcast_select_fusion), kind=kOutput, calls=%fused_computation.65 | convolution fusion | flops 29360128 | bytes 524288 | tf_op jit(solution)/shard_map/dot_general | solution.py:217
  41.1 0.2 copy.31
  41.4 0.6 convolution_bitcast_fusion
  42.0 1.1 %collective-permute-done.4 = f32[128,128]{1,0:T(8,128)S(1)} collective-permute-done((f32[128,128]{1,0:T(8,128)}, f32[128,128]{1,0:T(8,128)S(1)}, u32[]{:S(2)}, u32[]{:S(2)}) %collective-permute-start.4) | collective-permute-done | bytes 65568 | tf_op jit(solution)/shard_map/ppermute | solution.py:111
  43.1 0.2 multiply_convert_fusion.1
  43.3 0.6 fusion.3
  43.9 0.4 fusion.73
  44.3 0.4 add_convert_fusion
  44.9 1.8 %collective-permute-done.5 = bf16[2,128,896]{2,1,0:T(8,128)(2,1)S(1)} collective-permute-done((bf16[2,128,896]{2,1,0:T(8,128)(2,1)S(1)}, bf16[2,128,896]{2,1,0:T(8,128)(2,1)S(1)}, u32[]{:S(2)}, u32[]{:S(2)}) %collective-permute-start.5) | collective-permute-done | bytes 458784 | tf_op jit(solution)/shard_map/ppermute | solution.py:111
  46.9 1.6 %collective-permute-start.6 = (bf16[1,128,896]{2,1,0:T(8,128)(2,1)S(1)}, bf16[1,128,896]{2,1,0:T(8,128)(2,1)S(1)}, u32[]{:S(2)}, u32[]{:S(2)}) collective-permute-start(bf16[1,128,896]{2,1,0:T(8,128)(2,1)S(1)} %fusion.38), channel_id=1, source_target_pairs={{0,16},{8,24},{16,0},{24,8},{1,17},{9,25},{17,1},{25,9},{2,18},{10... | collective-permute-start | bytes 688136 | tf_op jit(solution)/shard_map/ppermute | solution.py:111
  48.5 6.1 %collective-permute-done.6 = bf16[1,128,896]{2,1,0:T(8,128)(2,1)S(1)} collective-permute-done((bf16[1,128,896]{2,1,0:T(8,128)(2,1)S(1)}, bf16[1,128,896]{2,1,0:T(8,128)(2,1)S(1)}, u32[]{:S(2)}, u32[]{:S(2)}) %collective-permute-start.6) | collective-permute-done | bytes 229408 | tf_op jit(solution)/shard_map/ppermute | solution.py:111
  54.6 0.7 %fusion.21 = bf16[1,128,896]{2,1,0:T(8,128)(2,1)} fusion(bf16[1,128,896]{2,1,0:T(8,128)(2,1)S(1)} %collective-permute-done.6, f32[1,2,128,896]{3,2,1,0:T(8,128)S(1)} %fusion.6, pred[]{:T(512)S(6)} %ne.18), kind=kLoop, calls=%fused_computation.37 | loop fusion | flops 458752 | bytes 1376257 | tf_op jit(solution)/shard_map/convert_element_type | solution.py:247
  55.4 3.6 %all-to-all-start.1 = ((bf16[8,16,896]{2,1,0:T(8,128)(2,1)}), bf16[8,16,896]{2,1,0:T(8,128)(2,1)S(1)}, u32[]{:S(2)}, u32[]{:S(2)}) async-start(bf16[8,16,896]{2,1,0:T(8,128)(2,1)} %bitcast.37), calls=%async_computation.1 | async-start | bytes 458752 | tf_op jit(solution)/shard_map/all_to_all | solution.py:248
  59.0 1.4 %convolution_convert_fusion = bf16[4,896,128]{2,1,0:T(8,128)(2,1)} fusion(pred[4]{0:T(512)(128)(4,1)S(1)} %get-tuple-element.18, pred[4]{0:T(512)(128)(4,1)S(1)} %get-tuple-element.19, pred[4]{0:T(512)(128)(4,1)S(1)} %iota_compare_fusion.3, bf16[128,896]{0,1:T(8,128)(2,1)S(1)} %copy.33, bf16[128,896]{0,1:T(8,128)(2,1)S(1)} %copy.32, ...), kind=kOutput, calls=%fused_computation.1 | convolution fusion | flops 119275520 | bytes 1867788 | tf_op jit(solution)/shard_map/dot_general | solution.py:240
  60.4 1.4 %convolution_convert_fusion.1 = bf16[4,896,128]{2,1,0:T(8,128)(2,1)} fusion(bf16[128,128,1]{1,0,2:T(8,128)(2,1)S(1)} %fusion.3, pred[4]{0:T(512)(128)(4,1)S(1)} %get-tuple-element.18, pred[4]{0:T(512)(128)(4,1)S(1)} %get-tuple-element.19, pred[4]{0:T(512)(128)(4,1)S(1)} %iota_compare_fusion.3, bf16[128,896]{0,1:T(8,128)(2,1)S(1)} %copy.33, ...), kind=kOutput, calls=%fused_computation.2 | convolution fusion | flops 119275520 | bytes 1867788 | tf_op jit(solution)/shard_map/dot_general | solution.py:237
  61.7 5.3 %all-to-all-done.1 = bf16[8,16,896]{2,1,0:T(8,128)(2,1)S(1)} async-done(((bf16[8,16,896]{2,1,0:T(8,128)(2,1)}), bf16[8,16,896]{2,1,0:T(8,128)(2,1)S(1)}, u32[]{:S(2)}, u32[]{:S(2)}) %all-to-all-start.1) | async-done | bytes 229408 | tf_op jit(solution)/shard_map/all_to_all | solution.py:248
  67.0 1.1 %convolution_convert_fusion.2 = bf16[256,896]{1,0:T(8,128)(2,1)} fusion(bf16[128,256]{1,0:T(8,128)(2,1)S(1)} %copy-done.3, bf16[128,896]{1,0:T(8,128)(2,1)S(1)} %bitcast.122), kind=kOutput, calls=%fused_computation.3 | convolution fusion | flops 58949632 | bytes 753664 | tf_op jit(solution)/shard_map/dot_general | solution.py:249
  (31 shorter events, 1.3 us)
Async XLA Ops:
  0.6 40.7 %copy-start = (bf16[1,3584,128]{2,1,0:T(8,128)(2,1)S(1)}, bf16[1,3584,128]{2,1,0:T(8,128)(2,1)}, u32[]{:S(2)}) copy-start(bf16[1,3584,128]{2,1,0:T(8,128)(2,1)} %param.13) | copy-start | bytes 2752516
  0.6 10.1 %copy-start.2 = (bf16[1,128,3584]{2,1,0:T(8,128)(2,1)S(1)}, bf16[1,128,3584]{2,1,0:T(8,128)(2,1)}, u32[]{:S(2)}) copy-start(bf16[1,128,3584]{2,1,0:T(8,128)(2,1)} %param.15) | copy-start | bytes 2752516
  3.5 21.1 %all-to-all-start = ((bf16[8,16,1920]{2,1,0:T(8,128)(2,1)}), bf16[8,16,1920]{2,1,0:T(8,128)(2,1)S(1)}, u32[]{:S(2)}, u32[]{:S(2)}) async-start(bf16[8,16,1920]{2,1,0:T(8,128)(2,1)} %bitcast.124), calls=%async_computation | async-start | bytes 983040 | tf_op jit(solution)/shard_map/all_to_all | solution.py:184
  11.6 23.8 %collective-permute-start.3 = (bf16[128,1792]{1,0:T(8,128)(2,1)}, bf16[128,1792]{1,0:T(8,128)(2,1)}, u32[]{:S(2)}, u32[]{:S(2)}) collective-permute-start(bf16[128,1792]{1,0:T(8,128)(2,1)} %get-tuple-element.11), channel_id=1, source_target_pairs={{0,16},{8,24},{16,0},{24,8},{1,17},{9,25},{17,1},{25,9},{2,18},{10... | collective-permute-start | bytes 1376264 | tf_op jit(solution)/shard_map/ppermute | solution.py:111
  26.1 8.2 %collective-permute-start.2 = (bf16[1,128,896]{2,1,0:T(8,128)(2,1)}, bf16[1,128,896]{2,1,0:T(8,128)(2,1)}, u32[]{:S(2)}, u32[]{:S(2)}) collective-permute-start(bf16[1,128,896]{2,1,0:T(8,128)(2,1)} %fusion.82), channel_id=1, source_target_pairs={{0,8},{8,0},{16,24},{24,16},{1,9},{9,1},{17,25},{25,17},{2,10},{10... | collective-permute-start | bytes 688136 | tf_op jit(solution)/shard_map/ppermute | solution.py:111
  26.1 8.0 %collective-permute-start = (bf16[1,128,896]{2,1,0:T(8,128)(2,1)S(1)}, bf16[1,128,896]{2,1,0:T(8,128)(2,1)S(1)}, u32[]{:S(2)}, u32[]{:S(2)}) collective-permute-start(bf16[1,128,896]{2,1,0:T(8,128)(2,1)S(1)} %get-tuple-element.12), channel_id=1, source_target_pairs={{0,16},{8,24},{16,0},{24,8},{1,17},{9,25},{17,1},{25,9},{2,18},{10... | collective-permute-start | bytes 688136 | tf_op jit(solution)/shard_map/ppermute | solution.py:111
  34.2 6.7 %collective-permute-start.1 = (bf16[2,128,896]{2,1,0:T(8,128)(2,1)S(1)}, bf16[2,128,896]{2,1,0:T(8,128)(2,1)S(1)}, u32[]{:S(2)}, u32[]{:S(2)}) collective-permute-start(bf16[2,128,896]{2,1,0:T(8,128)(2,1)S(1)} %pad_maximum_fusion), channel_id=1, source_target_pairs={{0,8},{8,0},{16,24},{24,16},{1,9},{9,1},{17,25},{25,17},{2,10},{10... | collective-permute-start | bytes 1376264 | tf_op jit(solution)/shard_map/ppermute | solution.py:111
  38.4 4.7 %collective-permute-start.4 = (f32[128,128]{1,0:T(8,128)}, f32[128,128]{1,0:T(8,128)S(1)}, u32[]{:S(2)}, u32[]{:S(2)}) collective-permute-start(f32[128,128]{1,0:T(8,128)} %convolution_add_fusion), channel_id=1, source_target_pairs={{0,16},{8,24},{16,0},{24,8},{1,17},{9,25},{17,1},{25,9},{2,18},{10... | collective-permute-start | bytes 196616 | tf_op jit(solution)/shard_map/ppermute | solution.py:111
  41.3 1.7 %copy-start.4 = (f32[128,128]{1,0:T(8,128)S(1)}, f32[128,128]{1,0:T(8,128)}, u32[]{:S(2)}) copy-start(f32[128,128]{1,0:T(8,128)} %fusion.43) | copy-start | bytes 196612
  41.3 2.0 %copy-start.1 = (bf16[1,3584,128]{2,1,0:T(8,128)(2,1)S(1)}, bf16[1,3584,128]{2,1,0:T(8,128)(2,1)}, u32[]{:S(2)}) copy-start(bf16[1,3584,128]{2,1,0:T(8,128)(2,1)} %param.14) | copy-start | bytes 2752516
  44.8 1.9 %collective-permute-start.5 = (bf16[2,128,896]{2,1,0:T(8,128)(2,1)S(1)}, bf16[2,128,896]{2,1,0:T(8,128)(2,1)S(1)}, u32[]{:S(2)}, u32[]{:S(2)}) collective-permute-start(bf16[2,128,896]{2,1,0:T(8,128)(2,1)S(1)} %fusion.19), channel_id=1, source_target_pairs={{0,8},{8,0},{16,24},{24,16},{1,9},{9,1},{17,25},{25,17},{2,10},{10... | collective-permute-start | bytes 1376264 | tf_op jit(solution)/shard_map/ppermute | solution.py:111
  46.9 7.7 %collective-permute-start.6 = (bf16[1,128,896]{2,1,0:T(8,128)(2,1)S(1)}, bf16[1,128,896]{2,1,0:T(8,128)(2,1)S(1)}, u32[]{:S(2)}, u32[]{:S(2)}) collective-permute-start(bf16[1,128,896]{2,1,0:T(8,128)(2,1)S(1)} %fusion.38), channel_id=1, source_target_pairs={{0,16},{8,24},{16,0},{24,8},{1,17},{9,25},{17,1},{25,9},{2,18},{10... | collective-permute-start | bytes 688136 | tf_op jit(solution)/shard_map/ppermute | solution.py:111
  55.4 11.6 %all-to-all-start.1 = ((bf16[8,16,896]{2,1,0:T(8,128)(2,1)}), bf16[8,16,896]{2,1,0:T(8,128)(2,1)S(1)}, u32[]{:S(2)}, u32[]{:S(2)}) async-start(bf16[8,16,896]{2,1,0:T(8,128)(2,1)} %bitcast.37), calls=%async_computation.1 | async-start | bytes 458752 | tf_op jit(solution)/shard_map/all_to_all | solution.py:248
  60.4 6.6 %copy-start.3 = (bf16[128,256]{1,0:T(8,128)(2,1)S(1)}, bf16[128,256]{1,0:T(8,128)(2,1)}, u32[]{:S(2)}) copy-start(bf16[128,256]{1,0:T(8,128)(2,1)} %get-tuple-element.6) | copy-start | bytes 196612

commit v10 on v9

--- a/solution.py
+++ b/solution.py
@@ -176,8 +176,8 @@
     half_cols = (n_dp * width) // 2
     if n_dp > 1:
         upper_half = (me_dp & top) != 0
-        lend = jnp.where(upper_half, w_down[:, :half_cols], w_down[:, half_cols:])
-        keep = jnp.where(upper_half, w_down[:, half_cols:], w_down[:, :half_cols])
+        lend = jnp.where(upper_half, w_down[:, :half_cols], w_down[:, half_cols:]).T
+        keep = jnp.where(upper_half, w_down[:, half_cols:], w_down[:, :half_cols]).T
         borrowed = partner(lend, top, n_dp)
     payload, pick_t = glue(expert_ids, gate_values, forget_flags, tokens, token_grads, n_dest)
     side = payload.shape[1] - 2 * width
@@ -211,19 +211,14 @@
     slot_tokens = gather_dp(part_tokens, n_dp)
     if n_dp > 1:
         half_grads, _ = gather_half(part_grads, n_dp)
-        hidden_grad = None
-        lent = None
-        for i in range(top):
-            mine = lax.dot_general(
-                half_grads[i], keep[:, i * width : (i + 1) * width],
-                last_dims, preferred_element_type=jnp.float32,
-            )
-            theirs = lax.dot_general(
-                half_grads[i], borrowed[:, i * width : (i + 1) * width], last_dims,
-                preferred_element_type=jnp.float32,
-            )
-            hidden_grad = mine if hidden_grad is None else hidden_grad + mine
-            lent = theirs if lent is None else lent + theirs
+        half_dims = (((0, 2), (0, 1)), ((), ()))
+        ff_down = w_down.shape[0]
+        hidden_grad = lax.dot_general(
+            half_grads, keep.reshape(top, width, ff_down), half_dims, preferred_element_type=jnp.float32
+        )
+        lent = lax.dot_general(
+            half_grads, borrowed.reshape(top, width, ff_down), half_dims, preferred_element_type=jnp.float32
+        )
         hidden_grad = hidden_grad + partner(lent, top, n_dp)
     else:
         hidden_grad = lax.dot_general(part_grads, w_down, last_dims, preferred_element_type=jnp.float32)

time: 68.5 us -> 68.3 us (level)
  starting transfers between devices: 17.2 us -> 19.2 us
  waiting for transfers between devices: 32 us -> 30.5 us
  matrix products: 10.2 us -> 8.76 us
    all_to_all x1, waiting for transfers between devices: 11.4 us -> 1.4 us  [on_device(): lax.all_to_all(payload, 'expert', split_axis=0, concat_axis=0, tiled=True)]
    ppermute x7, waiting for transfers between devices: 15.3 us -> 23.8 us  [partner(): return lax.ppermute(x, 'dp', [(i, i ^ bit) for i in range(n)])]
    select_n x2 -> x0, other arithmetic: 1.9 us -> none  [the longest x1 1.07 us: gather_half(): out = jnp.where(at == owner - base, piece[None], out)]
    dot_general x4 -> x2, matrix products: 4.06 us -> 2.66 us  [the longest x1 1.39 us: on_device(): lax.dot_general(half_grads, borrowed.reshape(top, width, ff_down), half_d...]
    all_to_all x1, starting transfers between devices: 3.64 us -> 4.95 us  [on_device(): lax.all_to_all(summed, 'expert', split_axis=0, concat_axis=0, tiled=True)]
    another operation x1, other arithmetic: 0.05 us -> 0.82 us  [gather_dp(): stacked = jnp.stack(held)]
    ppermute x7, starting transfers between devices: 6.23 us -> 6.96 us  [partner(): return lax.ppermute(x, 'dp', [(i, i ^ bit) for i in range(n)])]
    convert_element_type x1, other arithmetic: 0.1 us -> 0.79 us  [on_device(): (scale[:, None] * raw_grads.astype(jnp.float32)).astype(jnp.bfloat16)]
  transfers between devices with their start and end apart: 9 -> 9, of which waited for: 6 -> 8; matrix products, arithmetic and copies ran while one was open for 17% -> 13% of each run, Pallas kernels for 0% -> 0%
where the time goes in v10:
time: 68.3 us; the launch traced here: 67.9 us
  waiting for transfers between devices  30.5 us (45%)
  starting transfers between devices  19.2 us (28%)
  matrix products  8.76 us (13%)
  other arithmetic  4.49 us (7%)
  Pallas kernels  2.81 us (4%)
  local copies, waits for them, and re-layouts  1.3 us (2%)
  between operations  0.84 us (1%)
    ppermute x7, waiting for transfers between devices, partner(): return lax.ppermute(x, 'dp', [(i, i ^ bit) for i in range(n)])  23.8 us
    all_to_all x1, starting transfers between devices, on_device(): lax.all_to_all(payload, 'expert', split_axis=0, concat_axis=0, tiled=True)  7.31 us
    ppermute x7, starting transfers between devices, partner(): return lax.ppermute(x, 'dp', [(i, i ^ bit) for i in range(n)])  6.96 us
    all_to_all x1, waiting for transfers between devices, on_device(): lax.all_to_all(summed, 'expert', split_axis=0, concat_axis=0, tiled=True)  5.28 us
    all_to_all x1, starting transfers between devices, on_device(): lax.all_to_all(summed, 'expert', split_axis=0, concat_axis=0, tiled=True)  4.95 us
    pallas_call x1, Pallas kernels, glue(): pl.pallas_call(functools.partial(glue_kernel, n_dest, width, side, split)...  2.81 us
    all_to_all x1, waiting for transfers between devices, on_device(): lax.all_to_all(payload, 'expert', split_axis=0, concat_axis=0, tiled=True)  1.4 us
    dot_general x1, matrix products, on_device(): lax.dot_general(half_grads, borrowed.reshape(top, width, ff_down), half_d...  1.39 us
  transfers between devices with their start and end apart: 9, of which 8 were waited for; matrix products, arithmetic and copies ran while one was open for 13% of the time, Pallas kernels for 0%

profile of v10, /device:TPU:0, one launch (start us, length us, event | category | flops | bytes accessed | tf_op | source)
XLA Modules:
  0.0 67.9 jit_solution(14852133454137571798)
XLA Ops:
  0.7 2.8 %shard_map.103 = (bf16[128,1920]{1,0:T(8,128)(2,1)}, bf16[128,256]{1,0:T(8,128)(2,1)}) custom-call(s32[8,256]{1,0:T(8,128)} %bitcast.129, f32[8,256]{1,0:T(8,128)} %bitcast.130, s32[1,256]{1,0:T(1,128)} %bitcast.131, bf16[256,896]{1,0:T(8,128)(2,1)} %tok_ref.1, bf16[256,896]{1,0:T(8,128)(2,1)} %grd_ref.1), custom_call_target="tpu_custom_call" | custom-call | tf_op jit(solution)/shard_map/pallas_call | solution.py:90
  3.5 7.3 %all-to-all-start = ((bf16[8,16,1920]{2,1,0:T(8,128)(2,1)}), bf16[8,16,1920]{2,1,0:T(8,128)(2,1)S(1)}, u32[]{:S(2)}, u32[]{:S(2)}) async-start(bf16[8,16,1920]{2,1,0:T(8,128)(2,1)} %bitcast.126), calls=%async_computation | async-start | bytes 983040 | tf_op jit(solution)/shard_map/all_to_all | solution.py:184
  10.9 1.6 %collective-permute-start.3 = (bf16[1792,128]{0,1:T(8,128)(2,1)S(1)}, bf16[1792,128]{0,1:T(8,128)(2,1)S(1)}, u32[]{:S(2)}, u32[]{:S(2)}) collective-permute-start(bf16[1792,128]{0,1:T(8,128)(2,1)S(1)} %get-tuple-element.11), channel_id=1, source_target_pairs={{0,16},{8,24},{16,0},{24,8},{1,17},{9,25},{17,1},{25,9},{2,18},{10... | collective-permute-start | bytes 1376264 | tf_op jit(solution)/shard_map/ppermute | solution.py:111
  12.4 0.3 copy.48
  12.7 0.6 iota_compare_fusion
  13.2 9.6 %collective-permute-done.3 = bf16[1792,128]{0,1:T(8,128)(2,1)S(1)} collective-permute-done((bf16[1792,128]{0,1:T(8,128)(2,1)S(1)}, bf16[1792,128]{0,1:T(8,128)(2,1)S(1)}, u32[]{:S(2)}, u32[]{:S(2)}) %collective-permute-start.3) | collective-permute-done | bytes 458784 | tf_op jit(solution)/shard_map/ppermute | solution.py:111
  22.9 0.3 copy.39
  23.1 1.4 %all-to-all-done = bf16[8,16,1920]{2,1,0:T(8,128)(2,1)S(1)} async-done(((bf16[8,16,1920]{2,1,0:T(8,128)(2,1)}), bf16[8,16,1920]{2,1,0:T(8,128)(2,1)S(1)}, u32[]{:S(2)}, u32[]{:S(2)}) %all-to-all-start) | async-done | bytes 491552 | tf_op jit(solution)/shard_map/all_to_all | solution.py:184
  24.6 1.6 %collective-permute-start = (bf16[1,128,896]{2,1,0:T(8,128)(2,1)S(1)}, bf16[1,128,896]{2,1,0:T(8,128)(2,1)S(1)}, u32[]{:S(2)}, u32[]{:S(2)}) collective-permute-start(bf16[1,128,896]{2,1,0:T(8,128)(2,1)S(1)} %get-tuple-element.12), channel_id=1, source_target_pairs={{0,16},{8,24},{16,0},{24,8},{1,17},{9,25},{17,1},{25,9},{2,18},{10... | collective-permute-start | bytes 688136 | tf_op jit(solution)/shard_map/ppermute | solution.py:111
  26.9 4.0 %collective-permute-done = bf16[1,128,896]{2,1,0:T(8,128)(2,1)S(1)} collective-permute-done((bf16[1,128,896]{2,1,0:T(8,128)(2,1)S(1)}, bf16[1,128,896]{2,1,0:T(8,128)(2,1)S(1)}, u32[]{:S(2)}, u32[]{:S(2)}) %collective-permute-start) | collective-permute-done | bytes 229408 | tf_op jit(solution)/shard_map/ppermute | solution.py:111
  30.9 0.8 %pad_maximum_fusion = bf16[2,128,896]{2,1,0:T(8,128)(2,1)} fusion(bf16[1,128,896]{2,1,0:T(8,128)(2,1)S(1)} %collective-permute-done, bf16[1,128,896]{2,1,0:T(8,128)(2,1)S(1)} %get-tuple-element.12), kind=kLoop, calls=%fused_computation.36 | loop fusion | flops 229376 | bytes 917504 | tf_op jit(solution)/shard_map/stack | solution.py:120
  31.7 0.8 %fusion.84 = bf16[1,128,896]{2,1,0:T(8,128)(2,1)} fusion(bf16[128,1920]{1,0:T(8,128)(2,1)S(1)} %bitcast.119, f32[128]{0:T(128)S(1)} %fusion.56), kind=kLoop, calls=%fused_computation.110 | loop fusion | flops 344064 | bytes 459264 | tf_op jit(solution)/shard_map/stack | solution.py:140
  32.6 0.6 collective-permute-start.2
  33.2 0.8 %multiply_convert_fusion = bf16[128,896]{1,0:T(8,128)(2,1)} fusion(bf16[128,1920]{1,0:T(8,128)(2,1)S(1)} %bitcast.120, f32[128]{0:T(128)S(1)} %fusion.56), kind=kLoop, calls=%fused_computation.44 | loop fusion | flops 344064 | bytes 459264 | tf_op jit(solution)/shard_map/convert_element_type | solution.py:206
  34.2 0.5 collective-permute-done.2
  34.7 1.4 %convolution_bitcast_fusion.2 = f32[128,128]{1,0:T(8,128)S(1)} fusion(bf16[2,896,128]{2,1,0:T(8,128)(2,1)S(1)} %bitcast.128, pred[2]{0:T(512)(128)(4,1)} %iota_compare_fusion, bf16[128,896]{1,0:T(8,128)(2,1)} %multiply_convert_fusion, bf16[128,896]{1,0:T(8,128)(2,1)} %bitcast.14), kind=kOutput, calls=%fused_computation.8 | convolution fusion | flops 58949632 | bytes 983042 | tf_op jit(solution)/shard_map/dot_general | solution.py:219
  36.1 1.6 %collective-permute-start.4 = (f32[128,128]{1,0:T(8,128)S(1)}, f32[128,128]{1,0:T(8,128)S(1)}, u32[]{:S(2)}, u32[]{:S(2)}) collective-permute-start(f32[128,128]{1,0:T(8,128)S(1)} %convolution_bitcast_fusion.2), channel_id=1, source_target_pairs={{0,16},{8,24},{16,0},{24,8},{1,17},{9,25},{17,1},{25,9},{2,18},{10... | collective-permute-start | bytes 196616 | tf_op jit(solution)/shard_map/ppermute | solution.py:111
  38.1 0.6 convolution_bitcast_fusion
  38.7 1.8 %collective-permute-done.4 = f32[128,128]{1,0:T(8,128)S(1)} collective-permute-done((f32[128,128]{1,0:T(8,128)S(1)}, f32[128,128]{1,0:T(8,128)S(1)}, u32[]{:S(2)}, u32[]{:S(2)}) %collective-permute-start.4) | collective-permute-done | bytes 65568 | tf_op jit(solution)/shard_map/ppermute | solution.py:111
  40.5 1.3 %multiply_convert_fusion.1 = (bf16[128,128]{1,0:T(8,128)(2,1)S(1)}, f32[128,128]{1,0:T(8,128)S(1)}) fusion(f32[128,128]{1,0:T(8,128)S(1)} %convolution_bitcast_fusion, f32[128,128]{1,0:T(8,128)S(1)} %collective-permute-done.4, bf16[2,896,128]{2,1,0:T(8,128)(2,1)S(1)} %bitcast.127, pred[2]{0:T(512)(128)(4,1)S(1)} %copy-done.5, ...), kind=kOutput, calls=%fused_computation.76 | convolution fusion | flops 59064320 | bytes 1146882 | tf_op jit(solution)/shard_map/dot_general | solution.py:216
  41.8 0.6 fusion.4
  42.4 0.4 fusion.73
  42.8 0.4 add_convert_fusion
  43.4 1.8 %collective-permute-done.5 = bf16[2,128,896]{2,1,0:T(8,128)(2,1)S(1)} collective-permute-done((bf16[2,128,896]{2,1,0:T(8,128)(2,1)S(1)}, bf16[2,128,896]{2,1,0:T(8,128)(2,1)S(1)}, u32[]{:S(2)}, u32[]{:S(2)}) %collective-permute-start.5) | collective-permute-done | bytes 458784 | tf_op jit(solution)/shard_map/ppermute | solution.py:111
  45.4 1.6 %collective-permute-start.6 = (bf16[1,128,896]{2,1,0:T(8,128)(2,1)S(1)}, bf16[1,128,896]{2,1,0:T(8,128)(2,1)S(1)}, u32[]{:S(2)}, u32[]{:S(2)}) collective-permute-start(bf16[1,128,896]{2,1,0:T(8,128)(2,1)S(1)} %fusion.43), channel_id=1, source_target_pairs={{0,16},{8,24},{16,0},{24,8},{1,17},{9,25},{17,1},{25,9},{2,18},{10... | collective-permute-start | bytes 688136 | tf_op jit(solution)/shard_map/ppermute | solution.py:111
  47.0 6.1 %collective-permute-done.6 = bf16[1,128,896]{2,1,0:T(8,128)(2,1)S(1)} collective-permute-done((bf16[1,128,896]{2,1,0:T(8,128)(2,1)S(1)}, bf16[1,128,896]{2,1,0:T(8,128)(2,1)S(1)}, u32[]{:S(2)}, u32[]{:S(2)}) %collective-permute-start.6) | collective-permute-done | bytes 229408 | tf_op jit(solution)/shard_map/ppermute | solution.py:111
  53.1 0.7 %fusion.24 = bf16[1,128,896]{2,1,0:T(8,128)(2,1)} fusion(bf16[1,128,896]{2,1,0:T(8,128)(2,1)S(1)} %collective-permute-done.6, f32[1,2,128,896]{3,2,1,0:T(8,128)S(1)} %fusion.7, pred[]{:T(512)S(6)} %ne.18), kind=kLoop, calls=%fused_computation.40 | loop fusion | flops 458752 | bytes 1376257 | tf_op jit(solution)/shard_map/convert_element_type | solution.py:242
  53.9 5.0 %all-to-all-start.1 = ((bf16[8,16,896]{2,1,0:T(8,128)(2,1)}), bf16[8,16,896]{2,1,0:T(8,128)(2,1)S(1)}, u32[]{:S(2)}, u32[]{:S(2)}) async-start(bf16[8,16,896]{2,1,0:T(8,128)(2,1)} %bitcast.41), calls=%async_computation.1 | async-start | bytes 458752 | tf_op jit(solution)/shard_map/all_to_all | solution.py:243
  58.8 1.4 %convolution_convert_fusion = bf16[4,896,128]{2,1,0:T(8,128)(2,1)} fusion(pred[4]{0:T(512)(128)(4,1)S(1)} %get-tuple-element.18, pred[4]{0:T(512)(128)(4,1)S(1)} %get-tuple-element.19, pred[4]{0:T(512)(128)(4,1)S(1)} %iota_compare_fusion.3, bf16[128,896]{0,1:T(8,128)(2,1)S(1)} %copy.37, bf16[128,896]{0,1:T(8,128)(2,1)S(1)} %copy.36, ...), kind=kOutput, calls=%fused_computation.1 | convolution fusion | flops 119275520 | bytes 1867788 | tf_op jit(solution)/shard_map/dot_general | solution.py:235
  60.2 1.4 %convolution_convert_fusion.1 = bf16[4,896,128]{2,1,0:T(8,128)(2,1)} fusion(bf16[128,128,1]{1,0,2:T(8,128)(2,1)S(1)} %fusion.4, pred[4]{0:T(512)(128)(4,1)S(1)} %get-tuple-element.18, pred[4]{0:T(512)(128)(4,1)S(1)} %get-tuple-element.19, pred[4]{0:T(512)(128)(4,1)S(1)} %iota_compare_fusion.3, bf16[128,896]{0,1:T(8,128)(2,1)S(1)} %copy.37, ...), kind=kOutput, calls=%fused_computation.2 | convolution fusion | flops 119275520 | bytes 1867788 | tf_op jit(solution)/shard_map/dot_general | solution.py:232
  61.5 5.3 %all-to-all-done.1 = bf16[8,16,896]{2,1,0:T(8,128)(2,1)S(1)} async-done(((bf16[8,16,896]{2,1,0:T(8,128)(2,1)}), bf16[8,16,896]{2,1,0:T(8,128)(2,1)S(1)}, u32[]{:S(2)}, u32[]{:S(2)}) %all-to-all-start.1) | async-done | bytes 229408 | tf_op jit(solution)/shard_map/all_to_all | solution.py:243
  66.8 1.1 %convolution_convert_fusion.2 = bf16[256,896]{1,0:T(8,128)(2,1)} fusion(bf16[128,256]{1,0:T(8,128)(2,1)S(1)} %copy-done.4, bf16[128,896]{1,0:T(8,128)(2,1)S(1)} %bitcast.124), kind=kOutput, calls=%fused_computation.3 | convolution fusion | flops 58949632 | bytes 753664 | tf_op jit(solution)/shard_map/dot_general | solution.py:244
  (32 shorter events, 1.9 us)
Async XLA Ops:
  0.6 37.4 %copy-start = (bf16[1,3584,128]{2,1,0:T(8,128)(2,1)S(1)}, bf16[1,3584,128]{2,1,0:T(8,128)(2,1)}, u32[]{:S(2)}) copy-start(bf16[1,3584,128]{2,1,0:T(8,128)(2,1)} %param.13) | copy-start | bytes 2752516
  0.6 10.1 %copy-start.2 = (bf16[1,128,3584]{2,1,0:T(8,128)(2,1)S(1)}, bf16[1,128,3584]{2,1,0:T(8,128)(2,1)}, u32[]{:S(2)}) copy-start(bf16[1,128,3584]{2,1,0:T(8,128)(2,1)} %param.15) | copy-start | bytes 2752516
  3.5 21.1 %all-to-all-start = ((bf16[8,16,1920]{2,1,0:T(8,128)(2,1)}), bf16[8,16,1920]{2,1,0:T(8,128)(2,1)S(1)}, u32[]{:S(2)}, u32[]{:S(2)}) async-start(bf16[8,16,1920]{2,1,0:T(8,128)(2,1)} %bitcast.126), calls=%async_computation | async-start | bytes 983040 | tf_op jit(solution)/shard_map/all_to_all | solution.py:184
  10.9 12.0 %collective-permute-start.3 = (bf16[1792,128]{0,1:T(8,128)(2,1)S(1)}, bf16[1792,128]{0,1:T(8,128)(2,1)S(1)}, u32[]{:S(2)}, u32[]{:S(2)}) collective-permute-start(bf16[1792,128]{0,1:T(8,128)(2,1)S(1)} %get-tuple-element.11), channel_id=1, source_target_pairs={{0,16},{8,24},{16,0},{24,8},{1,17},{9,25},{17,1},{25,9},{2,18},{10... | collective-permute-start | bytes 1376264 | tf_op jit(solution)/shard_map/ppermute | solution.py:111
  24.6 6.3 %collective-permute-start = (bf16[1,128,896]{2,1,0:T(8,128)(2,1)S(1)}, bf16[1,128,896]{2,1,0:T(8,128)(2,1)S(1)}, u32[]{:S(2)}, u32[]{:S(2)}) collective-permute-start(bf16[1,128,896]{2,1,0:T(8,128)(2,1)S(1)} %get-tuple-element.12), channel_id=1, source_target_pairs={{0,16},{8,24},{16,0},{24,8},{1,17},{9,25},{17,1},{25,9},{2,18},{10... | collective-permute-start | bytes 688136 | tf_op jit(solution)/shard_map/ppermute | solution.py:111
  31.7 6.0 %collective-permute-start.1 = (bf16[2,128,896]{2,1,0:T(8,128)(2,1)}, bf16[2,128,896]{2,1,0:T(8,128)(2,1)S(1)}, u32[]{:S(2)}, u32[]{:S(2)}) collective-permute-start(bf16[2,128,896]{2,1,0:T(8,128)(2,1)} %pad_maximum_fusion), channel_id=1, source_target_pairs={{0,8},{8,0},{16,24},{24,16},{1,9},{9,1},{17,25},{25,17},{2,10},{10... | collective-permute-start | bytes 1376264 | tf_op jit(solution)/shard_map/ppermute | solution.py:111
  32.6 2.0 %collective-permute-start.2 = (bf16[1,128,896]{2,1,0:T(8,128)(2,1)}, bf16[1,128,896]{2,1,0:T(8,128)(2,1)}, u32[]{:S(2)}, u32[]{:S(2)}) collective-permute-start(bf16[1,128,896]{2,1,0:T(8,128)(2,1)} %fusion.84), channel_id=1, source_target_pairs={{0,8},{8,0},{16,24},{24,16},{1,9},{9,1},{17,25},{25,17},{2,10},{10... | collective-permute-start | bytes 688136 | tf_op jit(solution)/shard_map/ppermute | solution.py:111
  36.1 4.4 %collective-permute-start.4 = (f32[128,128]{1,0:T(8,128)S(1)}, f32[128,128]{1,0:T(8,128)S(1)}, u32[]{:S(2)}, u32[]{:S(2)}) collective-permute-start(f32[128,128]{1,0:T(8,128)S(1)} %convolution_bitcast_fusion.2), channel_id=1, source_target_pairs={{0,16},{8,24},{16,0},{24,8},{1,17},{9,25},{17,1},{25,9},{2,18},{10... | collective-permute-start | bytes 196616 | tf_op jit(solution)/shard_map/ppermute | solution.py:111
  38.1 2.4 %copy-start.3 = (bf16[128,896]{1,0:T(8,128)(2,1)S(1)}, bf16[128,896]{1,0:T(8,128)(2,1)}, u32[]{:S(2)}) copy-start(bf16[128,896]{1,0:T(8,128)(2,1)} %multiply_convert_fusion) | copy-start | bytes 688132
  38.1 2.4 %copy-start.5 = (pred[2]{0:T(512)(128)(4,1)S(1)}, pred[2]{0:T(512)(128)(4,1)}, u32[]{:S(2)}) copy-start(pred[2]{0:T(512)(128)(4,1)} %iota_compare_fusion) | copy-start | bytes 10
  38.1 3.7 %copy-start.1 = (bf16[1,3584,128]{2,1,0:T(8,128)(2,1)S(1)}, bf16[1,3584,128]{2,1,0:T(8,128)(2,1)}, u32[]{:S(2)}) copy-start(bf16[1,3584,128]{2,1,0:T(8,128)(2,1)} %param.14) | copy-start | bytes 2752516
  43.3 1.9 %collective-permute-start.5 = (bf16[2,128,896]{2,1,0:T(8,128)(2,1)S(1)}, bf16[2,128,896]{2,1,0:T(8,128)(2,1)S(1)}, u32[]{:S(2)}, u32[]{:S(2)}) collective-permute-start(bf16[2,128,896]{2,1,0:T(8,128)(2,1)S(1)} %fusion.22), channel_id=1, source_target_pairs={{0,8},{8,0},{16,24},{24,16},{1,9},{9,1},{17,25},{25,17},{2,10},{10... | collective-permute-start | bytes 1376264 | tf_op jit(solution)/shard_map/ppermute | solution.py:111
  45.4 7.7 %collective-permute-start.6 = (bf16[1,128,896]{2,1,0:T(8,128)(2,1)S(1)}, bf16[1,128,896]{2,1,0:T(8,128)(2,1)S(1)}, u32[]{:S(2)}, u32[]{:S(2)}) collective-permute-start(bf16[1,128,896]{2,1,0:T(8,128)(2,1)S(1)} %fusion.43), channel_id=1, source_target_pairs={{0,16},{8,24},{16,0},{24,8},{1,17},{9,25},{17,1},{25,9},{2,18},{10... | collective-permute-start | bytes 688136 | tf_op jit(solution)/shard_map/ppermute | solution.py:111
  53.9 13.0 %all-to-all-start.1 = ((bf16[8,16,896]{2,1,0:T(8,128)(2,1)}), bf16[8,16,896]{2,1,0:T(8,128)(2,1)S(1)}, u32[]{:S(2)}, u32[]{:S(2)}) async-start(bf16[8,16,896]{2,1,0:T(8,128)(2,1)} %bitcast.41), calls=%async_computation.1 | async-start | bytes 458752 | tf_op jit(solution)/shard_map/all_to_all | solution.py:243
  60.2 6.6 %copy-start.4 = (bf16[128,256]{1,0:T(8,128)(2,1)S(1)}, bf16[128,256]{1,0:T(8,128)(2,1)}, u32[]{:S(2)}) copy-start(bf16[128,256]{1,0:T(8,128)(2,1)} %get-tuple-element.6) | copy-start | bytes 196612

commit v11 on v10

--- a/solution.py
+++ b/solution.py
@@ -9,7 +9,7 @@
 CAP = 16
 
 
-def glue_kernel(n_dest, width, side, split, ids_ref, gates_ref, flags_ref, tok_ref, grd_ref, *outs):
+def glue_kernel(n_dest, width, side, split, ids_rows_ref, ids_ref, gates_ref, flags_ref, tok_ref, grd_ref, *outs):
     f32, bf16 = jnp.float32, jnp.bfloat16
     rows = tok_ref.shape[0]
     slots = n_dest * CAP
@@ -71,7 +71,25 @@
         pay_out[:, :width] = tok
         pay_out[:, width : 2 * width] = grd
         pay_out[:, 2 * width :] = side_v
-    pick_out[...] = pick_b
+    ids_rows = ids_rows_ref[...]
+    edited_row = lax.broadcasted_iota(jnp.int32, (rows, lanes), 1) * EXP_DEV
+    valid_row = lax.broadcasted_iota(jnp.int32, (rows, lanes), 1) < n_dest
+    hits_t = jnp.zeros((rows, lanes), f32)
+    for k in range(ids_rows.shape[1]):
+        hits_t = hits_t + jnp.where((ids_rows[:, k : k + 1] == edited_row) & valid_row, 1.0, 0.0)
+    after = jnp.where(
+        lax.broadcasted_iota(jnp.int32, (rows, rows), 1) < lax.broadcasted_iota(jnp.int32, (rows, rows), 0),
+        1.0, 0.0,
+    ).astype(bf16)
+    rank_t = jnp.dot(after, hits_t.astype(bf16), preferred_element_type=f32)
+    lane_of = lax.broadcasted_iota(jnp.int32, (lanes, slots), 0)
+    spread_t = jnp.where(
+        lax.shift_right_logical(lax.broadcasted_iota(jnp.int32, (lanes, slots), 1), 4) == lane_of, 1.0, 0.0
+    ).astype(bf16)
+    hit_at = jnp.dot(hits_t.astype(bf16), spread_t, preferred_element_type=f32)
+    rank_at = jnp.dot(rank_t.astype(bf16), spread_t, preferred_element_type=f32)
+    place_t = (lax.broadcasted_iota(jnp.int32, (rows, slots), 1) & (CAP - 1)).astype(f32)
+    pick_out[...] = jnp.where((hit_at == 1.0) & (rank_at == place_t), 1.0, 0.0).astype(bf16)
 
 
 def glue(expert_ids, gate_values, forget_flags, tokens, token_grads, n_dest):
@@ -83,16 +101,16 @@
     split = width % 128 != 0
     bf16 = jnp.bfloat16
     if split:
-        shapes = [(slots, width), (slots, width), (slots, side), (slots, rows)]
+        shapes = [(slots, width), (slots, width), (slots, side), (rows, slots)]
     else:
-        shapes = [(slots, 2 * width + side), (slots, rows)]
+        shapes = [(slots, 2 * width + side), (rows, slots)]
     vmem = pl.BlockSpec(memory_space=pltpu.VMEM)
     outs = pl.pallas_call(
         functools.partial(glue_kernel, n_dest, width, side, split),
         out_shape=[jax.ShapeDtypeStruct(s, bf16) for s in shapes],
-        in_specs=[vmem] * 5,
+        in_specs=[vmem] * 6,
         out_specs=[vmem] * len(shapes),
-    )(expert_ids.T, gate_values.T, forget_flags.reshape(1, rows), tokens, token_grads)
+    )(expert_ids, expert_ids.T, gate_values.T, forget_flags.reshape(1, rows), tokens, token_grads)
     if split:
         return jnp.concatenate(outs[:3], axis=1), outs[3]
     return outs[0], outs[1]
@@ -241,9 +259,7 @@
     part = (from_gate + from_up).astype(jnp.bfloat16)
     summed = scatter_dp(jnp.swapaxes(part, 1, 2), n_dp).astype(jnp.bfloat16)
     returned = lax.all_to_all(summed, "expert", split_axis=0, concat_axis=0, tiled=True)
-    input_grad = lax.dot_general(
-        pick_t, returned, (((0,), (0,)), ((), ())), preferred_element_type=jnp.float32
-    )
+    input_grad = jnp.dot(pick_t, returned, preferred_element_type=jnp.float32)
     return (
         grad_gate.reshape(1, n_dp * width, ff),
         grad_up.reshape(1, n_dp * width, ff),

time: 68.3 us -> 70.1 us (1.026)
  local copies, waits for them, and re-layouts: 1.3 us -> 2.92 us
    unnamed x12 -> x13, local copies, waits for them, and re-layouts: 0.03 us -> 1.65 us
where the time goes in v11:
time: 70.1 us; the launch traced here: 69.7 us
  waiting for transfers between devices  30.6 us (44%)
  starting transfers between devices  19.1 us (27%)
  matrix products  8.72 us (12%)
  other arithmetic  4.49 us (6%)
  Pallas kernels  3.04 us (4%)
  local copies, waits for them, and re-layouts  2.92 us (4%)
  between operations  0.84 us (1%)
    ppermute x7, waiting for transfers between devices, partner(): return lax.ppermute(x, 'dp', [(i, i ^ bit) for i in range(n)])  23.9 us
    all_to_all x1, starting transfers between devices, on_device(): lax.all_to_all(payload, 'expert', split_axis=0, concat_axis=0, tiled=True)  7.31 us
    ppermute x7, starting transfers between devices, partner(): return lax.ppermute(x, 'dp', [(i, i ^ bit) for i in range(n)])  6.86 us
    all_to_all x1, waiting for transfers between devices, on_device(): lax.all_to_all(summed, 'expert', split_axis=0, concat_axis=0, tiled=True)  5.28 us
    all_to_all x1, starting transfers between devices, on_device(): lax.all_to_all(summed, 'expert', split_axis=0, concat_axis=0, tiled=True)  4.95 us
    pallas_call x1, Pallas kernels, glue(): pl.pallas_call(functools.partial(glue_kernel, n_dest, width, side, split)...  3.04 us
    unnamed x13, local copies, waits for them, and re-layouts  1.65 us
    all_to_all x1, waiting for transfers between devices, on_device(): lax.all_to_all(payload, 'expert', split_axis=0, concat_axis=0, tiled=True)  1.4 us
  transfers between devices with their start and end apart: 9, of which 8 were waited for; matrix products, arithmetic and copies ran while one was open for 13% of the time, Pallas kernels for 0%

profile of v11, /device:TPU:0, one launch (start us, length us, event | category | flops | bytes accessed | tf_op | source)
XLA Modules:
  0.0 69.7 jit_solution(15101473646980276662)
XLA Ops:
  0.7 1.6 %copy.36.ids_rows_ref = s32[256,8]{1,0:T(8,128)} copy(s32[256,8]{0,1:T(8,128)} %param.10) | data formatting | bytes 16384 | tf_op args[2]
  2.3 3.0 %shard_map.103 = (bf16[128,1920]{1,0:T(8,128)(2,1)}, bf16[256,128]{1,0:T(8,128)(2,1)}) custom-call(s32[256,8]{1,0:T(8,128)} %copy.36.ids_rows_ref, s32[8,256]{1,0:T(8,128)} %bitcast.129, f32[8,256]{1,0:T(8,128)} %bitcast.130, s32[1,256]{1,0:T(1,128)} %bitcast.131, bf16[256,896]{1,0:T(8,128)(2,1)} %tok_ref.1, bf16[256,896]{1,0:T(8,128)(2,1)} %grd_ref.1), custom_call_target="tpu_custom_call" | custom-call | tf_op jit(solution)/shard_map/pallas_call | solution.py:108
  5.3 7.3 %all-to-all-start = ((bf16[8,16,1920]{2,1,0:T(8,128)(2,1)}), bf16[8,16,1920]{2,1,0:T(8,128)(2,1)S(1)}, u32[]{:S(2)}, u32[]{:S(2)}) async-start(bf16[8,16,1920]{2,1,0:T(8,128)(2,1)} %bitcast.126), calls=%async_computation | async-start | bytes 983040 | tf_op jit(solution)/shard_map/all_to_all | solution.py:202
  12.7 1.6 %collective-permute-start.3 = (bf16[1792,128]{0,1:T(8,128)(2,1)S(1)}, bf16[1792,128]{0,1:T(8,128)(2,1)S(1)}, u32[]{:S(2)}, u32[]{:S(2)}) collective-permute-start(bf16[1792,128]{0,1:T(8,128)(2,1)S(1)} %get-tuple-element.11), channel_id=1, source_target_pairs={{0,16},{8,24},{16,0},{24,8},{1,17},{9,25},{17,1},{25,9},{2,18},{10... | collective-permute-start | bytes 1376264 | tf_op jit(solution)/shard_map/ppermute | solution.py:129
  14.5 0.6 iota_compare_fusion
  15.1 9.7 %collective-permute-done.3 = bf16[1792,128]{0,1:T(8,128)(2,1)S(1)} collective-permute-done((bf16[1792,128]{0,1:T(8,128)(2,1)S(1)}, bf16[1792,128]{0,1:T(8,128)(2,1)S(1)}, u32[]{:S(2)}, u32[]{:S(2)}) %collective-permute-start.3) | collective-permute-done | bytes 458784 | tf_op jit(solution)/shard_map/ppermute | solution.py:129
  24.7 0.3 copy.42
  25.0 1.4 %all-to-all-done = bf16[8,16,1920]{2,1,0:T(8,128)(2,1)S(1)} async-done(((bf16[8,16,1920]{2,1,0:T(8,128)(2,1)}), bf16[8,16,1920]{2,1,0:T(8,128)(2,1)S(1)}, u32[]{:S(2)}, u32[]{:S(2)}) %all-to-all-start) | async-done | bytes 491552 | tf_op jit(solution)/shard_map/all_to_all | solution.py:202
  26.5 1.6 %collective-permute-start = (bf16[1,128,896]{2,1,0:T(8,128)(2,1)S(1)}, bf16[1,128,896]{2,1,0:T(8,128)(2,1)S(1)}, u32[]{:S(2)}, u32[]{:S(2)}) collective-permute-start(bf16[1,128,896]{2,1,0:T(8,128)(2,1)S(1)} %get-tuple-element.12), channel_id=1, source_target_pairs={{0,16},{8,24},{16,0},{24,8},{1,17},{9,25},{17,1},{25,9},{2,18},{10... | collective-permute-start | bytes 688136 | tf_op jit(solution)/shard_map/ppermute | solution.py:129
  28.7 4.0 %collective-permute-done = bf16[1,128,896]{2,1,0:T(8,128)(2,1)S(1)} collective-permute-done((bf16[1,128,896]{2,1,0:T(8,128)(2,1)S(1)}, bf16[1,128,896]{2,1,0:T(8,128)(2,1)S(1)}, u32[]{:S(2)}, u32[]{:S(2)}) %collective-permute-start) | collective-permute-done | bytes 229408 | tf_op jit(solution)/shard_map/ppermute | solution.py:129
  32.7 0.8 %pad_maximum_fusion = bf16[2,128,896]{2,1,0:T(8,128)(2,1)} fusion(bf16[1,128,896]{2,1,0:T(8,128)(2,1)S(1)} %collective-permute-done, bf16[1,128,896]{2,1,0:T(8,128)(2,1)S(1)} %get-tuple-element.12), kind=kLoop, calls=%fused_computation.36 | loop fusion | flops 229376 | bytes 917504 | tf_op jit(solution)/shard_map/stack | solution.py:138
  33.6 0.8 %fusion.84 = bf16[1,128,896]{2,1,0:T(8,128)(2,1)} fusion(bf16[128,1920]{1,0:T(8,128)(2,1)S(1)} %bitcast.119, f32[128]{0:T(128)S(1)} %fusion.56), kind=kLoop, calls=%fused_computation.110 | loop fusion | flops 344064 | bytes 459264 | tf_op jit(solution)/shard_map/stack | solution.py:158
  34.5 0.6 collective-permute-start.2
  35.1 0.8 %multiply_convert_fusion = bf16[128,896]{1,0:T(8,128)(2,1)} fusion(bf16[128,1920]{1,0:T(8,128)(2,1)S(1)} %bitcast.120, f32[128]{0:T(128)S(1)} %fusion.56), kind=kLoop, calls=%fused_computation.44 | loop fusion | flops 344064 | bytes 459264 | tf_op jit(solution)/shard_map/convert_element_type | solution.py:224
  36.1 0.5 collective-permute-done.2
  36.6 1.4 %convolution_bitcast_fusion.2 = f32[128,128]{1,0:T(8,128)S(1)} fusion(bf16[2,896,128]{2,1,0:T(8,128)(2,1)S(1)} %bitcast.128, pred[2]{0:T(512)(128)(4,1)} %iota_compare_fusion, bf16[128,896]{1,0:T(8,128)(2,1)} %multiply_convert_fusion, bf16[128,896]{1,0:T(8,128)(2,1)} %bitcast.14), kind=kOutput, calls=%fused_computation.8 | convolution fusion | flops 58949632 | bytes 983042 | tf_op jit(solution)/shard_map/dot_general | solution.py:237
  38.0 1.6 %collective-permute-start.4 = (f32[128,128]{1,0:T(8,128)S(1)}, f32[128,128]{1,0:T(8,128)S(1)}, u32[]{:S(2)}, u32[]{:S(2)}) collective-permute-start(f32[128,128]{1,0:T(8,128)S(1)} %convolution_bitcast_fusion.2), channel_id=1, source_target_pairs={{0,16},{8,24},{16,0},{24,8},{1,17},{9,25},{17,1},{25,9},{2,18},{10... | collective-permute-start | bytes 196616 | tf_op jit(solution)/shard_map/ppermute | solution.py:129
  40.0 0.6 convolution_bitcast_fusion
  40.6 1.8 %collective-permute-done.4 = f32[128,128]{1,0:T(8,128)S(1)} collective-permute-done((f32[128,128]{1,0:T(8,128)S(1)}, f32[128,128]{1,0:T(8,128)S(1)}, u32[]{:S(2)}, u32[]{:S(2)}) %collective-permute-start.4) | collective-permute-done | bytes 65568 | tf_op jit(solution)/shard_map/ppermute | solution.py:129
  42.4 1.3 %multiply_convert_fusion.1 = (bf16[128,128]{1,0:T(8,128)(2,1)S(1)}, f32[128,128]{1,0:T(8,128)S(1)}) fusion(f32[128,128]{1,0:T(8,128)S(1)} %convolution_bitcast_fusion, f32[128,128]{1,0:T(8,128)S(1)} %collective-permute-done.4, bf16[2,896,128]{2,1,0:T(8,128)(2,1)S(1)} %bitcast.127, pred[2]{0:T(512)(128)(4,1)S(1)} %copy-done.5, ...), kind=kOutput, calls=%fused_computation.76 | convolution fusion | flops 59064320 | bytes 1146882 | tf_op jit(solution)/shard_map/dot_general | solution.py:234
  43.7 0.6 fusion.4
  44.3 0.4 fusion.73
  44.7 0.4 add_convert_fusion
  45.3 1.8 %collective-permute-done.5 = bf16[2,128,896]{2,1,0:T(8,128)(2,1)S(1)} collective-permute-done((bf16[2,128,896]{2,1,0:T(8,128)(2,1)S(1)}, bf16[2,128,896]{2,1,0:T(8,128)(2,1)S(1)}, u32[]{:S(2)}, u32[]{:S(2)}) %collective-permute-start.5) | collective-permute-done | bytes 458784 | tf_op jit(solution)/shard_map/ppermute | solution.py:129
  47.3 1.6 %collective-permute-start.6 = (bf16[1,128,896]{2,1,0:T(8,128)(2,1)S(1)}, bf16[1,128,896]{2,1,0:T(8,128)(2,1)S(1)}, u32[]{:S(2)}, u32[]{:S(2)}) collective-permute-start(bf16[1,128,896]{2,1,0:T(8,128)(2,1)S(1)} %fusion.43), channel_id=1, source_target_pairs={{0,16},{8,24},{16,0},{24,8},{1,17},{9,25},{17,1},{25,9},{2,18},{10... | collective-permute-start | bytes 688136 | tf_op jit(solution)/shard_map/ppermute | solution.py:129
  48.8 6.2 %collective-permute-done.6 = bf16[1,128,896]{2,1,0:T(8,128)(2,1)S(1)} collective-permute-done((bf16[1,128,896]{2,1,0:T(8,128)(2,1)S(1)}, bf16[1,128,896]{2,1,0:T(8,128)(2,1)S(1)}, u32[]{:S(2)}, u32[]{:S(2)}) %collective-permute-start.6) | collective-permute-done | bytes 229408 | tf_op jit(solution)/shard_map/ppermute | solution.py:129
  55.0 0.7 %fusion.24 = bf16[1,128,896]{2,1,0:T(8,128)(2,1)} fusion(bf16[1,128,896]{2,1,0:T(8,128)(2,1)S(1)} %collective-permute-done.6, f32[1,2,128,896]{3,2,1,0:T(8,128)S(1)} %fusion.7, pred[]{:T(512)S(6)} %ne.18), kind=kLoop, calls=%fused_computation.40 | loop fusion | flops 458752 | bytes 1376257 | tf_op jit(solution)/shard_map/convert_element_type | solution.py:260
  55.7 5.0 %all-to-all-start.1 = ((bf16[8,16,896]{2,1,0:T(8,128)(2,1)}), bf16[8,16,896]{2,1,0:T(8,128)(2,1)S(1)}, u32[]{:S(2)}, u32[]{:S(2)}) async-start(bf16[8,16,896]{2,1,0:T(8,128)(2,1)} %bitcast.41), calls=%async_computation.1 | async-start | bytes 458752 | tf_op jit(solution)/shard_map/all_to_all | solution.py:261
  60.7 1.4 %convolution_convert_fusion = bf16[4,896,128]{2,1,0:T(8,128)(2,1)} fusion(pred[4]{0:T(512)(128)(4,1)S(1)} %get-tuple-element.18, pred[4]{0:T(512)(128)(4,1)S(1)} %get-tuple-element.19, pred[4]{0:T(512)(128)(4,1)S(1)} %iota_compare_fusion.3, bf16[128,896]{0,1:T(8,128)(2,1)S(1)} %copy.40, bf16[128,896]{0,1:T(8,128)(2,1)S(1)} %copy.39, ...), kind=kOutput, calls=%fused_computation.1 | convolution fusion | flops 119275520 | bytes 1867788 | tf_op jit(solution)/shard_map/dot_general | solution.py:253
  62.1 1.4 %convolution_convert_fusion.1 = bf16[4,896,128]{2,1,0:T(8,128)(2,1)} fusion(bf16[128,128,1]{1,0,2:T(8,128)(2,1)S(1)} %fusion.4, pred[4]{0:T(512)(128)(4,1)S(1)} %get-tuple-element.18, pred[4]{0:T(512)(128)(4,1)S(1)} %get-tuple-element.19, pred[4]{0:T(512)(128)(4,1)S(1)} %iota_compare_fusion.3, bf16[128,896]{0,1:T(8,128)(2,1)S(1)} %copy.40, ...), kind=kOutput, calls=%fused_computation.2 | convolution fusion | flops 119275520 | bytes 1867788 | tf_op jit(solution)/shard_map/dot_general | solution.py:250
  63.4 5.3 %all-to-all-done.1 = bf16[8,16,896]{2,1,0:T(8,128)(2,1)S(1)} async-done(((bf16[8,16,896]{2,1,0:T(8,128)(2,1)}), bf16[8,16,896]{2,1,0:T(8,128)(2,1)S(1)}, u32[]{:S(2)}, u32[]{:S(2)}) %all-to-all-start.1) | async-done | bytes 229408 | tf_op jit(solution)/shard_map/all_to_all | solution.py:261
  68.7 1.0 %convolution_convert_fusion.2 = bf16[256,896]{1,0:T(8,128)(2,1)} fusion(bf16[256,128]{1,0:T(8,128)(2,1)S(1)} %copy-done.4, bf16[128,896]{1,0:T(8,128)(2,1)S(1)} %bitcast.124), kind=kOutput, calls=%fused_computation.3 | convolution fusion | flops 58949632 | bytes 753664 | tf_op jit(solution)/shard_map/dot_general | solution.py:262
  (33 shorter events, 2.2 us)
Async XLA Ops:
  0.6 39.3 %copy-start = (bf16[1,3584,128]{2,1,0:T(8,128)(2,1)S(1)}, bf16[1,3584,128]{2,1,0:T(8,128)(2,1)}, u32[]{:S(2)}) copy-start(bf16[1,3584,128]{2,1,0:T(8,128)(2,1)} %param.13) | copy-start | bytes 2752516
  0.6 12.0 %copy-start.2 = (bf16[1,128,3584]{2,1,0:T(8,128)(2,1)S(1)}, bf16[1,128,3584]{2,1,0:T(8,128)(2,1)}, u32[]{:S(2)}) copy-start(bf16[1,128,3584]{2,1,0:T(8,128)(2,1)} %param.15) | copy-start | bytes 2752516
  5.3 21.1 %all-to-all-start = ((bf16[8,16,1920]{2,1,0:T(8,128)(2,1)}), bf16[8,16,1920]{2,1,0:T(8,128)(2,1)S(1)}, u32[]{:S(2)}, u32[]{:S(2)}) async-start(bf16[8,16,1920]{2,1,0:T(8,128)(2,1)} %bitcast.126), calls=%async_computation | async-start | bytes 983040 | tf_op jit(solution)/shard_map/all_to_all | solution.py:202
  12.7 12.0 %collective-permute-start.3 = (bf16[1792,128]{0,1:T(8,128)(2,1)S(1)}, bf16[1792,128]{0,1:T(8,128)(2,1)S(1)}, u32[]{:S(2)}, u32[]{:S(2)}) collective-permute-start(bf16[1792,128]{0,1:T(8,128)(2,1)S(1)} %get-tuple-element.11), channel_id=1, source_target_pairs={{0,16},{8,24},{16,0},{24,8},{1,17},{9,25},{17,1},{25,9},{2,18},{10... | collective-permute-start | bytes 1376264 | tf_op jit(solution)/shard_map/ppermute | solution.py:129
  26.5 6.3 %collective-permute-start = (bf16[1,128,896]{2,1,0:T(8,128)(2,1)S(1)}, bf16[1,128,896]{2,1,0:T(8,128)(2,1)S(1)}, u32[]{:S(2)}, u32[]{:S(2)}) collective-permute-start(bf16[1,128,896]{2,1,0:T(8,128)(2,1)S(1)} %get-tuple-element.12), channel_id=1, source_target_pairs={{0,16},{8,24},{16,0},{24,8},{1,17},{9,25},{17,1},{25,9},{2,18},{10... | collective-permute-start | bytes 688136 | tf_op jit(solution)/shard_map/ppermute | solution.py:129
  33.6 6.0 %collective-permute-start.1 = (bf16[2,128,896]{2,1,0:T(8,128)(2,1)}, bf16[2,128,896]{2,1,0:T(8,128)(2,1)S(1)}, u32[]{:S(2)}, u32[]{:S(2)}) collective-permute-start(bf16[2,128,896]{2,1,0:T(8,128)(2,1)} %pad_maximum_fusion), channel_id=1, source_target_pairs={{0,8},{8,0},{16,24},{24,16},{1,9},{9,1},{17,25},{25,17},{2,10},{10... | collective-permute-start | bytes 1376264 | tf_op jit(solution)/shard_map/ppermute | solution.py:129
  34.5 2.0 %collective-permute-start.2 = (bf16[1,128,896]{2,1,0:T(8,128)(2,1)}, bf16[1,128,896]{2,1,0:T(8,128)(2,1)}, u32[]{:S(2)}, u32[]{:S(2)}) collective-permute-start(bf16[1,128,896]{2,1,0:T(8,128)(2,1)} %fusion.84), channel_id=1, source_target_pairs={{0,8},{8,0},{16,24},{24,16},{1,9},{9,1},{17,25},{25,17},{2,10},{10... | collective-permute-start | bytes 688136 | tf_op jit(solution)/shard_map/ppermute | solution.py:129
  38.0 4.4 %collective-permute-start.4 = (f32[128,128]{1,0:T(8,128)S(1)}, f32[128,128]{1,0:T(8,128)S(1)}, u32[]{:S(2)}, u32[]{:S(2)}) collective-permute-start(f32[128,128]{1,0:T(8,128)S(1)} %convolution_bitcast_fusion.2), channel_id=1, source_target_pairs={{0,16},{8,24},{16,0},{24,8},{1,17},{9,25},{17,1},{25,9},{2,18},{10... | collective-permute-start | bytes 196616 | tf_op jit(solution)/shard_map/ppermute | solution.py:129
  39.9 2.5 %copy-start.3 = (bf16[128,896]{1,0:T(8,128)(2,1)S(1)}, bf16[128,896]{1,0:T(8,128)(2,1)}, u32[]{:S(2)}) copy-start(bf16[128,896]{1,0:T(8,128)(2,1)} %multiply_convert_fusion) | copy-start | bytes 688132
  39.9 2.5 %copy-start.5 = (pred[2]{0:T(512)(128)(4,1)S(1)}, pred[2]{0:T(512)(128)(4,1)}, u32[]{:S(2)}) copy-start(pred[2]{0:T(512)(128)(4,1)} %iota_compare_fusion) | copy-start | bytes 10
  39.9 3.7 %copy-start.1 = (bf16[1,3584,128]{2,1,0:T(8,128)(2,1)S(1)}, bf16[1,3584,128]{2,1,0:T(8,128)(2,1)}, u32[]{:S(2)}) copy-start(bf16[1,3584,128]{2,1,0:T(8,128)(2,1)} %param.14) | copy-start | bytes 2752516
  45.2 1.9 %collective-permute-start.5 = (bf16[2,128,896]{2,1,0:T(8,128)(2,1)S(1)}, bf16[2,128,896]{2,1,0:T(8,128)(2,1)S(1)}, u32[]{:S(2)}, u32[]{:S(2)}) collective-permute-start(bf16[2,128,896]{2,1,0:T(8,128)(2,1)S(1)} %fusion.22), channel_id=1, source_target_pairs={{0,8},{8,0},{16,24},{24,16},{1,9},{9,1},{17,25},{25,17},{2,10},{10... | collective-permute-start | bytes 1376264 | tf_op jit(solution)/shard_map/ppermute | solution.py:129
  47.3 7.7 %collective-permute-start.6 = (bf16[1,128,896]{2,1,0:T(8,128)(2,1)S(1)}, bf16[1,128,896]{2,1,0:T(8,128)(2,1)S(1)}, u32[]{:S(2)}, u32[]{:S(2)}) collective-permute-start(bf16[1,128,896]{2,1,0:T(8,128)(2,1)S(1)} %fusion.43), channel_id=1, source_target_pairs={{0,16},{8,24},{16,0},{24,8},{1,17},{9,25},{17,1},{25,9},{2,18},{10... | collective-permute-start | bytes 688136 | tf_op jit(solution)/shard_map/ppermute | solution.py:129
  55.7 13.0 %all-to-all-start.1 = ((bf16[8,16,896]{2,1,0:T(8,128)(2,1)}), bf16[8,16,896]{2,1,0:T(8,128)(2,1)S(1)}, u32[]{:S(2)}, u32[]{:S(2)}) async-start(bf16[8,16,896]{2,1,0:T(8,128)(2,1)} %bitcast.41), calls=%async_computation.1 | async-start | bytes 458752 | tf_op jit(solution)/shard_map/all_to_all | solution.py:261
  62.1 6.6 %copy-start.4 = (bf16[256,128]{1,0:T(8,128)(2,1)S(1)}, bf16[256,128]{1,0:T(8,128)(2,1)}, u32[]{:S(2)}) copy-start(bf16[256,128]{1,0:T(8,128)(2,1)} %get-tuple-element.6) | copy-start | bytes 196612

commit v12 on v10

--- a/solution.py
+++ b/solution.py
@@ -129,6 +129,20 @@
     return out
 
 
+def gather_from(held, owners, bit, n):
+    while bit >= 1:
+        stacked = jnp.stack(held)
+        got = partner(stacked, bit, n)
+        held = held + [got[i] for i in range(len(held))]
+        owners = owners + [o ^ bit for o in owners]
+        bit //= 2
+    at = lax.broadcasted_iota(jnp.int32, (n, 1, 1), 0)
+    out = jnp.broadcast_to(held[0][None], (n,) + held[0].shape)
+    for piece, owner in zip(held[1:], owners[1:]):
+        out = jnp.where(at == owner, piece[None], out)
+    return out
+
+
 def gather_half(x, n):
     me = lax.axis_index("dp")
     top = n // 2
@@ -208,20 +222,32 @@
     w_gate = gate_weight[0].reshape(n_dp, width, ff)
     w_up = up_weight[0].reshape(n_dp, width, ff)
     last_dims = (((1,), (1,)), ((), ()))
-    slot_tokens = gather_dp(part_tokens, n_dp)
     if n_dp > 1:
         half_grads, _ = gather_half(part_grads, n_dp)
         half_dims = (((0, 2), (0, 1)), ((), ()))
         ff_down = w_down.shape[0]
+        lent = lax.dot_general(
+            half_grads, borrowed.reshape(top, width, ff_down), half_dims, preferred_element_type=jnp.float32
+        )
+        lent_hi = bf16_part(lent)
+        lent_rest = lent - lent_hi
+        lent_mid = bf16_part(lent_rest)
+        lent_lo = lent_rest - lent_mid
+        outgoing = jnp.concatenate(
+            [part_tokens, lent_hi.astype(jnp.bfloat16), lent_mid.astype(jnp.bfloat16), lent_lo.astype(jnp.bfloat16)],
+            axis=1,
+        )
+        incoming = partner(outgoing, top, n_dp)
+        share = incoming[:, width:].astype(jnp.float32)
+        returned_share = (share[:, :ff_down] + share[:, ff_down : 2 * ff_down]) + share[:, 2 * ff_down :]
         hidden_grad = lax.dot_general(
             half_grads, keep.reshape(top, width, ff_down), half_dims, preferred_element_type=jnp.float32
         )
-        lent = lax.dot_general(
-            half_grads, borrowed.reshape(top, width, ff_down), half_dims, preferred_element_type=jnp.float32
-        )
-        hidden_grad = hidden_grad + partner(lent, top, n_dp)
+        hidden_grad = hidden_grad + returned_share
+        slot_tokens = gather_from([part_tokens, incoming[:, :width]], [me_dp, me_dp ^ top], top // 2, n_dp)
     else:
         hidden_grad = lax.dot_general(part_grads, w_down, last_dims, preferred_element_type=jnp.float32)
+        slot_tokens = part_tokens[None]
     chunk_dims = (((0, 2), (0, 1)), ((), ()))
     gate_pre = lax.dot_general(slot_tokens, w_gate, chunk_dims, preferred_element_type=jnp.float32)
     up_pre = lax.dot_general(slot_tokens, w_up, chunk_dims, preferred_element_type=jnp.float32)

time: 68.3 us -> 66.9 us (0.980)
  waiting for transfers between devices: 30.5 us -> 34.8 us
  starting transfers between devices: 19.2 us -> 15.9 us
  matrix products: 8.76 us -> 6.82 us
  other arithmetic: 4.49 us -> 2.64 us
  local copies, waits for them, and re-layouts: 1.3 us -> 2.57 us
    all_to_all x1, waiting for transfers between devices: 1.4 us -> 10.8 us  [on_device(): lax.all_to_all(payload, 'expert', split_axis=0, concat_axis=0, tiled=True)]
    ppermute x7 -> x6, waiting for transfers between devices: 23.8 us -> 18.8 us  [partner(): return lax.ppermute(x, 'dp', [(i, i ^ bit) for i in range(n)])]
    ppermute x7 -> x6, starting transfers between devices: 6.96 us -> 4.99 us  [partner(): return lax.ppermute(x, 'dp', [(i, i ^ bit) for i in range(n)])]
    unnamed x12 -> x15, local copies, waits for them, and re-layouts: 0.03 us -> 1.42 us
    all_to_all x1, starting transfers between devices: 4.95 us -> 3.64 us  [on_device(): lax.all_to_all(summed, 'expert', split_axis=0, concat_axis=0, tiled=True)]
    dot_general x1, matrix products: 1.39 us -> 0.37 us  [on_device(): lax.dot_general(half_grads, borrowed.reshape(top, width, ff_down), half_d...]
    dot_general x1, matrix products: 1.27 us -> 0.33 us  [on_device(): lax.dot_general(half_grads, keep.reshape(top, width, ff_down), half_dims,...]
    transpose x1, other arithmetic: 0.07 us -> 0.83 us  [on_device(): lend = jnp.where(upper_half, w_down[:, :half_cols], w_down[:, half_cols:]).T]
  transfers between devices with their start and end apart: 9 -> 8, of which waited for: 8 -> 7; matrix products, arithmetic and copies ran while one was open for 13% -> 8% of each run, Pallas kernels for 0% -> 0%
where the time goes in v12:
time: 66.9 us; the launch traced here: 66.5 us
  waiting for transfers between devices  34.8 us (52%)
  starting transfers between devices  15.9 us (24%)
  matrix products  6.82 us (10%)
  Pallas kernels  2.81 us (4%)
  other arithmetic  2.64 us (4%)
  local copies, waits for them, and re-layouts  2.57 us (4%)
  between operations  0.91 us (1%)
    ppermute x6, waiting for transfers between devices, partner(): return lax.ppermute(x, 'dp', [(i, i ^ bit) for i in range(n)])  18.8 us
    all_to_all x1, waiting for transfers between devices, on_device(): lax.all_to_all(payload, 'expert', split_axis=0, concat_axis=0, tiled=True)  10.8 us
    all_to_all x1, starting transfers between devices, on_device(): lax.all_to_all(payload, 'expert', split_axis=0, concat_axis=0, tiled=True)  7.31 us
    all_to_all x1, waiting for transfers between devices, on_device(): lax.all_to_all(summed, 'expert', split_axis=0, concat_axis=0, tiled=True)  5.27 us
    ppermute x6, starting transfers between devices, partner(): return lax.ppermute(x, 'dp', [(i, i ^ bit) for i in range(n)])  4.99 us
    all_to_all x1, starting transfers between devices, on_device(): lax.all_to_all(summed, 'expert', split_axis=0, concat_axis=0, tiled=True)  3.64 us
    pallas_call x1, Pallas kernels, glue(): pl.pallas_call(functools.partial(glue_kernel, n_dest, width, side, split)...  2.81 us
    unnamed x15, local copies, waits for them, and re-layouts  1.42 us
  transfers between devices with their start and end apart: 8, of which 7 were waited for; matrix products, arithmetic and copies ran while one was open for 8% of the time, Pallas kernels for 0%

profile of v12, /device:TPU:0, one launch (start us, length us, event | category | flops | bytes accessed | tf_op | source)
XLA Modules:
  0.0 66.5 jit_solution(4028906267139669176)
XLA Ops:
  0.7 2.8 %shard_map.103 = (bf16[128,1920]{1,0:T(8,128)(2,1)}, bf16[128,256]{1,0:T(8,128)(2,1)}) custom-call(s32[8,256]{1,0:T(8,128)} %bitcast.128, f32[8,256]{1,0:T(8,128)} %bitcast.129, s32[1,256]{1,0:T(1,128)} %bitcast.130, bf16[256,896]{1,0:T(8,128)(2,1)} %tok_ref.1, bf16[256,896]{1,0:T(8,128)(2,1)} %grd_ref.1), custom_call_target="tpu_custom_call" | custom-call | tf_op jit(solution)/shard_map/pallas_call | solution.py:90
  3.5 7.3 %all-to-all-start = ((bf16[8,16,1920]{2,1,0:T(8,128)(2,1)}), bf16[8,16,1920]{2,1,0:T(8,128)(2,1)S(1)}, u32[]{:S(2)}, u32[]{:S(2)}) async-start(bf16[8,16,1920]{2,1,0:T(8,128)(2,1)} %bitcast.126), calls=%async_computation | async-start | bytes 983040 | tf_op jit(solution)/shard_map/all_to_all | solution.py:198
  10.8 0.6 copy.25
  11.4 0.8 %select_bitcast_fusion = (bf16[1792,128]{1,0:T(8,128)(2,1)S(1)}, bf16[128,1792]{0,1:T(8,128)(2,1)}) fusion(pred[]{:T(512)S(6)} %ne.18, bf16[128,3584]{0,1:T(8,128)(2,1)S(1)} %bitcast.118), kind=kLoop, calls=%fused_computation.58 | loop fusion | flops 458752 | bytes 1835009 | tf_op jit(solution)/shard_map/transpose | solution.py:193
  12.2 1.5 %collective-permute-start.1 = (bf16[1792,128]{1,0:T(8,128)(2,1)S(1)}, bf16[1792,128]{1,0:T(8,128)(2,1)S(1)}, u32[]{:S(2)}, u32[]{:S(2)}) collective-permute-start(bf16[1792,128]{1,0:T(8,128)(2,1)S(1)} %get-tuple-element.10), channel_id=1, source_target_pairs={{0,16},{8,24},{16,0},{24,8},{1,17},{9,25},{17,1},{25,9},{2,18},{10... | collective-permute-start | bytes 1376264 | tf_op jit(solution)/shard_map/ppermute | solution.py:111
  13.7 10.8 %all-to-all-done = bf16[8,16,1920]{2,1,0:T(8,128)(2,1)S(1)} async-done(((bf16[8,16,1920]{2,1,0:T(8,128)(2,1)}), bf16[8,16,1920]{2,1,0:T(8,128)(2,1)S(1)}, u32[]{:S(2)}, u32[]{:S(2)}) %all-to-all-start) | async-done | bytes 491552 | tf_op jit(solution)/shard_map/all_to_all | solution.py:198
  24.6 0.2 slice_reduce_fusion
  24.8 0.2 fusion.50
  25.7 1.3 %collective-permute-done = bf16[1,128,896]{2,1,0:T(8,128)(2,1)S(1)} collective-permute-done((bf16[1,128,896]{2,1,0:T(8,128)(2,1)S(1)}, bf16[1,128,896]{2,1,0:T(8,128)(2,1)S(1)}, u32[]{:S(2)}, u32[]{:S(2)}) %collective-permute-start) | collective-permute-done | bytes 229408 | tf_op jit(solution)/shard_map/ppermute | solution.py:111
  27.0 0.4 reduce-precision_convert_fusion.1
  27.4 0.3 copy-done.5
  28.1 1.6 %collective-permute-start.2 = (bf16[128,1280]{1,0:T(8,128)(2,1)S(1)}, bf16[128,1280]{1,0:T(8,128)(2,1)S(1)}, u32[]{:S(2)}, u32[]{:S(2)}) collective-permute-start(bf16[128,1280]{1,0:T(8,128)(2,1)S(1)} %pad_maximum_fusion.1), channel_id=1, source_target_pairs={{0,16},{8,24},{16,0},{24,8},{1,17},{9,25},{17,1},{25,9},{2,18},{10... | collective-permute-start | bytes 983048 | tf_op jit(solution)/shard_map/ppermute | solution.py:111
  29.6 8.2 %collective-permute-done.2 = bf16[128,1280]{1,0:T(8,128)(2,1)S(1)} collective-permute-done((bf16[128,1280]{1,0:T(8,128)(2,1)S(1)}, bf16[128,1280]{1,0:T(8,128)(2,1)S(1)}, u32[]{:S(2)}, u32[]{:S(2)}) %collective-permute-start.2) | collective-permute-done | bytes 327712 | tf_op jit(solution)/shard_map/ppermute | solution.py:111
  38.3 0.2 copy.32
  38.5 1.4 %collective-permute-done.3 = bf16[2,128,896]{2,1,0:T(8,128)(2,1)S(1)} collective-permute-done((bf16[2,128,896]{2,1,0:T(8,128)(2,1)S(1)}, bf16[2,128,896]{2,1,0:T(8,128)(2,1)S(1)}, u32[]{:S(2)}, u32[]{:S(2)}) %collective-permute-start.3) | collective-permute-done | bytes 458784 | tf_op jit(solution)/shard_map/ppermute | solution.py:111
  40.1 0.2 copy.31
  40.3 0.6 convolution_bitcast_fusion
  40.9 0.4 copy-done.3
  41.4 0.3 multiply_convert_fusion.1
  41.7 0.6 fusion.4
  42.3 0.4 fusion.74
  42.8 0.4 add_convert_fusion
  43.2 0.2 collective-permute-start.4
  43.4 1.7 %collective-permute-done.4 = bf16[2,128,896]{2,1,0:T(8,128)(2,1)S(1)} collective-permute-done((bf16[2,128,896]{2,1,0:T(8,128)(2,1)S(1)}, bf16[2,128,896]{2,1,0:T(8,128)(2,1)S(1)}, u32[]{:S(2)}, u32[]{:S(2)}) %collective-permute-start.4) | collective-permute-done | bytes 458784 | tf_op jit(solution)/shard_map/ppermute | solution.py:111
  45.3 1.6 %collective-permute-start.5 = (bf16[1,128,896]{2,1,0:T(8,128)(2,1)S(1)}, bf16[1,128,896]{2,1,0:T(8,128)(2,1)S(1)}, u32[]{:S(2)}, u32[]{:S(2)}) collective-permute-start(bf16[1,128,896]{2,1,0:T(8,128)(2,1)S(1)} %fusion.43), channel_id=1, source_target_pairs={{0,16},{8,24},{16,0},{24,8},{1,17},{9,25},{17,1},{25,9},{2,18},{10... | collective-permute-start | bytes 688136 | tf_op jit(solution)/shard_map/ppermute | solution.py:111
  46.9 6.1 %collective-permute-done.5 = bf16[1,128,896]{2,1,0:T(8,128)(2,1)S(1)} collective-permute-done((bf16[1,128,896]{2,1,0:T(8,128)(2,1)S(1)}, bf16[1,128,896]{2,1,0:T(8,128)(2,1)S(1)}, u32[]{:S(2)}, u32[]{:S(2)}) %collective-permute-start.5) | collective-permute-done | bytes 229408 | tf_op jit(solution)/shard_map/ppermute | solution.py:111
  53.0 0.7 %fusion.24 = bf16[1,128,896]{2,1,0:T(8,128)(2,1)} fusion(bf16[1,128,896]{2,1,0:T(8,128)(2,1)S(1)} %collective-permute-done.5, f32[1,2,128,896]{3,2,1,0:T(8,128)S(1)} %fusion.7, pred[]{:T(512)S(6)} %ne.18), kind=kLoop, calls=%fused_computation.40 | loop fusion | flops 458752 | bytes 1376257 | tf_op jit(solution)/shard_map/convert_element_type | solution.py:268
  53.8 3.6 %all-to-all-start.1 = ((bf16[8,16,896]{2,1,0:T(8,128)(2,1)}), bf16[8,16,896]{2,1,0:T(8,128)(2,1)S(1)}, u32[]{:S(2)}, u32[]{:S(2)}) async-start(bf16[8,16,896]{2,1,0:T(8,128)(2,1)} %bitcast.41), calls=%async_computation.1 | async-start | bytes 458752 | tf_op jit(solution)/shard_map/all_to_all | solution.py:269
  57.4 1.4 %convolution_convert_fusion = bf16[4,896,128]{2,1,0:T(8,128)(2,1)} fusion(pred[4]{0:T(512)(128)(4,1)S(1)} %get-tuple-element.23, pred[4]{0:T(512)(128)(4,1)S(1)} %get-tuple-element.24, pred[4]{0:T(512)(128)(4,1)S(1)} %iota_compare_fusion.3, bf16[128,896]{0,1:T(8,128)(2,1)S(1)} %copy.33, bf16[128,896]{0,1:T(8,128)(2,1)S(1)} %copy.32, ...), kind=kOutput, calls=%fused_computation.1 | convolution fusion | flops 119275520 | bytes 1867788 | tf_op jit(solution)/shard_map/dot_general | solution.py:261
  58.8 1.4 %convolution_convert_fusion.1 = bf16[4,896,128]{2,1,0:T(8,128)(2,1)} fusion(bf16[128,128,1]{1,0,2:T(8,128)(2,1)S(1)} %fusion.4, pred[4]{0:T(512)(128)(4,1)S(1)} %get-tuple-element.23, pred[4]{0:T(512)(128)(4,1)S(1)} %get-tuple-element.24, pred[4]{0:T(512)(128)(4,1)S(1)} %iota_compare_fusion.3, bf16[128,896]{0,1:T(8,128)(2,1)S(1)} %copy.33, ...), kind=kOutput, calls=%fused_computation.2 | convolution fusion | flops 119275520 | bytes 1867788 | tf_op jit(solution)/shard_map/dot_general | solution.py:258
  60.2 5.3 %all-to-all-done.1 = bf16[8,16,896]{2,1,0:T(8,128)(2,1)S(1)} async-done(((bf16[8,16,896]{2,1,0:T(8,128)(2,1)}), bf16[8,16,896]{2,1,0:T(8,128)(2,1)S(1)}, u32[]{:S(2)}, u32[]{:S(2)}) %all-to-all-start.1) | async-done | bytes 229408 | tf_op jit(solution)/shard_map/all_to_all | solution.py:269
  65.4 1.1 %convolution_convert_fusion.2 = bf16[256,896]{1,0:T(8,128)(2,1)} fusion(bf16[128,256]{1,0:T(8,128)(2,1)S(1)} %copy-done.4, bf16[128,896]{1,0:T(8,128)(2,1)S(1)} %bitcast.125), kind=kOutput, calls=%fused_computation.3 | convolution fusion | flops 58949632 | bytes 753664 | tf_op jit(solution)/shard_map/dot_general | solution.py:270
  (37 shorter events, 2.0 us)
Async XLA Ops:
  0.6 39.6 %copy-start = (bf16[1,3584,128]{2,1,0:T(8,128)(2,1)S(1)}, bf16[1,3584,128]{2,1,0:T(8,128)(2,1)}, u32[]{:S(2)}) copy-start(bf16[1,3584,128]{2,1,0:T(8,128)(2,1)} %param.13) | copy-start | bytes 2752516
  0.6 10.1 %copy-start.2 = (bf16[1,128,3584]{2,1,0:T(8,128)(2,1)S(1)}, bf16[1,128,3584]{2,1,0:T(8,128)(2,1)}, u32[]{:S(2)}) copy-start(bf16[1,128,3584]{2,1,0:T(8,128)(2,1)} %param.15) | copy-start | bytes 2752516
  3.5 21.1 %all-to-all-start = ((bf16[8,16,1920]{2,1,0:T(8,128)(2,1)}), bf16[8,16,1920]{2,1,0:T(8,128)(2,1)S(1)}, u32[]{:S(2)}, u32[]{:S(2)}) async-start(bf16[8,16,1920]{2,1,0:T(8,128)(2,1)} %bitcast.126), calls=%async_computation | async-start | bytes 983040 | tf_op jit(solution)/shard_map/all_to_all | solution.py:198
  12.2 13.4 %collective-permute-start.1 = (bf16[1792,128]{1,0:T(8,128)(2,1)S(1)}, bf16[1792,128]{1,0:T(8,128)(2,1)S(1)}, u32[]{:S(2)}, u32[]{:S(2)}) collective-permute-start(bf16[1792,128]{1,0:T(8,128)(2,1)S(1)} %get-tuple-element.10), channel_id=1, source_target_pairs={{0,16},{8,24},{16,0},{24,8},{1,17},{9,25},{17,1},{25,9},{2,18},{10... | collective-permute-start | bytes 1376264 | tf_op jit(solution)/shard_map/ppermute | solution.py:111
  25.4 1.6 %collective-permute-start = (bf16[1,128,896]{2,1,0:T(8,128)(2,1)S(1)}, bf16[1,128,896]{2,1,0:T(8,128)(2,1)S(1)}, u32[]{:S(2)}, u32[]{:S(2)}) collective-permute-start(bf16[1,128,896]{2,1,0:T(8,128)(2,1)S(1)} %fusion.85), channel_id=1, source_target_pairs={{0,8},{8,0},{16,24},{24,16},{1,9},{9,1},{17,25},{25,17},{2,10},{10... | collective-permute-start | bytes 688136 | tf_op jit(solution)/shard_map/ppermute | solution.py:111
  27.0 0.7 %copy-start.5 = (bf16[1,128,896]{2,1,0:T(8,128)(2,1)}, bf16[1,128,896]{2,1,0:T(8,128)(2,1)S(1)}, u32[]{:S(2)}) copy-start(bf16[1,128,896]{2,1,0:T(8,128)(2,1)S(1)} %collective-permute-done) | copy-start | bytes 688132
  28.1 9.8 %collective-permute-start.2 = (bf16[128,1280]{1,0:T(8,128)(2,1)S(1)}, bf16[128,1280]{1,0:T(8,128)(2,1)S(1)}, u32[]{:S(2)}, u32[]{:S(2)}) collective-permute-start(bf16[128,1280]{1,0:T(8,128)(2,1)S(1)} %pad_maximum_fusion.1), channel_id=1, source_target_pairs={{0,16},{8,24},{16,0},{24,8},{1,17},{9,25},{17,1},{25,9},{2,18},{10... | collective-permute-start | bytes 983048 | tf_op jit(solution)/shard_map/ppermute | solution.py:111
  38.0 1.9 %collective-permute-start.3 = (bf16[2,128,896]{2,1,0:T(8,128)(2,1)S(1)}, bf16[2,128,896]{2,1,0:T(8,128)(2,1)S(1)}, u32[]{:S(2)}, u32[]{:S(2)}) collective-permute-start(bf16[2,128,896]{2,1,0:T(8,128)(2,1)S(1)} %pad_maximum_fusion), channel_id=1, source_target_pairs={{0,8},{8,0},{16,24},{24,16},{1,9},{9,1},{17,25},{25,17},{2,10},{10... | collective-permute-start | bytes 1376264 | tf_op jit(solution)/shard_map/ppermute | solution.py:111
  40.3 1.0 %copy-start.3 = (bf16[128,1792]{0,1:T(8,128)(2,1)S(1)}, bf16[128,1792]{0,1:T(8,128)(2,1)}, u32[]{:S(2)}) copy-start(bf16[128,1792]{0,1:T(8,128)(2,1)} %get-tuple-element.11) | copy-start | bytes 1376260
  40.3 1.1 %copy-start.6 = (bf16[1,128,896]{2,1,0:T(8,128)(2,1)S(1)}, bf16[1,128,896]{2,1,0:T(8,128)(2,1)}, u32[]{:S(2)}) copy-start(bf16[1,128,896]{2,1,0:T(8,128)(2,1)} %copy-done.5) | copy-start | bytes 688132
  40.3 1.4 %copy-start.1 = (bf16[1,3584,128]{2,1,0:T(8,128)(2,1)S(1)}, bf16[1,3584,128]{2,1,0:T(8,128)(2,1)}, u32[]{:S(2)}) copy-start(bf16[1,3584,128]{2,1,0:T(8,128)(2,1)} %param.14) | copy-start | bytes 2752516
  43.2 1.9 %collective-permute-start.4 = (bf16[2,128,896]{2,1,0:T(8,128)(2,1)S(1)}, bf16[2,128,896]{2,1,0:T(8,128)(2,1)S(1)}, u32[]{:S(2)}, u32[]{:S(2)}) collective-permute-start(bf16[2,128,896]{2,1,0:T(8,128)(2,1)S(1)} %fusion.22), channel_id=1, source_target_pairs={{0,8},{8,0},{16,24},{24,16},{1,9},{9,1},{17,25},{25,17},{2,10},{10... | collective-permute-start | bytes 1376264 | tf_op jit(solution)/shard_map/ppermute | solution.py:111
  45.3 7.7 %collective-permute-start.5 = (bf16[1,128,896]{2,1,0:T(8,128)(2,1)S(1)}, bf16[1,128,896]{2,1,0:T(8,128)(2,1)S(1)}, u32[]{:S(2)}, u32[]{:S(2)}) collective-permute-start(bf16[1,128,896]{2,1,0:T(8,128)(2,1)S(1)} %fusion.43), channel_id=1, source_target_pairs={{0,16},{8,24},{16,0},{24,8},{1,17},{9,25},{17,1},{25,9},{2,18},{10... | collective-permute-start | bytes 688136 | tf_op jit(solution)/shard_map/ppermute | solution.py:111
  53.8 11.6 %all-to-all-start.1 = ((bf16[8,16,896]{2,1,0:T(8,128)(2,1)}), bf16[8,16,896]{2,1,0:T(8,128)(2,1)S(1)}, u32[]{:S(2)}, u32[]{:S(2)}) async-start(bf16[8,16,896]{2,1,0:T(8,128)(2,1)} %bitcast.41), calls=%async_computation.1 | async-start | bytes 458752 | tf_op jit(solution)/shard_map/all_to_all | solution.py:269
  58.8 6.6 %copy-start.4 = (bf16[128,256]{1,0:T(8,128)(2,1)S(1)}, bf16[128,256]{1,0:T(8,128)(2,1)}, u32[]{:S(2)}) copy-start(bf16[128,256]{1,0:T(8,128)(2,1)} %get-tuple-element.6) | copy-start | bytes 196612

commit v13 on v12

--- a/solution.py
+++ b/solution.py
@@ -230,16 +230,13 @@
             half_grads, borrowed.reshape(top, width, ff_down), half_dims, preferred_element_type=jnp.float32
         )
         lent_hi = bf16_part(lent)
-        lent_rest = lent - lent_hi
-        lent_mid = bf16_part(lent_rest)
-        lent_lo = lent_rest - lent_mid
+        lent_lo = lent - lent_hi
         outgoing = jnp.concatenate(
-            [part_tokens, lent_hi.astype(jnp.bfloat16), lent_mid.astype(jnp.bfloat16), lent_lo.astype(jnp.bfloat16)],
-            axis=1,
+            [part_tokens, lent_hi.astype(jnp.bfloat16), lent_lo.astype(jnp.bfloat16)], axis=1
         )
         incoming = partner(outgoing, top, n_dp)
         share = incoming[:, width:].astype(jnp.float32)
-        returned_share = (share[:, :ff_down] + share[:, ff_down : 2 * ff_down]) + share[:, 2 * ff_down :]
+        returned_share = share[:, :ff_down] + share[:, ff_down:]
         hidden_grad = lax.dot_general(
             half_grads, keep.reshape(top, width, ff_down), half_dims, preferred_element_type=jnp.float32
         )

time: 66.9 us -> 66 us (0.987)
  waiting for transfers between devices: 34.8 us -> 34.1 us
    ppermute x6, waiting for transfers between devices: 18.8 us -> 18.1 us  [partner(): return lax.ppermute(x, 'dp', [(i, i ^ bit) for i in range(n)])]
where the time goes in v13:
time: 66 us; the launch traced here: 65.7 us
  waiting for transfers between devices  34.1 us (52%)
  starting transfers between devices  15.9 us (24%)
  matrix products  6.83 us (10%)
  Pallas kernels  2.81 us (4%)
  other arithmetic  2.63 us (4%)
  local copies, waits for them, and re-layouts  2.45 us (4%)
  between operations  0.91 us (1%)
    ppermute x6, waiting for transfers between devices, partner(): return lax.ppermute(x, 'dp', [(i, i ^ bit) for i in range(n)])  18.1 us
    all_to_all x1, waiting for transfers between devices, on_device(): lax.all_to_all(payload, 'expert', split_axis=0, concat_axis=0, tiled=True)  10.8 us
    all_to_all x1, starting transfers between devices, on_device(): lax.all_to_all(payload, 'expert', split_axis=0, concat_axis=0, tiled=True)  7.31 us
    all_to_all x1, waiting for transfers between devices, on_device(): lax.all_to_all(summed, 'expert', split_axis=0, concat_axis=0, tiled=True)  5.27 us
    ppermute x6, starting transfers between devices, partner(): return lax.ppermute(x, 'dp', [(i, i ^ bit) for i in range(n)])  4.98 us
    all_to_all x1, starting transfers between devices, on_device(): lax.all_to_all(summed, 'expert', split_axis=0, concat_axis=0, tiled=True)  3.64 us
    pallas_call x1, Pallas kernels, glue(): pl.pallas_call(functools.partial(glue_kernel, n_dest, width, side, split)...  2.81 us
    unnamed x15, local copies, waits for them, and re-layouts  1.42 us
  transfers between devices with their start and end apart: 8, of which 7 were waited for; matrix products, arithmetic and copies ran while one was open for 8% of the time, Pallas kernels for 0%

profile of v13, /device:TPU:0, one launch (start us, length us, event | category | flops | bytes accessed | tf_op | source)
XLA Modules:
  0.0 65.7 jit_solution(15853641933589846076)
XLA Ops:
  0.7 2.8 %shard_map.103 = (bf16[128,1920]{1,0:T(8,128)(2,1)}, bf16[128,256]{1,0:T(8,128)(2,1)}) custom-call(s32[8,256]{1,0:T(8,128)} %bitcast.128, f32[8,256]{1,0:T(8,128)} %bitcast.129, s32[1,256]{1,0:T(1,128)} %bitcast.130, bf16[256,896]{1,0:T(8,128)(2,1)} %tok_ref.1, bf16[256,896]{1,0:T(8,128)(2,1)} %grd_ref.1), custom_call_target="tpu_custom_call" | custom-call | tf_op jit(solution)/shard_map/pallas_call | solution.py:90
  3.5 7.3 %all-to-all-start = ((bf16[8,16,1920]{2,1,0:T(8,128)(2,1)}), bf16[8,16,1920]{2,1,0:T(8,128)(2,1)S(1)}, u32[]{:S(2)}, u32[]{:S(2)}) async-start(bf16[8,16,1920]{2,1,0:T(8,128)(2,1)} %bitcast.126), calls=%async_computation | async-start | bytes 983040 | tf_op jit(solution)/shard_map/all_to_all | solution.py:198
  10.8 0.6 copy.24
  11.4 0.8 %select_bitcast_fusion = (bf16[1792,128]{1,0:T(8,128)(2,1)S(1)}, bf16[128,1792]{0,1:T(8,128)(2,1)}) fusion(pred[]{:T(512)S(6)} %ne.18, bf16[128,3584]{0,1:T(8,128)(2,1)S(1)} %bitcast.118), kind=kLoop, calls=%fused_computation.58 | loop fusion | flops 458752 | bytes 1835009 | tf_op jit(solution)/shard_map/transpose | solution.py:193
  12.2 1.5 %collective-permute-start.1 = (bf16[1792,128]{1,0:T(8,128)(2,1)S(1)}, bf16[1792,128]{1,0:T(8,128)(2,1)S(1)}, u32[]{:S(2)}, u32[]{:S(2)}) collective-permute-start(bf16[1792,128]{1,0:T(8,128)(2,1)S(1)} %get-tuple-element.10), channel_id=1, source_target_pairs={{0,16},{8,24},{16,0},{24,8},{1,17},{9,25},{17,1},{25,9},{2,18},{10... | collective-permute-start | bytes 1376264 | tf_op jit(solution)/shard_map/ppermute | solution.py:111
  13.7 10.8 %all-to-all-done = bf16[8,16,1920]{2,1,0:T(8,128)(2,1)S(1)} async-done(((bf16[8,16,1920]{2,1,0:T(8,128)(2,1)}), bf16[8,16,1920]{2,1,0:T(8,128)(2,1)S(1)}, u32[]{:S(2)}, u32[]{:S(2)}) %all-to-all-start) | async-done | bytes 491552 | tf_op jit(solution)/shard_map/all_to_all | solution.py:198
  24.6 0.2 slice_reduce_fusion
  24.8 0.2 fusion.50
  25.7 1.3 %collective-permute-done = bf16[1,128,896]{2,1,0:T(8,128)(2,1)S(1)} collective-permute-done((bf16[1,128,896]{2,1,0:T(8,128)(2,1)S(1)}, bf16[1,128,896]{2,1,0:T(8,128)(2,1)S(1)}, u32[]{:S(2)}, u32[]{:S(2)}) %collective-permute-start) | collective-permute-done | bytes 229408 | tf_op jit(solution)/shard_map/ppermute | solution.py:111
  27.0 0.4 reduce-precision_convert_fusion
  27.3 0.3 copy-done.5
  27.9 1.6 %collective-permute-start.2 = (bf16[128,1152]{1,0:T(8,128)(2,1)S(1)}, bf16[128,1152]{1,0:T(8,128)(2,1)S(1)}, u32[]{:S(2)}, u32[]{:S(2)}) collective-permute-start(bf16[128,1152]{1,0:T(8,128)(2,1)S(1)} %pad_maximum_fusion.1), channel_id=1, source_target_pairs={{0,16},{8,24},{16,0},{24,8},{1,17},{9,25},{17,1},{25,9},{2,18},{10... | collective-permute-start | bytes 884744 | tf_op jit(solution)/shard_map/ppermute | solution.py:111
  29.5 7.5 %collective-permute-done.2 = bf16[128,1152]{1,0:T(8,128)(2,1)S(1)} collective-permute-done((bf16[128,1152]{1,0:T(8,128)(2,1)S(1)}, bf16[128,1152]{1,0:T(8,128)(2,1)S(1)}, u32[]{:S(2)}, u32[]{:S(2)}) %collective-permute-start.2) | collective-permute-done | bytes 294944 | tf_op jit(solution)/shard_map/ppermute | solution.py:111
  37.5 0.2 copy.30
  37.7 1.4 %collective-permute-done.3 = bf16[2,128,896]{2,1,0:T(8,128)(2,1)S(1)} collective-permute-done((bf16[2,128,896]{2,1,0:T(8,128)(2,1)S(1)}, bf16[2,128,896]{2,1,0:T(8,128)(2,1)S(1)}, u32[]{:S(2)}, u32[]{:S(2)}) %collective-permute-start.3) | collective-permute-done | bytes 458784 | tf_op jit(solution)/shard_map/ppermute | solution.py:111
  39.3 0.2 copy.29
  39.5 0.6 convolution_bitcast_fusion
  40.1 0.4 copy-done.3
  40.5 0.3 multiply_convert_fusion.1
  40.9 0.6 fusion.4
  41.5 0.4 fusion.74
  41.9 0.4 add_convert_fusion
  42.4 0.2 collective-permute-start.4
  42.6 1.7 %collective-permute-done.4 = bf16[2,128,896]{2,1,0:T(8,128)(2,1)S(1)} collective-permute-done((bf16[2,128,896]{2,1,0:T(8,128)(2,1)S(1)}, bf16[2,128,896]{2,1,0:T(8,128)(2,1)S(1)}, u32[]{:S(2)}, u32[]{:S(2)}) %collective-permute-start.4) | collective-permute-done | bytes 458784 | tf_op jit(solution)/shard_map/ppermute | solution.py:111
  44.5 1.6 %collective-permute-start.5 = (bf16[1,128,896]{2,1,0:T(8,128)(2,1)S(1)}, bf16[1,128,896]{2,1,0:T(8,128)(2,1)S(1)}, u32[]{:S(2)}, u32[]{:S(2)}) collective-permute-start(bf16[1,128,896]{2,1,0:T(8,128)(2,1)S(1)} %fusion.43), channel_id=1, source_target_pairs={{0,16},{8,24},{16,0},{24,8},{1,17},{9,25},{17,1},{25,9},{2,18},{10... | collective-permute-start | bytes 688136 | tf_op jit(solution)/shard_map/ppermute | solution.py:111
  46.1 6.1 %collective-permute-done.5 = bf16[1,128,896]{2,1,0:T(8,128)(2,1)S(1)} collective-permute-done((bf16[1,128,896]{2,1,0:T(8,128)(2,1)S(1)}, bf16[1,128,896]{2,1,0:T(8,128)(2,1)S(1)}, u32[]{:S(2)}, u32[]{:S(2)}) %collective-permute-start.5) | collective-permute-done | bytes 229408 | tf_op jit(solution)/shard_map/ppermute | solution.py:111
  52.2 0.7 %fusion.24 = bf16[1,128,896]{2,1,0:T(8,128)(2,1)} fusion(bf16[1,128,896]{2,1,0:T(8,128)(2,1)S(1)} %collective-permute-done.5, f32[1,2,128,896]{3,2,1,0:T(8,128)S(1)} %fusion.7, pred[]{:T(512)S(6)} %ne.18), kind=kLoop, calls=%fused_computation.40 | loop fusion | flops 458752 | bytes 1376257 | tf_op jit(solution)/shard_map/convert_element_type | solution.py:265
  53.0 3.6 %all-to-all-start.1 = ((bf16[8,16,896]{2,1,0:T(8,128)(2,1)}), bf16[8,16,896]{2,1,0:T(8,128)(2,1)S(1)}, u32[]{:S(2)}, u32[]{:S(2)}) async-start(bf16[8,16,896]{2,1,0:T(8,128)(2,1)} %bitcast.41), calls=%async_computation.1 | async-start | bytes 458752 | tf_op jit(solution)/shard_map/all_to_all | solution.py:266
  56.6 1.4 %convolution_convert_fusion = bf16[4,896,128]{2,1,0:T(8,128)(2,1)} fusion(pred[4]{0:T(512)(128)(4,1)S(1)} %get-tuple-element.22, pred[4]{0:T(512)(128)(4,1)S(1)} %get-tuple-element.23, pred[4]{0:T(512)(128)(4,1)S(1)} %iota_compare_fusion.3, bf16[128,896]{0,1:T(8,128)(2,1)S(1)} %copy.31, bf16[128,896]{0,1:T(8,128)(2,1)S(1)} %copy.30, ...), kind=kOutput, calls=%fused_computation.1 | convolution fusion | flops 119275520 | bytes 1867788 | tf_op jit(solution)/shard_map/dot_general | solution.py:258
  58.0 1.4 %convolution_convert_fusion.1 = bf16[4,896,128]{2,1,0:T(8,128)(2,1)} fusion(bf16[128,128,1]{1,0,2:T(8,128)(2,1)S(1)} %fusion.4, pred[4]{0:T(512)(128)(4,1)S(1)} %get-tuple-element.22, pred[4]{0:T(512)(128)(4,1)S(1)} %get-tuple-element.23, pred[4]{0:T(512)(128)(4,1)S(1)} %iota_compare_fusion.3, bf16[128,896]{0,1:T(8,128)(2,1)S(1)} %copy.31, ...), kind=kOutput, calls=%fused_computation.2 | convolution fusion | flops 119275520 | bytes 1867788 | tf_op jit(solution)/shard_map/dot_general | solution.py:255
  59.3 5.3 %all-to-all-done.1 = bf16[8,16,896]{2,1,0:T(8,128)(2,1)S(1)} async-done(((bf16[8,16,896]{2,1,0:T(8,128)(2,1)}), bf16[8,16,896]{2,1,0:T(8,128)(2,1)S(1)}, u32[]{:S(2)}, u32[]{:S(2)}) %all-to-all-start.1) | async-done | bytes 229408 | tf_op jit(solution)/shard_map/all_to_all | solution.py:266
  64.6 1.1 %convolution_convert_fusion.2 = bf16[256,896]{1,0:T(8,128)(2,1)} fusion(bf16[128,256]{1,0:T(8,128)(2,1)S(1)} %copy-done.4, bf16[128,896]{1,0:T(8,128)(2,1)S(1)} %bitcast.125), kind=kOutput, calls=%fused_computation.3 | convolution fusion | flops 58949632 | bytes 753664 | tf_op jit(solution)/shard_map/dot_general | solution.py:267
  (36 shorter events, 1.9 us)
Async XLA Ops:
  0.6 38.8 %copy-start = (bf16[1,3584,128]{2,1,0:T(8,128)(2,1)S(1)}, bf16[1,3584,128]{2,1,0:T(8,128)(2,1)}, u32[]{:S(2)}) copy-start(bf16[1,3584,128]{2,1,0:T(8,128)(2,1)} %param.13) | copy-start | bytes 2752516
  0.6 10.1 %copy-start.2 = (bf16[1,128,3584]{2,1,0:T(8,128)(2,1)S(1)}, bf16[1,128,3584]{2,1,0:T(8,128)(2,1)}, u32[]{:S(2)}) copy-start(bf16[1,128,3584]{2,1,0:T(8,128)(2,1)} %param.15) | copy-start | bytes 2752516
  3.5 21.1 %all-to-all-start = ((bf16[8,16,1920]{2,1,0:T(8,128)(2,1)}), bf16[8,16,1920]{2,1,0:T(8,128)(2,1)S(1)}, u32[]{:S(2)}, u32[]{:S(2)}) async-start(bf16[8,16,1920]{2,1,0:T(8,128)(2,1)} %bitcast.126), calls=%async_computation | async-start | bytes 983040 | tf_op jit(solution)/shard_map/all_to_all | solution.py:198
  12.2 13.4 %collective-permute-start.1 = (bf16[1792,128]{1,0:T(8,128)(2,1)S(1)}, bf16[1792,128]{1,0:T(8,128)(2,1)S(1)}, u32[]{:S(2)}, u32[]{:S(2)}) collective-permute-start(bf16[1792,128]{1,0:T(8,128)(2,1)S(1)} %get-tuple-element.10), channel_id=1, source_target_pairs={{0,16},{8,24},{16,0},{24,8},{1,17},{9,25},{17,1},{25,9},{2,18},{10... | collective-permute-start | bytes 1376264 | tf_op jit(solution)/shard_map/ppermute | solution.py:111
  25.4 1.6 %collective-permute-start = (bf16[1,128,896]{2,1,0:T(8,128)(2,1)S(1)}, bf16[1,128,896]{2,1,0:T(8,128)(2,1)S(1)}, u32[]{:S(2)}, u32[]{:S(2)}) collective-permute-start(bf16[1,128,896]{2,1,0:T(8,128)(2,1)S(1)} %fusion.85), channel_id=1, source_target_pairs={{0,8},{8,0},{16,24},{24,16},{1,9},{9,1},{17,25},{25,17},{2,10},{10... | collective-permute-start | bytes 688136 | tf_op jit(solution)/shard_map/ppermute | solution.py:111
  27.0 0.7 %copy-start.5 = (bf16[1,128,896]{2,1,0:T(8,128)(2,1)}, bf16[1,128,896]{2,1,0:T(8,128)(2,1)S(1)}, u32[]{:S(2)}) copy-start(bf16[1,128,896]{2,1,0:T(8,128)(2,1)S(1)} %collective-permute-done) | copy-start | bytes 688132
  27.9 9.1 %collective-permute-start.2 = (bf16[128,1152]{1,0:T(8,128)(2,1)S(1)}, bf16[128,1152]{1,0:T(8,128)(2,1)S(1)}, u32[]{:S(2)}, u32[]{:S(2)}) collective-permute-start(bf16[128,1152]{1,0:T(8,128)(2,1)S(1)} %pad_maximum_fusion.1), channel_id=1, source_target_pairs={{0,16},{8,24},{16,0},{24,8},{1,17},{9,25},{17,1},{25,9},{2,18},{10... | collective-permute-start | bytes 884744 | tf_op jit(solution)/shard_map/ppermute | solution.py:111
  37.2 1.9 %collective-permute-start.3 = (bf16[2,128,896]{2,1,0:T(8,128)(2,1)S(1)}, bf16[2,128,896]{2,1,0:T(8,128)(2,1)S(1)}, u32[]{:S(2)}, u32[]{:S(2)}) collective-permute-start(bf16[2,128,896]{2,1,0:T(8,128)(2,1)S(1)} %pad_maximum_fusion), channel_id=1, source_target_pairs={{0,8},{8,0},{16,24},{24,16},{1,9},{9,1},{17,25},{25,17},{2,10},{10... | collective-permute-start | bytes 1376264 | tf_op jit(solution)/shard_map/ppermute | solution.py:111
  39.5 1.0 %copy-start.3 = (bf16[128,1792]{0,1:T(8,128)(2,1)S(1)}, bf16[128,1792]{0,1:T(8,128)(2,1)}, u32[]{:S(2)}) copy-start(bf16[128,1792]{0,1:T(8,128)(2,1)} %get-tuple-element.11) | copy-start | bytes 1376260
  39.5 1.1 %copy-start.6 = (bf16[1,128,896]{2,1,0:T(8,128)(2,1)S(1)}, bf16[1,128,896]{2,1,0:T(8,128)(2,1)}, u32[]{:S(2)}) copy-start(bf16[1,128,896]{2,1,0:T(8,128)(2,1)} %copy-done.5) | copy-start | bytes 688132
  39.5 1.4 %copy-start.1 = (bf16[1,3584,128]{2,1,0:T(8,128)(2,1)S(1)}, bf16[1,3584,128]{2,1,0:T(8,128)(2,1)}, u32[]{:S(2)}) copy-start(bf16[1,3584,128]{2,1,0:T(8,128)(2,1)} %param.14) | copy-start | bytes 2752516
  42.4 1.9 %collective-permute-start.4 = (bf16[2,128,896]{2,1,0:T(8,128)(2,1)S(1)}, bf16[2,128,896]{2,1,0:T(8,128)(2,1)S(1)}, u32[]{:S(2)}, u32[]{:S(2)}) collective-permute-start(bf16[2,128,896]{2,1,0:T(8,128)(2,1)S(1)} %fusion.22), channel_id=1, source_target_pairs={{0,8},{8,0},{16,24},{24,16},{1,9},{9,1},{17,25},{25,17},{2,10},{10... | collective-permute-start | bytes 1376264 | tf_op jit(solution)/shard_map/ppermute | solution.py:111
  44.5 7.7 %collective-permute-start.5 = (bf16[1,128,896]{2,1,0:T(8,128)(2,1)S(1)}, bf16[1,128,896]{2,1,0:T(8,128)(2,1)S(1)}, u32[]{:S(2)}, u32[]{:S(2)}) collective-permute-start(bf16[1,128,896]{2,1,0:T(8,128)(2,1)S(1)} %fusion.43), channel_id=1, source_target_pairs={{0,16},{8,24},{16,0},{24,8},{1,17},{9,25},{17,1},{25,9},{2,18},{10... | collective-permute-start | bytes 688136 | tf_op jit(solution)/shard_map/ppermute | solution.py:111
  53.0 11.6 %all-to-all-start.1 = ((bf16[8,16,896]{2,1,0:T(8,128)(2,1)}), bf16[8,16,896]{2,1,0:T(8,128)(2,1)S(1)}, u32[]{:S(2)}, u32[]{:S(2)}) async-start(bf16[8,16,896]{2,1,0:T(8,128)(2,1)} %bitcast.41), calls=%async_computation.1 | async-start | bytes 458752 | tf_op jit(solution)/shard_map/all_to_all | solution.py:266
  58.0 6.6 %copy-start.4 = (bf16[128,256]{1,0:T(8,128)(2,1)S(1)}, bf16[128,256]{1,0:T(8,128)(2,1)}, u32[]{:S(2)}) copy-start(bf16[128,256]{1,0:T(8,128)(2,1)} %get-tuple-element.6) | copy-start | bytes 196612

commit v14 on v13

--- a/solution.py
+++ b/solution.py
@@ -164,9 +164,11 @@
 
 
 def scatter_dp(parts, n):
+    return scatter_from(parts, 1, n)
+
+
+def scatter_from(acc, bit, n):
     me = lax.axis_index("dp")
-    acc = parts
-    bit = 1
     while bit < n:
         pairs = acc.reshape((acc.shape[0] // 2, 2) + acc.shape[1:])
         mine = (me & bit) != 0
@@ -259,10 +261,29 @@
         slot_tokens, up_delta, slot_dims, preferred_element_type=jnp.float32
     ).astype(jnp.bfloat16)
     back_dims = (((2,), (1,)), ((), ()))
-    from_gate = lax.dot_general(w_gate, gate_delta, back_dims, preferred_element_type=jnp.float32)
-    from_up = lax.dot_general(w_up, up_delta, back_dims, preferred_element_type=jnp.float32)
-    part = (from_gate + from_up).astype(jnp.bfloat16)
-    summed = scatter_dp(jnp.swapaxes(part, 1, 2), n_dp).astype(jnp.bfloat16)
+    if n_dp > 1:
+        odd = (me_dp & 1) != 0
+        gate_pairs = w_gate.reshape(n_dp // 2, 2, width, ff)
+        up_pairs = w_up.reshape(n_dp // 2, 2, width, ff)
+        gate_send = jnp.where(odd, gate_pairs[:, 0], gate_pairs[:, 1])
+        gate_keep = jnp.where(odd, gate_pairs[:, 1], gate_pairs[:, 0])
+        up_send = jnp.where(odd, up_pairs[:, 0], up_pairs[:, 1])
+        up_keep = jnp.where(odd, up_pairs[:, 1], up_pairs[:, 0])
+        send_part = (
+            lax.dot_general(gate_send, gate_delta, back_dims, preferred_element_type=jnp.float32)
+            + lax.dot_general(up_send, up_delta, back_dims, preferred_element_type=jnp.float32)
+        ).astype(jnp.bfloat16)
+        got = partner(jnp.swapaxes(send_part, 1, 2), 1, n_dp)
+        keep_part = (
+            lax.dot_general(gate_keep, gate_delta, back_dims, preferred_element_type=jnp.float32)
+            + lax.dot_general(up_keep, up_delta, back_dims, preferred_element_type=jnp.float32)
+        ).astype(jnp.bfloat16)
+        first = jnp.swapaxes(keep_part, 1, 2).astype(jnp.float32) + got.astype(jnp.float32)
+        summed = scatter_from(first, 2, n_dp).astype(jnp.bfloat16)
+    else:
+        from_gate = lax.dot_general(w_gate, gate_delta, back_dims, preferred_element_type=jnp.float32)
+        from_up = lax.dot_general(w_up, up_delta, back_dims, preferred_element_type=jnp.float32)
+        summed = ((from_gate + from_up).astype(jnp.bfloat16)[0].T).astype(jnp.bfloat16)
     returned = lax.all_to_all(summed, "expert", split_axis=0, concat_axis=0, tiled=True)
     input_grad = lax.dot_general(
         pick_t, returned, (((0,), (0,)), ((), ())), preferred_element_type=jnp.float32

time: 66 us -> 66.8 us (1.012)
    ppermute x6, waiting for transfers between devices: 18.1 us -> 17.1 us  [partner(): return lax.ppermute(x, 'dp', [(i, i ^ bit) for i in range(n)])]
    transpose x1, other arithmetic: 0.83 us -> 0.07 us  [on_device(): lend = jnp.where(upper_half, w_down[:, :half_cols], w_down[:, half_cols:]).T]
    all_to_all x1, waiting for transfers between devices: 10.8 us -> 11.5 us  [on_device(): lax.all_to_all(payload, 'expert', split_axis=0, concat_axis=0, tiled=True)]
    unnamed x15 -> x19, local copies, waits for them, and re-layouts: 1.42 us -> 1.9 us
  transfers between devices with their start and end apart: 8 -> 8, of which waited for: 7 -> 7; matrix products, arithmetic and copies ran while one was open for 8% -> 9% of each run, Pallas kernels for 0% -> 0%
where the time goes in v14:
time: 66.8 us; the launch traced here: 66.4 us
  waiting for transfers between devices  34 us (51%)
  starting transfers between devices  16.3 us (24%)
  matrix products  7.16 us (11%)
  local copies, waits for them, and re-layouts  2.92 us (4%)
  Pallas kernels  2.76 us (4%)
  other arithmetic  2.32 us (3%)
  between operations  0.9 us (1%)
    ppermute x6, waiting for transfers between devices, partner(): return lax.ppermute(x, 'dp', [(i, i ^ bit) for i in range(n)])  17.1 us
    all_to_all x1, waiting for transfers between devices, on_device(): lax.all_to_all(payload, 'expert', split_axis=0, concat_axis=0, tiled=True)  11.5 us
    all_to_all x1, starting transfers between devices, on_device(): lax.all_to_all(payload, 'expert', split_axis=0, concat_axis=0, tiled=True)  7.31 us
    ppermute x6, starting transfers between devices, partner(): return lax.ppermute(x, 'dp', [(i, i ^ bit) for i in range(n)])  5.38 us
    all_to_all x1, waiting for transfers between devices, on_device(): lax.all_to_all(summed, 'expert', split_axis=0, concat_axis=0, tiled=True)  5.37 us
    all_to_all x1, starting transfers between devices, on_device(): lax.all_to_all(summed, 'expert', split_axis=0, concat_axis=0, tiled=True)  3.63 us
    pallas_call x1, Pallas kernels, glue(): pl.pallas_call(functools.partial(glue_kernel, n_dest, width, side, split)...  2.76 us
    unnamed x19, local copies, waits for them, and re-layouts  1.9 us
  transfers between devices with their start and end apart: 8, of which 7 were waited for; matrix products, arithmetic and copies ran while one was open for 9% of the time, Pallas kernels for 0%

profile of v14, /device:TPU:0, one launch (start us, length us, event | category | flops | bytes accessed | tf_op | source)
XLA Modules:
  0.0 66.4 jit_solution(7401048857025882124)
XLA Ops:
  0.6 2.8 %shard_map.103 = (bf16[128,1920]{1,0:T(8,128)(2,1)}, bf16[128,256]{1,0:T(8,128)(2,1)}) custom-call(s32[8,256]{1,0:T(8,128)} %bitcast.159, f32[8,256]{1,0:T(8,128)} %bitcast.160, s32[1,256]{1,0:T(1,128)} %bitcast.161, bf16[256,896]{1,0:T(8,128)(2,1)} %tok_ref.1, bf16[256,896]{1,0:T(8,128)(2,1)} %grd_ref.1), custom_call_target="tpu_custom_call" | custom-call | tf_op jit(solution)/shard_map/pallas_call | solution.py:90
  3.4 7.3 %all-to-all-start = ((bf16[8,16,1920]{2,1,0:T(8,128)(2,1)}), bf16[8,16,1920]{2,1,0:T(8,128)(2,1)S(1)}, u32[]{:S(2)}, u32[]{:S(2)}) async-start(bf16[8,16,1920]{2,1,0:T(8,128)(2,1)} %bitcast.157), calls=%async_computation | async-start | bytes 983040 | tf_op jit(solution)/shard_map/all_to_all | solution.py:200
  10.7 0.6 copy.26
  11.4 1.6 %collective-permute-start.1 = (bf16[1792,128]{1,0:T(8,128)(2,1)S(1)}, bf16[1792,128]{1,0:T(8,128)(2,1)S(1)}, u32[]{:S(2)}, u32[]{:S(2)}) collective-permute-start(bf16[1792,128]{1,0:T(8,128)(2,1)S(1)} %get-tuple-element.10), channel_id=1, source_target_pairs={{0,16},{8,24},{16,0},{24,8},{1,17},{9,25},{17,1},{25,9},{2,18},{10... | collective-permute-start | bytes 1376264 | tf_op jit(solution)/shard_map/ppermute | solution.py:111
  13.0 11.5 %all-to-all-done = bf16[8,16,1920]{2,1,0:T(8,128)(2,1)S(1)} async-done(((bf16[8,16,1920]{2,1,0:T(8,128)(2,1)}), bf16[8,16,1920]{2,1,0:T(8,128)(2,1)S(1)}, u32[]{:S(2)}, u32[]{:S(2)}) %all-to-all-start) | async-done | bytes 491552 | tf_op jit(solution)/shard_map/all_to_all | solution.py:200
  24.7 0.3 slice_reduce_fusion
  25.6 1.3 %collective-permute-done = bf16[1,128,896]{2,1,0:T(8,128)(2,1)S(1)} collective-permute-done((bf16[1,128,896]{2,1,0:T(8,128)(2,1)S(1)}, bf16[1,128,896]{2,1,0:T(8,128)(2,1)S(1)}, u32[]{:S(2)}, u32[]{:S(2)}) %collective-permute-start) | collective-permute-done | bytes 229408 | tf_op jit(solution)/shard_map/ppermute | solution.py:111
  26.9 0.4 reduce-precision_convert_fusion
  27.3 0.3 copy-done.7
  27.9 1.6 %collective-permute-start.2 = (bf16[128,1152]{1,0:T(8,128)(2,1)S(1)}, bf16[128,1152]{1,0:T(8,128)(2,1)S(1)}, u32[]{:S(2)}, u32[]{:S(2)}) collective-permute-start(bf16[128,1152]{1,0:T(8,128)(2,1)S(1)} %pad_maximum_fusion.1), channel_id=1, source_target_pairs={{0,16},{8,24},{16,0},{24,8},{1,17},{9,25},{17,1},{25,9},{2,18},{10... | collective-permute-start | bytes 884744 | tf_op jit(solution)/shard_map/ppermute | solution.py:111
  29.5 7.5 %collective-permute-done.2 = bf16[128,1152]{1,0:T(8,128)(2,1)S(1)} collective-permute-done((bf16[128,1152]{1,0:T(8,128)(2,1)S(1)}, bf16[128,1152]{1,0:T(8,128)(2,1)S(1)}, u32[]{:S(2)}, u32[]{:S(2)}) %collective-permute-start.2) | collective-permute-done | bytes 294944 | tf_op jit(solution)/shard_map/ppermute | solution.py:111
  37.6 0.7 %slice_convert_fusion = f32[128,256]{1,0:T(8,128)} fusion(bf16[128,1152]{1,0:T(8,128)(2,1)S(1)} %collective-permute-done.2), kind=kLoop, calls=%fused_computation.94 | loop fusion | flops 32768 | bytes 196608 | tf_op jit(solution)/shard_map/convert_element_type | solution.py:240
  38.2 0.7 %collective-permute-done.3 = bf16[2,128,896]{2,1,0:T(8,128)(2,1)S(1)} collective-permute-done((bf16[2,128,896]{2,1,0:T(8,128)(2,1)S(1)}, bf16[2,128,896]{2,1,0:T(8,128)(2,1)S(1)}, u32[]{:S(2)}, u32[]{:S(2)}) %collective-permute-start.3) | collective-permute-done | bytes 458784 | tf_op jit(solution)/shard_map/ppermute | solution.py:111
  39.4 0.6 convolution_bitcast_fusion
  40.1 0.3 copy-done.4
  40.5 0.3 multiply_convert_fusion.1
  40.9 0.4 copy-done.2
  41.3 0.6 fusion.9
  41.9 0.3 fusion.28
  42.2 0.3 fusion.4
  42.5 0.5 collective-permute-start.4
  43.0 0.3 fusion.33
  43.3 1.2 %collective-permute-done.4 = bf16[2,128,896]{2,1,0:T(8,128)(2,1)S(1)} collective-permute-done((bf16[2,128,896]{2,1,0:T(8,128)(2,1)S(1)}, bf16[2,128,896]{2,1,0:T(8,128)(2,1)S(1)}, u32[]{:S(2)}, u32[]{:S(2)}) %collective-permute-start.4) | collective-permute-done | bytes 458784 | tf_op jit(solution)/shard_map/ppermute | solution.py:111
  44.5 0.3 add_bitcast_fusion
  44.8 1.6 %collective-permute-start.5 = (bf16[1,128,896]{2,1,0:T(8,128)(2,1)S(1)}, bf16[1,128,896]{2,1,0:T(8,128)(2,1)S(1)}, u32[]{:S(2)}, u32[]{:S(2)}) collective-permute-start(bf16[1,128,896]{2,1,0:T(8,128)(2,1)S(1)} %fusion.61), channel_id=1, source_target_pairs={{0,16},{8,24},{16,0},{24,8},{1,17},{9,25},{17,1},{25,9},{2,18},{10... | collective-permute-start | bytes 688136 | tf_op jit(solution)/shard_map/ppermute | solution.py:111
  46.4 6.4 %collective-permute-done.5 = bf16[1,128,896]{2,1,0:T(8,128)(2,1)S(1)} collective-permute-done((bf16[1,128,896]{2,1,0:T(8,128)(2,1)S(1)}, bf16[1,128,896]{2,1,0:T(8,128)(2,1)S(1)}, u32[]{:S(2)}, u32[]{:S(2)}) %collective-permute-start.5) | collective-permute-done | bytes 229408 | tf_op jit(solution)/shard_map/ppermute | solution.py:111
  52.8 0.7 %fusion.26 = bf16[1,128,896]{2,1,0:T(8,128)(2,1)} fusion(bf16[1,128,896]{2,1,0:T(8,128)(2,1)S(1)} %collective-permute-done.5, f32[1,2,128,896]{3,2,1,0:T(8,128)S(1)} %add_bitcast_fusion, pred[]{:T(512)S(6)} %ne.18), kind=kLoop, calls=%fused_computation.45 | loop fusion | flops 458752 | bytes 1376257 | tf_op jit(solution)/shard_map/convert_element_type | solution.py:282
  53.5 3.6 %all-to-all-start.1 = ((bf16[8,16,896]{2,1,0:T(8,128)(2,1)}), bf16[8,16,896]{2,1,0:T(8,128)(2,1)S(1)}, u32[]{:S(2)}, u32[]{:S(2)}) async-start(bf16[8,16,896]{2,1,0:T(8,128)(2,1)} %bitcast.41), calls=%async_computation.1 | async-start | bytes 458752 | tf_op jit(solution)/shard_map/all_to_all | solution.py:287
  57.2 1.4 %convolution_convert_fusion = bf16[4,896,128]{2,1,0:T(8,128)(2,1)} fusion(pred[4]{0:T(512)(128)(4,1)S(1)} %get-tuple-element.22, pred[4]{0:T(512)(128)(4,1)S(1)} %get-tuple-element.23, pred[4]{0:T(512)(128)(4,1)S(1)} %iota_compare_fusion.3, bf16[128,896]{0,1:T(8,128)(2,1)S(1)} %copy.33, bf16[128,896]{0,1:T(8,128)(2,1)S(1)} %copy.32, ...), kind=kOutput, calls=%fused_computation | convolution fusion | flops 119275520 | bytes 1867788 | tf_op jit(solution)/shard_map/dot_general | solution.py:260
  58.5 1.4 %convolution_convert_fusion.1 = bf16[4,896,128]{2,1,0:T(8,128)(2,1)} fusion(bf16[128,128,1]{1,0,2:T(8,128)(2,1)S(1)} %fusion.9, pred[4]{0:T(512)(128)(4,1)S(1)} %get-tuple-element.22, pred[4]{0:T(512)(128)(4,1)S(1)} %get-tuple-element.23, pred[4]{0:T(512)(128)(4,1)S(1)} %iota_compare_fusion.3, bf16[128,896]{0,1:T(8,128)(2,1)S(1)} %copy.33, ...), kind=kOutput, calls=%fused_computation.1 | convolution fusion | flops 119275520 | bytes 1867788 | tf_op jit(solution)/shard_map/dot_general | solution.py:257
  59.9 5.4 %all-to-all-done.1 = bf16[8,16,896]{2,1,0:T(8,128)(2,1)S(1)} async-done(((bf16[8,16,896]{2,1,0:T(8,128)(2,1)}), bf16[8,16,896]{2,1,0:T(8,128)(2,1)S(1)}, u32[]{:S(2)}, u32[]{:S(2)}) %all-to-all-start.1) | async-done | bytes 229408 | tf_op jit(solution)/shard_map/all_to_all | solution.py:287
  65.3 1.1 %convolution_convert_fusion.2 = bf16[256,896]{1,0:T(8,128)(2,1)} fusion(bf16[128,256]{1,0:T(8,128)(2,1)S(1)} %copy-done.6, bf16[128,896]{1,0:T(8,128)(2,1)S(1)} %bitcast.150), kind=kOutput, calls=%fused_computation.8 | convolution fusion | flops 58949632 | bytes 753664 | tf_op jit(solution)/shard_map/dot_general | solution.py:288
  (40 shorter events, 2.3 us)
Async XLA Ops:
  0.6 10.1 %copy-start = (bf16[1,128,3584]{2,1,0:T(8,128)(2,1)S(1)}, bf16[1,128,3584]{2,1,0:T(8,128)(2,1)}, u32[]{:S(2)}) copy-start(bf16[1,128,3584]{2,1,0:T(8,128)(2,1)} %param.15) | copy-start | bytes 2752516
  3.4 21.1 %all-to-all-start = ((bf16[8,16,1920]{2,1,0:T(8,128)(2,1)}), bf16[8,16,1920]{2,1,0:T(8,128)(2,1)S(1)}, u32[]{:S(2)}, u32[]{:S(2)}) async-start(bf16[8,16,1920]{2,1,0:T(8,128)(2,1)} %bitcast.157), calls=%async_computation | async-start | bytes 983040 | tf_op jit(solution)/shard_map/all_to_all | solution.py:200
  11.4 14.2 %collective-permute-start.1 = (bf16[1792,128]{1,0:T(8,128)(2,1)S(1)}, bf16[1792,128]{1,0:T(8,128)(2,1)S(1)}, u32[]{:S(2)}, u32[]{:S(2)}) collective-permute-start(bf16[1792,128]{1,0:T(8,128)(2,1)S(1)} %get-tuple-element.10), channel_id=1, source_target_pairs={{0,16},{8,24},{16,0},{24,8},{1,17},{9,25},{17,1},{25,9},{2,18},{10... | collective-permute-start | bytes 1376264 | tf_op jit(solution)/shard_map/ppermute | solution.py:111
  25.4 1.6 %collective-permute-start = (bf16[1,128,896]{2,1,0:T(8,128)(2,1)S(1)}, bf16[1,128,896]{2,1,0:T(8,128)(2,1)S(1)}, u32[]{:S(2)}, u32[]{:S(2)}) collective-permute-start(bf16[1,128,896]{2,1,0:T(8,128)(2,1)S(1)} %fusion.102), channel_id=1, source_target_pairs={{0,8},{8,0},{16,24},{24,16},{1,9},{9,1},{17,25},{25,17},{2,10},{10... | collective-permute-start | bytes 688136 | tf_op jit(solution)/shard_map/ppermute | solution.py:111
  25.6 2.2 %copy-start.3 = (bf16[128,896]{1,0:T(8,128)(2,1)}, bf16[128,896]{1,0:T(8,128)(2,1)S(1)}, u32[]{:S(2)}) copy-start(bf16[128,896]{1,0:T(8,128)(2,1)S(1)} %multiply_convert_fusion) | copy-start | bytes 688132
  26.9 0.7 %copy-start.7 = (bf16[1,128,896]{2,1,0:T(8,128)(2,1)}, bf16[1,128,896]{2,1,0:T(8,128)(2,1)S(1)}, u32[]{:S(2)}) copy-start(bf16[1,128,896]{2,1,0:T(8,128)(2,1)S(1)} %collective-permute-done) | copy-start | bytes 688132
  27.9 9.1 %collective-permute-start.2 = (bf16[128,1152]{1,0:T(8,128)(2,1)S(1)}, bf16[128,1152]{1,0:T(8,128)(2,1)S(1)}, u32[]{:S(2)}, u32[]{:S(2)}) collective-permute-start(bf16[128,1152]{1,0:T(8,128)(2,1)S(1)} %pad_maximum_fusion.1), channel_id=1, source_target_pairs={{0,16},{8,24},{16,0},{24,8},{1,17},{9,25},{17,1},{25,9},{2,18},{10... | collective-permute-start | bytes 884744 | tf_op jit(solution)/shard_map/ppermute | solution.py:111
  37.1 1.9 %collective-permute-start.3 = (bf16[2,128,896]{2,1,0:T(8,128)(2,1)S(1)}, bf16[2,128,896]{2,1,0:T(8,128)(2,1)S(1)}, u32[]{:S(2)}, u32[]{:S(2)}) collective-permute-start(bf16[2,128,896]{2,1,0:T(8,128)(2,1)S(1)} %pad_maximum_fusion), channel_id=1, source_target_pairs={{0,8},{8,0},{16,24},{24,16},{1,9},{9,1},{17,25},{25,17},{2,10},{10... | collective-permute-start | bytes 1376264 | tf_op jit(solution)/shard_map/ppermute | solution.py:111
  38.2 1.2 %copy-start.1 = (bf16[1,3584,128]{2,1,0:T(8,128)(2,1)S(1)}, bf16[1,3584,128]{2,1,0:T(8,128)(2,1)}, u32[]{:S(2)}) copy-start(bf16[1,3584,128]{2,1,0:T(8,128)(2,1)} %param.13) | copy-start | bytes 2752516
  39.4 0.9 %copy-start.4 = (bf16[128,896]{1,0:T(8,128)(2,1)S(1)}, bf16[128,896]{1,0:T(8,128)(2,1)}, u32[]{:S(2)}) copy-start(bf16[128,896]{1,0:T(8,128)(2,1)} %copy-done.3) | copy-start | bytes 688132
  39.4 1.0 %copy-start.5 = (f32[128,256]{1,0:T(8,128)S(1)}, f32[128,256]{1,0:T(8,128)}, u32[]{:S(2)}) copy-start(f32[128,256]{1,0:T(8,128)} %slice_convert_fusion) | copy-start | bytes 393220
  39.4 1.1 %copy-start.8 = (bf16[1,128,896]{2,1,0:T(8,128)(2,1)S(1)}, bf16[1,128,896]{2,1,0:T(8,128)(2,1)}, u32[]{:S(2)}) copy-start(bf16[1,128,896]{2,1,0:T(8,128)(2,1)} %copy-done.7) | copy-start | bytes 688132
  40.0 1.3 %copy-start.2 = (bf16[1,3584,128]{2,1,0:T(8,128)(2,1)S(1)}, bf16[1,3584,128]{2,1,0:T(8,128)(2,1)}, u32[]{:S(2)}) copy-start(bf16[1,3584,128]{2,1,0:T(8,128)(2,1)} %param.14) | copy-start | bytes 2752516
  42.5 2.0 %collective-permute-start.4 = (bf16[2,128,896]{2,1,0:T(8,128)(2,1)S(1)}, bf16[2,128,896]{2,1,0:T(8,128)(2,1)S(1)}, u32[]{:S(2)}, u32[]{:S(2)}) collective-permute-start(bf16[2,128,896]{2,1,0:T(8,128)(2,1)S(1)} %fusion.4), channel_id=1, source_target_pairs={{0,8},{8,0},{16,24},{24,16},{1,9},{9,1},{17,25},{25,17},{2,10},{10... | collective-permute-start | bytes 1376264 | tf_op jit(solution)/shard_map/ppermute | solution.py:111
  44.8 7.9 %collective-permute-start.5 = (bf16[1,128,896]{2,1,0:T(8,128)(2,1)S(1)}, bf16[1,128,896]{2,1,0:T(8,128)(2,1)S(1)}, u32[]{:S(2)}, u32[]{:S(2)}) collective-permute-start(bf16[1,128,896]{2,1,0:T(8,128)(2,1)S(1)} %fusion.61), channel_id=1, source_target_pairs={{0,16},{8,24},{16,0},{24,8},{1,17},{9,25},{17,1},{25,9},{2,18},{10... | collective-permute-start | bytes 688136 | tf_op jit(solution)/shard_map/ppermute | solution.py:111
  53.5 11.7 %all-to-all-start.1 = ((bf16[8,16,896]{2,1,0:T(8,128)(2,1)}), bf16[8,16,896]{2,1,0:T(8,128)(2,1)S(1)}, u32[]{:S(2)}, u32[]{:S(2)}) async-start(bf16[8,16,896]{2,1,0:T(8,128)(2,1)} %bitcast.41), calls=%async_computation.1 | async-start | bytes 458752 | tf_op jit(solution)/shard_map/all_to_all | solution.py:287
  58.5 6.8 %copy-start.6 = (bf16[128,256]{1,0:T(8,128)(2,1)S(1)}, bf16[128,256]{1,0:T(8,128)(2,1)}, u32[]{:S(2)}) copy-start(bf16[128,256]{1,0:T(8,128)(2,1)} %get-tuple-element.6) | copy-start | bytes 196612

commit v15 on v13

--- a/solution.py
+++ b/solution.py
@@ -229,14 +229,9 @@
         lent = lax.dot_general(
             half_grads, borrowed.reshape(top, width, ff_down), half_dims, preferred_element_type=jnp.float32
         )
-        lent_hi = bf16_part(lent)
-        lent_lo = lent - lent_hi
-        outgoing = jnp.concatenate(
-            [part_tokens, lent_hi.astype(jnp.bfloat16), lent_lo.astype(jnp.bfloat16)], axis=1
-        )
+        outgoing = jnp.concatenate([part_tokens, lent.astype(jnp.bfloat16)], axis=1)
         incoming = partner(outgoing, top, n_dp)
-        share = incoming[:, width:].astype(jnp.float32)
-        returned_share = share[:, :ff_down] + share[:, ff_down:]
+        returned_share = incoming[:, width:].astype(jnp.float32)
         hidden_grad = lax.dot_general(
             half_grads, keep.reshape(top, width, ff_down), half_dims, preferred_element_type=jnp.float32
         )

time: 66 us -> 65.6 us (level)
  waiting for transfers between devices: 34.1 us -> 33.4 us
    ppermute x6, waiting for transfers between devices: 18.1 us -> 17.4 us  [partner(): return lax.ppermute(x, 'dp', [(i, i ^ bit) for i in range(n)])]
  transfers between devices with their start and end apart: 8 -> 8, of which waited for: 7 -> 7; matrix products, arithmetic and copies ran while one was open for 8% -> 9% of each run, Pallas kernels for 0% -> 0%
where the time goes in v15:
time: 65.6 us; the launch traced here: 65.2 us
  waiting for transfers between devices  33.4 us (51%)
  starting transfers between devices  15.9 us (24%)
  matrix products  6.83 us (10%)
  Pallas kernels  2.81 us (4%)
  local copies, waits for them, and re-layouts  2.7 us (4%)
  other arithmetic  2.62 us (4%)
  between operations  0.89 us (1%)
    ppermute x6, waiting for transfers between devices, partner(): return lax.ppermute(x, 'dp', [(i, i ^ bit) for i in range(n)])  17.4 us
    all_to_all x1, waiting for transfers between devices, on_device(): lax.all_to_all(payload, 'expert', split_axis=0, concat_axis=0, tiled=True)  10.8 us
    all_to_all x1, starting transfers between devices, on_device(): lax.all_to_all(payload, 'expert', split_axis=0, concat_axis=0, tiled=True)  7.31 us
    all_to_all x1, waiting for transfers between devices, on_device(): lax.all_to_all(summed, 'expert', split_axis=0, concat_axis=0, tiled=True)  5.27 us
    ppermute x6, starting transfers between devices, partner(): return lax.ppermute(x, 'dp', [(i, i ^ bit) for i in range(n)])  4.98 us
    all_to_all x1, starting transfers between devices, on_device(): lax.all_to_all(summed, 'expert', split_axis=0, concat_axis=0, tiled=True)  3.64 us
    pallas_call x1, Pallas kernels, glue(): pl.pallas_call(functools.partial(glue_kernel, n_dest, width, side, split)...  2.81 us
    unnamed x15, local copies, waits for them, and re-layouts  1.79 us
  transfers between devices with their start and end apart: 8, of which 7 were waited for; matrix products, arithmetic and copies ran while one was open for 9% of the time, Pallas kernels for 0%

profile of v15, /device:TPU:0, one launch (start us, length us, event | category | flops | bytes accessed | tf_op | source)
XLA Modules:
  0.0 65.2 jit_solution(2930209606167693591)
XLA Ops:
  0.7 2.8 %shard_map.103 = (bf16[128,1920]{1,0:T(8,128)(2,1)}, bf16[128,256]{1,0:T(8,128)(2,1)}) custom-call(s32[8,256]{1,0:T(8,128)} %bitcast.130, f32[8,256]{1,0:T(8,128)} %bitcast.131, s32[1,256]{1,0:T(1,128)} %bitcast.132, bf16[256,896]{1,0:T(8,128)(2,1)} %tok_ref.1, bf16[256,896]{1,0:T(8,128)(2,1)} %grd_ref.1), custom_call_target="tpu_custom_call" | custom-call | tf_op jit(solution)/shard_map/pallas_call | solution.py:90
  3.5 7.3 %all-to-all-start = ((bf16[8,16,1920]{2,1,0:T(8,128)(2,1)}), bf16[8,16,1920]{2,1,0:T(8,128)(2,1)S(1)}, u32[]{:S(2)}, u32[]{:S(2)}) async-start(bf16[8,16,1920]{2,1,0:T(8,128)(2,1)} %bitcast.128), calls=%async_computation | async-start | bytes 983040 | tf_op jit(solution)/shard_map/all_to_all | solution.py:198
  10.8 0.6 copy.23
  11.4 0.8 %select_bitcast_fusion = (bf16[1792,128]{1,0:T(8,128)(2,1)S(1)}, bf16[128,1792]{0,1:T(8,128)(2,1)}) fusion(pred[]{:T(512)S(6)} %ne.18, bf16[128,3584]{0,1:T(8,128)(2,1)S(1)} %bitcast.120), kind=kLoop, calls=%fused_computation.59 | loop fusion | flops 458752 | bytes 1835009 | tf_op jit(solution)/shard_map/transpose | solution.py:193
  12.2 1.5 %collective-permute-start.1 = (bf16[1792,128]{1,0:T(8,128)(2,1)S(1)}, bf16[1792,128]{1,0:T(8,128)(2,1)S(1)}, u32[]{:S(2)}, u32[]{:S(2)}) collective-permute-start(bf16[1792,128]{1,0:T(8,128)(2,1)S(1)} %get-tuple-element.10), channel_id=1, source_target_pairs={{0,16},{8,24},{16,0},{24,8},{1,17},{9,25},{17,1},{25,9},{2,18},{10... | collective-permute-start | bytes 1376264 | tf_op jit(solution)/shard_map/ppermute | solution.py:111
  13.7 10.8 %all-to-all-done = bf16[8,16,1920]{2,1,0:T(8,128)(2,1)S(1)} async-done(((bf16[8,16,1920]{2,1,0:T(8,128)(2,1)}), bf16[8,16,1920]{2,1,0:T(8,128)(2,1)S(1)}, u32[]{:S(2)}, u32[]{:S(2)}) %all-to-all-start) | async-done | bytes 491552 | tf_op jit(solution)/shard_map/all_to_all | solution.py:198
  24.6 0.2 slice_reduce_fusion
  24.8 0.2 fusion.50
  25.7 1.3 %collective-permute-done = bf16[1,128,896]{2,1,0:T(8,128)(2,1)S(1)} collective-permute-done((bf16[1,128,896]{2,1,0:T(8,128)(2,1)S(1)}, bf16[1,128,896]{2,1,0:T(8,128)(2,1)S(1)}, u32[]{:S(2)}, u32[]{:S(2)}) %collective-permute-start) | collective-permute-done | bytes 229408 | tf_op jit(solution)/shard_map/ppermute | solution.py:111
  27.0 0.7 %copy-done.5 = bf16[1,128,896]{2,1,0:T(8,128)(2,1)} copy-done((bf16[1,128,896]{2,1,0:T(8,128)(2,1)}, bf16[1,128,896]{2,1,0:T(8,128)(2,1)S(1)}, u32[]{:S(2)}) %copy-start.5) | copy-done | bytes 229400
  27.7 0.4 fusion.3
  28.2 1.6 %collective-permute-start.2 = (bf16[128,1024]{1,0:T(8,128)(2,1)S(1)}, bf16[128,1024]{1,0:T(8,128)(2,1)S(1)}, u32[]{:S(2)}, u32[]{:S(2)}) collective-permute-start(bf16[128,1024]{1,0:T(8,128)(2,1)S(1)} %pad_maximum_fusion.1), channel_id=1, source_target_pairs={{0,16},{8,24},{16,0},{24,8},{1,17},{9,25},{17,1},{25,9},{2,18},{10... | collective-permute-start | bytes 786440 | tf_op jit(solution)/shard_map/ppermute | solution.py:111
  29.8 6.8 %collective-permute-done.2 = bf16[128,1024]{1,0:T(8,128)(2,1)S(1)} collective-permute-done((bf16[128,1024]{1,0:T(8,128)(2,1)S(1)}, bf16[128,1024]{1,0:T(8,128)(2,1)S(1)}, u32[]{:S(2)}, u32[]{:S(2)}) %collective-permute-start.2) | collective-permute-done | bytes 262176 | tf_op jit(solution)/shard_map/ppermute | solution.py:111
  37.0 0.2 copy.28
  37.2 1.4 %collective-permute-done.3 = bf16[2,128,896]{2,1,0:T(8,128)(2,1)S(1)} collective-permute-done((bf16[2,128,896]{2,1,0:T(8,128)(2,1)S(1)}, bf16[2,128,896]{2,1,0:T(8,128)(2,1)S(1)}, u32[]{:S(2)}, u32[]{:S(2)}) %collective-permute-start.3) | collective-permute-done | bytes 458784 | tf_op jit(solution)/shard_map/ppermute | solution.py:111
  38.8 0.2 copy.27
  39.0 0.6 convolution_bitcast_fusion
  39.6 0.4 copy-done.3
  40.1 0.3 multiply_convert_fusion.1
  40.4 0.6 fusion.5
  41.1 0.4 fusion.74
  41.5 0.4 add_convert_fusion
  41.9 0.2 collective-permute-start.4
  42.1 1.7 %collective-permute-done.4 = bf16[2,128,896]{2,1,0:T(8,128)(2,1)S(1)} collective-permute-done((bf16[2,128,896]{2,1,0:T(8,128)(2,1)S(1)}, bf16[2,128,896]{2,1,0:T(8,128)(2,1)S(1)}, u32[]{:S(2)}, u32[]{:S(2)}) %collective-permute-start.4) | collective-permute-done | bytes 458784 | tf_op jit(solution)/shard_map/ppermute | solution.py:111
  44.0 1.6 %collective-permute-start.5 = (bf16[1,128,896]{2,1,0:T(8,128)(2,1)S(1)}, bf16[1,128,896]{2,1,0:T(8,128)(2,1)S(1)}, u32[]{:S(2)}, u32[]{:S(2)}) collective-permute-start(bf16[1,128,896]{2,1,0:T(8,128)(2,1)S(1)} %fusion.44), channel_id=1, source_target_pairs={{0,16},{8,24},{16,0},{24,8},{1,17},{9,25},{17,1},{25,9},{2,18},{10... | collective-permute-start | bytes 688136 | tf_op jit(solution)/shard_map/ppermute | solution.py:111
  45.6 6.1 %collective-permute-done.5 = bf16[1,128,896]{2,1,0:T(8,128)(2,1)S(1)} collective-permute-done((bf16[1,128,896]{2,1,0:T(8,128)(2,1)S(1)}, bf16[1,128,896]{2,1,0:T(8,128)(2,1)S(1)}, u32[]{:S(2)}, u32[]{:S(2)}) %collective-permute-start.5) | collective-permute-done | bytes 229408 | tf_op jit(solution)/shard_map/ppermute | solution.py:111
  51.8 0.7 %fusion.25 = bf16[1,128,896]{2,1,0:T(8,128)(2,1)} fusion(bf16[1,128,896]{2,1,0:T(8,128)(2,1)S(1)} %collective-permute-done.5, f32[1,2,128,896]{3,2,1,0:T(8,128)S(1)} %fusion.8, pred[]{:T(512)S(6)} %ne.18), kind=kLoop, calls=%fused_computation.41 | loop fusion | flops 458752 | bytes 1376257 | tf_op jit(solution)/shard_map/convert_element_type | solution.py:260
  52.5 3.6 %all-to-all-start.1 = ((bf16[8,16,896]{2,1,0:T(8,128)(2,1)}), bf16[8,16,896]{2,1,0:T(8,128)(2,1)S(1)}, u32[]{:S(2)}, u32[]{:S(2)}) async-start(bf16[8,16,896]{2,1,0:T(8,128)(2,1)} %bitcast.41), calls=%async_computation.1 | async-start | bytes 458752 | tf_op jit(solution)/shard_map/all_to_all | solution.py:261
  56.1 1.4 %convolution_convert_fusion = bf16[4,896,128]{2,1,0:T(8,128)(2,1)} fusion(pred[4]{0:T(512)(128)(4,1)S(1)} %get-tuple-element.20, pred[4]{0:T(512)(128)(4,1)S(1)} %get-tuple-element.21, pred[4]{0:T(512)(128)(4,1)S(1)} %iota_compare_fusion.3, bf16[128,896]{0,1:T(8,128)(2,1)S(1)} %copy.29, bf16[128,896]{0,1:T(8,128)(2,1)S(1)} %copy.28, ...), kind=kOutput, calls=%fused_computation.1 | convolution fusion | flops 119275520 | bytes 1867788 | tf_op jit(solution)/shard_map/dot_general | solution.py:253
  57.5 1.4 %convolution_convert_fusion.1 = bf16[4,896,128]{2,1,0:T(8,128)(2,1)} fusion(bf16[128,128,1]{1,0,2:T(8,128)(2,1)S(1)} %fusion.5, pred[4]{0:T(512)(128)(4,1)S(1)} %get-tuple-element.20, pred[4]{0:T(512)(128)(4,1)S(1)} %get-tuple-element.21, pred[4]{0:T(512)(128)(4,1)S(1)} %iota_compare_fusion.3, bf16[128,896]{0,1:T(8,128)(2,1)S(1)} %copy.29, ...), kind=kOutput, calls=%fused_computation.2 | convolution fusion | flops 119275520 | bytes 1867788 | tf_op jit(solution)/shard_map/dot_general | solution.py:250
  58.9 5.3 %all-to-all-done.1 = bf16[8,16,896]{2,1,0:T(8,128)(2,1)S(1)} async-done(((bf16[8,16,896]{2,1,0:T(8,128)(2,1)}), bf16[8,16,896]{2,1,0:T(8,128)(2,1)S(1)}, u32[]{:S(2)}, u32[]{:S(2)}) %all-to-all-start.1) | async-done | bytes 229408 | tf_op jit(solution)/shard_map/all_to_all | solution.py:261
  64.1 1.1 %convolution_convert_fusion.2 = bf16[256,896]{1,0:T(8,128)(2,1)} fusion(bf16[128,256]{1,0:T(8,128)(2,1)S(1)} %copy-done.4, bf16[128,896]{1,0:T(8,128)(2,1)S(1)} %bitcast.127), kind=kOutput, calls=%fused_computation.3 | convolution fusion | flops 58949632 | bytes 753664 | tf_op jit(solution)/shard_map/dot_general | solution.py:262
  (34 shorter events, 1.7 us)
Async XLA Ops:
  0.6 38.4 %copy-start = (bf16[1,3584,128]{2,1,0:T(8,128)(2,1)S(1)}, bf16[1,3584,128]{2,1,0:T(8,128)(2,1)}, u32[]{:S(2)}) copy-start(bf16[1,3584,128]{2,1,0:T(8,128)(2,1)} %param.13) | copy-start | bytes 2752516
  0.6 10.1 %copy-start.2 = (bf16[1,128,3584]{2,1,0:T(8,128)(2,1)S(1)}, bf16[1,128,3584]{2,1,0:T(8,128)(2,1)}, u32[]{:S(2)}) copy-start(bf16[1,128,3584]{2,1,0:T(8,128)(2,1)} %param.15) | copy-start | bytes 2752516
  3.5 21.1 %all-to-all-start = ((bf16[8,16,1920]{2,1,0:T(8,128)(2,1)}), bf16[8,16,1920]{2,1,0:T(8,128)(2,1)S(1)}, u32[]{:S(2)}, u32[]{:S(2)}) async-start(bf16[8,16,1920]{2,1,0:T(8,128)(2,1)} %bitcast.128), calls=%async_computation | async-start | bytes 983040 | tf_op jit(solution)/shard_map/all_to_all | solution.py:198
  12.2 13.4 %collective-permute-start.1 = (bf16[1792,128]{1,0:T(8,128)(2,1)S(1)}, bf16[1792,128]{1,0:T(8,128)(2,1)S(1)}, u32[]{:S(2)}, u32[]{:S(2)}) collective-permute-start(bf16[1792,128]{1,0:T(8,128)(2,1)S(1)} %get-tuple-element.10), channel_id=1, source_target_pairs={{0,16},{8,24},{16,0},{24,8},{1,17},{9,25},{17,1},{25,9},{2,18},{10... | collective-permute-start | bytes 1376264 | tf_op jit(solution)/shard_map/ppermute | solution.py:111
  25.4 1.6 %collective-permute-start = (bf16[1,128,896]{2,1,0:T(8,128)(2,1)S(1)}, bf16[1,128,896]{2,1,0:T(8,128)(2,1)S(1)}, u32[]{:S(2)}, u32[]{:S(2)}) collective-permute-start(bf16[1,128,896]{2,1,0:T(8,128)(2,1)S(1)} %fusion.85), channel_id=1, source_target_pairs={{0,8},{8,0},{16,24},{24,16},{1,9},{9,1},{17,25},{25,17},{2,10},{10... | collective-permute-start | bytes 688136 | tf_op jit(solution)/shard_map/ppermute | solution.py:111
  27.0 0.7 %copy-start.5 = (bf16[1,128,896]{2,1,0:T(8,128)(2,1)}, bf16[1,128,896]{2,1,0:T(8,128)(2,1)S(1)}, u32[]{:S(2)}) copy-start(bf16[1,128,896]{2,1,0:T(8,128)(2,1)S(1)} %collective-permute-done) | copy-start | bytes 688132
  28.2 8.4 %collective-permute-start.2 = (bf16[128,1024]{1,0:T(8,128)(2,1)S(1)}, bf16[128,1024]{1,0:T(8,128)(2,1)S(1)}, u32[]{:S(2)}, u32[]{:S(2)}) collective-permute-start(bf16[128,1024]{1,0:T(8,128)(2,1)S(1)} %pad_maximum_fusion.1), channel_id=1, source_target_pairs={{0,16},{8,24},{16,0},{24,8},{1,17},{9,25},{17,1},{25,9},{2,18},{10... | collective-permute-start | bytes 786440 | tf_op jit(solution)/shard_map/ppermute | solution.py:111
  36.7 1.9 %collective-permute-start.3 = (bf16[2,128,896]{2,1,0:T(8,128)(2,1)S(1)}, bf16[2,128,896]{2,1,0:T(8,128)(2,1)S(1)}, u32[]{:S(2)}, u32[]{:S(2)}) collective-permute-start(bf16[2,128,896]{2,1,0:T(8,128)(2,1)S(1)} %pad_maximum_fusion), channel_id=1, source_target_pairs={{0,8},{8,0},{16,24},{24,16},{1,9},{9,1},{17,25},{25,17},{2,10},{10... | collective-permute-start | bytes 1376264 | tf_op jit(solution)/shard_map/ppermute | solution.py:111
  39.0 1.0 %copy-start.3 = (bf16[128,1792]{0,1:T(8,128)(2,1)S(1)}, bf16[128,1792]{0,1:T(8,128)(2,1)}, u32[]{:S(2)}) copy-start(bf16[128,1792]{0,1:T(8,128)(2,1)} %get-tuple-element.11) | copy-start | bytes 1376260
  39.0 1.1 %copy-start.6 = (bf16[1,128,896]{2,1,0:T(8,128)(2,1)S(1)}, bf16[1,128,896]{2,1,0:T(8,128)(2,1)}, u32[]{:S(2)}) copy-start(bf16[1,128,896]{2,1,0:T(8,128)(2,1)} %copy-done.5) | copy-start | bytes 688132
  39.0 1.4 %copy-start.1 = (bf16[1,3584,128]{2,1,0:T(8,128)(2,1)S(1)}, bf16[1,3584,128]{2,1,0:T(8,128)(2,1)}, u32[]{:S(2)}) copy-start(bf16[1,3584,128]{2,1,0:T(8,128)(2,1)} %param.14) | copy-start | bytes 2752516
  41.9 1.9 %collective-permute-start.4 = (bf16[2,128,896]{2,1,0:T(8,128)(2,1)S(1)}, bf16[2,128,896]{2,1,0:T(8,128)(2,1)S(1)}, u32[]{:S(2)}, u32[]{:S(2)}) collective-permute-start(bf16[2,128,896]{2,1,0:T(8,128)(2,1)S(1)} %fusion.23), channel_id=1, source_target_pairs={{0,8},{8,0},{16,24},{24,16},{1,9},{9,1},{17,25},{25,17},{2,10},{10... | collective-permute-start | bytes 1376264 | tf_op jit(solution)/shard_map/ppermute | solution.py:111
  44.0 7.7 %collective-permute-start.5 = (bf16[1,128,896]{2,1,0:T(8,128)(2,1)S(1)}, bf16[1,128,896]{2,1,0:T(8,128)(2,1)S(1)}, u32[]{:S(2)}, u32[]{:S(2)}) collective-permute-start(bf16[1,128,896]{2,1,0:T(8,128)(2,1)S(1)} %fusion.44), channel_id=1, source_target_pairs={{0,16},{8,24},{16,0},{24,8},{1,17},{9,25},{17,1},{25,9},{2,18},{10... | collective-permute-start | bytes 688136 | tf_op jit(solution)/shard_map/ppermute | solution.py:111
  52.5 11.6 %all-to-all-start.1 = ((bf16[8,16,896]{2,1,0:T(8,128)(2,1)}), bf16[8,16,896]{2,1,0:T(8,128)(2,1)S(1)}, u32[]{:S(2)}, u32[]{:S(2)}) async-start(bf16[8,16,896]{2,1,0:T(8,128)(2,1)} %bitcast.41), calls=%async_computation.1 | async-start | bytes 458752 | tf_op jit(solution)/shard_map/all_to_all | solution.py:261
  57.5 6.6 %copy-start.4 = (bf16[128,256]{1,0:T(8,128)(2,1)S(1)}, bf16[128,256]{1,0:T(8,128)(2,1)}, u32[]{:S(2)}) copy-start(bf16[128,256]{1,0:T(8,128)(2,1)} %get-tuple-element.6) | copy-start | bytes 196612

commit v16 on v13

--- a/solution.py
+++ b/solution.py
@@ -9,7 +9,12 @@
 CAP = 16
 
 
-def glue_kernel(n_dest, width, side, split, ids_ref, gates_ref, flags_ref, tok_ref, grd_ref, *outs):
+def glue_kernel(n_dest, width, side, split, ids_ref, gates_ref, flags_ref, tok_hbm, grd_hbm, *rest):
+    outs, (tok_ref, grd_ref, sems) = rest[:-3], rest[-3:]
+    tok_copy = pltpu.make_async_copy(tok_hbm, tok_ref, sems.at[0])
+    grd_copy = pltpu.make_async_copy(grd_hbm, grd_ref, sems.at[1])
+    tok_copy.start()
+    grd_copy.start()
     f32, bf16 = jnp.float32, jnp.bfloat16
     rows = tok_ref.shape[0]
     slots = n_dest * CAP
@@ -40,6 +45,8 @@
     place = (lax.broadcasted_iota(jnp.int32, (slots, rows), 0) & (CAP - 1)).astype(f32)
     pick = jnp.where((hit_s == 1.0) & (rank_s == place), 1.0, 0.0)
     pick_b = pick.astype(bf16)
+    tok_copy.wait()
+    grd_copy.wait()
     tok = jnp.dot(pick_b, tok_ref[...], preferred_element_type=f32).astype(bf16)
     grd = jnp.dot(pick_b, grd_ref[...], preferred_element_type=f32).astype(bf16)
     hi = gsel.astype(bf16).astype(f32)
@@ -90,8 +97,13 @@
     outs = pl.pallas_call(
         functools.partial(glue_kernel, n_dest, width, side, split),
         out_shape=[jax.ShapeDtypeStruct(s, bf16) for s in shapes],
-        in_specs=[vmem] * 5,
+        in_specs=[vmem] * 3 + [pl.BlockSpec(memory_space=pl.ANY)] * 2,
         out_specs=[vmem] * len(shapes),
+        scratch_shapes=[
+            pltpu.VMEM((rows, width), bf16),
+            pltpu.VMEM((rows, width), bf16),
+            pltpu.SemaphoreType.DMA((2,)),
+        ],
     )(expert_ids.T, gate_values.T, forget_flags.reshape(1, rows), tokens, token_grads)
     if split:
         return jnp.concatenate(outs[:3], axis=1), outs[3]

time: 66 us -> 66.5 us (level)
  no operation moved by 1% of the time
where the time goes in v16:
time: 66.5 us; the launch traced here: 66.2 us
  waiting for transfers between devices  34.2 us (51%)
  starting transfers between devices  15.9 us (24%)
  matrix products  6.83 us (10%)
  Pallas kernels  3.25 us (5%)
  other arithmetic  2.63 us (4%)
  local copies, waits for them, and re-layouts  2.45 us (4%)
  between operations  0.91 us (1%)
    ppermute x6, waiting for transfers between devices, partner(): return lax.ppermute(x, 'dp', [(i, i ^ bit) for i in range(n)])  18.1 us
    all_to_all x1, waiting for transfers between devices, on_device(): lax.all_to_all(payload, 'expert', split_axis=0, concat_axis=0, tiled=True)  10.8 us
    all_to_all x1, starting transfers between devices, on_device(): lax.all_to_all(payload, 'expert', split_axis=0, concat_axis=0, tiled=True)  7.32 us
    all_to_all x1, waiting for transfers between devices, on_device(): lax.all_to_all(summed, 'expert', split_axis=0, concat_axis=0, tiled=True)  5.27 us
    ppermute x6, starting transfers between devices, partner(): return lax.ppermute(x, 'dp', [(i, i ^ bit) for i in range(n)])  4.94 us
    all_to_all x1, starting transfers between devices, on_device(): lax.all_to_all(summed, 'expert', split_axis=0, concat_axis=0, tiled=True)  3.64 us
    pallas_call x1, Pallas kernels, glue(): pl.pallas_call(functools.partial(glue_kernel, n_dest, width, side, split)...  3.25 us
    unnamed x15, local copies, waits for them, and re-layouts  1.42 us
  transfers between devices with their start and end apart: 8, of which 7 were waited for; matrix products, arithmetic and copies ran while one was open for 8% of the time, Pallas kernels for 0%

profile of v16, /device:TPU:0, one launch (start us, length us, event | category | flops | bytes accessed | tf_op | source)
XLA Modules:
  0.0 66.2 jit_solution(1070006107306987231)
XLA Ops:
  0.7 3.2 %shard_map.103 = (bf16[128,1920]{1,0:T(8,128)(2,1)}, bf16[128,256]{1,0:T(8,128)(2,1)}) custom-call(s32[8,256]{1,0:T(8,128)} %bitcast.128, f32[8,256]{1,0:T(8,128)} %bitcast.129, s32[1,256]{1,0:T(1,128)} %bitcast.130, bf16[256,896]{1,0:T(8,128)(2,1)} %tok_hbm.1, bf16[256,896]{1,0:T(8,128)(2,1)} %grd_hbm.1), custom_call_target="tpu_custom_call" | custom-call | tf_op jit(solution)/shard_map/pallas_call | solution.py:97
  3.9 7.3 %all-to-all-start = ((bf16[8,16,1920]{2,1,0:T(8,128)(2,1)}), bf16[8,16,1920]{2,1,0:T(8,128)(2,1)S(1)}, u32[]{:S(2)}, u32[]{:S(2)}) async-start(bf16[8,16,1920]{2,1,0:T(8,128)(2,1)} %bitcast.126), calls=%async_computation | async-start | bytes 983040 | tf_op jit(solution)/shard_map/all_to_all | solution.py:210
  11.2 0.6 copy.24
  11.9 0.8 %select_bitcast_fusion = (bf16[1792,128]{1,0:T(8,128)(2,1)S(1)}, bf16[128,1792]{0,1:T(8,128)(2,1)}) fusion(pred[]{:T(512)S(6)} %ne.18, bf16[128,3584]{0,1:T(8,128)(2,1)S(1)} %bitcast.118), kind=kLoop, calls=%fused_computation.58 | loop fusion | flops 458752 | bytes 1835009 | tf_op jit(solution)/shard_map/transpose | solution.py:205
  12.7 1.5 %collective-permute-start.1 = (bf16[1792,128]{1,0:T(8,128)(2,1)S(1)}, bf16[1792,128]{1,0:T(8,128)(2,1)S(1)}, u32[]{:S(2)}, u32[]{:S(2)}) collective-permute-start(bf16[1792,128]{1,0:T(8,128)(2,1)S(1)} %get-tuple-element.10), channel_id=1, source_target_pairs={{0,16},{8,24},{16,0},{24,8},{1,17},{9,25},{17,1},{25,9},{2,18},{10... | collective-permute-start | bytes 1376264 | tf_op jit(solution)/shard_map/ppermute | solution.py:123
  14.2 10.8 %all-to-all-done = bf16[8,16,1920]{2,1,0:T(8,128)(2,1)S(1)} async-done(((bf16[8,16,1920]{2,1,0:T(8,128)(2,1)}), bf16[8,16,1920]{2,1,0:T(8,128)(2,1)S(1)}, u32[]{:S(2)}, u32[]{:S(2)}) %all-to-all-start) | async-done | bytes 491552 | tf_op jit(solution)/shard_map/all_to_all | solution.py:210
  25.0 0.2 slice_reduce_fusion
  25.3 0.2 fusion.50
  26.1 1.3 %collective-permute-done = bf16[1,128,896]{2,1,0:T(8,128)(2,1)S(1)} collective-permute-done((bf16[1,128,896]{2,1,0:T(8,128)(2,1)S(1)}, bf16[1,128,896]{2,1,0:T(8,128)(2,1)S(1)}, u32[]{:S(2)}, u32[]{:S(2)}) %collective-permute-start) | collective-permute-done | bytes 229408 | tf_op jit(solution)/shard_map/ppermute | solution.py:123
  27.5 0.4 reduce-precision_convert_fusion
  27.8 0.3 copy-done.5
  28.4 1.6 %collective-permute-start.2 = (bf16[128,1152]{1,0:T(8,128)(2,1)S(1)}, bf16[128,1152]{1,0:T(8,128)(2,1)S(1)}, u32[]{:S(2)}, u32[]{:S(2)}) collective-permute-start(bf16[128,1152]{1,0:T(8,128)(2,1)S(1)} %pad_maximum_fusion.1), channel_id=1, source_target_pairs={{0,16},{8,24},{16,0},{24,8},{1,17},{9,25},{17,1},{25,9},{2,18},{10... | collective-permute-start | bytes 884744 | tf_op jit(solution)/shard_map/ppermute | solution.py:123
  30.0 7.6 %collective-permute-done.2 = bf16[128,1152]{1,0:T(8,128)(2,1)S(1)} collective-permute-done((bf16[128,1152]{1,0:T(8,128)(2,1)S(1)}, bf16[128,1152]{1,0:T(8,128)(2,1)S(1)}, u32[]{:S(2)}, u32[]{:S(2)}) %collective-permute-start.2) | collective-permute-done | bytes 294944 | tf_op jit(solution)/shard_map/ppermute | solution.py:123
  37.9 0.2 copy.30
  38.1 1.4 %collective-permute-done.3 = bf16[2,128,896]{2,1,0:T(8,128)(2,1)S(1)} collective-permute-done((bf16[2,128,896]{2,1,0:T(8,128)(2,1)S(1)}, bf16[2,128,896]{2,1,0:T(8,128)(2,1)S(1)}, u32[]{:S(2)}, u32[]{:S(2)}) %collective-permute-start.3) | collective-permute-done | bytes 458784 | tf_op jit(solution)/shard_map/ppermute | solution.py:123
  39.7 0.2 copy.29
  40.0 0.6 convolution_bitcast_fusion
  40.6 0.4 copy-done.3
  41.0 0.3 multiply_convert_fusion.1
  41.4 0.6 fusion.4
  42.0 0.4 fusion.74
  42.4 0.4 add_convert_fusion
  42.9 0.2 collective-permute-start.4
  43.1 1.7 %collective-permute-done.4 = bf16[2,128,896]{2,1,0:T(8,128)(2,1)S(1)} collective-permute-done((bf16[2,128,896]{2,1,0:T(8,128)(2,1)S(1)}, bf16[2,128,896]{2,1,0:T(8,128)(2,1)S(1)}, u32[]{:S(2)}, u32[]{:S(2)}) %collective-permute-start.4) | collective-permute-done | bytes 458784 | tf_op jit(solution)/shard_map/ppermute | solution.py:123
  45.0 1.5 %collective-permute-start.5 = (bf16[1,128,896]{2,1,0:T(8,128)(2,1)S(1)}, bf16[1,128,896]{2,1,0:T(8,128)(2,1)S(1)}, u32[]{:S(2)}, u32[]{:S(2)}) collective-permute-start(bf16[1,128,896]{2,1,0:T(8,128)(2,1)S(1)} %fusion.43), channel_id=1, source_target_pairs={{0,16},{8,24},{16,0},{24,8},{1,17},{9,25},{17,1},{25,9},{2,18},{10... | collective-permute-start | bytes 688136 | tf_op jit(solution)/shard_map/ppermute | solution.py:123
  46.5 6.2 %collective-permute-done.5 = bf16[1,128,896]{2,1,0:T(8,128)(2,1)S(1)} collective-permute-done((bf16[1,128,896]{2,1,0:T(8,128)(2,1)S(1)}, bf16[1,128,896]{2,1,0:T(8,128)(2,1)S(1)}, u32[]{:S(2)}, u32[]{:S(2)}) %collective-permute-start.5) | collective-permute-done | bytes 229408 | tf_op jit(solution)/shard_map/ppermute | solution.py:123
  52.7 0.7 %fusion.24 = bf16[1,128,896]{2,1,0:T(8,128)(2,1)} fusion(bf16[1,128,896]{2,1,0:T(8,128)(2,1)S(1)} %collective-permute-done.5, f32[1,2,128,896]{3,2,1,0:T(8,128)S(1)} %fusion.7, pred[]{:T(512)S(6)} %ne.18), kind=kLoop, calls=%fused_computation.40 | loop fusion | flops 458752 | bytes 1376257 | tf_op jit(solution)/shard_map/convert_element_type | solution.py:277
  53.4 3.6 %all-to-all-start.1 = ((bf16[8,16,896]{2,1,0:T(8,128)(2,1)}), bf16[8,16,896]{2,1,0:T(8,128)(2,1)S(1)}, u32[]{:S(2)}, u32[]{:S(2)}) async-start(bf16[8,16,896]{2,1,0:T(8,128)(2,1)} %bitcast.41), calls=%async_computation.1 | async-start | bytes 458752 | tf_op jit(solution)/shard_map/all_to_all | solution.py:278
  57.1 1.4 %convolution_convert_fusion = bf16[4,896,128]{2,1,0:T(8,128)(2,1)} fusion(pred[4]{0:T(512)(128)(4,1)S(1)} %get-tuple-element.22, pred[4]{0:T(512)(128)(4,1)S(1)} %get-tuple-element.23, pred[4]{0:T(512)(128)(4,1)S(1)} %iota_compare_fusion.3, bf16[128,896]{0,1:T(8,128)(2,1)S(1)} %copy.31, bf16[128,896]{0,1:T(8,128)(2,1)S(1)} %copy.30, ...), kind=kOutput, calls=%fused_computation.1 | convolution fusion | flops 119275520 | bytes 1867788 | tf_op jit(solution)/shard_map/dot_general | solution.py:270
  58.4 1.4 %convolution_convert_fusion.1 = bf16[4,896,128]{2,1,0:T(8,128)(2,1)} fusion(bf16[128,128,1]{1,0,2:T(8,128)(2,1)S(1)} %fusion.4, pred[4]{0:T(512)(128)(4,1)S(1)} %get-tuple-element.22, pred[4]{0:T(512)(128)(4,1)S(1)} %get-tuple-element.23, pred[4]{0:T(512)(128)(4,1)S(1)} %iota_compare_fusion.3, bf16[128,896]{0,1:T(8,128)(2,1)S(1)} %copy.31, ...), kind=kOutput, calls=%fused_computation.2 | convolution fusion | flops 119275520 | bytes 1867788 | tf_op jit(solution)/shard_map/dot_general | solution.py:267
  59.8 5.3 %all-to-all-done.1 = bf16[8,16,896]{2,1,0:T(8,128)(2,1)S(1)} async-done(((bf16[8,16,896]{2,1,0:T(8,128)(2,1)}), bf16[8,16,896]{2,1,0:T(8,128)(2,1)S(1)}, u32[]{:S(2)}, u32[]{:S(2)}) %all-to-all-start.1) | async-done | bytes 229408 | tf_op jit(solution)/shard_map/all_to_all | solution.py:278
  65.1 1.1 %convolution_convert_fusion.2 = bf16[256,896]{1,0:T(8,128)(2,1)} fusion(bf16[128,256]{1,0:T(8,128)(2,1)S(1)} %copy-done.4, bf16[128,896]{1,0:T(8,128)(2,1)S(1)} %bitcast.125), kind=kOutput, calls=%fused_computation.3 | convolution fusion | flops 58949632 | bytes 753664 | tf_op jit(solution)/shard_map/dot_general | solution.py:279
  (36 shorter events, 1.9 us)
Async XLA Ops:
  0.6 39.3 %copy-start = (bf16[1,3584,128]{2,1,0:T(8,128)(2,1)S(1)}, bf16[1,3584,128]{2,1,0:T(8,128)(2,1)}, u32[]{:S(2)}) copy-start(bf16[1,3584,128]{2,1,0:T(8,128)(2,1)} %param.13) | copy-start | bytes 2752516
  0.6 10.6 %copy-start.2 = (bf16[1,128,3584]{2,1,0:T(8,128)(2,1)S(1)}, bf16[1,128,3584]{2,1,0:T(8,128)(2,1)}, u32[]{:S(2)}) copy-start(bf16[1,128,3584]{2,1,0:T(8,128)(2,1)} %param.15) | copy-start | bytes 2752516
  3.9 21.1 %all-to-all-start = ((bf16[8,16,1920]{2,1,0:T(8,128)(2,1)}), bf16[8,16,1920]{2,1,0:T(8,128)(2,1)S(1)}, u32[]{:S(2)}, u32[]{:S(2)}) async-start(bf16[8,16,1920]{2,1,0:T(8,128)(2,1)} %bitcast.126), calls=%async_computation | async-start | bytes 983040 | tf_op jit(solution)/shard_map/all_to_all | solution.py:210
  12.7 13.4 %collective-permute-start.1 = (bf16[1792,128]{1,0:T(8,128)(2,1)S(1)}, bf16[1792,128]{1,0:T(8,128)(2,1)S(1)}, u32[]{:S(2)}, u32[]{:S(2)}) collective-permute-start(bf16[1792,128]{1,0:T(8,128)(2,1)S(1)} %get-tuple-element.10), channel_id=1, source_target_pairs={{0,16},{8,24},{16,0},{24,8},{1,17},{9,25},{17,1},{25,9},{2,18},{10... | collective-permute-start | bytes 1376264 | tf_op jit(solution)/shard_map/ppermute | solution.py:123
  25.9 1.6 %collective-permute-start = (bf16[1,128,896]{2,1,0:T(8,128)(2,1)S(1)}, bf16[1,128,896]{2,1,0:T(8,128)(2,1)S(1)}, u32[]{:S(2)}, u32[]{:S(2)}) collective-permute-start(bf16[1,128,896]{2,1,0:T(8,128)(2,1)S(1)} %fusion.85), channel_id=1, source_target_pairs={{0,8},{8,0},{16,24},{24,16},{1,9},{9,1},{17,25},{25,17},{2,10},{10... | collective-permute-start | bytes 688136 | tf_op jit(solution)/shard_map/ppermute | solution.py:123
  27.5 0.7 %copy-start.5 = (bf16[1,128,896]{2,1,0:T(8,128)(2,1)}, bf16[1,128,896]{2,1,0:T(8,128)(2,1)S(1)}, u32[]{:S(2)}) copy-start(bf16[1,128,896]{2,1,0:T(8,128)(2,1)S(1)} %collective-permute-done) | copy-start | bytes 688132
  28.4 9.1 %collective-permute-start.2 = (bf16[128,1152]{1,0:T(8,128)(2,1)S(1)}, bf16[128,1152]{1,0:T(8,128)(2,1)S(1)}, u32[]{:S(2)}, u32[]{:S(2)}) collective-permute-start(bf16[128,1152]{1,0:T(8,128)(2,1)S(1)} %pad_maximum_fusion.1), channel_id=1, source_target_pairs={{0,16},{8,24},{16,0},{24,8},{1,17},{9,25},{17,1},{25,9},{2,18},{10... | collective-permute-start | bytes 884744 | tf_op jit(solution)/shard_map/ppermute | solution.py:123
  37.6 1.9 %collective-permute-start.3 = (bf16[2,128,896]{2,1,0:T(8,128)(2,1)S(1)}, bf16[2,128,896]{2,1,0:T(8,128)(2,1)S(1)}, u32[]{:S(2)}, u32[]{:S(2)}) collective-permute-start(bf16[2,128,896]{2,1,0:T(8,128)(2,1)S(1)} %pad_maximum_fusion), channel_id=1, source_target_pairs={{0,8},{8,0},{16,24},{24,16},{1,9},{9,1},{17,25},{25,17},{2,10},{10... | collective-permute-start | bytes 1376264 | tf_op jit(solution)/shard_map/ppermute | solution.py:123
  39.9 1.0 %copy-start.3 = (bf16[128,1792]{0,1:T(8,128)(2,1)S(1)}, bf16[128,1792]{0,1:T(8,128)(2,1)}, u32[]{:S(2)}) copy-start(bf16[128,1792]{0,1:T(8,128)(2,1)} %get-tuple-element.11) | copy-start | bytes 1376260
  39.9 1.1 %copy-start.6 = (bf16[1,128,896]{2,1,0:T(8,128)(2,1)S(1)}, bf16[1,128,896]{2,1,0:T(8,128)(2,1)}, u32[]{:S(2)}) copy-start(bf16[1,128,896]{2,1,0:T(8,128)(2,1)} %copy-done.5) | copy-start | bytes 688132
  40.0 1.4 %copy-start.1 = (bf16[1,3584,128]{2,1,0:T(8,128)(2,1)S(1)}, bf16[1,3584,128]{2,1,0:T(8,128)(2,1)}, u32[]{:S(2)}) copy-start(bf16[1,3584,128]{2,1,0:T(8,128)(2,1)} %param.14) | copy-start | bytes 2752516
  42.9 1.9 %collective-permute-start.4 = (bf16[2,128,896]{2,1,0:T(8,128)(2,1)S(1)}, bf16[2,128,896]{2,1,0:T(8,128)(2,1)S(1)}, u32[]{:S(2)}, u32[]{:S(2)}) collective-permute-start(bf16[2,128,896]{2,1,0:T(8,128)(2,1)S(1)} %fusion.22), channel_id=1, source_target_pairs={{0,8},{8,0},{16,24},{24,16},{1,9},{9,1},{17,25},{25,17},{2,10},{10... | collective-permute-start | bytes 1376264 | tf_op jit(solution)/shard_map/ppermute | solution.py:123
  45.0 7.7 %collective-permute-start.5 = (bf16[1,128,896]{2,1,0:T(8,128)(2,1)S(1)}, bf16[1,128,896]{2,1,0:T(8,128)(2,1)S(1)}, u32[]{:S(2)}, u32[]{:S(2)}) collective-permute-start(bf16[1,128,896]{2,1,0:T(8,128)(2,1)S(1)} %fusion.43), channel_id=1, source_target_pairs={{0,16},{8,24},{16,0},{24,8},{1,17},{9,25},{17,1},{25,9},{2,18},{10... | collective-permute-start | bytes 688136 | tf_op jit(solution)/shard_map/ppermute | solution.py:123
  53.4 11.6 %all-to-all-start.1 = ((bf16[8,16,896]{2,1,0:T(8,128)(2,1)}), bf16[8,16,896]{2,1,0:T(8,128)(2,1)S(1)}, u32[]{:S(2)}, u32[]{:S(2)}) async-start(bf16[8,16,896]{2,1,0:T(8,128)(2,1)} %bitcast.41), calls=%async_computation.1 | async-start | bytes 458752 | tf_op jit(solution)/shard_map/all_to_all | solution.py:278
  58.4 6.6 %copy-start.4 = (bf16[128,256]{1,0:T(8,128)(2,1)S(1)}, bf16[128,256]{1,0:T(8,128)(2,1)}, u32[]{:S(2)}) copy-start(bf16[128,256]{1,0:T(8,128)(2,1)} %get-tuple-element.6) | copy-start | bytes 196612

commit v17 on v13

--- a/solution.py
+++ b/solution.py
@@ -241,13 +241,34 @@
             half_grads, keep.reshape(top, width, ff_down), half_dims, preferred_element_type=jnp.float32
         )
         hidden_grad = hidden_grad + returned_share
-        slot_tokens = gather_from([part_tokens, incoming[:, :width]], [me_dp, me_dp ^ top], top // 2, n_dp)
+        held, offs = [part_tokens, incoming[:, :width]], [0, top]
+        bit = top // 2
+        while bit >= 1:
+            got = partner(jnp.stack(held), bit, n_dp)
+            held = held + [got[i] for i in range(len(held))]
+            offs = offs + [o ^ bit for o in offs]
+            bit //= 2
+        order = me_dp ^ jnp.array(offs, jnp.int32)
+        gate_rel = jnp.take(w_gate, order, axis=0)
+        up_rel = jnp.take(w_up, order, axis=0)
+        early, late = jnp.stack(held[:top]), jnp.stack(held[top:])
+        rel_dims = (((0, 2), (0, 1)), ((), ()))
+        gate_pre = lax.dot_general(early, gate_rel[:top], rel_dims, preferred_element_type=jnp.float32) + lax.dot_general(
+            late, gate_rel[top:], rel_dims, preferred_element_type=jnp.float32
+        )
+        up_pre = lax.dot_general(early, up_rel[:top], rel_dims, preferred_element_type=jnp.float32) + lax.dot_general(
+            late, up_rel[top:], rel_dims, preferred_element_type=jnp.float32
+        )
+        at = lax.broadcasted_iota(jnp.int32, (n_dp, 1, 1), 0)
+        slot_tokens = jnp.broadcast_to(held[0][None], (n_dp,) + held[0].shape)
+        for piece, o in zip(held[1:], offs[1:]):
+            slot_tokens = jnp.where(at == (me_dp ^ o), piece[None], slot_tokens)
     else:
         hidden_grad = lax.dot_general(part_grads, w_down, last_dims, preferred_element_type=jnp.float32)
         slot_tokens = part_tokens[None]
-    chunk_dims = (((0, 2), (0, 1)), ((), ()))
-    gate_pre = lax.dot_general(slot_tokens, w_gate, chunk_dims, preferred_element_type=jnp.float32)
-    up_pre = lax.dot_general(slot_tokens, w_up, chunk_dims, preferred_element_type=jnp.float32)
+        chunk_dims = (((0, 2), (0, 1)), ((), ()))
+        gate_pre = lax.dot_general(slot_tokens, w_gate, chunk_dims, preferred_element_type=jnp.float32)
+        up_pre = lax.dot_general(slot_tokens, w_up, chunk_dims, preferred_element_type=jnp.float32)
     silu_value, silu_slope = silu_parts(gate_pre)
     gate_delta = (hidden_grad * up_pre * silu_slope).astype(jnp.bfloat16)
     up_delta = (hidden_grad * silu_value).astype(jnp.bfloat16)

time: 66 us -> 70.6 us (1.070)
  waiting for transfers between devices: 34.1 us -> 29.2 us
  local copies, waits for them, and re-layouts: 2.45 us -> 7.06 us
  other arithmetic: 2.63 us -> 6.4 us
  matrix products: 6.83 us -> 7.85 us
    ppermute x6, waiting for transfers between devices: 18.1 us -> 13.3 us  [partner(): return lax.ppermute(x, 'dp', [(i, i ^ bit) for i in range(n)])]
    gather x0 -> x2, local copies, waits for them, and re-layouts: none -> 2.31 us  [the longest x1 1.59 us: on_device(): gate_rel = jnp.take(w_gate, order, axis=0)]
    slice x1 -> x2, local copies, waits for them, and re-layouts: 0.17 us -> 1.83 us  [on_device(): held, offs = ([part_tokens, incoming[:, :width]], [0, top])]
    dot_general x1, matrix products: 0.36 us -> 1.47 us  [on_device(): lax.dot_general(half_grads, borrowed.reshape(top, width, ff_down), half_d...]
    reshape x1, other arithmetic: 0.15 us -> 1.17 us  [scatter_dp(): pairs = acc.reshape((acc.shape[0] // 2, 2) + acc.shape[1:])]
    convert_element_type x1, other arithmetic: 0.01 us -> 0.93 us  [on_device(): share = incoming[:, width:].astype(jnp.float32)]
    unnamed x15 -> x31, local copies, waits for them, and re-layouts: 1.42 us -> 0.69 us
    concatenate x1, other arithmetic: 0.03 us -> 0.75 us  [on_device(): jnp.concatenate([part_tokens, lent_hi.astype(jnp.bfloat16), lent_lo.astyp...]
  transfers between devices with their start and end apart: 8 -> 8, of which waited for: 7 -> 7; matrix products, arithmetic and copies ran while one was open for 8% -> 16% of each run, Pallas kernels for 0% -> 0%
where the time goes in v17:
time: 70.6 us; the launch traced here: 70.1 us
  waiting for transfers between devices  29.2 us (41%)
  starting transfers between devices  15.8 us (22%)
  matrix products  7.85 us (11%)
  local copies, waits for them, and re-layouts  7.06 us (10%)
  other arithmetic  6.4 us (9%)
  Pallas kernels  2.81 us (4%)
  between operations  0.99 us (1%)
    ppermute x6, waiting for transfers between devices, partner(): return lax.ppermute(x, 'dp', [(i, i ^ bit) for i in range(n)])  13.3 us
    all_to_all x1, waiting for transfers between devices, on_device(): lax.all_to_all(payload, 'expert', split_axis=0, concat_axis=0, tiled=True)  10.7 us
    all_to_all x1, starting transfers between devices, on_device(): lax.all_to_all(payload, 'expert', split_axis=0, concat_axis=0, tiled=True)  7.31 us
    all_to_all x1, waiting for transfers between devices, on_device(): lax.all_to_all(summed, 'expert', split_axis=0, concat_axis=0, tiled=True)  5.26 us
    ppermute x6, starting transfers between devices, partner(): return lax.ppermute(x, 'dp', [(i, i ^ bit) for i in range(n)])  4.85 us
    all_to_all x1, starting transfers between devices, on_device(): lax.all_to_all(summed, 'expert', split_axis=0, concat_axis=0, tiled=True)  3.63 us
    pallas_call x1, Pallas kernels, glue(): pl.pallas_call(functools.partial(glue_kernel, n_dest, width, side, split)...  2.81 us
    slice x2, local copies, waits for them, and re-layouts, on_device(): held, offs = ([part_tokens, incoming[:, :width]], [0, top])  1.83 us
  transfers between devices with their start and end apart: 8, of which 7 were waited for; matrix products, arithmetic and copies ran while one was open for 16% of the time, Pallas kernels for 0%

profile of v17, /device:TPU:0, one launch (start us, length us, event | category | flops | bytes accessed | tf_op | source)
XLA Modules:
  0.0 70.1 jit_solution(15646511689802937509)
XLA Ops:
  0.7 2.8 %shard_map.112 = (bf16[128,1920]{1,0:T(8,128)(2,1)}, bf16[128,256]{1,0:T(8,128)(2,1)}) custom-call(s32[8,256]{1,0:T(8,128)} %bitcast.136, f32[8,256]{1,0:T(8,128)} %bitcast.137, s32[1,256]{1,0:T(1,128)} %bitcast.138, bf16[256,896]{1,0:T(8,128)(2,1)} %tok_ref.1, bf16[256,896]{1,0:T(8,128)(2,1)} %grd_ref.1), custom_call_target="tpu_custom_call" | custom-call | tf_op jit(solution)/shard_map/pallas_call | solution.py:90
  3.5 7.3 %all-to-all-start = ((bf16[8,16,1920]{2,1,0:T(8,128)(2,1)}), bf16[8,16,1920]{2,1,0:T(8,128)(2,1)S(1)}, u32[]{:S(2)}, u32[]{:S(2)}) async-start(bf16[8,16,1920]{2,1,0:T(8,128)(2,1)} %bitcast.134), calls=%async_computation | async-start | bytes 983040 | tf_op jit(solution)/shard_map/all_to_all | solution.py:198
  10.8 0.6 copy.23
  11.4 1.0 %select_bitcast_fusion = (bf16[1792,128]{1,0:T(8,128)(2,1)}, bf16[128,1792]{0,1:T(8,128)(2,1)}) fusion(pred[]{:T(512)S(6)} %ne.18, bf16[128,3584]{0,1:T(8,128)(2,1)S(1)} %bitcast.128), kind=kLoop, calls=%fused_computation.56 | loop fusion | flops 458752 | bytes 1835009 | tf_op jit(solution)/shard_map/transpose | solution.py:193
  12.4 1.5 %collective-permute-start.1 = (bf16[1792,128]{1,0:T(8,128)(2,1)}, bf16[1792,128]{1,0:T(8,128)(2,1)}, u32[]{:S(2)}, u32[]{:S(2)}) collective-permute-start(bf16[1792,128]{1,0:T(8,128)(2,1)} %get-tuple-element.13), channel_id=1, source_target_pairs={{0,16},{8,24},{16,0},{24,8},{1,17},{9,25},{17,1},{25,9},{2,18},{10... | collective-permute-start | bytes 1376264 | tf_op jit(solution)/shard_map/ppermute | solution.py:111
  13.9 10.7 %all-to-all-done = bf16[8,16,1920]{2,1,0:T(8,128)(2,1)S(1)} async-done(((bf16[8,16,1920]{2,1,0:T(8,128)(2,1)}), bf16[8,16,1920]{2,1,0:T(8,128)(2,1)S(1)}, u32[]{:S(2)}, u32[]{:S(2)}) %all-to-all-start) | async-done | bytes 491552 | tf_op jit(solution)/shard_map/all_to_all | solution.py:198
  25.6 0.8 %slice_bitcast_fusion.3 = (bf16[1,128,896]{2,1,0:T(8,128)(2,1)}, bf16[128,896]{1,0:T(8,128)(2,1)S(1)}) fusion(bf16[128,1920]{1,0:T(8,128)(2,1)S(1)} %bitcast.132), kind=kLoop, calls=%fused_computation.116 | loop fusion | bytes 688128 | tf_op jit(solution)/shard_map/stack | solution.py:247
  26.4 0.6 collective-permute-done
  27.0 1.5 %reduce-precision_convert_fusion = (bf16[128,128]{0,1:T(8,128)(2,1)S(1)}, bf16[128,128]{0,1:T(8,128)(2,1)S(1)}) fusion(bf16[2,896,128]{2,1,0:T(8,128)(2,1)} %bitcast.14, pred[2]{0:T(512)(128)(4,1)S(1)} %iota_compare_fusion.2, bf16[128,896]{1,0:T(8,128)(2,1)S(1)} %multiply_convert_fusion, bf16[128,896]{1,0:T(8,128)(2,1)S(1)} %bitcast.139), kind=kOutput, calls=%fused_computation.70 | convolution fusion | flops 59015168 | bytes 983042 | tf_op jit(solution)/shard_map/dot_general | solution.py:229
  28.7 0.8 %pad_maximum_fusion.1 = bf16[128,1152]{1,0:T(8,128)(2,1)} fusion(bf16[128,128]{1,0:T(8,128)(2,1)S(1)} %copy.26, bf16[128,128]{1,0:T(8,128)(2,1)S(1)} %copy.25, bf16[128,896]{1,0:T(8,128)(2,1)S(1)} %get-tuple-element.16), kind=kLoop, calls=%fused_computation.61 | loop fusion | flops 884736 | bytes 589824 | tf_op jit(solution)/shard_map/concatenate | solution.py:234
  29.5 1.5 %collective-permute-start.2 = (bf16[128,1152]{1,0:T(8,128)(2,1)}, bf16[128,1152]{1,0:T(8,128)(2,1)}, u32[]{:S(2)}, u32[]{:S(2)}) collective-permute-start(bf16[128,1152]{1,0:T(8,128)(2,1)} %pad_maximum_fusion.1), channel_id=1, source_target_pairs={{0,16},{8,24},{16,0},{24,8},{1,17},{9,25},{17,1},{25,9},{2,18},{10... | collective-permute-start | bytes 884744 | tf_op jit(solution)/shard_map/ppermute | solution.py:111
  31.0 0.7 %gather_fusion = bf16[4,896,128]{2,1,0:T(8,128)(2,1)S(1)} fusion(bf16[4,896,128]{2,1,0:T(8,128)(2,1)S(1)} %bitcast.126, s32[1024]{0:T(1024)S(1)} %pad_clamp_fusion), kind=kCustom, calls=%fused_computation.clone | custom fusion | bytes 1835024 | tf_op jit(solution)/shard_map/jit(_take)/gather | solution.py:253
  31.8 1.6 %gather_fusion.1 = bf16[4,896,128]{2,1,0:T(8,128)(2,1)} fusion(bf16[4,896,128]{2,1,0:T(8,128)(2,1)S(1)} %bitcast.122, s32[1024]{0:T(1024)S(1)} %pad_clamp_fusion), kind=kCustom, calls=%fused_computation.1.clone | custom fusion | bytes 1835024 | tf_op jit(solution)/shard_map/jit(_take)/gather | solution.py:252
  33.4 5.5 %collective-permute-done.2 = bf16[128,1152]{1,0:T(8,128)(2,1)} collective-permute-done((bf16[128,1152]{1,0:T(8,128)(2,1)}, bf16[128,1152]{1,0:T(8,128)(2,1)}, u32[]{:S(2)}, u32[]{:S(2)}) %collective-permute-start.2) | collective-permute-done | bytes 294944 | tf_op jit(solution)/shard_map/ppermute | solution.py:111
  38.8 1.7 %fusion.66 = (bf16[128,896]{1,0:T(8,128)(2,1)}, bf16[1,128,896]{2,1,0:T(8,128)(2,1)S(1)}) fusion(bf16[128,1152]{1,0:T(8,128)(2,1)} %collective-permute-done.2), kind=kLoop, calls=%fused_computation.117 | loop fusion | bytes 688128 | tf_op jit(solution)/shard_map/slice | solution.py:244
  40.9 0.9 %slice_convert_fusion = f32[128,256]{1,0:T(8,128)S(1)} fusion(bf16[128,1152]{1,0:T(8,128)(2,1)} %collective-permute-done.2), kind=kLoop, calls=%fused_computation.73 | loop fusion | flops 32768 | bytes 196608 | tf_op jit(solution)/shard_map/convert_element_type | solution.py:238
  41.9 0.5 collective-permute-done.3
  43.0 0.3 multiply_convert_fusion.1
  44.0 0.4 fusion.67
  44.4 0.4 add_convert_fusion
  45.1 0.8 %copy.30 = bf16[128,896]{0,1:T(8,128)(2,1)} copy(bf16[128,896]{1,0:T(8,128)(2,1)S(1)} %get-tuple-element.16) | data formatting | bytes 458752 | tf_op jit(solution)/shard_map/slice | solution.py:200
  46.1 0.8 %collective-permute-done.4 = bf16[2,128,896]{2,1,0:T(8,128)(2,1)} collective-permute-done((bf16[2,128,896]{2,1,0:T(8,128)(2,1)S(1)}, bf16[2,128,896]{2,1,0:T(8,128)(2,1)}, u32[]{:S(2)}, u32[]{:S(2)}) %collective-permute-start.4) | collective-permute-done | bytes 458784 | tf_op jit(solution)/shard_map/ppermute | solution.py:111
  46.9 1.2 %fusion.9 = f32[1,2,128,896]{3,2,1,0:T(8,128)S(1)} fusion(bf16[2,128,896]{2,1,0:T(8,128)(2,1)} %collective-permute-done.4, pred[]{:T(512)S(6)} %ne.19, bf16[2,2,128,896]{3,2,1,0:T(8,128)(2,1)S(1)} %bitcast.125), kind=kLoop, calls=%fused_computation.24 | loop fusion | flops 917504 | bytes 2293761 | tf_op jit(solution)/shard_map/reshape | solution.py:171
  48.0 0.7 %fusion.35 = bf16[1,128,896]{2,1,0:T(8,128)(2,1)} fusion(f32[1,2,128,896]{3,2,1,0:T(8,128)S(1)} %fusion.9, pred[]{:T(512)S(6)} %ne.18), kind=kLoop, calls=%fused_computation.62 | loop fusion | flops 114688 | bytes 688129 | tf_op jit(solution)/shard_map/convert_element_type | solution.py:175
  48.8 1.5 %collective-permute-start.5 = (bf16[1,128,896]{2,1,0:T(8,128)(2,1)}, bf16[1,128,896]{2,1,0:T(8,128)(2,1)S(1)}, u32[]{:S(2)}, u32[]{:S(2)}) collective-permute-start(bf16[1,128,896]{2,1,0:T(8,128)(2,1)} %fusion.35), channel_id=1, source_target_pairs={{0,16},{8,24},{16,0},{24,8},{1,17},{9,25},{17,1},{25,9},{2,18},{10... | collective-permute-start | bytes 688136 | tf_op jit(solution)/shard_map/ppermute | solution.py:111
  50.7 6.0 %collective-permute-done.5 = bf16[1,128,896]{2,1,0:T(8,128)(2,1)S(1)} collective-permute-done((bf16[1,128,896]{2,1,0:T(8,128)(2,1)}, bf16[1,128,896]{2,1,0:T(8,128)(2,1)S(1)}, u32[]{:S(2)}, u32[]{:S(2)}) %collective-permute-start.5) | collective-permute-done | bytes 229408 | tf_op jit(solution)/shard_map/ppermute | solution.py:111
  56.6 0.7 %fusion.24 = bf16[1,128,896]{2,1,0:T(8,128)(2,1)} fusion(bf16[1,128,896]{2,1,0:T(8,128)(2,1)S(1)} %collective-permute-done.5, f32[1,2,128,896]{3,2,1,0:T(8,128)S(1)} %fusion.9, pred[]{:T(512)S(6)} %ne.18), kind=kLoop, calls=%fused_computation.46 | loop fusion | flops 458752 | bytes 1376257 | tf_op jit(solution)/shard_map/convert_element_type | solution.py:286
  57.4 3.6 %all-to-all-start.1 = ((bf16[8,16,896]{2,1,0:T(8,128)(2,1)}), bf16[8,16,896]{2,1,0:T(8,128)(2,1)S(1)}, u32[]{:S(2)}, u32[]{:S(2)}) async-start(bf16[8,16,896]{2,1,0:T(8,128)(2,1)} %bitcast.43), calls=%async_computation.1 | async-start | bytes 458752 | tf_op jit(solution)/shard_map/all_to_all | solution.py:287
  61.0 1.4 %convolution_convert_fusion = bf16[4,896,128]{2,1,0:T(8,128)(2,1)} fusion(pred[4]{0:T(512)(128)(4,1)S(1)} %get-tuple-element.27, pred[4]{0:T(512)(128)(4,1)S(1)} %get-tuple-element.28, pred[4]{0:T(512)(128)(4,1)S(1)} %iota_compare_fusion.3, bf16[128,896]{0,1:T(8,128)(2,1)S(1)} %copy-done.8, bf16[128,896]{0,1:T(8,128)(2,1)S(1)} %copy.29, ...), kind=kOutput, calls=%fused_computation.3 | convolution fusion | flops 119275520 | bytes 1867788 | tf_op jit(solution)/shard_map/dot_general | solution.py:279
  62.4 1.4 %convolution_convert_fusion.1 = bf16[4,896,128]{2,1,0:T(8,128)(2,1)} fusion(bf16[128,128,1]{1,0,2:T(8,128)(2,1)S(1)} %fusion.6, pred[4]{0:T(512)(128)(4,1)S(1)} %get-tuple-element.27, pred[4]{0:T(512)(128)(4,1)S(1)} %get-tuple-element.28, pred[4]{0:T(512)(128)(4,1)S(1)} %iota_compare_fusion.3, bf16[128,896]{0,1:T(8,128)(2,1)S(1)} %copy-done.8, ...), kind=kOutput, calls=%fused_computation.4 | convolution fusion | flops 119275520 | bytes 1867788 | tf_op jit(solution)/shard_map/dot_general | solution.py:276
  63.8 5.3 %all-to-all-done.1 = bf16[8,16,896]{2,1,0:T(8,128)(2,1)S(1)} async-done(((bf16[8,16,896]{2,1,0:T(8,128)(2,1)}), bf16[8,16,896]{2,1,0:T(8,128)(2,1)S(1)}, u32[]{:S(2)}, u32[]{:S(2)}) %all-to-all-start.1) | async-done | bytes 229408 | tf_op jit(solution)/shard_map/all_to_all | solution.py:287
  69.0 1.1 %convolution_convert_fusion.2 = bf16[256,896]{1,0:T(8,128)(2,1)} fusion(bf16[128,256]{1,0:T(8,128)(2,1)S(1)} %copy-done.11, bf16[128,896]{1,0:T(8,128)(2,1)S(1)} %bitcast.133), kind=kOutput, calls=%fused_computation.5 | convolution fusion | flops 58949632 | bytes 753664 | tf_op jit(solution)/shard_map/dot_general | solution.py:288
  (59 shorter events, 3.7 us)
Async XLA Ops:
  0.6 31.1 %copy-start = (bf16[1,3584,128]{2,1,0:T(8,128)(2,1)S(1)}, bf16[1,3584,128]{2,1,0:T(8,128)(2,1)}, u32[]{:S(2)}) copy-start(bf16[1,3584,128]{2,1,0:T(8,128)(2,1)} %param.16) | copy-start | bytes 2752516
  0.6 10.1 %copy-start.3 = (bf16[1,128,3584]{2,1,0:T(8,128)(2,1)S(1)}, bf16[1,128,3584]{2,1,0:T(8,128)(2,1)}, u32[]{:S(2)}) copy-start(bf16[1,128,3584]{2,1,0:T(8,128)(2,1)} %param.18) | copy-start | bytes 2752516
  3.5 21.1 %all-to-all-start = ((bf16[8,16,1920]{2,1,0:T(8,128)(2,1)}), bf16[8,16,1920]{2,1,0:T(8,128)(2,1)S(1)}, u32[]{:S(2)}, u32[]{:S(2)}) async-start(bf16[8,16,1920]{2,1,0:T(8,128)(2,1)} %bitcast.134), calls=%async_computation | async-start | bytes 983040 | tf_op jit(solution)/shard_map/all_to_all | solution.py:198
  12.4 14.0 %collective-permute-start.1 = (bf16[1792,128]{1,0:T(8,128)(2,1)}, bf16[1792,128]{1,0:T(8,128)(2,1)}, u32[]{:S(2)}, u32[]{:S(2)}) collective-permute-start(bf16[1792,128]{1,0:T(8,128)(2,1)} %get-tuple-element.13), channel_id=1, source_target_pairs={{0,16},{8,24},{16,0},{24,8},{1,17},{9,25},{17,1},{25,9},{2,18},{10... | collective-permute-start | bytes 1376264 | tf_op jit(solution)/shard_map/ppermute | solution.py:111
  24.8 6.2 %copy-start.12 = (s32[4]{0:T(128)S(1)}, s32[4]{0:T(128)}, u32[]{:S(2)}) copy-start(s32[4]{0:T(128)} %constant.57.clone) | copy-start | bytes 52
  24.8 6.2 %copy-start.1 = (bf16[1,3584,128]{2,1,0:T(8,128)(2,1)S(1)}, bf16[1,3584,128]{2,1,0:T(8,128)(2,1)}, u32[]{:S(2)}) copy-start(bf16[1,3584,128]{2,1,0:T(8,128)(2,1)} %param.17) | copy-start | bytes 2752516
  25.4 1.6 %collective-permute-start = (bf16[1,128,896]{2,1,0:T(8,128)(2,1)S(1)}, bf16[1,128,896]{2,1,0:T(8,128)(2,1)S(1)}, u32[]{:S(2)}, u32[]{:S(2)}) collective-permute-start(bf16[1,128,896]{2,1,0:T(8,128)(2,1)S(1)} %fusion.78), channel_id=1, source_target_pairs={{0,8},{8,0},{16,24},{24,16},{1,9},{9,1},{17,25},{25,17},{2,10},{10... | collective-permute-start | bytes 688136 | tf_op jit(solution)/shard_map/ppermute | solution.py:111
  25.6 5.4 %copy-start.9 = (bf16[128,896]{1,0:T(8,128)(2,1)}, bf16[128,896]{1,0:T(8,128)(2,1)S(1)}, u32[]{:S(2)}) copy-start(bf16[128,896]{1,0:T(8,128)(2,1)S(1)} %multiply_convert_fusion) | copy-start | bytes 688132
  27.0 4.0 %copy-start.13 = (bf16[1,128,896]{2,1,0:T(8,128)(2,1)}, bf16[1,128,896]{2,1,0:T(8,128)(2,1)S(1)}, u32[]{:S(2)}) copy-start(bf16[1,128,896]{2,1,0:T(8,128)(2,1)S(1)} %collective-permute-done) | copy-start | bytes 688132
  29.5 9.4 %collective-permute-start.2 = (bf16[128,1152]{1,0:T(8,128)(2,1)}, bf16[128,1152]{1,0:T(8,128)(2,1)}, u32[]{:S(2)}, u32[]{:S(2)}) collective-permute-start(bf16[128,1152]{1,0:T(8,128)(2,1)} %pad_maximum_fusion.1), channel_id=1, source_target_pairs={{0,16},{8,24},{16,0},{24,8},{1,17},{9,25},{17,1},{25,9},{2,18},{10... | collective-permute-start | bytes 884744 | tf_op jit(solution)/shard_map/ppermute | solution.py:111
  31.0 9.5 %copy-start.4 = (bf16[1,128,896]{2,1,0:T(8,128)(2,1)S(1)}, bf16[1,128,896]{2,1,0:T(8,128)(2,1)}, u32[]{:S(2)}) copy-start(bf16[1,128,896]{2,1,0:T(8,128)(2,1)} %get-tuple-element.15) | copy-start | bytes 688132
  33.4 7.3 %copy-start.2 = (bf16[4,896,128]{2,1,0:T(8,128)(2,1)S(1)}, bf16[4,896,128]{2,1,0:T(8,128)(2,1)}, u32[]{:S(2)}) copy-start(bf16[4,896,128]{2,1,0:T(8,128)(2,1)} %gather_fusion.1) | copy-start | bytes 2752516
  40.5 1.9 %collective-permute-start.3 = (bf16[2,128,896]{2,1,0:T(8,128)(2,1)S(1)}, bf16[2,128,896]{2,1,0:T(8,128)(2,1)S(1)}, u32[]{:S(2)}, u32[]{:S(2)}) collective-permute-start(bf16[2,128,896]{2,1,0:T(8,128)(2,1)S(1)} %pad_maximum_fusion), channel_id=1, source_target_pairs={{0,8},{8,0},{16,24},{24,16},{1,9},{9,1},{17,25},{25,17},{2,10},{10... | collective-permute-start | bytes 1376264 | tf_op jit(solution)/shard_map/ppermute | solution.py:111
  40.6 2.1 %copy-start.5 = (bf16[1,128,896]{2,1,0:T(8,128)(2,1)S(1)}, bf16[1,128,896]{2,1,0:T(8,128)(2,1)}, u32[]{:S(2)}) copy-start(bf16[1,128,896]{2,1,0:T(8,128)(2,1)} %get-tuple-element.15) | copy-start | bytes 688132
  40.9 2.1 %copy-start.7 = (bf16[128,1792]{0,1:T(8,128)(2,1)S(1)}, bf16[128,1792]{0,1:T(8,128)(2,1)}, u32[]{:S(2)}) copy-start(bf16[128,1792]{0,1:T(8,128)(2,1)} %get-tuple-element.14) | copy-start | bytes 1376260
  40.9 2.1 %copy-start.10 = (bf16[128,896]{1,0:T(8,128)(2,1)S(1)}, bf16[128,896]{1,0:T(8,128)(2,1)}, u32[]{:S(2)}) copy-start(bf16[128,896]{1,0:T(8,128)(2,1)} %copy-done.9) | copy-start | bytes 688132
  40.9 2.1 %copy-start.14 = (bf16[1,128,896]{2,1,0:T(8,128)(2,1)S(1)}, bf16[1,128,896]{2,1,0:T(8,128)(2,1)}, u32[]{:S(2)}) copy-start(bf16[1,128,896]{2,1,0:T(8,128)(2,1)} %copy-done.13) | copy-start | bytes 688132
  44.8 1.1 %copy-start.6 = (bf16[128,896]{1,0:T(8,128)(2,1)S(1)}, bf16[128,896]{1,0:T(8,128)(2,1)}, u32[]{:S(2)}) copy-start(bf16[128,896]{1,0:T(8,128)(2,1)} %get-tuple-element.19) | copy-start | bytes 688132
  44.9 2.0 %collective-permute-start.4 = (bf16[2,128,896]{2,1,0:T(8,128)(2,1)S(1)}, bf16[2,128,896]{2,1,0:T(8,128)(2,1)}, u32[]{:S(2)}, u32[]{:S(2)}) collective-permute-start(bf16[2,128,896]{2,1,0:T(8,128)(2,1)S(1)} %fusion.18), channel_id=1, source_target_pairs={{0,8},{8,0},{16,24},{24,16},{1,9},{9,1},{17,25},{25,17},{2,10},{10... | collective-permute-start | bytes 1376264 | tf_op jit(solution)/shard_map/ppermute | solution.py:111
  48.8 12.2 %copy-start.8 = (bf16[128,896]{0,1:T(8,128)(2,1)S(1)}, bf16[128,896]{0,1:T(8,128)(2,1)}, u32[]{:S(2)}) copy-start(bf16[128,896]{0,1:T(8,128)(2,1)} %copy.30) | copy-start | bytes 688132
  48.8 7.9 %collective-permute-start.5 = (bf16[1,128,896]{2,1,0:T(8,128)(2,1)}, bf16[1,128,896]{2,1,0:T(8,128)(2,1)S(1)}, u32[]{:S(2)}, u32[]{:S(2)}) collective-permute-start(bf16[1,128,896]{2,1,0:T(8,128)(2,1)} %fusion.35), channel_id=1, source_target_pairs={{0,16},{8,24},{16,0},{24,8},{1,17},{9,25},{17,1},{25,9},{2,18},{10... | collective-permute-start | bytes 688136 | tf_op jit(solution)/shard_map/ppermute | solution.py:111
  57.4 11.6 %all-to-all-start.1 = ((bf16[8,16,896]{2,1,0:T(8,128)(2,1)}), bf16[8,16,896]{2,1,0:T(8,128)(2,1)S(1)}, u32[]{:S(2)}, u32[]{:S(2)}) async-start(bf16[8,16,896]{2,1,0:T(8,128)(2,1)} %bitcast.43), calls=%async_computation.1 | async-start | bytes 458752 | tf_op jit(solution)/shard_map/all_to_all | solution.py:287
  62.4 6.6 %copy-start.11 = (bf16[128,256]{1,0:T(8,128)(2,1)S(1)}, bf16[128,256]{1,0:T(8,128)(2,1)}, u32[]{:S(2)}) copy-start(bf16[128,256]{1,0:T(8,128)(2,1)} %get-tuple-element.7) | copy-start | bytes 196612

commit v18 on v13

--- a/solution.py
+++ b/solution.py
@@ -226,9 +226,23 @@
         half_grads, _ = gather_half(part_grads, n_dp)
         half_dims = (((0, 2), (0, 1)), ((), ()))
         ff_down = w_down.shape[0]
-        lent = lax.dot_general(
-            half_grads, borrowed.reshape(top, width, ff_down), half_dims, preferred_element_type=jnp.float32
+        offs = [0]
+        bit = top // 2
+        while bit >= 1:
+            offs = offs + [o ^ bit for o in offs]
+            bit //= 2
+        own_pos = me_dp & (top - 1)
+        lent_rel = jnp.take(
+            borrowed.reshape(top, width, ff_down), own_pos ^ jnp.array(offs, jnp.int32), axis=0
         )
+        lent = lax.dot_general(part_grads, lent_rel[0], (((1,), (0,)), ((), ())), preferred_element_type=jnp.float32)
+        if top > 1:
+            rest = jnp.stack([half_grads[0]] * 0 + [
+                jnp.sum(jnp.where(
+                    lax.broadcasted_iota(jnp.int32, (top, 1, 1), 0) == (own_pos ^ o), half_grads, 0
+                ), axis=0).astype(jnp.bfloat16) for o in offs[1:]
+            ])
+            lent = lent + lax.dot_general(rest, lent_rel[1:], half_dims, preferred_element_type=jnp.float32)
         lent_hi = bf16_part(lent)
         lent_lo = lent - lent_hi
         outgoing = jnp.concatenate(

time: 66 us -> 69.8 us (1.058)
  local copies, waits for them, and re-layouts: 2.45 us -> 4.67 us
  starting transfers between devices: 15.9 us -> 17.3 us
  waiting for transfers between devices: 34.1 us -> 33 us
  other arithmetic: 2.63 us -> 3.73 us
    all_to_all x1, waiting for transfers between devices: 10.8 us -> 0.64 us  [on_device(): lax.all_to_all(payload, 'expert', split_axis=0, concat_axis=0, tiled=True)]
    ppermute x6, waiting for transfers between devices: 18.1 us -> 27.1 us  [partner(): return lax.ppermute(x, 'dp', [(i, i ^ bit) for i in range(n)])]
    convert_element_type x1, other arithmetic: 0.01 us -> 1.56 us  [on_device(): share = incoming[:, width:].astype(jnp.float32)]
    all_to_all x1, starting transfers between devices: 3.64 us -> 5.09 us  [on_device(): lax.all_to_all(summed, 'expert', split_axis=0, concat_axis=0, tiled=True)]
    transpose x1, other arithmetic: 0.83 us -> 0.07 us  [on_device(): lend = jnp.where(upper_half, w_down[:, :half_cols], w_down[:, half_cols:]).T]
    unnamed x15 -> x20, local copies, waits for them, and re-layouts: 1.42 us -> 1.18 us
  transfers between devices with their start and end apart: 8 -> 8, of which waited for: 7 -> 7; matrix products, arithmetic and copies ran while one was open for 8% -> 11% of each run, Pallas kernels for 0% -> 0%
where the time goes in v18:
time: 69.8 us; the launch traced here: 69.4 us
  waiting for transfers between devices  33 us (47%)
  starting transfers between devices  17.3 us (25%)
  matrix products  7.01 us (10%)
  local copies, waits for them, and re-layouts  4.67 us (7%)
  other arithmetic  3.73 us (5%)
  Pallas kernels  2.81 us (4%)
  between operations  0.95 us (1%)
    ppermute x6, waiting for transfers between devices, partner(): return lax.ppermute(x, 'dp', [(i, i ^ bit) for i in range(n)])  27.1 us
    all_to_all x1, starting transfers between devices, on_device(): lax.all_to_all(payload, 'expert', split_axis=0, concat_axis=0, tiled=True)  7.31 us
    all_to_all x1, waiting for transfers between devices, on_device(): lax.all_to_all(summed, 'expert', split_axis=0, concat_axis=0, tiled=True)  5.26 us
    all_to_all x1, starting transfers between devices, on_device(): lax.all_to_all(summed, 'expert', split_axis=0, concat_axis=0, tiled=True)  5.09 us
    ppermute x6, starting transfers between devices, partner(): return lax.ppermute(x, 'dp', [(i, i ^ bit) for i in range(n)])  4.91 us
    pallas_call x1, Pallas kernels, glue(): pl.pallas_call(functools.partial(glue_kernel, n_dest, width, side, split)...  2.81 us
    convert_element_type x1, other arithmetic, on_device(): share = incoming[:, width:].astype(jnp.float32)  1.56 us
  transfers between devices with their start and end apart: 8, of which 7 were waited for; matrix products, arithmetic and copies ran while one was open for 11% of the time, Pallas kernels for 0%

profile of v18, /device:TPU:0, one launch (start us, length us, event | category | flops | bytes accessed | tf_op | source)
XLA Modules:
  0.0 69.4 jit_solution(16579163407924191655)
XLA Ops:
  0.7 2.8 %shard_map.112 = (bf16[128,1920]{1,0:T(8,128)(2,1)}, bf16[128,256]{1,0:T(8,128)(2,1)}) custom-call(s32[8,256]{1,0:T(8,128)} %bitcast.138, f32[8,256]{1,0:T(8,128)} %bitcast.139, s32[1,256]{1,0:T(1,128)} %bitcast.140, bf16[256,896]{1,0:T(8,128)(2,1)} %tok_ref.1, bf16[256,896]{1,0:T(8,128)(2,1)} %grd_ref.1), custom_call_target="tpu_custom_call" | custom-call | tf_op jit(solution)/shard_map/pallas_call | solution.py:90
  3.5 7.3 %all-to-all-start = ((bf16[8,16,1920]{2,1,0:T(8,128)(2,1)}), bf16[8,16,1920]{2,1,0:T(8,128)(2,1)S(1)}, u32[]{:S(2)}, u32[]{:S(2)}) async-start(bf16[8,16,1920]{2,1,0:T(8,128)(2,1)} %bitcast.134), calls=%async_computation | async-start | bytes 983040 | tf_op jit(solution)/shard_map/all_to_all | solution.py:198
  10.9 1.6 %collective-permute-start = (bf16[1792,128]{0,1:T(8,128)(2,1)S(1)}, bf16[1792,128]{0,1:T(8,128)(2,1)S(1)}, u32[]{:S(2)}, u32[]{:S(2)}) collective-permute-start(bf16[1792,128]{0,1:T(8,128)(2,1)S(1)} %get-tuple-element.10), channel_id=1, source_target_pairs={{0,16},{8,24},{16,0},{24,8},{1,17},{9,25},{17,1},{25,9},{2,18},{10... | collective-permute-start | bytes 1376264 | tf_op jit(solution)/shard_map/ppermute | solution.py:111
  12.5 10.4 %collective-permute-done = bf16[1792,128]{0,1:T(8,128)(2,1)S(1)} collective-permute-done((bf16[1792,128]{0,1:T(8,128)(2,1)S(1)}, bf16[1792,128]{0,1:T(8,128)(2,1)S(1)}, u32[]{:S(2)}, u32[]{:S(2)}) %collective-permute-start) | collective-permute-done | bytes 458784 | tf_op jit(solution)/shard_map/ppermute | solution.py:111
  22.9 0.3 copy.25
  23.1 0.6 gather_fusion
  23.9 0.6 all-to-all-done
  25.6 0.3 fusion.43
  25.9 1.2 %collective-permute-done.1 = bf16[1,128,896]{2,1,0:T(8,128)(2,1)S(1)} collective-permute-done((bf16[1,128,896]{2,1,0:T(8,128)(2,1)S(1)}, bf16[1,128,896]{2,1,0:T(8,128)(2,1)S(1)}, u32[]{:S(2)}, u32[]{:S(2)}) %collective-permute-start.1) | collective-permute-done | bytes 229408 | tf_op jit(solution)/shard_map/ppermute | solution.py:111
  27.3 0.3 reduce-precision_convert_fusion
  28.1 1.6 %collective-permute-start.2 = (bf16[128,1152]{1,0:T(8,128)(2,1)S(1)}, bf16[128,1152]{1,0:T(8,128)(2,1)S(1)}, u32[]{:S(2)}, u32[]{:S(2)}) collective-permute-start(bf16[128,1152]{1,0:T(8,128)(2,1)S(1)} %pad_maximum_fusion.1), channel_id=1, source_target_pairs={{0,16},{8,24},{16,0},{24,8},{1,17},{9,25},{17,1},{25,9},{2,18},{10... | collective-permute-start | bytes 884744 | tf_op jit(solution)/shard_map/ppermute | solution.py:111
  29.6 7.5 %collective-permute-done.2 = bf16[128,1152]{1,0:T(8,128)(2,1)S(1)} collective-permute-done((bf16[128,1152]{1,0:T(8,128)(2,1)S(1)}, bf16[128,1152]{1,0:T(8,128)(2,1)S(1)}, u32[]{:S(2)}, u32[]{:S(2)}) %collective-permute-start.2) | collective-permute-done | bytes 294944 | tf_op jit(solution)/shard_map/ppermute | solution.py:111
  37.4 0.5 copy-done.3
  37.9 0.3 copy.41
  38.2 0.8 %copy.31 = bf16[128,896]{0,1:T(8,128)(2,1)} copy(bf16[128,896]{1,0:T(8,128)(2,1)S(1)} %get-tuple-element.13) | data formatting | bytes 458752 | tf_op jit(solution)/shard_map/slice | solution.py:200
  39.0 0.8 %copy.30 = bf16[128,896]{0,1:T(8,128)(2,1)} copy(bf16[128,896]{1,0:T(8,128)(2,1)S(1)} %get-tuple-element.17) | data formatting | bytes 458752 | tf_op jit(solution)/shard_map/slice | solution.py:258
  39.8 1.6 %slice_convert_fusion = f32[128,256]{1,0:T(8,128)} fusion(bf16[128,1152]{1,0:T(8,128)(2,1)} %copy-done.3), kind=kLoop, calls=%fused_computation.78 | loop fusion | flops 32768 | bytes 196608 | tf_op jit(solution)/shard_map/convert_element_type | solution.py:252
  41.9 0.6 convolution_bitcast_fusion
  42.5 0.3 copy-done.7
  42.9 0.3 multiply_convert_fusion.1
  43.2 0.6 fusion.4
  43.8 0.4 fusion.72
  44.2 0.4 add_convert_fusion
  44.8 1.8 %collective-permute-done.4 = bf16[2,128,896]{2,1,0:T(8,128)(2,1)S(1)} collective-permute-done((bf16[2,128,896]{2,1,0:T(8,128)(2,1)S(1)}, bf16[2,128,896]{2,1,0:T(8,128)(2,1)S(1)}, u32[]{:S(2)}, u32[]{:S(2)}) %collective-permute-start.4) | collective-permute-done | bytes 458784 | tf_op jit(solution)/shard_map/ppermute | solution.py:111
  46.8 1.6 %collective-permute-start.5 = (bf16[1,128,896]{2,1,0:T(8,128)(2,1)S(1)}, bf16[1,128,896]{2,1,0:T(8,128)(2,1)S(1)}, u32[]{:S(2)}, u32[]{:S(2)}) collective-permute-start(bf16[1,128,896]{2,1,0:T(8,128)(2,1)S(1)} %fusion.42), channel_id=1, source_target_pairs={{0,16},{8,24},{16,0},{24,8},{1,17},{9,25},{17,1},{25,9},{2,18},{10... | collective-permute-start | bytes 688136 | tf_op jit(solution)/shard_map/ppermute | solution.py:111
  48.4 6.1 %collective-permute-done.5 = bf16[1,128,896]{2,1,0:T(8,128)(2,1)S(1)} collective-permute-done((bf16[1,128,896]{2,1,0:T(8,128)(2,1)S(1)}, bf16[1,128,896]{2,1,0:T(8,128)(2,1)S(1)}, u32[]{:S(2)}, u32[]{:S(2)}) %collective-permute-start.5) | collective-permute-done | bytes 229408 | tf_op jit(solution)/shard_map/ppermute | solution.py:111
  54.5 0.7 %fusion.24 = bf16[1,128,896]{2,1,0:T(8,128)(2,1)} fusion(bf16[1,128,896]{2,1,0:T(8,128)(2,1)S(1)} %collective-permute-done.5, f32[1,2,128,896]{3,2,1,0:T(8,128)S(1)} %fusion.7, pred[]{:T(512)S(6)} %ne.18), kind=kLoop, calls=%fused_computation.42 | loop fusion | flops 458752 | bytes 1376257 | tf_op jit(solution)/shard_map/convert_element_type | solution.py:279
  55.3 5.1 %all-to-all-start.1 = ((bf16[8,16,896]{2,1,0:T(8,128)(2,1)}), bf16[8,16,896]{2,1,0:T(8,128)(2,1)S(1)}, u32[]{:S(2)}, u32[]{:S(2)}) async-start(bf16[8,16,896]{2,1,0:T(8,128)(2,1)} %bitcast.42), calls=%async_computation.1 | async-start | bytes 458752 | tf_op jit(solution)/shard_map/all_to_all | solution.py:280
  60.4 1.4 %convolution_convert_fusion = bf16[4,896,128]{2,1,0:T(8,128)(2,1)} fusion(pred[4]{0:T(512)(128)(4,1)S(1)} %get-tuple-element.22, pred[4]{0:T(512)(128)(4,1)S(1)} %get-tuple-element.23, pred[4]{0:T(512)(128)(4,1)S(1)} %iota_compare_fusion.4, bf16[128,896]{0,1:T(8,128)(2,1)S(1)} %copy-done.4, bf16[128,896]{0,1:T(8,128)(2,1)S(1)} %copy-done.5, ...), kind=kOutput, calls=%fused_computation.2 | convolution fusion | flops 119275520 | bytes 1867788 | tf_op jit(solution)/shard_map/dot_general | solution.py:272
  61.7 1.4 %convolution_convert_fusion.1 = bf16[4,896,128]{2,1,0:T(8,128)(2,1)} fusion(bf16[128,128,1]{1,0,2:T(8,128)(2,1)S(1)} %fusion.4, pred[4]{0:T(512)(128)(4,1)S(1)} %get-tuple-element.22, pred[4]{0:T(512)(128)(4,1)S(1)} %get-tuple-element.23, pred[4]{0:T(512)(128)(4,1)S(1)} %iota_compare_fusion.4, bf16[128,896]{0,1:T(8,128)(2,1)S(1)} %copy-done.4, ...), kind=kOutput, calls=%fused_computation.3 | convolution fusion | flops 119275520 | bytes 1867788 | tf_op jit(solution)/shard_map/dot_general | solution.py:269
  63.1 5.3 %all-to-all-done.1 = bf16[8,16,896]{2,1,0:T(8,128)(2,1)S(1)} async-done(((bf16[8,16,896]{2,1,0:T(8,128)(2,1)}), bf16[8,16,896]{2,1,0:T(8,128)(2,1)S(1)}, u32[]{:S(2)}, u32[]{:S(2)}) %all-to-all-start.1) | async-done | bytes 229408 | tf_op jit(solution)/shard_map/all_to_all | solution.py:280
  68.4 1.1 %convolution_convert_fusion.2 = bf16[256,896]{1,0:T(8,128)(2,1)} fusion(bf16[128,256]{1,0:T(8,128)(2,1)S(1)} %copy-done.9, bf16[128,896]{1,0:T(8,128)(2,1)S(1)} %bitcast.132), kind=kOutput, calls=%fused_computation.4 | convolution fusion | flops 58949632 | bytes 753664 | tf_op jit(solution)/shard_map/dot_general | solution.py:281
  (51 shorter events, 3.0 us)
Async XLA Ops:
  0.6 41.2 %copy-start = (bf16[1,3584,128]{2,1,0:T(8,128)(2,1)S(1)}, bf16[1,3584,128]{2,1,0:T(8,128)(2,1)}, u32[]{:S(2)}) copy-start(bf16[1,3584,128]{2,1,0:T(8,128)(2,1)} %param.14) | copy-start | bytes 2752516
  0.6 10.1 %copy-start.2 = (bf16[1,128,3584]{2,1,0:T(8,128)(2,1)S(1)}, bf16[1,128,3584]{2,1,0:T(8,128)(2,1)}, u32[]{:S(2)}) copy-start(bf16[1,128,3584]{2,1,0:T(8,128)(2,1)} %param.16) | copy-start | bytes 2752516
  3.5 21.1 %all-to-all-start = ((bf16[8,16,1920]{2,1,0:T(8,128)(2,1)}), bf16[8,16,1920]{2,1,0:T(8,128)(2,1)S(1)}, u32[]{:S(2)}, u32[]{:S(2)}) async-start(bf16[8,16,1920]{2,1,0:T(8,128)(2,1)} %bitcast.134), calls=%async_computation | async-start | bytes 983040 | tf_op jit(solution)/shard_map/all_to_all | solution.py:198
  10.9 12.0 %collective-permute-start = (bf16[1792,128]{0,1:T(8,128)(2,1)S(1)}, bf16[1792,128]{0,1:T(8,128)(2,1)S(1)}, u32[]{:S(2)}, u32[]{:S(2)}) collective-permute-start(bf16[1792,128]{0,1:T(8,128)(2,1)S(1)} %get-tuple-element.10), channel_id=1, source_target_pairs={{0,16},{8,24},{16,0},{24,8},{1,17},{9,25},{17,1},{25,9},{2,18},{10... | collective-permute-start | bytes 1376264 | tf_op jit(solution)/shard_map/ppermute | solution.py:111
  25.5 1.6 %collective-permute-start.1 = (bf16[1,128,896]{2,1,0:T(8,128)(2,1)S(1)}, bf16[1,128,896]{2,1,0:T(8,128)(2,1)S(1)}, u32[]{:S(2)}, u32[]{:S(2)}) collective-permute-start(bf16[1,128,896]{2,1,0:T(8,128)(2,1)S(1)} %fusion.84), channel_id=1, source_target_pairs={{0,8},{8,0},{16,24},{24,16},{1,9},{9,1},{17,25},{25,17},{2,10},{10... | collective-permute-start | bytes 688136 | tf_op jit(solution)/shard_map/ppermute | solution.py:111
  27.1 0.7 copy-start.6
  28.1 9.1 %collective-permute-start.2 = (bf16[128,1152]{1,0:T(8,128)(2,1)S(1)}, bf16[128,1152]{1,0:T(8,128)(2,1)S(1)}, u32[]{:S(2)}, u32[]{:S(2)}) collective-permute-start(bf16[128,1152]{1,0:T(8,128)(2,1)S(1)} %pad_maximum_fusion.1), channel_id=1, source_target_pairs={{0,16},{8,24},{16,0},{24,8},{1,17},{9,25},{17,1},{25,9},{2,18},{10... | collective-permute-start | bytes 884744 | tf_op jit(solution)/shard_map/ppermute | solution.py:111
  37.2 0.7 %copy-start.3 = (bf16[128,1152]{1,0:T(8,128)(2,1)}, bf16[128,1152]{1,0:T(8,128)(2,1)S(1)}, u32[]{:S(2)}) copy-start(bf16[128,1152]{1,0:T(8,128)(2,1)S(1)} %collective-permute-done.2) | copy-start | bytes 884740
  37.3 4.1 %collective-permute-start.3 = (bf16[2,128,896]{2,1,0:T(8,128)(2,1)S(1)}, bf16[2,128,896]{2,1,0:T(8,128)(2,1)S(1)}, u32[]{:S(2)}, u32[]{:S(2)}) collective-permute-start(bf16[2,128,896]{2,1,0:T(8,128)(2,1)S(1)} %pad_maximum_fusion), channel_id=1, source_target_pairs={{0,8},{8,0},{16,24},{24,16},{1,9},{9,1},{17,25},{25,17},{2,10},{10... | collective-permute-start | bytes 1376264 | tf_op jit(solution)/shard_map/ppermute | solution.py:111
  39.0 2.8 %copy-start.4 = (bf16[128,896]{0,1:T(8,128)(2,1)S(1)}, bf16[128,896]{0,1:T(8,128)(2,1)}, u32[]{:S(2)}) copy-start(bf16[128,896]{0,1:T(8,128)(2,1)} %copy.31) | copy-start | bytes 688132
  39.8 2.0 %copy-start.5 = (bf16[128,896]{0,1:T(8,128)(2,1)S(1)}, bf16[128,896]{0,1:T(8,128)(2,1)}, u32[]{:S(2)}) copy-start(bf16[128,896]{0,1:T(8,128)(2,1)} %copy.30) | copy-start | bytes 688132
  41.8 0.9 %copy-start.7 = (bf16[1,128,896]{2,1,0:T(8,128)(2,1)S(1)}, bf16[1,128,896]{2,1,0:T(8,128)(2,1)}, u32[]{:S(2)}) copy-start(bf16[1,128,896]{2,1,0:T(8,128)(2,1)} %copy-done.6) | copy-start | bytes 688132
  41.8 1.0 %copy-start.8 = (f32[128,256]{1,0:T(8,128)S(1)}, f32[128,256]{1,0:T(8,128)}, u32[]{:S(2)}) copy-start(f32[128,256]{1,0:T(8,128)} %slice_convert_fusion) | copy-start | bytes 393220
  41.9 1.4 %copy-start.1 = (bf16[1,3584,128]{2,1,0:T(8,128)(2,1)S(1)}, bf16[1,3584,128]{2,1,0:T(8,128)(2,1)}, u32[]{:S(2)}) copy-start(bf16[1,3584,128]{2,1,0:T(8,128)(2,1)} %param.15) | copy-start | bytes 2752516
  44.7 1.9 %collective-permute-start.4 = (bf16[2,128,896]{2,1,0:T(8,128)(2,1)S(1)}, bf16[2,128,896]{2,1,0:T(8,128)(2,1)S(1)}, u32[]{:S(2)}, u32[]{:S(2)}) collective-permute-start(bf16[2,128,896]{2,1,0:T(8,128)(2,1)S(1)} %fusion.22), channel_id=1, source_target_pairs={{0,8},{8,0},{16,24},{24,16},{1,9},{9,1},{17,25},{25,17},{2,10},{10... | collective-permute-start | bytes 1376264 | tf_op jit(solution)/shard_map/ppermute | solution.py:111
  46.8 7.7 %collective-permute-start.5 = (bf16[1,128,896]{2,1,0:T(8,128)(2,1)S(1)}, bf16[1,128,896]{2,1,0:T(8,128)(2,1)S(1)}, u32[]{:S(2)}, u32[]{:S(2)}) collective-permute-start(bf16[1,128,896]{2,1,0:T(8,128)(2,1)S(1)} %fusion.42), channel_id=1, source_target_pairs={{0,16},{8,24},{16,0},{24,8},{1,17},{9,25},{17,1},{25,9},{2,18},{10... | collective-permute-start | bytes 688136 | tf_op jit(solution)/shard_map/ppermute | solution.py:111
  55.3 13.1 %all-to-all-start.1 = ((bf16[8,16,896]{2,1,0:T(8,128)(2,1)}), bf16[8,16,896]{2,1,0:T(8,128)(2,1)S(1)}, u32[]{:S(2)}, u32[]{:S(2)}) async-start(bf16[8,16,896]{2,1,0:T(8,128)(2,1)} %bitcast.42), calls=%async_computation.1 | async-start | bytes 458752 | tf_op jit(solution)/shard_map/all_to_all | solution.py:280
  61.7 6.6 %copy-start.9 = (bf16[128,256]{1,0:T(8,128)(2,1)S(1)}, bf16[128,256]{1,0:T(8,128)(2,1)}, u32[]{:S(2)}) copy-start(bf16[128,256]{1,0:T(8,128)(2,1)} %get-tuple-element.6) | copy-start | bytes 196612

commit v19 on v13

--- a/solution.py
+++ b/solution.py
@@ -47,20 +47,20 @@
     mid = rest.astype(bf16).astype(f32)
     lo = rest - mid
 
-    def per_slot(x):
-        spread = jnp.dot(expand, x.astype(bf16), preferred_element_type=f32)
-        return jnp.sum(spread * pick, axis=1, keepdims=True)
-
-    s_hi, s_mid, s_lo = per_slot(hi), per_slot(mid), per_slot(lo)
-    s_flag = jnp.sum(pick * flags, axis=1, keepdims=True)
+    into = lax.broadcasted_iota(jnp.int32, (rows, side), 1)
+
+    def to_column(x, c):
+        return jnp.dot(x.astype(bf16), jnp.where(into == c, 1.0, 0.0).astype(bf16), preferred_element_type=f32)
+
+    side_v = to_column(jnp.dot(expand, hi.astype(bf16), preferred_element_type=f32) * pick, 0)
+    side_v = side_v + to_column(jnp.dot(expand, mid.astype(bf16), preferred_element_type=f32) * pick, 1)
+    side_v = side_v + to_column(jnp.dot(expand, lo.astype(bf16), preferred_element_type=f32) * pick, 2)
+    side_v = side_v + to_column(pick * flags, 3)
     count = jnp.sum(flags, axis=1, keepdims=True)
     c_hi = jnp.floor(count / 256.0)
     c_lo = count - 256.0 * c_hi
     col = lax.broadcasted_iota(jnp.int32, (slots, side), 1)
-    side_v = jnp.where(col == 0, s_hi, 0.0)
-    for c, v in ((1, s_mid), (2, s_lo), (3, s_flag), (4, c_hi), (5, c_lo)):
-        side_v = jnp.where(col == c, v, side_v)
-    side_v = side_v.astype(bf16)
+    side_v = jnp.where(col == 4, c_hi, jnp.where(col == 5, c_lo, side_v)).astype(bf16)
     if split:
         tok_out, grd_out, side_out, pick_out = outs
         tok_out[...] = tok

time: 66 us -> 66.2 us (level)
  no operation moved by 1% of the time
where the time goes in v19:
time: 66.2 us; the launch traced here: 65.9 us
  waiting for transfers between devices  34.2 us (52%)
  starting transfers between devices  15.9 us (24%)
  matrix products  6.83 us (10%)
  Pallas kernels  3.01 us (5%)
  other arithmetic  2.63 us (4%)
  local copies, waits for them, and re-layouts  2.45 us (4%)
  between operations  0.91 us (1%)
    ppermute x6, waiting for transfers between devices, partner(): return lax.ppermute(x, 'dp', [(i, i ^ bit) for i in range(n)])  18.1 us
    all_to_all x1, waiting for transfers between devices, on_device(): lax.all_to_all(payload, 'expert', split_axis=0, concat_axis=0, tiled=True)  10.8 us
    all_to_all x1, starting transfers between devices, on_device(): lax.all_to_all(payload, 'expert', split_axis=0, concat_axis=0, tiled=True)  7.31 us
    all_to_all x1, waiting for transfers between devices, on_device(): lax.all_to_all(summed, 'expert', split_axis=0, concat_axis=0, tiled=True)  5.27 us
    ppermute x6, starting transfers between devices, partner(): return lax.ppermute(x, 'dp', [(i, i ^ bit) for i in range(n)])  4.96 us
    all_to_all x1, starting transfers between devices, on_device(): lax.all_to_all(summed, 'expert', split_axis=0, concat_axis=0, tiled=True)  3.63 us
    pallas_call x1, Pallas kernels, glue(): pl.pallas_call(functools.partial(glue_kernel, n_dest, width, side, split)...  3.01 us
    unnamed x15, local copies, waits for them, and re-layouts  1.42 us
  transfers between devices with their start and end apart: 8, of which 7 were waited for; matrix products, arithmetic and copies ran while one was open for 8% of the time, Pallas kernels for 0%

profile of v19, /device:TPU:0, one launch (start us, length us, event | category | flops | bytes accessed | tf_op | source)
XLA Modules:
  0.0 65.9 jit_solution(10952629459901909614)
XLA Ops:
  0.7 3.0 %shard_map.103 = (bf16[128,1920]{1,0:T(8,128)(2,1)}, bf16[128,256]{1,0:T(8,128)(2,1)}) custom-call(s32[8,256]{1,0:T(8,128)} %bitcast.128, f32[8,256]{1,0:T(8,128)} %bitcast.129, s32[1,256]{1,0:T(1,128)} %bitcast.130, bf16[256,896]{1,0:T(8,128)(2,1)} %tok_ref.1, bf16[256,896]{1,0:T(8,128)(2,1)} %grd_ref.1), custom_call_target="tpu_custom_call" | custom-call | tf_op jit(solution)/shard_map/pallas_call | solution.py:90
  3.7 7.3 %all-to-all-start = ((bf16[8,16,1920]{2,1,0:T(8,128)(2,1)}), bf16[8,16,1920]{2,1,0:T(8,128)(2,1)S(1)}, u32[]{:S(2)}, u32[]{:S(2)}) async-start(bf16[8,16,1920]{2,1,0:T(8,128)(2,1)} %bitcast.126), calls=%async_computation | async-start | bytes 983040 | tf_op jit(solution)/shard_map/all_to_all | solution.py:198
  11.0 0.6 copy.24
  11.6 0.8 %select_bitcast_fusion = (bf16[1792,128]{1,0:T(8,128)(2,1)S(1)}, bf16[128,1792]{0,1:T(8,128)(2,1)}) fusion(pred[]{:T(512)S(6)} %ne.18, bf16[128,3584]{0,1:T(8,128)(2,1)S(1)} %bitcast.118), kind=kLoop, calls=%fused_computation.58 | loop fusion | flops 458752 | bytes 1835009 | tf_op jit(solution)/shard_map/transpose | solution.py:193
  12.4 1.5 %collective-permute-start.1 = (bf16[1792,128]{1,0:T(8,128)(2,1)S(1)}, bf16[1792,128]{1,0:T(8,128)(2,1)S(1)}, u32[]{:S(2)}, u32[]{:S(2)}) collective-permute-start(bf16[1792,128]{1,0:T(8,128)(2,1)S(1)} %get-tuple-element.10), channel_id=1, source_target_pairs={{0,16},{8,24},{16,0},{24,8},{1,17},{9,25},{17,1},{25,9},{2,18},{10... | collective-permute-start | bytes 1376264 | tf_op jit(solution)/shard_map/ppermute | solution.py:111
  13.9 10.8 %all-to-all-done = bf16[8,16,1920]{2,1,0:T(8,128)(2,1)S(1)} async-done(((bf16[8,16,1920]{2,1,0:T(8,128)(2,1)}), bf16[8,16,1920]{2,1,0:T(8,128)(2,1)S(1)}, u32[]{:S(2)}, u32[]{:S(2)}) %all-to-all-start) | async-done | bytes 491552 | tf_op jit(solution)/shard_map/all_to_all | solution.py:198
  24.8 0.2 slice_reduce_fusion
  25.0 0.2 fusion.50
  25.9 1.3 %collective-permute-done = bf16[1,128,896]{2,1,0:T(8,128)(2,1)S(1)} collective-permute-done((bf16[1,128,896]{2,1,0:T(8,128)(2,1)S(1)}, bf16[1,128,896]{2,1,0:T(8,128)(2,1)S(1)}, u32[]{:S(2)}, u32[]{:S(2)}) %collective-permute-start) | collective-permute-done | bytes 229408 | tf_op jit(solution)/shard_map/ppermute | solution.py:111
  27.2 0.4 reduce-precision_convert_fusion
  27.6 0.3 copy-done.5
  28.2 1.6 %collective-permute-start.2 = (bf16[128,1152]{1,0:T(8,128)(2,1)S(1)}, bf16[128,1152]{1,0:T(8,128)(2,1)S(1)}, u32[]{:S(2)}, u32[]{:S(2)}) collective-permute-start(bf16[128,1152]{1,0:T(8,128)(2,1)S(1)} %pad_maximum_fusion.1), channel_id=1, source_target_pairs={{0,16},{8,24},{16,0},{24,8},{1,17},{9,25},{17,1},{25,9},{2,18},{10... | collective-permute-start | bytes 884744 | tf_op jit(solution)/shard_map/ppermute | solution.py:111
  29.7 7.5 %collective-permute-done.2 = bf16[128,1152]{1,0:T(8,128)(2,1)S(1)} collective-permute-done((bf16[128,1152]{1,0:T(8,128)(2,1)S(1)}, bf16[128,1152]{1,0:T(8,128)(2,1)S(1)}, u32[]{:S(2)}, u32[]{:S(2)}) %collective-permute-start.2) | collective-permute-done | bytes 294944 | tf_op jit(solution)/shard_map/ppermute | solution.py:111
  37.7 0.2 copy.30
  37.9 1.4 %collective-permute-done.3 = bf16[2,128,896]{2,1,0:T(8,128)(2,1)S(1)} collective-permute-done((bf16[2,128,896]{2,1,0:T(8,128)(2,1)S(1)}, bf16[2,128,896]{2,1,0:T(8,128)(2,1)S(1)}, u32[]{:S(2)}, u32[]{:S(2)}) %collective-permute-start.3) | collective-permute-done | bytes 458784 | tf_op jit(solution)/shard_map/ppermute | solution.py:111
  39.5 0.2 copy.29
  39.7 0.6 convolution_bitcast_fusion
  40.3 0.4 copy-done.3
  40.7 0.3 multiply_convert_fusion.1
  41.1 0.6 fusion.4
  41.7 0.4 fusion.74
  42.1 0.4 add_convert_fusion
  42.6 0.2 collective-permute-start.4
  42.8 1.7 %collective-permute-done.4 = bf16[2,128,896]{2,1,0:T(8,128)(2,1)S(1)} collective-permute-done((bf16[2,128,896]{2,1,0:T(8,128)(2,1)S(1)}, bf16[2,128,896]{2,1,0:T(8,128)(2,1)S(1)}, u32[]{:S(2)}, u32[]{:S(2)}) %collective-permute-start.4) | collective-permute-done | bytes 458784 | tf_op jit(solution)/shard_map/ppermute | solution.py:111
  44.7 1.6 %collective-permute-start.5 = (bf16[1,128,896]{2,1,0:T(8,128)(2,1)S(1)}, bf16[1,128,896]{2,1,0:T(8,128)(2,1)S(1)}, u32[]{:S(2)}, u32[]{:S(2)}) collective-permute-start(bf16[1,128,896]{2,1,0:T(8,128)(2,1)S(1)} %fusion.43), channel_id=1, source_target_pairs={{0,16},{8,24},{16,0},{24,8},{1,17},{9,25},{17,1},{25,9},{2,18},{10... | collective-permute-start | bytes 688136 | tf_op jit(solution)/shard_map/ppermute | solution.py:111
  46.3 6.1 %collective-permute-done.5 = bf16[1,128,896]{2,1,0:T(8,128)(2,1)S(1)} collective-permute-done((bf16[1,128,896]{2,1,0:T(8,128)(2,1)S(1)}, bf16[1,128,896]{2,1,0:T(8,128)(2,1)S(1)}, u32[]{:S(2)}, u32[]{:S(2)}) %collective-permute-start.5) | collective-permute-done | bytes 229408 | tf_op jit(solution)/shard_map/ppermute | solution.py:111
  52.4 0.7 %fusion.24 = bf16[1,128,896]{2,1,0:T(8,128)(2,1)} fusion(bf16[1,128,896]{2,1,0:T(8,128)(2,1)S(1)} %collective-permute-done.5, f32[1,2,128,896]{3,2,1,0:T(8,128)S(1)} %fusion.7, pred[]{:T(512)S(6)} %ne.18), kind=kLoop, calls=%fused_computation.40 | loop fusion | flops 458752 | bytes 1376257 | tf_op jit(solution)/shard_map/convert_element_type | solution.py:265
  53.2 3.6 %all-to-all-start.1 = ((bf16[8,16,896]{2,1,0:T(8,128)(2,1)}), bf16[8,16,896]{2,1,0:T(8,128)(2,1)S(1)}, u32[]{:S(2)}, u32[]{:S(2)}) async-start(bf16[8,16,896]{2,1,0:T(8,128)(2,1)} %bitcast.41), calls=%async_computation.1 | async-start | bytes 458752 | tf_op jit(solution)/shard_map/all_to_all | solution.py:266
  56.8 1.4 %convolution_convert_fusion = bf16[4,896,128]{2,1,0:T(8,128)(2,1)} fusion(pred[4]{0:T(512)(128)(4,1)S(1)} %get-tuple-element.22, pred[4]{0:T(512)(128)(4,1)S(1)} %get-tuple-element.23, pred[4]{0:T(512)(128)(4,1)S(1)} %iota_compare_fusion.3, bf16[128,896]{0,1:T(8,128)(2,1)S(1)} %copy.31, bf16[128,896]{0,1:T(8,128)(2,1)S(1)} %copy.30, ...), kind=kOutput, calls=%fused_computation.1 | convolution fusion | flops 119275520 | bytes 1867788 | tf_op jit(solution)/shard_map/dot_general | solution.py:258
  58.2 1.4 %convolution_convert_fusion.1 = bf16[4,896,128]{2,1,0:T(8,128)(2,1)} fusion(bf16[128,128,1]{1,0,2:T(8,128)(2,1)S(1)} %fusion.4, pred[4]{0:T(512)(128)(4,1)S(1)} %get-tuple-element.22, pred[4]{0:T(512)(128)(4,1)S(1)} %get-tuple-element.23, pred[4]{0:T(512)(128)(4,1)S(1)} %iota_compare_fusion.3, bf16[128,896]{0,1:T(8,128)(2,1)S(1)} %copy.31, ...), kind=kOutput, calls=%fused_computation.2 | convolution fusion | flops 119275520 | bytes 1867788 | tf_op jit(solution)/shard_map/dot_general | solution.py:255
  59.5 5.3 %all-to-all-done.1 = bf16[8,16,896]{2,1,0:T(8,128)(2,1)S(1)} async-done(((bf16[8,16,896]{2,1,0:T(8,128)(2,1)}), bf16[8,16,896]{2,1,0:T(8,128)(2,1)S(1)}, u32[]{:S(2)}, u32[]{:S(2)}) %all-to-all-start.1) | async-done | bytes 229408 | tf_op jit(solution)/shard_map/all_to_all | solution.py:266
  64.8 1.1 %convolution_convert_fusion.2 = bf16[256,896]{1,0:T(8,128)(2,1)} fusion(bf16[128,256]{1,0:T(8,128)(2,1)S(1)} %copy-done.4, bf16[128,896]{1,0:T(8,128)(2,1)S(1)} %bitcast.125), kind=kOutput, calls=%fused_computation.3 | convolution fusion | flops 58949632 | bytes 753664 | tf_op jit(solution)/shard_map/dot_general | solution.py:267
  (36 shorter events, 1.9 us)
Async XLA Ops:
  0.6 39.0 %copy-start = (bf16[1,3584,128]{2,1,0:T(8,128)(2,1)S(1)}, bf16[1,3584,128]{2,1,0:T(8,128)(2,1)}, u32[]{:S(2)}) copy-start(bf16[1,3584,128]{2,1,0:T(8,128)(2,1)} %param.13) | copy-start | bytes 2752516
  0.6 10.3 %copy-start.2 = (bf16[1,128,3584]{2,1,0:T(8,128)(2,1)S(1)}, bf16[1,128,3584]{2,1,0:T(8,128)(2,1)}, u32[]{:S(2)}) copy-start(bf16[1,128,3584]{2,1,0:T(8,128)(2,1)} %param.15) | copy-start | bytes 2752516
  3.7 21.1 %all-to-all-start = ((bf16[8,16,1920]{2,1,0:T(8,128)(2,1)}), bf16[8,16,1920]{2,1,0:T(8,128)(2,1)S(1)}, u32[]{:S(2)}, u32[]{:S(2)}) async-start(bf16[8,16,1920]{2,1,0:T(8,128)(2,1)} %bitcast.126), calls=%async_computation | async-start | bytes 983040 | tf_op jit(solution)/shard_map/all_to_all | solution.py:198
  12.4 13.4 %collective-permute-start.1 = (bf16[1792,128]{1,0:T(8,128)(2,1)S(1)}, bf16[1792,128]{1,0:T(8,128)(2,1)S(1)}, u32[]{:S(2)}, u32[]{:S(2)}) collective-permute-start(bf16[1792,128]{1,0:T(8,128)(2,1)S(1)} %get-tuple-element.10), channel_id=1, source_target_pairs={{0,16},{8,24},{16,0},{24,8},{1,17},{9,25},{17,1},{25,9},{2,18},{10... | collective-permute-start | bytes 1376264 | tf_op jit(solution)/shard_map/ppermute | solution.py:111
  25.6 1.6 %collective-permute-start = (bf16[1,128,896]{2,1,0:T(8,128)(2,1)S(1)}, bf16[1,128,896]{2,1,0:T(8,128)(2,1)S(1)}, u32[]{:S(2)}, u32[]{:S(2)}) collective-permute-start(bf16[1,128,896]{2,1,0:T(8,128)(2,1)S(1)} %fusion.85), channel_id=1, source_target_pairs={{0,8},{8,0},{16,24},{24,16},{1,9},{9,1},{17,25},{25,17},{2,10},{10... | collective-permute-start | bytes 688136 | tf_op jit(solution)/shard_map/ppermute | solution.py:111
  27.2 0.7 %copy-start.5 = (bf16[1,128,896]{2,1,0:T(8,128)(2,1)}, bf16[1,128,896]{2,1,0:T(8,128)(2,1)S(1)}, u32[]{:S(2)}) copy-start(bf16[1,128,896]{2,1,0:T(8,128)(2,1)S(1)} %collective-permute-done) | copy-start | bytes 688132
  28.2 9.1 %collective-permute-start.2 = (bf16[128,1152]{1,0:T(8,128)(2,1)S(1)}, bf16[128,1152]{1,0:T(8,128)(2,1)S(1)}, u32[]{:S(2)}, u32[]{:S(2)}) collective-permute-start(bf16[128,1152]{1,0:T(8,128)(2,1)S(1)} %pad_maximum_fusion.1), channel_id=1, source_target_pairs={{0,16},{8,24},{16,0},{24,8},{1,17},{9,25},{17,1},{25,9},{2,18},{10... | collective-permute-start | bytes 884744 | tf_op jit(solution)/shard_map/ppermute | solution.py:111
  37.4 1.9 %collective-permute-start.3 = (bf16[2,128,896]{2,1,0:T(8,128)(2,1)S(1)}, bf16[2,128,896]{2,1,0:T(8,128)(2,1)S(1)}, u32[]{:S(2)}, u32[]{:S(2)}) collective-permute-start(bf16[2,128,896]{2,1,0:T(8,128)(2,1)S(1)} %pad_maximum_fusion), channel_id=1, source_target_pairs={{0,8},{8,0},{16,24},{24,16},{1,9},{9,1},{17,25},{25,17},{2,10},{10... | collective-permute-start | bytes 1376264 | tf_op jit(solution)/shard_map/ppermute | solution.py:111
  39.7 1.0 %copy-start.3 = (bf16[128,1792]{0,1:T(8,128)(2,1)S(1)}, bf16[128,1792]{0,1:T(8,128)(2,1)}, u32[]{:S(2)}) copy-start(bf16[128,1792]{0,1:T(8,128)(2,1)} %get-tuple-element.11) | copy-start | bytes 1376260
  39.7 1.1 %copy-start.6 = (bf16[1,128,896]{2,1,0:T(8,128)(2,1)S(1)}, bf16[1,128,896]{2,1,0:T(8,128)(2,1)}, u32[]{:S(2)}) copy-start(bf16[1,128,896]{2,1,0:T(8,128)(2,1)} %copy-done.5) | copy-start | bytes 688132
  39.7 1.4 %copy-start.1 = (bf16[1,3584,128]{2,1,0:T(8,128)(2,1)S(1)}, bf16[1,3584,128]{2,1,0:T(8,128)(2,1)}, u32[]{:S(2)}) copy-start(bf16[1,3584,128]{2,1,0:T(8,128)(2,1)} %param.14) | copy-start | bytes 2752516
  42.6 1.9 %collective-permute-start.4 = (bf16[2,128,896]{2,1,0:T(8,128)(2,1)S(1)}, bf16[2,128,896]{2,1,0:T(8,128)(2,1)S(1)}, u32[]{:S(2)}, u32[]{:S(2)}) collective-permute-start(bf16[2,128,896]{2,1,0:T(8,128)(2,1)S(1)} %fusion.22), channel_id=1, source_target_pairs={{0,8},{8,0},{16,24},{24,16},{1,9},{9,1},{17,25},{25,17},{2,10},{10... | collective-permute-start | bytes 1376264 | tf_op jit(solution)/shard_map/ppermute | solution.py:111
  44.7 7.7 %collective-permute-start.5 = (bf16[1,128,896]{2,1,0:T(8,128)(2,1)S(1)}, bf16[1,128,896]{2,1,0:T(8,128)(2,1)S(1)}, u32[]{:S(2)}, u32[]{:S(2)}) collective-permute-start(bf16[1,128,896]{2,1,0:T(8,128)(2,1)S(1)} %fusion.43), channel_id=1, source_target_pairs={{0,16},{8,24},{16,0},{24,8},{1,17},{9,25},{17,1},{25,9},{2,18},{10... | collective-permute-start | bytes 688136 | tf_op jit(solution)/shard_map/ppermute | solution.py:111
  53.2 11.6 %all-to-all-start.1 = ((bf16[8,16,896]{2,1,0:T(8,128)(2,1)}), bf16[8,16,896]{2,1,0:T(8,128)(2,1)S(1)}, u32[]{:S(2)}, u32[]{:S(2)}) async-start(bf16[8,16,896]{2,1,0:T(8,128)(2,1)} %bitcast.41), calls=%async_computation.1 | async-start | bytes 458752 | tf_op jit(solution)/shard_map/all_to_all | solution.py:266
  58.2 6.6 %copy-start.4 = (bf16[128,256]{1,0:T(8,128)(2,1)S(1)}, bf16[128,256]{1,0:T(8,128)(2,1)}, u32[]{:S(2)}) copy-start(bf16[128,256]{1,0:T(8,128)(2,1)} %get-tuple-element.6) | copy-start | bytes 196612
